TPU v7x, 32 devices: a whole 2x2x4 slice. The times are simulated.
32 devices in a mesh: dp: 8 (over z, x), own: 4 (over y, core).
Axes of the slice: x: 2, y: 2, z: 4, core: 2. Of those that a mesh axis runs over, the one named last changes fastest.
Arguments:
- grads_fc: bfloat16 [8, 4, 8, 200, 1600], P('dp', 'own'), may hold values from -180 to 180
- grads_ln: bfloat16 [8, 4, 1600], P('dp'), may hold values from -48 to 48
- grads_emb: bfloat16 [8, 4, 8, 4, 1600], P('dp', 'own'), may hold values from -48 to 48
- weights_fc: bfloat16 [4, 8, 200, 1600], P('own'), may hold values from -0.15625 to 0.15625
- basis: float32 [1600, 256], replicated, may hold values from -0.15625 to 0.15625
- fc_m: float32 [4, 8, 200, 256], P('own', 'dp'), may hold values from -0.6 to 0.6
- fc_v: float32 [4, 8, 200, 256], P('own', 'dp'), may hold values from 0.001 to 0.1
- ln_params: float32 [4, 1600], replicated, may hold values from -3 to 3
- ln_m: float32 [4, 1600], replicated, may hold values from -0.6 to 0.6
- ln_v: float32 [4, 1600], replicated, may hold values from 0.001 to 0.1
- emb_weights: bfloat16 [4, 8, 4, 1600], P('own'), may hold values from -0.29882812 to 0.29882812
- emb_m: float32 [4, 8, 4, 1600], P('own', 'dp'), may hold values from -0.6 to 0.6
- emb_v: float32 [4, 8, 4, 1600], P('own', 'dp'), may hold values from 0.001 to 0.1
- step_count: int32 [1], replicated, may hold values from 1 to 63
Outputs:
- fc_m_next: float32 [4, 8, 200, 256], P('own', 'dp')
- fc_v_next: float32 [4, 8, 200, 256], P('own', 'dp')
- fc_direction: float32 [4, 8, 200, 256], P('own', 'dp')
- weights_next: bfloat16 [4, 8, 200, 1600], P('own')
- basis_next: float32 [1600, 256], replicated
- ln_next: float32 [4, 1600], replicated
- ln_m_next: float32 [4, 1600], replicated
- ln_v_next: float32 [4, 1600], replicated
- emb_next: bfloat16 [4, 8, 4, 1600], P('own')
- emb_m_next: float32 [4, 8, 4, 1600], P('own', 'dp')
- emb_v_next: float32 [4, 8, 4, 1600], P('own', 'dp')
All inputs are finite; a program needn't handle non-finite values.
Results may differ from a plain program's by a relative error of at most 0.009.
Values may be sent and summed in bfloat16 or wider, within the bound.
No kernel may reach another device: no remote copies, remote signals or barrier semaphores. Data moves between devices by JAX's collectives and lax.ppermute only.
A program may use at most 128 MiB of HBM per device.

v0:
```python
import math

import jax
import jax.numpy as jnp
from jax import lax
from jax.sharding import PartitionSpec as P

FF = 6400
RANK = 256
NS_STEPS = 5


beta_one = 0.9
beta_two = 0.999
adam_eps = 1e-08
learn_rate = 0.02
galore_scale = 0.25


def adam_update(moment_one, moment_two, gradient, correct_one, correct_two):
    moment_one_new = beta_one * moment_one + (1.0 - beta_one) * gradient
    moment_two_new = beta_two * moment_two + (1.0 - beta_two) * gradient * gradient
    direction = moment_one_new / correct_one / (jnp.sqrt(moment_two_new / correct_two) + adam_eps)
    return (moment_one_new, moment_two_new, direction)


def orthogonalize(subspace):
    highest = lax.Precision.HIGH
    iterate = subspace * lax.rsqrt(jnp.sum(subspace * subspace) + 1e-06)
    for sweep_index in range(NS_STEPS):
        gram_matrix = jnp.dot(iterate.T, iterate, precision=highest)
        iterate = 1.5 * iterate - 0.5 * jnp.dot(iterate, gram_matrix, precision=highest)
    return iterate


def row_count_of(piece, cols):
    return -(-piece.size // cols)


def pack_rows(pieces, cols):
    rows = []
    for piece in pieces:
        if piece.ndim == 2 and piece.shape[1] == cols:
            rows.append(piece)
            continue
        flat = piece.reshape(-1)
        flat = jnp.pad(flat, (0, row_count_of(piece, cols) * cols - flat.size))
        rows.append(flat.reshape(-1, cols))
    return jnp.concatenate(rows, axis=0)


def unpack_rows(packed, pieces):
    cols = packed.shape[1]
    out = []
    start = 0
    for piece in pieces:
        count = row_count_of(piece, cols)
        block = packed[start : start + count]
        start += count
        out.append(block.reshape(-1)[: piece.size].reshape(piece.shape))
    return out


def axis_steps(axes):
    steps = []
    for name in axes:
        size = lax.axis_size(name)
        if size & (size - 1):
            return None
        bit = 1
        while bit < size:
            steps.append((name, bit, size))
            bit *= 2
    return steps


def swap_with(values, name, bit, size):
    return lax.ppermute(values, name, [(index, index ^ bit) for index in range(size)])


def run_steps(parts, steps):
    sides = []
    for name, bit, size in steps:
        side = (lax.axis_index(name) // bit) % 2
        half = parts.shape[0] // 2
        keep = lax.dynamic_slice_in_dim(parts, side * half, half, 0)
        send = lax.dynamic_slice_in_dim(parts, (1 - side) * half, half, 0)
        parts = keep + swap_with(send, name, bit, size)
        sides.append(side)
    for (name, bit, size), side in zip(reversed(steps), reversed(sides)):
        other = swap_with(parts, name, bit, size)
        first = jnp.where(side == 0, parts, other)
        second = jnp.where(side == 0, other, parts)
        parts = jnp.concatenate([first, second], axis=0)
    return parts


def butterfly_sum(packed, axes):
    steps = axis_steps(axes)
    if steps is None:
        return lax.psum(packed, axes)
    count = 2 ** len(steps)
    rows, cols = packed.shape
    padded = -(-rows // (8 * count)) * 8 * count
    parts = jnp.pad(packed, ((0, padded - rows), (0, 0)))
    low = 1 if len(axes) > 1 else 0
    high = len(steps) - 1
    if cols % 256 or high - low < 2:
        return run_steps(parts, steps)[:rows]
    middle = steps[low:high]
    other = steps[:low] + middle[1:] + middle[:1] + steps[high:]
    half = cols // 2
    left = run_steps(parts[:, :half], steps)
    right = run_steps(parts[:, half:], other)
    return jnp.concatenate([left, right], axis=1)[:rows]


def small_sum(values, axes):
    steps = axis_steps(axes)
    if steps is None:
        return lax.psum(values, axes)
    for name, bit, size in steps:
        values = values + swap_with(values, name, bit, size)
    return values


def butterfly_gather(piece, name):
    size = lax.axis_size(name)
    if size & (size - 1):
        return lax.all_gather(piece, name, axis=0, tiled=False)
    parts = piece[None]
    bit = size // 2
    levels = 0
    while bit >= 1:
        side = (lax.axis_index(name) // bit) % 2
        other = swap_with(parts, name, bit, size)
        first = jnp.where(side == 0, parts, other)
        second = jnp.where(side == 0, other, parts)
        parts = jnp.concatenate([first, second], axis=0)
        bit //= 2
        levels += 1
    parts = parts.reshape((2,) * levels + piece.shape)
    order = tuple(reversed(range(levels))) + tuple(range(levels, levels + piece.ndim))
    return parts.transpose(order).reshape((size,) + piece.shape)


def split3(values):
    first = values.astype(jnp.bfloat16)
    rest = values - first.astype(jnp.float32)
    second = rest.astype(jnp.bfloat16)
    third = (rest - second.astype(jnp.float32)).astype(jnp.bfloat16)
    return jnp.concatenate([first, second, third], axis=1)


def exact_dot(lhs_bf16, rhs_f32, contract):
    cols = rhs_f32.shape[1]
    wide = lax.dot_general(
        lhs_bf16,
        split3(rhs_f32),
        ((contract, (0,)), ((), ())),
        preferred_element_type=jnp.float32,
    )
    return wide[:, :cols] + wide[:, cols : 2 * cols] + wide[:, 2 * cols :]


def shards(
    grads_fc,
    grads_ln,
    grads_emb,
    weights_fc,
    basis,
    fc_m,
    fc_v,
    ln_params,
    ln_m,
    ln_v,
    emb_weights,
    emb_m,
    emb_v,
    step_count,
):
    highest = lax.Precision.HIGHEST
    replicas = lax.axis_size("dp")
    owners = lax.axis_size("own")
    replica = lax.axis_index("dp")
    blocks = grads_fc.shape[2]
    row_count = grads_fc.shape[3]
    width = grads_fc.shape[4]
    rank_cols = basis.shape[1]
    emb_count = grads_emb.shape[3]
    local_rows = grads_fc.reshape(blocks * row_count, width)
    local_proj = exact_dot(local_rows, basis, (1,))
    emb_local = grads_emb.reshape(blocks, emb_count, width).astype(jnp.float32)
    ln_local = grads_ln.reshape(4, width).astype(jnp.float32)
    proj_own, emb_own, ln_sum = unpack_rows(
        butterfly_sum(pack_rows((local_proj, emb_local, ln_local), rank_cols), ("dp",)),
        (local_proj, emb_local, ln_local),
    )
    partial_value = exact_dot(local_rows, proj_own, (0,))
    own_square = jnp.sum(proj_own * proj_own) + jnp.sum(emb_own * emb_own)
    square_total = small_sum(jnp.full((8, 128), own_square), ("own",))[0, 0]
    grad_norm = jnp.sqrt(square_total + jnp.sum(ln_sum * ln_sum) + 1e-06)
    clip_limit = math.sqrt(FF * RANK + emb_count * replicas * owners * width + 4 * width)
    factor = jnp.minimum(1.0, clip_limit / grad_norm)
    count = step_count[0].astype(jnp.float32)
    correct_one = 1.0 - jnp.power(jnp.float32(beta_one), count)
    correct_two = 1.0 - jnp.power(jnp.float32(beta_two), count)
    proj_rows = lax.dynamic_slice_in_dim(proj_own, replica * row_count, row_count, 0)
    fc_grad = factor * proj_rows.reshape(1, 1, row_count, rank_cols)
    fc_m_next, fc_v_next, fc_direction = adam_update(fc_m, fc_v, fc_grad, correct_one, correct_two)
    ln_m_next, ln_v_next, ln_direction = adam_update(
        ln_m, ln_v, factor * ln_sum, correct_one, correct_two
    )
    ln_next = ln_params - learn_rate * ln_direction
    emb_rows = lax.dynamic_index_in_dim(emb_own, replica, 0, keepdims=True).reshape(
        1, 1, emb_count, width
    )
    emb_m_next, emb_v_next, emb_direction = adam_update(
        emb_m, emb_v, factor * emb_rows, correct_one, correct_two
    )
    fc_dir_mine = fc_direction.reshape(row_count, rank_cols).astype(jnp.bfloat16)
    emb_dir_f32 = emb_direction.reshape(emb_count, width)
    emb_dir_high = emb_dir_f32.astype(jnp.bfloat16)
    emb_dir_low = (emb_dir_f32 - emb_dir_high.astype(jnp.float32)).astype(jnp.bfloat16)
    emb_dir_mine = jnp.stack([emb_dir_high, emb_dir_low])
    gathered = butterfly_gather(pack_rows((fc_dir_mine, emb_dir_mine), rank_cols), "dp")
    fc_dir_all, emb_dir_all = jax.vmap(
        lambda packed: unpack_rows(packed, (fc_dir_mine, emb_dir_mine))
    )(gathered)
    fc_dir_all = fc_dir_all.reshape(replicas * row_count, rank_cols)
    emb_dir_all = emb_dir_all[:, 0].astype(jnp.float32) + emb_dir_all[:, 1].astype(jnp.float32)
    pieces = split3(basis)
    stacked = jnp.concatenate(
        [pieces[:, :rank_cols], pieces[:, rank_cols : 2 * rank_cols], pieces[:, 2 * rank_cols :]], axis=1
    )
    update_rows = lax.dot_general(
        jnp.concatenate([fc_dir_all] * 3, axis=1),
        stacked,
        (((1,), (1,)), ((), ())),
        preferred_element_type=jnp.float32,
    )
    weights_next = (
        weights_fc.astype(jnp.float32)
        - learn_rate * galore_scale * update_rows.reshape(weights_fc.shape)
    ).astype(jnp.bfloat16)
    emb_next = (
        emb_weights.astype(jnp.float32) - learn_rate * emb_dir_all.reshape(emb_weights.shape)
    ).astype(jnp.bfloat16)
    subspace = butterfly_sum(partial_value, ("own", "dp"))
    basis_next = orthogonalize(subspace)
    return (
        fc_m_next,
        fc_v_next,
        fc_direction,
        weights_next,
        basis_next,
        ln_next,
        ln_m_next,
        ln_v_next,
        emb_next,
        emb_m_next,
        emb_v_next,
    )


def solution(mesh):
    in_specs = (
        P("dp", "own", None, None, None),
        P("dp", None, None),
        P("dp", "own", None, None, None),
        P("own", None, None, None),
        P(),
        P("own", "dp", None, None),
        P("own", "dp", None, None),
        P(),
        P(),
        P(),
        P("own", None, None, None),
        P("own", "dp", None, None),
        P("own", "dp", None, None),
        P(),
    )
    out_specs = (
        P("own", "dp", None, None),
        P("own", "dp", None, None),
        P("own", "dp", None, None),
        P("own", None, None, None),
        P(),
        P(),
        P(),
        P(),
        P("own", None, None, None),
        P("own", "dp", None, None),
        P("own", "dp", None, None),
    )
    return jax.shard_map(shards, mesh=mesh, in_specs=in_specs, out_specs=out_specs, check_vma=False)
```

profile of v0, /device:TPU:0, one launch (start us, length us, event | category | flops | bytes accessed | tf_op | source)
XLA Modules:
  0.0 206.3 jit_solution(963042684573770192)
XLA Ops:
  1.5 1.1 reshape.192
  2.5 2.3 %fusion.42 = (bf16[1600,256]{1,0:T(8,128)(2,1)S(1)}, bf16[1600,256]{1,0:T(8,128)(2,1)S(1)}, bf16[1600,256]{1,0:T(8,128)(2,1)S(1)}) fusion(f32[1600,256]{1,0:T(8,128)} %param.18), kind=kLoop, calls=%fused_computation.174 | loop fusion | flops 2867200 | bytes 4096000 | tf_op jit(solution)/shard_map/convert_element_type | solution.py:148
  6.1 6.7 %convolution_bitcast_fusion = f32[1600,768]{1,0:T(8,128)S(1)} fusion(bf16[1600,1600]{1,0:T(8,128)(2,1)} %bitcast.71, bf16[1600,256]{1,0:T(8,128)(2,1)S(1)} %get-tuple-element.36, bf16[1600,256]{1,0:T(8,128)(2,1)S(1)} %get-tuple-element.37, bf16[1600,256]{1,0:T(8,128)(2,1)S(1)} %get-tuple-element.35), kind=kOutput, calls=%fused_computation.2 | convolution fusion | flops 3939532800 | bytes 12492800 | tf_op jit(solution)/shard_map/dot_general | solution.py:157
  13.4 3.1 %collective-permute-start.6 = (f32[928,128]{1,0:T(8,128)S(1)}, f32[928,128]{1,0:T(8,128)S(1)}, u32[]{:S(2)}, u32[]{:S(2)}) collective-permute-start(f32[928,128]{1,0:T(8,128)S(1)} %constant_dynamic-slice_fusion.12), channel_id=1, source_target_pairs={{0,8},{4,12},{8,0},{12,4},{16,24},{20,28},{24,16},{28,20},{1,9},{5... | collective-permute-start | bytes 1425416 | tf_op jit(solution)/shard_map/ppermute | solution.py:78
  16.6 1.6 collective-permute-start
  18.1 9.3 %collective-permute-done.6 = f32[928,128]{1,0:T(8,128)S(1)} collective-permute-done((f32[928,128]{1,0:T(8,128)S(1)}, f32[928,128]{1,0:T(8,128)S(1)}, u32[]{:S(2)}, u32[]{:S(2)}) %collective-permute-start.6) | collective-permute-done | bytes 475168 | tf_op jit(solution)/shard_map/ppermute | solution.py:78
  27.5 1.7 collective-permute-start.7
  29.2 1.1 dynamic-slice_add_fusion.1
  30.3 1.6 collective-permute-start.1
  32.0 2.7 %collective-permute-done.7 = f32[464,128]{1,0:T(8,128)S(1)} collective-permute-done((f32[464,128]{1,0:T(8,128)S(1)}, f32[464,128]{1,0:T(8,128)S(1)}, u32[]{:S(2)}, u32[]{:S(2)}) %collective-permute-start.7) | collective-permute-done | bytes 237600 | tf_op jit(solution)/shard_map/ppermute | solution.py:78
  34.7 2.5 %collective-permute-start.8 = (f32[232,128]{1,0:T(8,128)S(1)}, f32[232,128]{1,0:T(8,128)S(1)}, u32[]{:S(2)}, u32[]{:S(2)}) collective-permute-start(f32[232,128]{1,0:T(8,128)S(1)} %constant_dynamic-slice_fusion.10), channel_id=1, source_target_pairs={{0,16},{4,20},{8,24},{12,28},{16,0},{20,4},{24,8},{28,12},{1,17},{... | collective-permute-start | bytes 356360 | tf_op jit(solution)/shard_map/ppermute | solution.py:78
  37.7 3.5 %collective-permute-start.2 = (f32[232,128]{1,0:T(8,128)S(1)}, f32[232,128]{1,0:T(8,128)S(1)}, u32[]{:S(2)}, u32[]{:S(2)}) collective-permute-start(f32[232,128]{1,0:T(8,128)S(1)} %constant_dynamic-slice_fusion.13), channel_id=1, source_target_pairs={{0,16},{4,20},{8,24},{12,28},{16,0},{20,4},{24,8},{28,12},{1,17},{... | collective-permute-start | bytes 356360 | tf_op jit(solution)/shard_map/ppermute | solution.py:78
  41.2 4.7 %collective-permute-done.8 = f32[232,128]{1,0:T(8,128)S(1)} collective-permute-done((f32[232,128]{1,0:T(8,128)S(1)}, f32[232,128]{1,0:T(8,128)S(1)}, u32[]{:S(2)}, u32[]{:S(2)}) %collective-permute-start.8) | collective-permute-done | bytes 118816 | tf_op jit(solution)/shard_map/ppermute | solution.py:78
  46.0 2.2 %collective-permute-done.2 = f32[232,128]{1,0:T(8,128)S(1)} collective-permute-done((f32[232,128]{1,0:T(8,128)S(1)}, f32[232,128]{1,0:T(8,128)S(1)}, u32[]{:S(2)}, u32[]{:S(2)}) %collective-permute-start.2) | collective-permute-done | bytes 118816 | tf_op jit(solution)/shard_map/ppermute | solution.py:78
  49.0 5.1 %collective-permute-done.9 = f32[232,128]{1,0:T(8,128)S(1)} collective-permute-done((f32[232,128]{1,0:T(8,128)S(1)}, f32[232,128]{1,0:T(8,128)S(1)}, u32[]{:S(2)}, u32[]{:S(2)}) %collective-permute-start.9) | collective-permute-done | bytes 118816 | tf_op jit(solution)/shard_map/ppermute | solution.py:78
  54.1 1.7 collective-permute-start.10
  56.7 2.8 %collective-permute-start.4 = (f32[464,128]{1,0:T(8,128)S(1)}, f32[464,128]{1,0:T(8,128)S(1)}, u32[]{:S(2)}, u32[]{:S(2)}) collective-permute-start(f32[464,128]{1,0:T(8,128)S(1)} %pad_maximum_fusion.12), channel_id=1, source_target_pairs={{0,8},{4,12},{8,0},{12,4},{16,24},{20,28},{24,16},{28,20},{1,9},{5... | collective-permute-start | bytes 712712 | tf_op jit(solution)/shard_map/ppermute | solution.py:78
  60.4 2.5 %collective-permute-start.11 = (f32[928,128]{1,0:T(8,128)S(1)}, f32[928,128]{1,0:T(8,128)S(1)}, u32[]{:S(2)}, u32[]{:S(2)}) collective-permute-start(f32[928,128]{1,0:T(8,128)S(1)} %pad_maximum_fusion.8), channel_id=1, source_target_pairs={{0,8},{4,12},{8,0},{12,4},{16,24},{20,28},{24,16},{28,20},{1,9},{5... | collective-permute-start | bytes 1425416 | tf_op jit(solution)/shard_map/ppermute | solution.py:78
  62.9 3.1 %collective-permute-done.4 = f32[464,128]{1,0:T(8,128)S(1)} collective-permute-done((f32[464,128]{1,0:T(8,128)S(1)}, f32[464,128]{1,0:T(8,128)S(1)}, u32[]{:S(2)}, u32[]{:S(2)}) %collective-permute-start.4) | collective-permute-done | bytes 237600 | tf_op jit(solution)/shard_map/ppermute | solution.py:78
  66.9 2.3 %collective-permute-start.5 = (f32[928,128]{1,0:T(8,128)}, f32[928,128]{1,0:T(8,128)S(1)}, u32[]{:S(2)}, u32[]{:S(2)}) collective-permute-start(f32[928,128]{1,0:T(8,128)} %pad_maximum_fusion.7), channel_id=1, source_target_pairs={{0,4},{4,0},{8,12},{12,8},{16,20},{20,16},{24,28},{28,24},{1,5},{5... | collective-permute-start | bytes 1425416 | tf_op jit(solution)/shard_map/ppermute | solution.py:78
  69.9 3.3 %collective-permute-done.11 = f32[928,128]{1,0:T(8,128)S(1)} collective-permute-done((f32[928,128]{1,0:T(8,128)S(1)}, f32[928,128]{1,0:T(8,128)S(1)}, u32[]{:S(2)}, u32[]{:S(2)}) %collective-permute-start.11) | collective-permute-done | bytes 475168 | tf_op jit(solution)/shard_map/ppermute | solution.py:78
  73.3 2.7 %collective-permute-done.5 = f32[928,128]{1,0:T(8,128)S(1)} collective-permute-done((f32[928,128]{1,0:T(8,128)}, f32[928,128]{1,0:T(8,128)S(1)}, u32[]{:S(2)}, u32[]{:S(2)}) %collective-permute-start.5) | collective-permute-done | bytes 475168 | tf_op jit(solution)/shard_map/ppermute | solution.py:78
  76.8 1.0 slice.111
  77.8 2.4 %fusion.20 = (bf16[1600,256]{1,0:T(8,128)(2,1)S(1)}, f32[]{:T(128)}, bf16[1600,256]{1,0:T(8,128)(2,1)}, f32[1600,256]{1,0:T(8,128)}) fusion(f32[1856,256]{1,0:T(8,128)S(1)} %maximum_maximum_fusion), kind=kLoop, calls=%fused_computation.48 | loop fusion | flops 3686399 | bytes 4915204 | tf_op jit(solution)/shard_map/convert_element_type | solution.py:150
  81.6 8.2 %convolution_bitcast_fusion.1 = f32[1600,768]{1,0:T(8,128)S(1)} fusion(bf16[1600,1600]{1,0:T(8,128)(2,1)} %bitcast.72, bf16[1600,256]{1,0:T(8,128)(2,1)} %get-tuple-element.29, bf16[1600,256]{1,0:T(8,128)(2,1)S(1)} %get-tuple-element.27, bf16[1600,256]{1,0:T(8,128)(2,1)} %slice.111), kind=kOutput, calls=%fused_computation.3 | convolution fusion | flops 3939532800 | bytes 12492800 | tf_op jit(solution)/shard_map/dot_general | solution.py:157
  90.3 0.9 constant_dynamic-slice_fusion.4
  91.2 1.6 collective-permute-start.13
  96.7 1.4 multiply_divide_fusion.2
  98.3 2.0 convert_bitcast_fusion
  100.3 2.8 %collective-permute-start.14 = (bf16[1,250,256]{2,1,0:T(8,128)(2,1)S(1)}, bf16[1,250,256]{2,1,0:T(8,128)(2,1)S(1)}, u32[]{:S(2)}, u32[]{:S(2)}) collective-permute-start(bf16[1,250,256]{2,1,0:T(8,128)(2,1)S(1)} %maximum_bitcast_fusion), channel_id=1, source_target_pairs={{0,16},{4,20},{8,24},{12,28},{16,0},{20,4},{24,8},{28,12},{1,17},{... | collective-permute-start | bytes 384008 | tf_op jit(solution)/shard_map/ppermute | solution.py:78
  103.2 5.9 %collective-permute-done.14 = bf16[1,250,256]{2,1,0:T(8,128)(2,1)S(1)} collective-permute-done((bf16[1,250,256]{2,1,0:T(8,128)(2,1)S(1)}, bf16[1,250,256]{2,1,0:T(8,128)(2,1)S(1)}, u32[]{:S(2)}, u32[]{:S(2)}) %collective-permute-start.14) | collective-permute-done | bytes 128032 | tf_op jit(solution)/shard_map/ppermute | solution.py:78
  110.7 5.8 %collective-permute-done.15 = bf16[2,250,256]{2,1,0:T(8,128)(2,1)S(1)} collective-permute-done((bf16[2,250,256]{2,1,0:T(8,128)(2,1)S(1)}, bf16[2,250,256]{2,1,0:T(8,128)(2,1)S(1)}, u32[]{:S(2)}, u32[]{:S(2)}) %collective-permute-start.15) | collective-permute-done | bytes 256032 | tf_op jit(solution)/shard_map/ppermute | solution.py:78
  116.6 2.5 %collective-permute-start.16 = (bf16[4,250,256]{2,1,0:T(8,128)(2,1)S(1)}, bf16[4,250,256]{2,1,0:T(8,128)(2,1)S(1)}, u32[]{:S(2)}, u32[]{:S(2)}) collective-permute-start(bf16[4,250,256]{2,1,0:T(8,128)(2,1)S(1)} %pad_maximum_fusion.6), channel_id=1, source_target_pairs={{0,4},{4,0},{8,12},{12,8},{16,20},{20,16},{24,28},{28,24},{1,5},{5... | collective-permute-start | bytes 1536008 | tf_op jit(solution)/shard_map/ppermute | solution.py:78
  119.5 1.4 collective-permute-start.18
  120.9 14.5 %collective-permute-done.28 = f32[448,128]{1,0:T(8,128)S(1)} collective-permute-done((f32[448,128]{1,0:T(8,128)S(1)}, f32[448,128]{1,0:T(8,128)S(1)}, u32[]{:S(2)}, u32[]{:S(2)}) %collective-permute-start.28) | collective-permute-done | bytes 229408 | tf_op jit(solution)/shard_map/ppermute | solution.py:78
  135.4 1.1 collective-permute-start.29
  136.5 1.4 collective-permute-start.19
  138.0 2.3 %collective-permute-done.29 = f32[224,128]{1,0:T(8,128)S(1)} collective-permute-done((f32[224,128]{1,0:T(8,128)S(1)}, f32[224,128]{1,0:T(8,128)S(1)}, u32[]{:S(2)}, u32[]{:S(2)}) %collective-permute-start.29) | collective-permute-done | bytes 114720 | tf_op jit(solution)/shard_map/ppermute | solution.py:78
  140.3 1.4 collective-permute-start.30
  142.5 2.0 collective-permute-done.30
  144.6 3.0 %collective-permute-start.31 = (f32[56,128]{1,0:T(8,128)S(1)}, f32[56,128]{1,0:T(8,128)S(1)}, u32[]{:S(2)}, u32[]{:S(2)}) collective-permute-start(f32[56,128]{1,0:T(8,128)S(1)} %constant_dynamic-slice_fusion), channel_id=1, source_target_pairs={{0,16},{4,20},{8,24},{12,28},{16,0},{20,4},{24,8},{28,12},{1,17},{... | collective-permute-start | bytes 86024 | tf_op jit(solution)/shard_map/ppermute | solution.py:78
  147.7 1.8 collective-permute-start.21
  149.8 3.0 %collective-permute-start.32 = (f32[56,128]{1,0:T(8,128)S(1)}, f32[56,128]{1,0:T(8,128)S(1)}, u32[]{:S(2)}, u32[]{:S(2)}) collective-permute-start(f32[56,128]{1,0:T(8,128)S(1)} %dynamic-slice_add_fusion.14), channel_id=1, source_target_pairs={{0,16},{4,20},{8,24},{12,28},{16,0},{20,4},{24,8},{28,12},{1,17},{... | collective-permute-start | bytes 86024 | tf_op jit(solution)/shard_map/ppermute | solution.py:78
  152.8 1.5 collective-permute-start.22
  154.6 1.0 copy-done.3
  156.1 7.3 %convolution_multiply_fusion = f32[1600,1600]{1,0:T(8,128)} fusion(bf16[1600,256]{1,0:T(8,128)(2,1)S(1)} %bitcast.70, bf16[1600,256]{1,0:T(8,128)(2,1)S(1)} %copy-done.5, bf16[1600,256]{1,0:T(8,128)(2,1)S(1)} %copy-done.7, bf16[1600,256]{1,0:T(8,128)(2,1)S(1)} %copy-done.3), kind=kOutput, calls=%fused_computation.1 | convolution fusion | flops 3949465600 | bytes 13516800 | tf_op jit(solution)/shard_map/dot_general | solution.py:236
  163.3 9.0 %subtract_convert_fusion = bf16[1,8,200,1600]{3,2,1,0:T(8,128)(2,1)} fusion(f32[1,8,200,1600]{3,2,1,0:T(8,128)} %bitcast.66, bf16[1,8,200,1600]{3,2,1,0:T(8,128)(2,1)} %param.17), kind=kLoop, calls=%fused_computation | loop fusion | flops 7680000 | bytes 20480000 | tf_op jit(solution)/shard_map/convert_element_type | solution.py:245
  172.6 1.1 collective-permute-start.33
  173.8 1.0 collective-permute-start.23
  174.7 2.1 %collective-permute-done.33 = f32[112,128]{1,0:T(8,128)S(1)} collective-permute-done((f32[112,128]{1,0:T(8,128)S(1)}, f32[112,128]{1,0:T(8,128)S(1)}, u32[]{:S(2)}, u32[]{:S(2)}) %collective-permute-start.33) | collective-permute-done | bytes 57376 | tf_op jit(solution)/shard_map/ppermute | solution.py:78
  176.9 1.1 collective-permute-start.34
  178.8 3.0 %collective-permute-done.34 = f32[224,128]{1,0:T(8,128)S(1)} collective-permute-done((f32[224,128]{1,0:T(8,128)S(1)}, f32[224,128]{1,0:T(8,128)S(1)}, u32[]{:S(2)}, u32[]{:S(2)}) %collective-permute-start.34) | collective-permute-done | bytes 114720 | tf_op jit(solution)/shard_map/ppermute | solution.py:78
  183.0 1.1 collective-permute-start.25
  184.0 3.9 %collective-permute-done.35 = f32[448,128]{1,0:T(8,128)S(1)} collective-permute-done((f32[448,128]{1,0:T(8,128)S(1)}, f32[448,128]{1,0:T(8,128)S(1)}, u32[]{:S(2)}, u32[]{:S(2)}) %collective-permute-start.35) | collective-permute-done | bytes 229408 | tf_op jit(solution)/shard_map/ppermute | solution.py:78
  188.1 1.0 collective-permute-done.25
  190.0 1.0 collective-permute-done.26
  191.1 1.0 multiply_reduce_fusion
  192.8 1.5 fusion.16
  195.1 1.6 fusion.43
  197.6 1.6 fusion.44
  200.0 1.6 fusion.45
  201.6 1.1 fusion.1
  202.7 1.6 fusion.46
  204.3 2.0 fusion
  (147 shorter events, 20.9 us)
Async XLA Ops:
  4.9 0.9 copy-start.2
  4.9 1.2 copy-start.4
  4.9 7.9 %copy-start.6 = (bf16[1600,256]{1,0:T(8,128)(2,1)}, bf16[1600,256]{1,0:T(8,128)(2,1)S(1)}, u32[]{:S(2)}) copy-start(bf16[1600,256]{1,0:T(8,128)(2,1)S(1)} %get-tuple-element.37) | copy-start | bytes 2457604
  13.4 14.0 %collective-permute-start.6 = (f32[928,128]{1,0:T(8,128)S(1)}, f32[928,128]{1,0:T(8,128)S(1)}, u32[]{:S(2)}, u32[]{:S(2)}) collective-permute-start(f32[928,128]{1,0:T(8,128)S(1)} %constant_dynamic-slice_fusion.12), channel_id=1, source_target_pairs={{0,8},{4,12},{8,0},{12,4},{16,24},{20,28},{24,16},{28,20},{1,9},{5... | collective-permute-start | bytes 1425416 | tf_op jit(solution)/shard_map/ppermute | solution.py:78
  16.6 12.6 %collective-permute-start = (f32[928,128]{1,0:T(8,128)S(1)}, f32[928,128]{1,0:T(8,128)}, u32[]{:S(2)}, u32[]{:S(2)}) collective-permute-start(f32[928,128]{1,0:T(8,128)S(1)} %constant_dynamic-slice_fusion.15), channel_id=1, source_target_pairs={{0,4},{4,0},{8,12},{12,8},{16,20},{20,16},{24,28},{28,24},{1,5},{5... | collective-permute-start | bytes 1425416 | tf_op jit(solution)/shard_map/ppermute | solution.py:78
  27.5 7.1 %collective-permute-start.7 = (f32[464,128]{1,0:T(8,128)S(1)}, f32[464,128]{1,0:T(8,128)S(1)}, u32[]{:S(2)}, u32[]{:S(2)}) collective-permute-start(f32[464,128]{1,0:T(8,128)S(1)} %constant_dynamic-slice_fusion.11), channel_id=1, source_target_pairs={{0,4},{4,0},{8,12},{12,8},{16,20},{20,16},{24,28},{28,24},{1,5},{5... | collective-permute-start | bytes 712712 | tf_op jit(solution)/shard_map/ppermute | solution.py:78
  30.3 7.3 %collective-permute-start.1 = (f32[464,128]{1,0:T(8,128)S(1)}, f32[464,128]{1,0:T(8,128)S(1)}, u32[]{:S(2)}, u32[]{:S(2)}) collective-permute-start(f32[464,128]{1,0:T(8,128)S(1)} %constant_dynamic-slice_fusion.14), channel_id=1, source_target_pairs={{0,8},{4,12},{8,0},{12,4},{16,24},{20,28},{24,16},{28,20},{1,9},{5... | collective-permute-start | bytes 712712 | tf_op jit(solution)/shard_map/ppermute | solution.py:78
  34.7 11.2 %collective-permute-start.8 = (f32[232,128]{1,0:T(8,128)S(1)}, f32[232,128]{1,0:T(8,128)S(1)}, u32[]{:S(2)}, u32[]{:S(2)}) collective-permute-start(f32[232,128]{1,0:T(8,128)S(1)} %constant_dynamic-slice_fusion.10), channel_id=1, source_target_pairs={{0,16},{4,20},{8,24},{12,28},{16,0},{20,4},{24,8},{28,12},{1,17},{... | collective-permute-start | bytes 356360 | tf_op jit(solution)/shard_map/ppermute | solution.py:78
  37.7 10.5 %collective-permute-start.2 = (f32[232,128]{1,0:T(8,128)S(1)}, f32[232,128]{1,0:T(8,128)S(1)}, u32[]{:S(2)}, u32[]{:S(2)}) collective-permute-start(f32[232,128]{1,0:T(8,128)S(1)} %constant_dynamic-slice_fusion.13), channel_id=1, source_target_pairs={{0,16},{4,20},{8,24},{12,28},{16,0},{20,4},{24,8},{28,12},{1,17},{... | collective-permute-start | bytes 356360 | tf_op jit(solution)/shard_map/ppermute | solution.py:78
  45.9 8.2 %collective-permute-start.9 = (f32[232,128]{1,0:T(8,128)S(1)}, f32[232,128]{1,0:T(8,128)S(1)}, u32[]{:S(2)}, u32[]{:S(2)}) collective-permute-start(f32[232,128]{1,0:T(8,128)S(1)} %dynamic-slice_add_fusion.8), channel_id=1, source_target_pairs={{0,16},{4,20},{8,24},{12,28},{16,0},{20,4},{24,8},{28,12},{1,17},{... | collective-permute-start | bytes 356360 | tf_op jit(solution)/shard_map/ppermute | solution.py:78
  48.2 8.4 %collective-permute-start.3 = (f32[232,128]{1,0:T(8,128)S(1)}, f32[232,128]{1,0:T(8,128)S(1)}, u32[]{:S(2)}, u32[]{:S(2)}) collective-permute-start(f32[232,128]{1,0:T(8,128)S(1)} %dynamic-slice_add_fusion.9), channel_id=1, source_target_pairs={{0,16},{4,20},{8,24},{12,28},{16,0},{20,4},{24,8},{28,12},{1,17},{... | collective-permute-start | bytes 356360 | tf_op jit(solution)/shard_map/ppermute | solution.py:78
  54.1 6.2 %collective-permute-start.10 = (f32[464,128]{1,0:T(8,128)S(1)}, f32[464,128]{1,0:T(8,128)S(1)}, u32[]{:S(2)}, u32[]{:S(2)}) collective-permute-start(f32[464,128]{1,0:T(8,128)S(1)} %pad_maximum_fusion.13), channel_id=1, source_target_pairs={{0,4},{4,0},{8,12},{12,8},{16,20},{20,16},{24,28},{28,24},{1,5},{5... | collective-permute-start | bytes 712712 | tf_op jit(solution)/shard_map/ppermute | solution.py:78
  56.7 9.4 %collective-permute-start.4 = (f32[464,128]{1,0:T(8,128)S(1)}, f32[464,128]{1,0:T(8,128)S(1)}, u32[]{:S(2)}, u32[]{:S(2)}) collective-permute-start(f32[464,128]{1,0:T(8,128)S(1)} %pad_maximum_fusion.12), channel_id=1, source_target_pairs={{0,8},{4,12},{8,0},{12,4},{16,24},{20,28},{24,16},{28,20},{1,9},{5... | collective-permute-start | bytes 712712 | tf_op jit(solution)/shard_map/ppermute | solution.py:78
  60.4 12.8 %collective-permute-start.11 = (f32[928,128]{1,0:T(8,128)S(1)}, f32[928,128]{1,0:T(8,128)S(1)}, u32[]{:S(2)}, u32[]{:S(2)}) collective-permute-start(f32[928,128]{1,0:T(8,128)S(1)} %pad_maximum_fusion.8), channel_id=1, source_target_pairs={{0,8},{4,12},{8,0},{12,4},{16,24},{20,28},{24,16},{28,20},{1,9},{5... | collective-permute-start | bytes 1425416 | tf_op jit(solution)/shard_map/ppermute | solution.py:78
  66.9 9.1 %collective-permute-start.5 = (f32[928,128]{1,0:T(8,128)}, f32[928,128]{1,0:T(8,128)S(1)}, u32[]{:S(2)}, u32[]{:S(2)}) collective-permute-start(f32[928,128]{1,0:T(8,128)} %pad_maximum_fusion.7), channel_id=1, source_target_pairs={{0,4},{4,0},{8,12},{12,8},{16,20},{20,16},{24,28},{28,24},{1,5},{5... | collective-permute-start | bytes 1425416 | tf_op jit(solution)/shard_map/ppermute | solution.py:78
  81.5 9.7 %collective-permute-start.12 = (f32[8,128]{1,0:T(8,128)S(1)}, f32[8,128]{1,0:T(8,128)S(1)}, u32[]{:S(2)}, u32[]{:S(2)}) collective-permute-start(f32[8,128]{1,0:T(8,128)S(1)} %broadcast_in_dim.6), channel_id=1, source_target_pairs={{0,1},{1,0},{2,3},{3,2},{4,5},{5,4},{6,7},{7,6},{8,9},{9,8},{10,11... | collective-permute-start | bytes 12296 | tf_op jit(solution)/shard_map/ppermute | solution.py:78
  90.3 3.2 %copy-start = (f32[1792,128]{1,0:T(8,128)}, f32[1792,128]{1,0:T(8,128)S(1)}, u32[]{:S(2)}) copy-start(f32[1792,128]{1,0:T(8,128)S(1)} %get-tuple-element.34) | copy-start | bytes 2752516
  91.2 3.6 %collective-permute-start.13 = (f32[8,128]{1,0:T(8,128)S(1)}, f32[8,128]{1,0:T(8,128)S(1)}, u32[]{:S(2)}, u32[]{:S(2)}) collective-permute-start(f32[8,128]{1,0:T(8,128)S(1)} %broadcast_add_fusion), channel_id=1, source_target_pairs={{0,2},{1,3},{2,0},{3,1},{4,6},{5,7},{6,4},{7,5},{8,10},{9,11},{10,... | collective-permute-start | bytes 12296 | tf_op jit(solution)/shard_map/ppermute | solution.py:78
  93.7 16.4 %copy-start.9 = (f32[4,1600]{1,0:T(4,128)S(1)}, f32[4,1600]{1,0:T(4,128)}, u32[]{:S(2)}) copy-start(f32[4,1600]{1,0:T(4,128)} %param.21) | copy-start | bytes 76804
  93.7 16.4 %copy-start.10 = (f32[4,1600]{1,0:T(4,128)S(1)}, f32[4,1600]{1,0:T(4,128)}, u32[]{:S(2)}) copy-start(f32[4,1600]{1,0:T(4,128)} %param.23) | copy-start | bytes 76804
  93.7 16.4 %copy-start.11 = (f32[4,1600]{1,0:T(4,128)S(1)}, f32[4,1600]{1,0:T(4,128)}, u32[]{:S(2)}) copy-start(f32[4,1600]{1,0:T(4,128)} %param.22) | copy-start | bytes 76804
  93.7 25.5 %collective-permute-start.27 = (f32[896,128]{1,0:T(8,128)}, f32[896,128]{1,0:T(8,128)S(1)}, u32[]{:S(2)}, u32[]{:S(2)}) collective-permute-start(f32[896,128]{1,0:T(8,128)} %constant_dynamic-slice_fusion.4), channel_id=1, source_target_pairs={{0,1},{1,0},{2,3},{3,2},{4,5},{5,4},{6,7},{7,6},{8,9},{9,8},{10,11... | collective-permute-start | bytes 1376264 | tf_op jit(solution)/shard_map/ppermute | solution.py:78
  94.0 25.4 %collective-permute-start.17 = (f32[896,128]{1,0:T(8,128)S(1)}, f32[896,128]{1,0:T(8,128)S(1)}, u32[]{:S(2)}, u32[]{:S(2)}) collective-permute-start(f32[896,128]{1,0:T(8,128)S(1)} %constant_dynamic-slice_fusion.9), channel_id=1, source_target_pairs={{0,1},{1,0},{2,3},{3,2},{4,5},{5,4},{6,7},{7,6},{8,9},{9,8},{10,11... | collective-permute-start | bytes 1376264 | tf_op jit(solution)/shard_map/ppermute | solution.py:78
  100.3 8.9 %collective-permute-start.14 = (bf16[1,250,256]{2,1,0:T(8,128)(2,1)S(1)}, bf16[1,250,256]{2,1,0:T(8,128)(2,1)S(1)}, u32[]{:S(2)}, u32[]{:S(2)}) collective-permute-start(bf16[1,250,256]{2,1,0:T(8,128)(2,1)S(1)} %maximum_bitcast_fusion), channel_id=1, source_target_pairs={{0,16},{4,20},{8,24},{12,28},{16,0},{20,4},{24,8},{28,12},{1,17},{... | collective-permute-start | bytes 384008 | tf_op jit(solution)/shard_map/ppermute | solution.py:78
  103.2 16.0 %copy-start.1 = (f32[1792,128]{1,0:T(8,128)S(1)}, f32[1792,128]{1,0:T(8,128)}, u32[]{:S(2)}) copy-start(f32[1792,128]{1,0:T(8,128)} %copy-done) | copy-start | bytes 2752516
  109.3 7.3 %collective-permute-start.15 = (bf16[2,250,256]{2,1,0:T(8,128)(2,1)S(1)}, bf16[2,250,256]{2,1,0:T(8,128)(2,1)S(1)}, u32[]{:S(2)}, u32[]{:S(2)}) collective-permute-start(bf16[2,250,256]{2,1,0:T(8,128)(2,1)S(1)} %pad_maximum_fusion.11), channel_id=1, source_target_pairs={{0,8},{4,12},{8,0},{12,4},{16,24},{20,28},{24,16},{28,20},{1,9},{5... | collective-permute-start | bytes 768008 | tf_op jit(solution)/shard_map/ppermute | solution.py:78
  116.6 37.6 %collective-permute-start.16 = (bf16[4,250,256]{2,1,0:T(8,128)(2,1)S(1)}, bf16[4,250,256]{2,1,0:T(8,128)(2,1)S(1)}, u32[]{:S(2)}, u32[]{:S(2)}) collective-permute-start(bf16[4,250,256]{2,1,0:T(8,128)(2,1)S(1)} %pad_maximum_fusion.6), channel_id=1, source_target_pairs={{0,4},{4,0},{8,12},{12,8},{16,20},{20,16},{24,28},{28,24},{1,5},{5... | collective-permute-start | bytes 1536008 | tf_op jit(solution)/shard_map/ppermute | solution.py:78
  119.3 16.1 %collective-permute-start.28 = (f32[448,128]{1,0:T(8,128)S(1)}, f32[448,128]{1,0:T(8,128)S(1)}, u32[]{:S(2)}, u32[]{:S(2)}) collective-permute-start(f32[448,128]{1,0:T(8,128)S(1)} %constant_dynamic-slice_fusion.3), channel_id=1, source_target_pairs={{0,4},{4,0},{8,12},{12,8},{16,20},{20,16},{24,28},{28,24},{1,5},{5... | collective-permute-start | bytes 688136 | tf_op jit(solution)/shard_map/ppermute | solution.py:78
  119.5 17.0 %collective-permute-start.18 = (f32[448,128]{1,0:T(8,128)S(1)}, f32[448,128]{1,0:T(8,128)S(1)}, u32[]{:S(2)}, u32[]{:S(2)}) collective-permute-start(f32[448,128]{1,0:T(8,128)S(1)} %constant_dynamic-slice_fusion.8), channel_id=1, source_target_pairs={{0,2},{1,3},{2,0},{3,1},{4,6},{5,7},{6,4},{7,5},{8,10},{9,11},{10,... | collective-permute-start | bytes 688136 | tf_op jit(solution)/shard_map/ppermute | solution.py:78
  135.4 4.9 %collective-permute-start.29 = (f32[224,128]{1,0:T(8,128)S(1)}, f32[224,128]{1,0:T(8,128)S(1)}, u32[]{:S(2)}, u32[]{:S(2)}) collective-permute-start(f32[224,128]{1,0:T(8,128)S(1)} %constant_dynamic-slice_fusion.2), channel_id=1, source_target_pairs={{0,8},{4,12},{8,0},{12,4},{16,24},{20,28},{24,16},{28,20},{1,9},{5... | collective-permute-start | bytes 344072 | tf_op jit(solution)/shard_map/ppermute | solution.py:78
  136.5 5.2 %collective-permute-start.19 = (f32[224,128]{1,0:T(8,128)S(1)}, f32[224,128]{1,0:T(8,128)S(1)}, u32[]{:S(2)}, u32[]{:S(2)}) collective-permute-start(f32[224,128]{1,0:T(8,128)S(1)} %constant_dynamic-slice_fusion.7), channel_id=1, source_target_pairs={{0,4},{4,0},{8,12},{12,8},{16,20},{20,16},{24,28},{28,24},{1,5},{5... | collective-permute-start | bytes 344072 | tf_op jit(solution)/shard_map/ppermute | solution.py:78
  140.3 4.2 %collective-permute-start.30 = (f32[112,128]{1,0:T(8,128)S(1)}, f32[112,128]{1,0:T(8,128)S(1)}, u32[]{:S(2)}, u32[]{:S(2)}) collective-permute-start(f32[112,128]{1,0:T(8,128)S(1)} %constant_dynamic-slice_fusion.1), channel_id=1, source_target_pairs={{0,2},{1,3},{2,0},{3,1},{4,6},{5,7},{6,4},{7,5},{8,10},{9,11},{10,... | collective-permute-start | bytes 172040 | tf_op jit(solution)/shard_map/ppermute | solution.py:78
  141.7 5.9 %collective-permute-start.20 = (f32[112,128]{1,0:T(8,128)S(1)}, f32[112,128]{1,0:T(8,128)S(1)}, u32[]{:S(2)}, u32[]{:S(2)}) collective-permute-start(f32[112,128]{1,0:T(8,128)S(1)} %constant_dynamic-slice_fusion.6), channel_id=1, source_target_pairs={{0,8},{4,12},{8,0},{12,4},{16,24},{20,28},{24,16},{28,20},{1,9},{5... | collective-permute-start | bytes 172040 | tf_op jit(solution)/shard_map/ppermute | solution.py:78
  144.6 5.2 %collective-permute-start.31 = (f32[56,128]{1,0:T(8,128)S(1)}, f32[56,128]{1,0:T(8,128)S(1)}, u32[]{:S(2)}, u32[]{:S(2)}) collective-permute-start(f32[56,128]{1,0:T(8,128)S(1)} %constant_dynamic-slice_fusion), channel_id=1, source_target_pairs={{0,16},{4,20},{8,24},{12,28},{16,0},{20,4},{24,8},{28,12},{1,17},{... | collective-permute-start | bytes 86024 | tf_op jit(solution)/shard_map/ppermute | solution.py:78
  147.7 5.1 %collective-permute-start.21 = (f32[56,128]{1,0:T(8,128)S(1)}, f32[56,128]{1,0:T(8,128)S(1)}, u32[]{:S(2)}, u32[]{:S(2)}) collective-permute-start(f32[56,128]{1,0:T(8,128)S(1)} %constant_dynamic-slice_fusion.5), channel_id=1, source_target_pairs={{0,16},{4,20},{8,24},{12,28},{16,0},{20,4},{24,8},{28,12},{1,17},{... | collective-permute-start | bytes 86024 | tf_op jit(solution)/shard_map/ppermute | solution.py:78
  149.8 22.8 %collective-permute-start.32 = (f32[56,128]{1,0:T(8,128)S(1)}, f32[56,128]{1,0:T(8,128)S(1)}, u32[]{:S(2)}, u32[]{:S(2)}) collective-permute-start(f32[56,128]{1,0:T(8,128)S(1)} %dynamic-slice_add_fusion.14), channel_id=1, source_target_pairs={{0,16},{4,20},{8,24},{12,28},{16,0},{20,4},{24,8},{28,12},{1,17},{... | collective-permute-start | bytes 86024 | tf_op jit(solution)/shard_map/ppermute | solution.py:78
  152.8 21.0 %collective-permute-start.22 = (f32[56,128]{1,0:T(8,128)S(1)}, f32[56,128]{1,0:T(8,128)S(1)}, u32[]{:S(2)}, u32[]{:S(2)}) collective-permute-start(f32[56,128]{1,0:T(8,128)S(1)} %dynamic-slice_add_fusion.15), channel_id=1, source_target_pairs={{0,16},{4,20},{8,24},{12,28},{16,0},{20,4},{24,8},{28,12},{1,17},{... | collective-permute-start | bytes 86024 | tf_op jit(solution)/shard_map/ppermute | solution.py:78
  154.4 1.1 copy-start.3
  154.4 1.4 copy-start.5
  154.5 1.6 copy-start.7
  172.6 4.2 %collective-permute-start.33 = (f32[112,128]{1,0:T(8,128)S(1)}, f32[112,128]{1,0:T(8,128)S(1)}, u32[]{:S(2)}, u32[]{:S(2)}) collective-permute-start(f32[112,128]{1,0:T(8,128)S(1)} %pad_maximum_fusion.19), channel_id=1, source_target_pairs={{0,2},{1,3},{2,0},{3,1},{4,6},{5,7},{6,4},{7,5},{8,10},{9,11},{10,... | collective-permute-start | bytes 172040 | tf_op jit(solution)/shard_map/ppermute | solution.py:78
  173.8 4.2 %collective-permute-start.23 = (f32[112,128]{1,0:T(8,128)S(1)}, f32[112,128]{1,0:T(8,128)S(1)}, u32[]{:S(2)}, u32[]{:S(2)}) collective-permute-start(f32[112,128]{1,0:T(8,128)S(1)} %pad_maximum_fusion.18), channel_id=1, source_target_pairs={{0,8},{4,12},{8,0},{12,4},{16,24},{20,28},{24,16},{28,20},{1,9},{5... | collective-permute-start | bytes 172040 | tf_op jit(solution)/shard_map/ppermute | solution.py:78
  176.9 4.9 %collective-permute-start.34 = (f32[224,128]{1,0:T(8,128)S(1)}, f32[224,128]{1,0:T(8,128)S(1)}, u32[]{:S(2)}, u32[]{:S(2)}) collective-permute-start(f32[224,128]{1,0:T(8,128)S(1)} %pad_maximum_fusion.17), channel_id=1, source_target_pairs={{0,8},{4,12},{8,0},{12,4},{16,24},{20,28},{24,16},{28,20},{1,9},{5... | collective-permute-start | bytes 344072 | tf_op jit(solution)/shard_map/ppermute | solution.py:78
  178.0 4.9 %collective-permute-start.24 = (f32[224,128]{1,0:T(8,128)S(1)}, f32[224,128]{1,0:T(8,128)S(1)}, u32[]{:S(2)}, u32[]{:S(2)}) collective-permute-start(f32[224,128]{1,0:T(8,128)S(1)} %pad_maximum_fusion.16), channel_id=1, source_target_pairs={{0,4},{4,0},{8,12},{12,8},{16,20},{20,16},{24,28},{28,24},{1,5},{5... | collective-permute-start | bytes 344072 | tf_op jit(solution)/shard_map/ppermute | solution.py:78
  181.8 6.1 %collective-permute-start.35 = (f32[448,128]{1,0:T(8,128)S(1)}, f32[448,128]{1,0:T(8,128)S(1)}, u32[]{:S(2)}, u32[]{:S(2)}) collective-permute-start(f32[448,128]{1,0:T(8,128)S(1)} %pad_maximum_fusion.15), channel_id=1, source_target_pairs={{0,4},{4,0},{8,12},{12,8},{16,20},{20,16},{24,28},{28,24},{1,5},{5... | collective-permute-start | bytes 688136 | tf_op jit(solution)/shard_map/ppermute | solution.py:78
  182.9 6.3 %copy-start.8 = (bf16[1,8,4,1600]{3,2,1,0:T(4,128)(2,1)S(1)}, bf16[1,8,4,1600]{3,2,1,0:T(4,128)(2,1)}, u32[]{:S(2)}) copy-start(bf16[1,8,4,1600]{3,2,1,0:T(4,128)(2,1)} %param.24) | copy-start | bytes 307204
  183.0 6.1 %collective-permute-start.25 = (f32[448,128]{1,0:T(8,128)S(1)}, f32[448,128]{1,0:T(8,128)S(1)}, u32[]{:S(2)}, u32[]{:S(2)}) collective-permute-start(f32[448,128]{1,0:T(8,128)S(1)} %pad_maximum_fusion.14), channel_id=1, source_target_pairs={{0,2},{1,3},{2,0},{3,1},{4,6},{5,7},{6,4},{7,5},{8,10},{9,11},{10,... | collective-permute-start | bytes 688136 | tf_op jit(solution)/shard_map/ppermute | solution.py:78
  188.0 2.0 collective-permute-start.36
  189.1 1.9 collective-permute-start.26
where the time goes:
time: 207 us; the launch traced here: 206 us
  waiting for transfers between devices  78.2 us (38%)
  starting transfers between devices  53.5 us (26%)
  matrix products  35.6 us (17%)
  other arithmetic  25.1 us (12%)
  local copies, waits for them, and re-layouts  8.34 us (4%)
  between operations  5.53 us (3%)
    ppermute x37, waiting for transfers between devices, swap_with(): lax.ppermute(values, name, [(index, index ^ bit) for index in range(size)])  78.2 us
    ppermute x37, starting transfers between devices, swap_with(): lax.ppermute(values, name, [(index, index ^ bit) for index in range(size)])  53.5 us
    dot_general x2, matrix products, exact_dot(): lax.dot_general(lhs_bf16, split3(rhs_f32), ((contract, (0,)), ((), ())),...  14.9 us
    convert_element_type x1, other arithmetic, shards(): weights_next = (weights_fc.astype(jnp.float32) - learn_rate * galore_scal...  8.97 us
    dot_general x5, matrix products, orthogonalize(): gram_matrix = jnp.dot(iterate.T, iterate, precision=highest)  7.84 us
    dot_general x1, matrix products, shards(): lax.dot_general(jnp.concatenate([fc_dir_all] * 3, axis=1), stacked, (((1,...  7.26 us
    dot_general x5, matrix products, orthogonalize(): jnp.dot(iterate, gram_matrix, precision=highest)  5.63 us
  transfers between devices with their start and end apart: 37, of which 24 were waited for; matrix products, arithmetic and copies ran while one was open for 17% of the time, Pallas kernels for 0%

commit v1 on v0

--- a/solution.py
+++ b/solution.py
@@ -93,6 +93,29 @@
         second = jnp.where(side == 0, other, parts)
         parts = jnp.concatenate([first, second], axis=0)
     return parts
+
+
+def half_orders(axes):
+    steps = axis_steps(axes)
+    if steps is None:
+        return None
+    low = 1 if len(axes) > 1 else 0
+    high = len(steps) - 1
+    if high - low < 2:
+        return steps, steps
+    middle = steps[low:high]
+    return steps, steps[:low] + middle[1:] + middle[:1] + steps[high:]
+
+
+def half_sum(piece, axes, which):
+    orders = half_orders(axes)
+    if orders is None:
+        return lax.psum(piece, axes)
+    steps = orders[which]
+    count = 2 ** len(steps)
+    rows = piece.shape[0]
+    padded = -(-rows // (8 * count)) * 8 * count
+    return run_steps(jnp.pad(piece, ((0, padded - rows), (0, 0))), steps)[:rows]
 
 
 def butterfly_sum(packed, axes):
@@ -144,23 +167,21 @@
     return parts.transpose(order).reshape((size,) + piece.shape)
 
 
-def split3(values):
+def split2(values):
     first = values.astype(jnp.bfloat16)
-    rest = values - first.astype(jnp.float32)
-    second = rest.astype(jnp.bfloat16)
-    third = (rest - second.astype(jnp.float32)).astype(jnp.bfloat16)
-    return jnp.concatenate([first, second, third], axis=1)
+    second = (values - first.astype(jnp.float32)).astype(jnp.bfloat16)
+    return jnp.concatenate([first, second], axis=1)
 
 
 def exact_dot(lhs_bf16, rhs_f32, contract):
     cols = rhs_f32.shape[1]
     wide = lax.dot_general(
         lhs_bf16,
-        split3(rhs_f32),
+        split2(rhs_f32),
         ((contract, (0,)), ((), ())),
         preferred_element_type=jnp.float32,
     )
-    return wide[:, :cols] + wide[:, cols : 2 * cols] + wide[:, 2 * cols :]
+    return wide[:, :cols] + wide[:, cols:]
 
 
 def shards(
@@ -189,14 +210,25 @@
     rank_cols = basis.shape[1]
     emb_count = grads_emb.shape[3]
     local_rows = grads_fc.reshape(blocks * row_count, width)
-    local_proj = exact_dot(local_rows, basis, (1,))
     emb_local = grads_emb.reshape(blocks, emb_count, width).astype(jnp.float32)
     ln_local = grads_ln.reshape(4, width).astype(jnp.float32)
-    proj_own, emb_own, ln_sum = unpack_rows(
-        butterfly_sum(pack_rows((local_proj, emb_local, ln_local), rank_cols), ("dp",)),
-        (local_proj, emb_local, ln_local),
-    )
-    partial_value = exact_dot(local_rows, proj_own, (0,))
+    half = rank_cols // 2
+    small = pack_rows((emb_local, ln_local), half)
+    small_rows = -(-small.shape[0] // 2)
+    small = jnp.pad(small, ((0, 2 * small_rows - small.shape[0]), (0, 0)))
+    proj_halves, small_halves, value_halves = [], [], []
+    for which in range(2):
+        proj_half = exact_dot(local_rows, basis[:, which * half : (which + 1) * half], (1,))
+        summed = half_sum(
+            jnp.concatenate([proj_half, small[which * small_rows : (which + 1) * small_rows]]),
+            ("dp",),
+            which,
+        )
+        proj_halves.append(summed[: proj_half.shape[0]])
+        small_halves.append(summed[proj_half.shape[0] :])
+        value_halves.append(exact_dot(local_rows, proj_halves[-1], (0,)))
+    proj_own = jnp.concatenate(proj_halves, axis=1)
+    emb_own, ln_sum = unpack_rows(jnp.concatenate(small_halves), (emb_local, ln_local))
     own_square = jnp.sum(proj_own * proj_own) + jnp.sum(emb_own * emb_own)
     square_total = small_sum(jnp.full((8, 128), own_square), ("own",))[0, 0]
     grad_norm = jnp.sqrt(square_total + jnp.sum(ln_sum * ln_sum) + 1e-06)
@@ -229,13 +261,9 @@
     )(gathered)
     fc_dir_all = fc_dir_all.reshape(replicas * row_count, rank_cols)
     emb_dir_all = emb_dir_all[:, 0].astype(jnp.float32) + emb_dir_all[:, 1].astype(jnp.float32)
-    pieces = split3(basis)
-    stacked = jnp.concatenate(
-        [pieces[:, :rank_cols], pieces[:, rank_cols : 2 * rank_cols], pieces[:, 2 * rank_cols :]], axis=1
-    )
     update_rows = lax.dot_general(
-        jnp.concatenate([fc_dir_all] * 3, axis=1),
-        stacked,
+        jnp.concatenate([fc_dir_all] * 2, axis=1),
+        split2(basis),
         (((1,), (1,)), ((), ())),
         preferred_element_type=jnp.float32,
     )
@@ -246,7 +274,9 @@
     emb_next = (
         emb_weights.astype(jnp.float32) - learn_rate * emb_dir_all.reshape(emb_weights.shape)
     ).astype(jnp.bfloat16)
-    subspace = butterfly_sum(partial_value, ("own", "dp"))
+    subspace = jnp.concatenate(
+        [half_sum(value_halves[which], ("own", "dp"), which) for which in range(2)], axis=1
+    )
     basis_next = orthogonalize(subspace)
     return (
         fc_m_next,

time: 207 us -> 208 us (level)
  waiting for transfers between devices: 78.2 us -> 74.3 us
  other arithmetic: 25.1 us -> 28.4 us
    ppermute x37, waiting for transfers between devices: 78.2 us -> 74.3 us  [swap_with(): lax.ppermute(values, name, [(index, index ^ bit) for index in range(size)])]
    dot_general x3 -> x5, matrix products: 22.2 us -> 23.8 us  [the longest x4 18.1 us: exact_dot(): lax.dot_general(lhs_bf16, split2(rhs_f32), ((contract, (0,)), ((), ())),...]
    convert_element_type x2 -> x3, other arithmetic: 4.76 us -> 4.75 us  [split2(): second = (values - first.astype(jnp.float32)).astype(jnp.bfloat16)]
  transfers between devices with their start and end apart: 37 -> 37, of which waited for: 24 -> 24; matrix products, arithmetic and copies ran while one was open for 17% -> 22% of each run, Pallas kernels for 0% -> 0%
where the time goes in v1:
time: 208 us; the launch traced here: 207 us
  waiting for transfers between devices  74.3 us (36%)
  starting transfers between devices  53.7 us (26%)
  matrix products  37.3 us (18%)
  other arithmetic  28.4 us (14%)
  local copies, waits for them, and re-layouts  8.08 us (4%)
  between operations  5.61 us (3%)
    ppermute x37, waiting for transfers between devices, swap_with(): lax.ppermute(values, name, [(index, index ^ bit) for index in range(size)])  74.3 us
    ppermute x37, starting transfers between devices, swap_with(): lax.ppermute(values, name, [(index, index ^ bit) for index in range(size)])  53.7 us
    dot_general x4, matrix products, exact_dot(): lax.dot_general(lhs_bf16, split2(rhs_f32), ((contract, (0,)), ((), ())),...  18.1 us
    convert_element_type x1, other arithmetic, shards(): weights_next = (weights_fc.astype(jnp.float32) - learn_rate * galore_scal...  8.97 us
    dot_general x5, matrix products, orthogonalize(): gram_matrix = jnp.dot(iterate.T, iterate, precision=highest)  7.84 us
    dot_general x1, matrix products, shards(): lax.dot_general(jnp.concatenate([fc_dir_all] * 2, axis=1), split2(basis),...  5.77 us
    dot_general x5, matrix products, orthogonalize(): jnp.dot(iterate, gram_matrix, precision=highest)  5.6 us
    convert_element_type x3, other arithmetic, split2(): second = (values - first.astype(jnp.float32)).astype(jnp.bfloat16)  4.75 us
  transfers between devices with their start and end apart: 37, of which 24 were waited for; matrix products, arithmetic and copies ran while one was open for 22% of the time, Pallas kernels for 0%

profile of v1, /device:TPU:0, one launch (start us, length us, event | category | flops | bytes accessed | tf_op | source)
XLA Modules:
  0.0 207.4 jit_solution(2973903463774853305)
XLA Ops:
  1.7 2.2 %subtract_convert_fusion.5 = (bf16[1600,128]{1,0:T(8,128)(2,1)S(1)}, bf16[1600,128]{1,0:T(8,128)(2,1)S(1)}, bf16[1600,128]{1,0:T(8,128)(2,1)S(1)}, bf16[1600,128]{1,0:T(8,128)(2,1)S(1)}) fusion(f32[1600,256]{1,0:T(8,128)} %param.18), kind=kLoop, calls=%fused_computation.70 | loop fusion | flops 1228800 | bytes 4096000 | tf_op jit(solution)/shard_map/convert_element_type | solution.py:172
  3.9 4.2 %convolution_bitcast_fusion.1 = f32[1600,256]{1,0:T(8,128)S(1)} fusion(bf16[1600,1600]{1,0:T(8,128)(2,1)} %bitcast.77, bf16[1600,128]{1,0:T(8,128)(2,1)S(1)} %get-tuple-element.33, bf16[1600,128]{1,0:T(8,128)(2,1)S(1)} %get-tuple-element.34), kind=kOutput, calls=%fused_computation.13 | convolution fusion | flops 1312358400 | bytes 7577600 | tf_op jit(solution)/shard_map/dot_general | solution.py:178
  9.1 3.0 %collective-permute-start = (f32[928,128]{1,0:T(8,128)S(1)}, f32[928,128]{1,0:T(8,128)}, u32[]{:S(2)}, u32[]{:S(2)}) collective-permute-start(f32[928,128]{1,0:T(8,128)S(1)} %constant_dynamic-slice_fusion.12), channel_id=1, source_target_pairs={{0,4},{4,0},{8,12},{12,8},{16,20},{20,16},{24,28},{28,24},{1,5},{5... | collective-permute-start | bytes 1425416 | tf_op jit(solution)/shard_map/ppermute | solution.py:78
  12.2 4.2 %convolution_bitcast_fusion = f32[1600,256]{1,0:T(8,128)S(1)} fusion(bf16[1600,1600]{1,0:T(8,128)(2,1)} %bitcast.78, bf16[1600,128]{1,0:T(8,128)(2,1)S(1)} %get-tuple-element.37, bf16[1600,128]{1,0:T(8,128)(2,1)S(1)} %get-tuple-element.38), kind=kOutput, calls=%fused_computation.12 | convolution fusion | flops 1312358400 | bytes 7577600 | tf_op jit(solution)/shard_map/dot_general | solution.py:178
  17.5 1.6 collective-permute-start.6
  19.2 4.0 %collective-permute-done = f32[928,128]{1,0:T(8,128)} collective-permute-done((f32[928,128]{1,0:T(8,128)S(1)}, f32[928,128]{1,0:T(8,128)}, u32[]{:S(2)}, u32[]{:S(2)}) %collective-permute-start) | collective-permute-done | bytes 475168 | tf_op jit(solution)/shard_map/ppermute | solution.py:78
  23.1 1.1 dynamic-slice_add_fusion
  24.2 1.9 collective-permute-start.1
  26.1 5.3 %collective-permute-done.6 = f32[928,128]{1,0:T(8,128)S(1)} collective-permute-done((f32[928,128]{1,0:T(8,128)S(1)}, f32[928,128]{1,0:T(8,128)S(1)}, u32[]{:S(2)}, u32[]{:S(2)}) %collective-permute-start.6) | collective-permute-done | bytes 475168 | tf_op jit(solution)/shard_map/ppermute | solution.py:78
  31.6 3.4 %collective-permute-done.1 = f32[464,128]{1,0:T(8,128)S(1)} collective-permute-done((f32[464,128]{1,0:T(8,128)S(1)}, f32[464,128]{1,0:T(8,128)S(1)}, u32[]{:S(2)}, u32[]{:S(2)}) %collective-permute-start.1) | collective-permute-done | bytes 237600 | tf_op jit(solution)/shard_map/ppermute | solution.py:78
  35.1 2.6 %collective-permute-start.2 = (f32[232,128]{1,0:T(8,128)S(1)}, f32[232,128]{1,0:T(8,128)S(1)}, u32[]{:S(2)}, u32[]{:S(2)}) collective-permute-start(f32[232,128]{1,0:T(8,128)S(1)} %constant_dynamic-slice_fusion.10), channel_id=1, source_target_pairs={{0,16},{4,20},{8,24},{12,28},{16,0},{20,4},{24,8},{28,12},{1,17},{... | collective-permute-start | bytes 356360 | tf_op jit(solution)/shard_map/ppermute | solution.py:78
  37.8 2.6 %collective-permute-start.8 = (f32[232,128]{1,0:T(8,128)S(1)}, f32[232,128]{1,0:T(8,128)S(1)}, u32[]{:S(2)}, u32[]{:S(2)}) collective-permute-start(f32[232,128]{1,0:T(8,128)S(1)} %constant_dynamic-slice_fusion.8), channel_id=1, source_target_pairs={{0,16},{4,20},{8,24},{12,28},{16,0},{20,4},{24,8},{28,12},{1,17},{... | collective-permute-start | bytes 356360 | tf_op jit(solution)/shard_map/ppermute | solution.py:78
  40.4 5.7 %collective-permute-done.2 = f32[232,128]{1,0:T(8,128)S(1)} collective-permute-done((f32[232,128]{1,0:T(8,128)S(1)}, f32[232,128]{1,0:T(8,128)S(1)}, u32[]{:S(2)}, u32[]{:S(2)}) %collective-permute-start.2) | collective-permute-done | bytes 118816 | tf_op jit(solution)/shard_map/ppermute | solution.py:78
  46.2 2.4 %collective-permute-done.8 = f32[232,128]{1,0:T(8,128)S(1)} collective-permute-done((f32[232,128]{1,0:T(8,128)S(1)}, f32[232,128]{1,0:T(8,128)S(1)}, u32[]{:S(2)}, u32[]{:S(2)}) %collective-permute-start.8) | collective-permute-done | bytes 118816 | tf_op jit(solution)/shard_map/ppermute | solution.py:78
  49.2 5.9 %collective-permute-done.3 = f32[232,128]{1,0:T(8,128)S(1)} collective-permute-done((f32[232,128]{1,0:T(8,128)S(1)}, f32[232,128]{1,0:T(8,128)S(1)}, u32[]{:S(2)}, u32[]{:S(2)}) %collective-permute-start.3) | collective-permute-done | bytes 118816 | tf_op jit(solution)/shard_map/ppermute | solution.py:78
  55.1 1.8 collective-permute-start.4
  57.5 4.9 %collective-permute-done.4 = f32[464,128]{1,0:T(8,128)S(1)} collective-permute-done((f32[464,128]{1,0:T(8,128)S(1)}, f32[464,128]{1,0:T(8,128)S(1)}, u32[]{:S(2)}, u32[]{:S(2)}) %collective-permute-start.4) | collective-permute-done | bytes 237600 | tf_op jit(solution)/shard_map/ppermute | solution.py:78
  64.2 4.7 %collective-permute-start.11 = (f32[928,128]{1,0:T(8,128)S(1)}, f32[928,128]{1,0:T(8,128)S(1)}, u32[]{:S(2)}, u32[]{:S(2)}) collective-permute-start(f32[928,128]{1,0:T(8,128)S(1)} %pad_maximum_fusion.9), channel_id=1, source_target_pairs={{0,8},{4,12},{8,0},{12,4},{16,24},{20,28},{24,16},{28,20},{1,9},{5... | collective-permute-start | bytes 1425416 | tf_op jit(solution)/shard_map/ppermute | solution.py:78
  68.9 1.4 subtract_convert_fusion.1
  71.0 3.2 %collective-permute-done.5 = f32[928,128]{1,0:T(8,128)S(1)} collective-permute-done((f32[928,128]{1,0:T(8,128)S(1)}, f32[928,128]{1,0:T(8,128)S(1)}, u32[]{:S(2)}, u32[]{:S(2)}) %collective-permute-start.5) | collective-permute-done | bytes 475168 | tf_op jit(solution)/shard_map/ppermute | solution.py:78
  74.3 2.6 %collective-permute-done.11 = f32[928,128]{1,0:T(8,128)S(1)} collective-permute-done((f32[928,128]{1,0:T(8,128)S(1)}, f32[928,128]{1,0:T(8,128)S(1)}, u32[]{:S(2)}, u32[]{:S(2)}) %collective-permute-start.11) | collective-permute-done | bytes 475168 | tf_op jit(solution)/shard_map/ppermute | solution.py:78
  77.6 1.2 subtract_convert_fusion.2
  81.3 4.8 %convolution_bitcast_fusion.2 = f32[1600,256]{1,0:T(8,128)S(1)} fusion(bf16[1600,1600]{1,0:T(8,128)(2,1)} %bitcast.79, bf16[1600,128]{1,0:T(8,128)(2,1)S(1)} %get-tuple-element.17, bf16[1600,128]{1,0:T(8,128)(2,1)S(1)} %get-tuple-element.18), kind=kOutput, calls=%fused_computation.14 | convolution fusion | flops 1312358400 | bytes 7577600 | tf_op jit(solution)/shard_map/dot_general | solution.py:178
  87.6 4.8 %convolution_bitcast_fusion.3 = f32[1600,256]{1,0:T(8,128)S(1)} fusion(bf16[1600,1600]{1,0:T(8,128)(2,1)} %bitcast.80, bf16[1600,128]{1,0:T(8,128)(2,1)S(1)} %copy-done.6, bf16[1600,128]{1,0:T(8,128)(2,1)S(1)} %copy-done.7), kind=kOutput, calls=%fused_computation.15 | convolution fusion | flops 1312358400 | bytes 7577600 | tf_op jit(solution)/shard_map/dot_general | solution.py:178
  92.5 1.4 multiply_reduce_fusion.2
  94.8 1.5 collective-permute-start.13
  97.2 1.2 collective-permute-done.13
  100.3 1.4 multiply_divide_fusion.2
  101.9 1.9 convert_bitcast_fusion
  103.8 2.6 %collective-permute-start.14 = (bf16[1,250,256]{2,1,0:T(8,128)(2,1)S(1)}, bf16[1,250,256]{2,1,0:T(8,128)(2,1)S(1)}, u32[]{:S(2)}, u32[]{:S(2)}) collective-permute-start(bf16[1,250,256]{2,1,0:T(8,128)(2,1)S(1)} %maximum_bitcast_fusion), channel_id=1, source_target_pairs={{0,16},{4,20},{8,24},{12,28},{16,0},{20,4},{24,8},{28,12},{1,17},{... | collective-permute-start | bytes 384008 | tf_op jit(solution)/shard_map/ppermute | solution.py:78
  107.3 5.0 %collective-permute-done.14 = bf16[1,250,256]{2,1,0:T(8,128)(2,1)S(1)} collective-permute-done((bf16[1,250,256]{2,1,0:T(8,128)(2,1)S(1)}, bf16[1,250,256]{2,1,0:T(8,128)(2,1)S(1)}, u32[]{:S(2)}, u32[]{:S(2)}) %collective-permute-start.14) | collective-permute-done | bytes 128032 | tf_op jit(solution)/shard_map/ppermute | solution.py:78
  113.7 5.6 %collective-permute-done.15 = bf16[2,250,256]{2,1,0:T(8,128)(2,1)S(1)} collective-permute-done((bf16[2,250,256]{2,1,0:T(8,128)(2,1)S(1)}, bf16[2,250,256]{2,1,0:T(8,128)(2,1)S(1)}, u32[]{:S(2)}, u32[]{:S(2)}) %collective-permute-start.15) | collective-permute-done | bytes 256032 | tf_op jit(solution)/shard_map/ppermute | solution.py:78
  119.3 1.6 collective-permute-start.16
  120.9 1.1 fusion.34
  122.6 1.1 fusion.33
  123.7 1.4 collective-permute-start.18
  125.1 11.2 %collective-permute-done.28 = f32[448,128]{1,0:T(8,128)S(1)} collective-permute-done((f32[448,128]{1,0:T(8,128)S(1)}, f32[448,128]{1,0:T(8,128)S(1)}, u32[]{:S(2)}, u32[]{:S(2)}) %collective-permute-start.28) | collective-permute-done | bytes 229408 | tf_op jit(solution)/shard_map/ppermute | solution.py:78
  136.4 2.5 %collective-permute-start.29 = (f32[224,128]{1,0:T(8,128)S(1)}, f32[224,128]{1,0:T(8,128)S(1)}, u32[]{:S(2)}, u32[]{:S(2)}) collective-permute-start(f32[224,128]{1,0:T(8,128)S(1)} %constant_dynamic-slice_fusion.2), channel_id=1, source_target_pairs={{0,8},{4,12},{8,0},{12,4},{16,24},{20,28},{24,16},{28,20},{1,9},{5... | collective-permute-start | bytes 344072 | tf_op jit(solution)/shard_map/ppermute | solution.py:78
  139.0 1.6 collective-permute-start.19
  140.6 1.1 collective-permute-done.29
  141.7 1.3 collective-permute-start.30
  143.9 1.3 collective-permute-start.20
  146.0 4.0 %collective-permute-start.31 = (f32[56,128]{1,0:T(8,128)S(1)}, f32[56,128]{1,0:T(8,128)S(1)}, u32[]{:S(2)}, u32[]{:S(2)}) collective-permute-start(f32[56,128]{1,0:T(8,128)S(1)} %constant_dynamic-slice_fusion), channel_id=1, source_target_pairs={{0,16},{4,20},{8,24},{12,28},{16,0},{20,4},{24,8},{28,12},{1,17},{... | collective-permute-start | bytes 86024 | tf_op jit(solution)/shard_map/ppermute | solution.py:78
  150.1 1.7 collective-permute-start.21
  152.1 3.0 %collective-permute-start.32 = (f32[56,128]{1,0:T(8,128)S(1)}, f32[56,128]{1,0:T(8,128)S(1)}, u32[]{:S(2)}, u32[]{:S(2)}) collective-permute-start(f32[56,128]{1,0:T(8,128)S(1)} %dynamic-slice_add_fusion.11), channel_id=1, source_target_pairs={{0,16},{4,20},{8,24},{12,28},{16,0},{20,4},{24,8},{28,12},{1,17},{... | collective-permute-start | bytes 86024 | tf_op jit(solution)/shard_map/ppermute | solution.py:78
  155.0 1.5 collective-permute-start.22
  158.1 5.8 %convolution_multiply_fusion = f32[1600,1600]{1,0:T(8,128)} fusion(bf16[1600,256]{1,0:T(8,128)(2,1)S(1)} %bitcast.76, bf16[1600,256]{1,0:T(8,128)(2,1)S(1)} %copy-done.4, bf16[1600,256]{1,0:T(8,128)(2,1)S(1)} %copy-done.5), kind=kOutput, calls=%fused_computation.1 | convolution fusion | flops 2630553600 | bytes 12697600 | tf_op jit(solution)/shard_map/dot_general | solution.py:264
  163.9 9.0 %subtract_convert_fusion = bf16[1,8,200,1600]{3,2,1,0:T(8,128)(2,1)} fusion(f32[1,8,200,1600]{3,2,1,0:T(8,128)} %bitcast.72, bf16[1,8,200,1600]{3,2,1,0:T(8,128)(2,1)} %param.17), kind=kLoop, calls=%fused_computation | loop fusion | flops 7680000 | bytes 20480000 | tf_op jit(solution)/shard_map/convert_element_type | solution.py:273
  173.2 1.1 collective-permute-start.33
  175.4 2.0 collective-permute-done.33
  177.5 1.1 collective-permute-start.34
  178.7 1.6 collective-permute-start.24
  180.2 2.1 %collective-permute-done.34 = f32[224,128]{1,0:T(8,128)S(1)} collective-permute-done((f32[224,128]{1,0:T(8,128)S(1)}, f32[224,128]{1,0:T(8,128)S(1)}, u32[]{:S(2)}, u32[]{:S(2)}) %collective-permute-start.34) | collective-permute-done | bytes 114720 | tf_op jit(solution)/shard_map/ppermute | solution.py:78
  182.4 1.6 collective-permute-start.35
  184.1 1.1 collective-permute-start.25
  185.2 3.3 %collective-permute-done.35 = f32[448,128]{1,0:T(8,128)S(1)} collective-permute-done((f32[448,128]{1,0:T(8,128)S(1)}, f32[448,128]{1,0:T(8,128)S(1)}, u32[]{:S(2)}, u32[]{:S(2)}) %collective-permute-start.35) | collective-permute-done | bytes 229408 | tf_op jit(solution)/shard_map/ppermute | solution.py:78
  188.6 1.5 collective-permute-done.25
  193.9 1.5 fusion.14
  196.2 1.6 fusion.57
  198.7 1.6 fusion.58
  201.1 1.6 fusion.59
  202.7 1.1 fusion.1
  203.8 1.6 fusion.60
  205.4 2.0 fusion
  (160 shorter events, 26.3 us)
Async XLA Ops:
  1.7 2.2 %copy-start.2 = (f32[400,128]{1,0:T(8,128)}, f32[400,128]{1,0:T(8,128)S(1)}, u32[]{:S(2)}) copy-start(f32[400,128]{1,0:T(8,128)S(1)} %reshape.192) | copy-start | bytes 614404
  8.1 0.9 slice-start
  8.2 3.9 %copy-start.14 = (bf16[1,4,1600]{2,1,0:T(4,128)(2,1)S(1)}, bf16[1,4,1600]{2,1,0:T(4,128)(2,1)}, u32[]{:S(2)}) copy-start(bf16[1,4,1600]{2,1,0:T(4,128)(2,1)} %param.15) | copy-start | bytes 38404
  9.1 14.0 %collective-permute-start = (f32[928,128]{1,0:T(8,128)S(1)}, f32[928,128]{1,0:T(8,128)}, u32[]{:S(2)}, u32[]{:S(2)}) collective-permute-start(f32[928,128]{1,0:T(8,128)S(1)} %constant_dynamic-slice_fusion.12), channel_id=1, source_target_pairs={{0,4},{4,0},{8,12},{12,8},{16,20},{20,16},{24,28},{28,24},{1,5},{5... | collective-permute-start | bytes 1425416 | tf_op jit(solution)/shard_map/ppermute | solution.py:78
  16.4 0.9 copy-start.3
  17.5 13.9 %collective-permute-start.6 = (f32[928,128]{1,0:T(8,128)S(1)}, f32[928,128]{1,0:T(8,128)S(1)}, u32[]{:S(2)}, u32[]{:S(2)}) collective-permute-start(f32[928,128]{1,0:T(8,128)S(1)} %pad_dynamic-slice_fusion.6), channel_id=1, source_target_pairs={{0,8},{4,12},{8,0},{12,4},{16,24},{20,28},{24,16},{28,20},{1,9},{5... | collective-permute-start | bytes 1425416 | tf_op jit(solution)/shard_map/ppermute | solution.py:78
  24.2 10.8 %collective-permute-start.1 = (f32[464,128]{1,0:T(8,128)S(1)}, f32[464,128]{1,0:T(8,128)S(1)}, u32[]{:S(2)}, u32[]{:S(2)}) collective-permute-start(f32[464,128]{1,0:T(8,128)S(1)} %constant_dynamic-slice_fusion.11), channel_id=1, source_target_pairs={{0,8},{4,12},{8,0},{12,4},{16,24},{20,28},{24,16},{28,20},{1,9},{5... | collective-permute-start | bytes 712712 | tf_op jit(solution)/shard_map/ppermute | solution.py:78
  31.5 6.2 %collective-permute-start.7 = (f32[464,128]{1,0:T(8,128)S(1)}, f32[464,128]{1,0:T(8,128)S(1)}, u32[]{:S(2)}, u32[]{:S(2)}) collective-permute-start(f32[464,128]{1,0:T(8,128)S(1)} %constant_dynamic-slice_fusion.9), channel_id=1, source_target_pairs={{0,4},{4,0},{8,12},{12,8},{16,20},{20,16},{24,28},{28,24},{1,5},{5... | collective-permute-start | bytes 712712 | tf_op jit(solution)/shard_map/ppermute | solution.py:78
  35.1 11.0 %collective-permute-start.2 = (f32[232,128]{1,0:T(8,128)S(1)}, f32[232,128]{1,0:T(8,128)S(1)}, u32[]{:S(2)}, u32[]{:S(2)}) collective-permute-start(f32[232,128]{1,0:T(8,128)S(1)} %constant_dynamic-slice_fusion.10), channel_id=1, source_target_pairs={{0,16},{4,20},{8,24},{12,28},{16,0},{20,4},{24,8},{28,12},{1,17},{... | collective-permute-start | bytes 356360 | tf_op jit(solution)/shard_map/ppermute | solution.py:78
  37.8 10.9 %collective-permute-start.8 = (f32[232,128]{1,0:T(8,128)S(1)}, f32[232,128]{1,0:T(8,128)S(1)}, u32[]{:S(2)}, u32[]{:S(2)}) collective-permute-start(f32[232,128]{1,0:T(8,128)S(1)} %constant_dynamic-slice_fusion.8), channel_id=1, source_target_pairs={{0,16},{4,20},{8,24},{12,28},{16,0},{20,4},{24,8},{28,12},{1,17},{... | collective-permute-start | bytes 356360 | tf_op jit(solution)/shard_map/ppermute | solution.py:78
  46.1 9.0 %collective-permute-start.3 = (f32[232,128]{1,0:T(8,128)S(1)}, f32[232,128]{1,0:T(8,128)S(1)}, u32[]{:S(2)}, u32[]{:S(2)}) collective-permute-start(f32[232,128]{1,0:T(8,128)S(1)} %dynamic-slice_add_fusion.6), channel_id=1, source_target_pairs={{0,16},{4,20},{8,24},{12,28},{16,0},{20,4},{24,8},{28,12},{1,17},{... | collective-permute-start | bytes 356360 | tf_op jit(solution)/shard_map/ppermute | solution.py:78
  48.6 8.2 %collective-permute-start.9 = (f32[232,128]{1,0:T(8,128)S(1)}, f32[232,128]{1,0:T(8,128)S(1)}, u32[]{:S(2)}, u32[]{:S(2)}) collective-permute-start(f32[232,128]{1,0:T(8,128)S(1)} %dynamic-slice_add_fusion.5), channel_id=1, source_target_pairs={{0,16},{4,20},{8,24},{12,28},{16,0},{20,4},{24,8},{28,12},{1,17},{... | collective-permute-start | bytes 356360 | tf_op jit(solution)/shard_map/ppermute | solution.py:78
  55.1 7.4 %collective-permute-start.4 = (f32[464,128]{1,0:T(8,128)S(1)}, f32[464,128]{1,0:T(8,128)S(1)}, u32[]{:S(2)}, u32[]{:S(2)}) collective-permute-start(f32[464,128]{1,0:T(8,128)S(1)} %pad_maximum_fusion.13), channel_id=1, source_target_pairs={{0,8},{4,12},{8,0},{12,4},{16,24},{20,28},{24,16},{28,20},{1,9},{5... | collective-permute-start | bytes 712712 | tf_op jit(solution)/shard_map/ppermute | solution.py:78
  56.9 7.2 %collective-permute-start.10 = (f32[464,128]{1,0:T(8,128)S(1)}, f32[464,128]{1,0:T(8,128)S(1)}, u32[]{:S(2)}, u32[]{:S(2)}) collective-permute-start(f32[464,128]{1,0:T(8,128)S(1)} %pad_maximum_fusion.14), channel_id=1, source_target_pairs={{0,4},{4,0},{8,12},{12,8},{16,20},{20,16},{24,28},{28,24},{1,5},{5... | collective-permute-start | bytes 712712 | tf_op jit(solution)/shard_map/ppermute | solution.py:78
  62.5 6.4 %copy-start = (f32[1600,256]{1,0:T(8,128)S(1)}, f32[1600,256]{1,0:T(8,128)}, u32[]{:S(2)}) copy-start(f32[1600,256]{1,0:T(8,128)} %param.18) | copy-start | bytes 4915204
  62.5 11.7 %collective-permute-start.5 = (f32[928,128]{1,0:T(8,128)S(1)}, f32[928,128]{1,0:T(8,128)S(1)}, u32[]{:S(2)}, u32[]{:S(2)}) collective-permute-start(f32[928,128]{1,0:T(8,128)S(1)} %pad_maximum_fusion.8), channel_id=1, source_target_pairs={{0,4},{4,0},{8,12},{12,8},{16,20},{20,16},{24,28},{28,24},{1,5},{5... | collective-permute-start | bytes 1425416 | tf_op jit(solution)/shard_map/ppermute | solution.py:78
  64.2 12.7 %collective-permute-start.11 = (f32[928,128]{1,0:T(8,128)S(1)}, f32[928,128]{1,0:T(8,128)S(1)}, u32[]{:S(2)}, u32[]{:S(2)}) collective-permute-start(f32[928,128]{1,0:T(8,128)S(1)} %pad_maximum_fusion.9), channel_id=1, source_target_pairs={{0,8},{4,12},{8,0},{12,4},{16,24},{20,28},{24,16},{28,20},{1,9},{5... | collective-permute-start | bytes 1425416 | tf_op jit(solution)/shard_map/ppermute | solution.py:78
  77.0 1.9 copy-start.1
  81.2 13.6 %collective-permute-start.12 = (f32[8,128]{1,0:T(8,128)S(1)}, f32[8,128]{1,0:T(8,128)S(1)}, u32[]{:S(2)}, u32[]{:S(2)}) collective-permute-start(f32[8,128]{1,0:T(8,128)S(1)} %broadcast_in_dim.6), channel_id=1, source_target_pairs={{0,1},{1,0},{2,3},{3,2},{4,5},{5,4},{6,7},{7,6},{8,9},{9,8},{10,11... | collective-permute-start | bytes 12296 | tf_op jit(solution)/shard_map/ppermute | solution.py:78
  86.1 1.5 copy-start.6
  86.1 1.4 copy-start.7
  87.1 33.9 %collective-permute-start.27 = (f32[896,128]{1,0:T(8,128)}, f32[896,128]{1,0:T(8,128)}, u32[]{:S(2)}, u32[]{:S(2)}) collective-permute-start(f32[896,128]{1,0:T(8,128)} %pad_dynamic-slice_fusion.2), channel_id=1, source_target_pairs={{0,1},{1,0},{2,3},{3,2},{4,5},{5,4},{6,7},{7,6},{8,9},{9,8},{10,11... | collective-permute-start | bytes 1376264 | tf_op jit(solution)/shard_map/ppermute | solution.py:78
  92.4 7.9 %copy-start.9 = (f32[1,1,4,1600]{3,2,1,0:T(4,128)S(1)}, f32[1,1,4,1600]{3,2,1,0:T(4,128)}, u32[]{:S(2)}) copy-start(f32[1,1,4,1600]{3,2,1,0:T(4,128)} %param.26) | copy-start | bytes 76804
  92.4 7.9 %copy-start.10 = (f32[1,1,4,1600]{3,2,1,0:T(4,128)S(1)}, f32[1,1,4,1600]{3,2,1,0:T(4,128)}, u32[]{:S(2)}) copy-start(f32[1,1,4,1600]{3,2,1,0:T(4,128)} %param.25) | copy-start | bytes 76804
  94.8 3.6 %collective-permute-start.13 = (f32[8,128]{1,0:T(8,128)S(1)}, f32[8,128]{1,0:T(8,128)S(1)}, u32[]{:S(2)}, u32[]{:S(2)}) collective-permute-start(f32[8,128]{1,0:T(8,128)S(1)} %broadcast_add_fusion), channel_id=1, source_target_pairs={{0,2},{1,3},{2,0},{3,1},{4,6},{5,7},{6,4},{7,5},{8,10},{9,11},{10,... | collective-permute-start | bytes 12296 | tf_op jit(solution)/shard_map/ppermute | solution.py:78
  97.1 25.5 %collective-permute-start.17 = (f32[896,128]{1,0:T(8,128)}, f32[896,128]{1,0:T(8,128)}, u32[]{:S(2)}, u32[]{:S(2)}) collective-permute-start(f32[896,128]{1,0:T(8,128)} %pad_dynamic-slice_fusion.4), channel_id=1, source_target_pairs={{0,1},{1,0},{2,3},{3,2},{4,5},{5,4},{6,7},{7,6},{8,9},{9,8},{10,11... | collective-permute-start | bytes 1376264 | tf_op jit(solution)/shard_map/ppermute | solution.py:78
  101.8 11.2 %copy-start.11 = (f32[4,1600]{1,0:T(4,128)S(1)}, f32[4,1600]{1,0:T(4,128)}, u32[]{:S(2)}) copy-start(f32[4,1600]{1,0:T(4,128)} %param.21) | copy-start | bytes 76804
  101.8 11.1 %copy-start.12 = (f32[4,1600]{1,0:T(4,128)S(1)}, f32[4,1600]{1,0:T(4,128)}, u32[]{:S(2)}) copy-start(f32[4,1600]{1,0:T(4,128)} %param.23) | copy-start | bytes 76804
  101.9 11.1 %copy-start.13 = (f32[4,1600]{1,0:T(4,128)S(1)}, f32[4,1600]{1,0:T(4,128)}, u32[]{:S(2)}) copy-start(f32[4,1600]{1,0:T(4,128)} %param.22) | copy-start | bytes 76804
  103.8 8.4 %collective-permute-start.14 = (bf16[1,250,256]{2,1,0:T(8,128)(2,1)S(1)}, bf16[1,250,256]{2,1,0:T(8,128)(2,1)S(1)}, u32[]{:S(2)}, u32[]{:S(2)}) collective-permute-start(bf16[1,250,256]{2,1,0:T(8,128)(2,1)S(1)} %maximum_bitcast_fusion), channel_id=1, source_target_pairs={{0,16},{4,20},{8,24},{12,28},{16,0},{20,4},{24,8},{28,12},{1,17},{... | collective-permute-start | bytes 384008 | tf_op jit(solution)/shard_map/ppermute | solution.py:78
  112.3 6.9 %collective-permute-start.15 = (bf16[2,250,256]{2,1,0:T(8,128)(2,1)S(1)}, bf16[2,250,256]{2,1,0:T(8,128)(2,1)S(1)}, u32[]{:S(2)}, u32[]{:S(2)}) collective-permute-start(bf16[2,250,256]{2,1,0:T(8,128)(2,1)S(1)} %pad_maximum_fusion.12), channel_id=1, source_target_pairs={{0,8},{4,12},{8,0},{12,4},{16,24},{20,28},{24,16},{28,20},{1,9},{5... | collective-permute-start | bytes 768008 | tf_op jit(solution)/shard_map/ppermute | solution.py:78
  119.3 37.2 %collective-permute-start.16 = (bf16[4,250,256]{2,1,0:T(8,128)(2,1)S(1)}, bf16[4,250,256]{2,1,0:T(8,128)(2,1)S(1)}, u32[]{:S(2)}, u32[]{:S(2)}) collective-permute-start(bf16[4,250,256]{2,1,0:T(8,128)(2,1)S(1)} %pad_maximum_fusion.7), channel_id=1, source_target_pairs={{0,4},{4,0},{8,12},{12,8},{16,20},{20,16},{24,28},{28,24},{1,5},{5... | collective-permute-start | bytes 1536008 | tf_op jit(solution)/shard_map/ppermute | solution.py:78
  122.0 14.3 %collective-permute-start.28 = (f32[448,128]{1,0:T(8,128)S(1)}, f32[448,128]{1,0:T(8,128)S(1)}, u32[]{:S(2)}, u32[]{:S(2)}) collective-permute-start(f32[448,128]{1,0:T(8,128)S(1)} %constant_dynamic-slice_fusion.3), channel_id=1, source_target_pairs={{0,4},{4,0},{8,12},{12,8},{16,20},{20,16},{24,28},{28,24},{1,5},{5... | collective-permute-start | bytes 688136 | tf_op jit(solution)/shard_map/ppermute | solution.py:78
  123.7 15.2 %collective-permute-start.18 = (f32[448,128]{1,0:T(8,128)S(1)}, f32[448,128]{1,0:T(8,128)S(1)}, u32[]{:S(2)}, u32[]{:S(2)}) collective-permute-start(f32[448,128]{1,0:T(8,128)S(1)} %constant_dynamic-slice_fusion.7), channel_id=1, source_target_pairs={{0,2},{1,3},{2,0},{3,1},{4,6},{5,7},{6,4},{7,5},{8,10},{9,11},{10,... | collective-permute-start | bytes 688136 | tf_op jit(solution)/shard_map/ppermute | solution.py:78
  136.4 5.3 %collective-permute-start.29 = (f32[224,128]{1,0:T(8,128)S(1)}, f32[224,128]{1,0:T(8,128)S(1)}, u32[]{:S(2)}, u32[]{:S(2)}) collective-permute-start(f32[224,128]{1,0:T(8,128)S(1)} %constant_dynamic-slice_fusion.2), channel_id=1, source_target_pairs={{0,8},{4,12},{8,0},{12,4},{16,24},{20,28},{24,16},{28,20},{1,9},{5... | collective-permute-start | bytes 344072 | tf_op jit(solution)/shard_map/ppermute | solution.py:78
  139.0 4.9 %collective-permute-start.19 = (f32[224,128]{1,0:T(8,128)S(1)}, f32[224,128]{1,0:T(8,128)S(1)}, u32[]{:S(2)}, u32[]{:S(2)}) collective-permute-start(f32[224,128]{1,0:T(8,128)S(1)} %constant_dynamic-slice_fusion.6), channel_id=1, source_target_pairs={{0,4},{4,0},{8,12},{12,8},{16,20},{20,16},{24,28},{28,24},{1,5},{5... | collective-permute-start | bytes 344072 | tf_op jit(solution)/shard_map/ppermute | solution.py:78
  141.7 4.2 %collective-permute-start.30 = (f32[112,128]{1,0:T(8,128)S(1)}, f32[112,128]{1,0:T(8,128)S(1)}, u32[]{:S(2)}, u32[]{:S(2)}) collective-permute-start(f32[112,128]{1,0:T(8,128)S(1)} %constant_dynamic-slice_fusion.1), channel_id=1, source_target_pairs={{0,2},{1,3},{2,0},{3,1},{4,6},{5,7},{6,4},{7,5},{8,10},{9,11},{10,... | collective-permute-start | bytes 172040 | tf_op jit(solution)/shard_map/ppermute | solution.py:78
  143.9 6.2 %collective-permute-start.20 = (f32[112,128]{1,0:T(8,128)S(1)}, f32[112,128]{1,0:T(8,128)S(1)}, u32[]{:S(2)}, u32[]{:S(2)}) collective-permute-start(f32[112,128]{1,0:T(8,128)S(1)} %constant_dynamic-slice_fusion.5), channel_id=1, source_target_pairs={{0,8},{4,12},{8,0},{12,4},{16,24},{20,28},{24,16},{28,20},{1,9},{5... | collective-permute-start | bytes 172040 | tf_op jit(solution)/shard_map/ppermute | solution.py:78
  146.0 6.0 %collective-permute-start.31 = (f32[56,128]{1,0:T(8,128)S(1)}, f32[56,128]{1,0:T(8,128)S(1)}, u32[]{:S(2)}, u32[]{:S(2)}) collective-permute-start(f32[56,128]{1,0:T(8,128)S(1)} %constant_dynamic-slice_fusion), channel_id=1, source_target_pairs={{0,16},{4,20},{8,24},{12,28},{16,0},{20,4},{24,8},{28,12},{1,17},{... | collective-permute-start | bytes 86024 | tf_op jit(solution)/shard_map/ppermute | solution.py:78
  150.1 5.0 %collective-permute-start.21 = (f32[56,128]{1,0:T(8,128)S(1)}, f32[56,128]{1,0:T(8,128)S(1)}, u32[]{:S(2)}, u32[]{:S(2)}) collective-permute-start(f32[56,128]{1,0:T(8,128)S(1)} %constant_dynamic-slice_fusion.4), channel_id=1, source_target_pairs={{0,16},{4,20},{8,24},{12,28},{16,0},{20,4},{24,8},{28,12},{1,17},{... | collective-permute-start | bytes 86024 | tf_op jit(solution)/shard_map/ppermute | solution.py:78
  152.1 21.1 %collective-permute-start.32 = (f32[56,128]{1,0:T(8,128)S(1)}, f32[56,128]{1,0:T(8,128)S(1)}, u32[]{:S(2)}, u32[]{:S(2)}) collective-permute-start(f32[56,128]{1,0:T(8,128)S(1)} %dynamic-slice_add_fusion.11), channel_id=1, source_target_pairs={{0,16},{4,20},{8,24},{12,28},{16,0},{20,4},{24,8},{28,12},{1,17},{... | collective-permute-start | bytes 86024 | tf_op jit(solution)/shard_map/ppermute | solution.py:78
  155.0 19.3 %collective-permute-start.22 = (f32[56,128]{1,0:T(8,128)S(1)}, f32[56,128]{1,0:T(8,128)S(1)}, u32[]{:S(2)}, u32[]{:S(2)}) collective-permute-start(f32[56,128]{1,0:T(8,128)S(1)} %dynamic-slice_add_fusion.12), channel_id=1, source_target_pairs={{0,16},{4,20},{8,24},{12,28},{16,0},{20,4},{24,8},{28,12},{1,17},{... | collective-permute-start | bytes 86024 | tf_op jit(solution)/shard_map/ppermute | solution.py:78
  156.7 1.1 copy-start.4
  156.8 1.4 copy-start.5
  173.2 4.2 %collective-permute-start.33 = (f32[112,128]{1,0:T(8,128)S(1)}, f32[112,128]{1,0:T(8,128)S(1)}, u32[]{:S(2)}, u32[]{:S(2)}) collective-permute-start(f32[112,128]{1,0:T(8,128)S(1)} %pad_maximum_fusion.21), channel_id=1, source_target_pairs={{0,2},{1,3},{2,0},{3,1},{4,6},{5,7},{6,4},{7,5},{8,10},{9,11},{10,... | collective-permute-start | bytes 172040 | tf_op jit(solution)/shard_map/ppermute | solution.py:78
  174.4 4.2 %collective-permute-start.23 = (f32[112,128]{1,0:T(8,128)S(1)}, f32[112,128]{1,0:T(8,128)S(1)}, u32[]{:S(2)}, u32[]{:S(2)}) collective-permute-start(f32[112,128]{1,0:T(8,128)S(1)} %pad_maximum_fusion.20), channel_id=1, source_target_pairs={{0,8},{4,12},{8,0},{12,4},{16,24},{20,28},{24,16},{28,20},{1,9},{5... | collective-permute-start | bytes 172040 | tf_op jit(solution)/shard_map/ppermute | solution.py:78
  177.5 4.9 %collective-permute-start.34 = (f32[224,128]{1,0:T(8,128)S(1)}, f32[224,128]{1,0:T(8,128)S(1)}, u32[]{:S(2)}, u32[]{:S(2)}) collective-permute-start(f32[224,128]{1,0:T(8,128)S(1)} %pad_maximum_fusion.19), channel_id=1, source_target_pairs={{0,8},{4,12},{8,0},{12,4},{16,24},{20,28},{24,16},{28,20},{1,9},{5... | collective-permute-start | bytes 344072 | tf_op jit(solution)/shard_map/ppermute | solution.py:78
  178.7 5.3 %collective-permute-start.24 = (f32[224,128]{1,0:T(8,128)S(1)}, f32[224,128]{1,0:T(8,128)S(1)}, u32[]{:S(2)}, u32[]{:S(2)}) collective-permute-start(f32[224,128]{1,0:T(8,128)S(1)} %pad_maximum_fusion.18), channel_id=1, source_target_pairs={{0,4},{4,0},{8,12},{12,8},{16,20},{20,16},{24,28},{28,24},{1,5},{5... | collective-permute-start | bytes 344072 | tf_op jit(solution)/shard_map/ppermute | solution.py:78
  182.4 6.1 %collective-permute-start.35 = (f32[448,128]{1,0:T(8,128)S(1)}, f32[448,128]{1,0:T(8,128)S(1)}, u32[]{:S(2)}, u32[]{:S(2)}) collective-permute-start(f32[448,128]{1,0:T(8,128)S(1)} %pad_maximum_fusion.16), channel_id=1, source_target_pairs={{0,4},{4,0},{8,12},{12,8},{16,20},{20,16},{24,28},{28,24},{1,5},{5... | collective-permute-start | bytes 688136 | tf_op jit(solution)/shard_map/ppermute | solution.py:78
  184.1 6.3 %copy-start.8 = (bf16[1,8,4,1600]{3,2,1,0:T(4,128)(2,1)S(1)}, bf16[1,8,4,1600]{3,2,1,0:T(4,128)(2,1)}, u32[]{:S(2)}) copy-start(bf16[1,8,4,1600]{3,2,1,0:T(4,128)(2,1)} %param.24) | copy-start | bytes 307204
  184.1 6.1 %collective-permute-start.25 = (f32[448,128]{1,0:T(8,128)S(1)}, f32[448,128]{1,0:T(8,128)S(1)}, u32[]{:S(2)}, u32[]{:S(2)}) collective-permute-start(f32[448,128]{1,0:T(8,128)S(1)} %pad_maximum_fusion.15), channel_id=1, source_target_pairs={{0,2},{1,3},{2,0},{3,1},{4,6},{5,7},{6,4},{7,5},{8,10},{9,11},{10,... | collective-permute-start | bytes 688136 | tf_op jit(solution)/shard_map/ppermute | solution.py:78
  188.6 2.5 %collective-permute-start.36 = (f32[896,128]{1,0:T(8,128)S(1)}, f32[896,128]{1,0:T(8,128)S(1)}, u32[]{:S(2)}, u32[]{:S(2)}) collective-permute-start(f32[896,128]{1,0:T(8,128)S(1)} %pad_maximum_fusion.11), channel_id=1, source_target_pairs={{0,1},{1,0},{2,3},{3,2},{4,5},{5,4},{6,7},{7,6},{8,9},{9,8},{10,11... | collective-permute-start | bytes 1376264 | tf_op jit(solution)/shard_map/ppermute | solution.py:78
  190.2 1.9 collective-permute-start.26

commit v2 on v1

--- a/solution.py
+++ b/solution.py
@@ -3,6 +3,7 @@
 import jax
 import jax.numpy as jnp
 from jax import lax
+from jax.experimental import pallas as pl
 from jax.sharding import PartitionSpec as P
 
 FF = 6400
@@ -165,6 +166,36 @@
     parts = parts.reshape((2,) * levels + piece.shape)
     order = tuple(reversed(range(levels))) + tuple(range(levels, levels + piece.ndim))
     return parts.transpose(order).reshape((size,) + piece.shape)
+
+
+def update_kernel(direction_ref, basis_ref, weight_ref, out_ref):
+    update = lax.dot_general(
+        direction_ref[0],
+        basis_ref[...],
+        (((1,), (1,)), ((), ())),
+        preferred_element_type=jnp.float32,
+    )
+    out_ref[0] = (
+        weight_ref[0].astype(jnp.float32) - learn_rate * galore_scale * update
+    ).astype(out_ref.dtype)
+
+
+def updated_weights(direction_bf16, basis, weights):
+    blocks, rows, width = weights.shape
+    pieces = split2(basis)
+    depth = pieces.shape[1]
+    doubled = jnp.concatenate([direction_bf16] * 2, axis=1).reshape(blocks, rows, depth)
+    return pl.pallas_call(
+        update_kernel,
+        out_shape=jax.ShapeDtypeStruct(weights.shape, jnp.bfloat16),
+        grid=(blocks,),
+        in_specs=[
+            pl.BlockSpec((1, rows, depth), lambda index: (index, 0, 0)),
+            pl.BlockSpec((width, depth), lambda index: (0, 0)),
+            pl.BlockSpec((1, rows, width), lambda index: (index, 0, 0)),
+        ],
+        out_specs=pl.BlockSpec((1, rows, width), lambda index: (index, 0, 0)),
+    )(doubled, pieces, weights)
 
 
 def split2(values):
@@ -261,16 +292,7 @@
     )(gathered)
     fc_dir_all = fc_dir_all.reshape(replicas * row_count, rank_cols)
     emb_dir_all = emb_dir_all[:, 0].astype(jnp.float32) + emb_dir_all[:, 1].astype(jnp.float32)
-    update_rows = lax.dot_general(
-        jnp.concatenate([fc_dir_all] * 2, axis=1),
-        split2(basis),
-        (((1,), (1,)), ((), ())),
-        preferred_element_type=jnp.float32,
-    )
-    weights_next = (
-        weights_fc.astype(jnp.float32)
-        - learn_rate * galore_scale * update_rows.reshape(weights_fc.shape)
-    ).astype(jnp.bfloat16)
+    weights_next = updated_weights(fc_dir_all, basis, weights_fc[0]).reshape(weights_fc.shape)
     emb_next = (
         emb_weights.astype(jnp.float32) - learn_rate * emb_dir_all.reshape(emb_weights.shape)
     ).astype(jnp.bfloat16)

time: 208 us -> 206 us (level)
  Pallas kernels: 0 us -> 10.6 us
  other arithmetic: 28.4 us -> 22 us
  matrix products: 37.3 us -> 31.3 us
  starting transfers between devices: 53.7 us -> 51.4 us
    pallas_call x0 -> x1, Pallas kernels: none -> 10.6 us  [updated_weights(): pl.pallas_call(update_kernel, out_shape=jax.ShapeDtypeStruct(weights.shap...]
    convert_element_type x1 -> x0, other arithmetic: 8.97 us -> none  [shards(): weights_next = (weights_fc.astype(jnp.float32) - learn_rate * galore_scal...]
    dot_general x1 -> x0, matrix products: 5.77 us -> none  [shards(): lax.dot_general(jnp.concatenate([fc_dir_all] * 2, axis=1), split2(basis),...]
    concatenate x0 -> x2, other arithmetic: none -> 2.63 us  [the longest x1 1.34 us: split2(): return jnp.concatenate([first, second], axis=1)]
    ppermute x37, starting transfers between devices: 53.7 us -> 51.4 us  [swap_with(): lax.ppermute(values, name, [(index, index ^ bit) for index in range(size)])]
  transfers between devices with their start and end apart: 37 -> 37, of which waited for: 24 -> 26; matrix products, arithmetic and copies ran while one was open for 22% -> 17% of each run, Pallas kernels for 0% -> 5%
where the time goes in v2:
time: 206 us; the launch traced here: 205 us
  waiting for transfers between devices  75.1 us (36%)
  starting transfers between devices  51.4 us (25%)
  matrix products  31.3 us (15%)
  other arithmetic  22 us (11%)
  Pallas kernels  10.6 us (5%)
  local copies, waits for them, and re-layouts  8.5 us (4%)
  between operations  5.76 us (3%)
    ppermute x37, waiting for transfers between devices, swap_with(): lax.ppermute(values, name, [(index, index ^ bit) for index in range(size)])  75.1 us
    ppermute x37, starting transfers between devices, swap_with(): lax.ppermute(values, name, [(index, index ^ bit) for index in range(size)])  51.4 us
    dot_general x4, matrix products, exact_dot(): lax.dot_general(lhs_bf16, split2(rhs_f32), ((contract, (0,)), ((), ())),...  18 us
    pallas_call x1, Pallas kernels, updated_weights(): pl.pallas_call(update_kernel, out_shape=jax.ShapeDtypeStruct(weights.shap...  10.6 us
    dot_general x5, matrix products, orthogonalize(): gram_matrix = jnp.dot(iterate.T, iterate, precision=highest)  7.84 us
    dot_general x5, matrix products, orthogonalize(): jnp.dot(iterate, gram_matrix, precision=highest)  5.37 us
    add x16, other arithmetic, run_steps(): parts = keep + swap_with(send, name, bit, size)  4.51 us
  transfers between devices with their start and end apart: 37, of which 26 were waited for; matrix products, arithmetic and copies ran while one was open for 17% of the time, Pallas kernels for 5%

profile of v2, /device:TPU:0, one launch (start us, length us, event | category | flops | bytes accessed | tf_op | source)
XLA Modules:
  0.0 204.7 jit_solution(15377257669103934254)
XLA Ops:
  0.7 1.0 reshape.183
  1.7 2.2 %subtract_convert_fusion.4 = (bf16[1600,128]{1,0:T(8,128)(2,1)S(1)}, bf16[1600,128]{1,0:T(8,128)(2,1)S(1)}, bf16[1600,128]{1,0:T(8,128)(2,1)S(1)}, bf16[1600,128]{1,0:T(8,128)(2,1)S(1)}) fusion(f32[1600,256]{1,0:T(8,128)} %param.18), kind=kLoop, calls=%fused_computation.64 | loop fusion | flops 1228800 | bytes 4096000 | tf_op jit(solution)/shard_map/convert_element_type | solution.py:203
  3.9 4.2 %convolution_bitcast_fusion.1 = f32[1600,256]{1,0:T(8,128)S(1)} fusion(bf16[1600,1600]{1,0:T(8,128)(2,1)} %bitcast.77, bf16[1600,128]{1,0:T(8,128)(2,1)S(1)} %get-tuple-element.33, bf16[1600,128]{1,0:T(8,128)(2,1)S(1)} %get-tuple-element.34), kind=kOutput, calls=%fused_computation.11 | convolution fusion | flops 1312358400 | bytes 7577600 | tf_op jit(solution)/shard_map/dot_general | solution.py:209
  9.9 2.9 %collective-permute-start = (f32[928,128]{1,0:T(8,128)}, f32[928,128]{1,0:T(8,128)}, u32[]{:S(2)}, u32[]{:S(2)}) collective-permute-start(f32[928,128]{1,0:T(8,128)} %constant_dynamic-slice_fusion.12), channel_id=1, source_target_pairs={{0,4},{4,0},{8,12},{12,8},{16,20},{20,16},{24,28},{28,24},{1,5},{5... | collective-permute-start | bytes 1425416 | tf_op jit(solution)/shard_map/ppermute | solution.py:79
  12.9 4.2 %convolution_bitcast_fusion = f32[1600,256]{1,0:T(8,128)S(1)} fusion(bf16[1600,1600]{1,0:T(8,128)(2,1)} %bitcast.78, bf16[1600,128]{1,0:T(8,128)(2,1)S(1)} %get-tuple-element.37, bf16[1600,128]{1,0:T(8,128)(2,1)S(1)} %get-tuple-element.38), kind=kOutput, calls=%fused_computation.10 | convolution fusion | flops 1312358400 | bytes 7577600 | tf_op jit(solution)/shard_map/dot_general | solution.py:209
  19.0 1.6 collective-permute-start.6
  21.8 2.3 %collective-permute-done = f32[928,128]{1,0:T(8,128)} collective-permute-done((f32[928,128]{1,0:T(8,128)}, f32[928,128]{1,0:T(8,128)}, u32[]{:S(2)}, u32[]{:S(2)}) %collective-permute-start) | collective-permute-done | bytes 475168 | tf_op jit(solution)/shard_map/ppermute | solution.py:79
  24.0 1.1 dynamic-slice_add_fusion
  25.1 1.9 collective-permute-start.1
  27.0 6.1 %collective-permute-done.6 = f32[928,128]{1,0:T(8,128)} collective-permute-done((f32[928,128]{1,0:T(8,128)}, f32[928,128]{1,0:T(8,128)}, u32[]{:S(2)}, u32[]{:S(2)}) %collective-permute-start.6) | collective-permute-done | bytes 475168 | tf_op jit(solution)/shard_map/ppermute | solution.py:79
  33.1 1.1 fusion.26
  34.3 2.3 %collective-permute-done.1 = f32[464,128]{1,0:T(8,128)S(1)} collective-permute-done((f32[464,128]{1,0:T(8,128)S(1)}, f32[464,128]{1,0:T(8,128)S(1)}, u32[]{:S(2)}, u32[]{:S(2)}) %collective-permute-start.1) | collective-permute-done | bytes 237600 | tf_op jit(solution)/shard_map/ppermute | solution.py:79
  36.7 2.7 %collective-permute-start.2 = (f32[232,128]{1,0:T(8,128)S(1)}, f32[232,128]{1,0:T(8,128)S(1)}, u32[]{:S(2)}, u32[]{:S(2)}) collective-permute-start(f32[232,128]{1,0:T(8,128)S(1)} %constant_dynamic-slice_fusion.10), channel_id=1, source_target_pairs={{0,16},{4,20},{8,24},{12,28},{16,0},{20,4},{24,8},{28,12},{1,17},{... | collective-permute-start | bytes 356360 | tf_op jit(solution)/shard_map/ppermute | solution.py:79
  39.3 1.1 collective-permute-done.7
  40.5 2.7 %collective-permute-start.8 = (f32[232,128]{1,0:T(8,128)S(1)}, f32[232,128]{1,0:T(8,128)S(1)}, u32[]{:S(2)}, u32[]{:S(2)}) collective-permute-start(f32[232,128]{1,0:T(8,128)S(1)} %constant_dynamic-slice_fusion.8), channel_id=1, source_target_pairs={{0,16},{4,20},{8,24},{12,28},{16,0},{20,4},{24,8},{28,12},{1,17},{... | collective-permute-start | bytes 356360 | tf_op jit(solution)/shard_map/ppermute | solution.py:79
  43.1 4.6 %collective-permute-done.2 = f32[232,128]{1,0:T(8,128)S(1)} collective-permute-done((f32[232,128]{1,0:T(8,128)S(1)}, f32[232,128]{1,0:T(8,128)S(1)}, u32[]{:S(2)}, u32[]{:S(2)}) %collective-permute-start.2) | collective-permute-done | bytes 118816 | tf_op jit(solution)/shard_map/ppermute | solution.py:79
  47.8 2.4 %collective-permute-done.8 = f32[232,128]{1,0:T(8,128)S(1)} collective-permute-done((f32[232,128]{1,0:T(8,128)S(1)}, f32[232,128]{1,0:T(8,128)S(1)}, u32[]{:S(2)}, u32[]{:S(2)}) %collective-permute-start.8) | collective-permute-done | bytes 118816 | tf_op jit(solution)/shard_map/ppermute | solution.py:79
  50.8 5.9 %collective-permute-done.3 = f32[232,128]{1,0:T(8,128)S(1)} collective-permute-done((f32[232,128]{1,0:T(8,128)S(1)}, f32[232,128]{1,0:T(8,128)S(1)}, u32[]{:S(2)}, u32[]{:S(2)}) %collective-permute-start.3) | collective-permute-done | bytes 118816 | tf_op jit(solution)/shard_map/ppermute | solution.py:79
  56.7 1.9 collective-permute-start.4
  60.3 3.7 %collective-permute-done.4 = f32[464,128]{1,0:T(8,128)S(1)} collective-permute-done((f32[464,128]{1,0:T(8,128)S(1)}, f32[464,128]{1,0:T(8,128)S(1)}, u32[]{:S(2)}, u32[]{:S(2)}) %collective-permute-start.4) | collective-permute-done | bytes 237600 | tf_op jit(solution)/shard_map/ppermute | solution.py:79
  65.8 3.7 %collective-permute-start.11 = (f32[928,128]{1,0:T(8,128)S(1)}, f32[928,128]{1,0:T(8,128)S(1)}, u32[]{:S(2)}, u32[]{:S(2)}) collective-permute-start(f32[928,128]{1,0:T(8,128)S(1)} %pad_maximum_fusion.11), channel_id=1, source_target_pairs={{0,8},{4,12},{8,0},{12,4},{16,24},{20,28},{24,16},{28,20},{1,9},{5... | collective-permute-start | bytes 1425416 | tf_op jit(solution)/shard_map/ppermute | solution.py:79
  69.5 1.3 pad_maximum_fusion.4.basis_ref
  70.8 4.9 %collective-permute-done.5 = f32[928,128]{1,0:T(8,128)S(1)} collective-permute-done((f32[928,128]{1,0:T(8,128)S(1)}, f32[928,128]{1,0:T(8,128)S(1)}, u32[]{:S(2)}, u32[]{:S(2)}) %collective-permute-start.5) | collective-permute-done | bytes 475168 | tf_op jit(solution)/shard_map/ppermute | solution.py:79
  79.6 4.8 %convolution_bitcast_fusion.2 = f32[1600,256]{1,0:T(8,128)S(1)} fusion(bf16[1600,1600]{1,0:T(8,128)(2,1)} %bitcast.79, bf16[1600,128]{1,0:T(8,128)(2,1)S(1)} %get-tuple-element.17, bf16[1600,128]{1,0:T(8,128)(2,1)S(1)} %get-tuple-element.18), kind=kOutput, calls=%fused_computation.12 | convolution fusion | flops 1312358400 | bytes 7577600 | tf_op jit(solution)/shard_map/dot_general | solution.py:209
  85.9 4.8 %convolution_bitcast_fusion.3 = f32[1600,256]{1,0:T(8,128)S(1)} fusion(bf16[1600,1600]{1,0:T(8,128)(2,1)} %bitcast.80, bf16[1600,128]{1,0:T(8,128)(2,1)S(1)} %get-tuple-element.77, bf16[1600,128]{1,0:T(8,128)(2,1)S(1)} %get-tuple-element.78), kind=kOutput, calls=%fused_computation.13 | convolution fusion | flops 1312358400 | bytes 7577600 | tf_op jit(solution)/shard_map/dot_general | solution.py:209
  90.9 1.4 multiply_reduce_fusion.2
  92.2 1.0 reshape_reshape.4
  93.3 1.5 collective-permute-start.13
  95.6 1.3 collective-permute-done.13
  98.8 1.4 multiply_divide_fusion.2
  100.3 1.9 convert_bitcast_fusion
  102.3 4.5 %collective-permute-start.14 = (bf16[1,250,256]{2,1,0:T(8,128)(2,1)S(1)}, bf16[1,250,256]{2,1,0:T(8,128)(2,1)S(1)}, u32[]{:S(2)}, u32[]{:S(2)}) collective-permute-start(bf16[1,250,256]{2,1,0:T(8,128)(2,1)S(1)} %maximum_bitcast_fusion), channel_id=1, source_target_pairs={{0,16},{4,20},{8,24},{12,28},{16,0},{20,4},{24,8},{28,12},{1,17},{... | collective-permute-start | bytes 384008 | tf_op jit(solution)/shard_map/ppermute | solution.py:79
  107.6 4.9 %collective-permute-done.14 = bf16[1,250,256]{2,1,0:T(8,128)(2,1)S(1)} collective-permute-done((bf16[1,250,256]{2,1,0:T(8,128)(2,1)S(1)}, bf16[1,250,256]{2,1,0:T(8,128)(2,1)S(1)}, u32[]{:S(2)}, u32[]{:S(2)}) %collective-permute-start.14) | collective-permute-done | bytes 128032 | tf_op jit(solution)/shard_map/ppermute | solution.py:79
  114.0 5.6 %collective-permute-done.15 = bf16[2,250,256]{2,1,0:T(8,128)(2,1)S(1)} collective-permute-done((bf16[2,250,256]{2,1,0:T(8,128)(2,1)S(1)}, bf16[2,250,256]{2,1,0:T(8,128)(2,1)S(1)}, u32[]{:S(2)}, u32[]{:S(2)}) %collective-permute-start.15) | collective-permute-done | bytes 256032 | tf_op jit(solution)/shard_map/ppermute | solution.py:79
  119.7 1.6 collective-permute-start.16
  121.3 1.1 fusion.28
  123.0 1.1 fusion.27
  124.7 11.9 %collective-permute-done.28 = f32[448,128]{1,0:T(8,128)S(1)} collective-permute-done((f32[448,128]{1,0:T(8,128)S(1)}, f32[448,128]{1,0:T(8,128)S(1)}, u32[]{:S(2)}, u32[]{:S(2)}) %collective-permute-start.28) | collective-permute-done | bytes 229408 | tf_op jit(solution)/shard_map/ppermute | solution.py:79
  136.7 2.5 %collective-permute-start.29 = (f32[224,128]{1,0:T(8,128)S(1)}, f32[224,128]{1,0:T(8,128)S(1)}, u32[]{:S(2)}, u32[]{:S(2)}) collective-permute-start(f32[224,128]{1,0:T(8,128)S(1)} %constant_dynamic-slice_fusion.2), channel_id=1, source_target_pairs={{0,8},{4,12},{8,0},{12,4},{16,24},{20,28},{24,16},{28,20},{1,9},{5... | collective-permute-start | bytes 344072 | tf_op jit(solution)/shard_map/ppermute | solution.py:79
  139.3 1.5 collective-permute-start.19
  140.9 1.2 collective-permute-done.29
  142.2 2.0 collective-permute-done.19
  144.3 2.0 collective-permute-done.30
  146.4 4.0 %collective-permute-start.31 = (f32[56,128]{1,0:T(8,128)S(1)}, f32[56,128]{1,0:T(8,128)S(1)}, u32[]{:S(2)}, u32[]{:S(2)}) collective-permute-start(f32[56,128]{1,0:T(8,128)S(1)} %constant_dynamic-slice_fusion), channel_id=1, source_target_pairs={{0,16},{4,20},{8,24},{12,28},{16,0},{20,4},{24,8},{28,12},{1,17},{... | collective-permute-start | bytes 86024 | tf_op jit(solution)/shard_map/ppermute | solution.py:79
  150.4 1.7 collective-permute-start.21
  152.4 3.1 %collective-permute-start.32 = (f32[56,128]{1,0:T(8,128)S(1)}, f32[56,128]{1,0:T(8,128)S(1)}, u32[]{:S(2)}, u32[]{:S(2)}) collective-permute-start(f32[56,128]{1,0:T(8,128)S(1)} %dynamic-slice_add_fusion.11), channel_id=1, source_target_pairs={{0,16},{4,20},{8,24},{12,28},{16,0},{20,4},{24,8},{28,12},{1,17},{... | collective-permute-start | bytes 86024 | tf_op jit(solution)/shard_map/ppermute | solution.py:79
  155.5 1.5 collective-permute-start.22
  158.1 2.2 %collective-permute-done.22 = f32[56,128]{1,0:T(8,128)S(1)} collective-permute-done((f32[56,128]{1,0:T(8,128)S(1)}, f32[56,128]{1,0:T(8,128)S(1)}, u32[]{:S(2)}, u32[]{:S(2)}) %collective-permute-start.22) | collective-permute-done | bytes 28704 | tf_op jit(solution)/shard_map/ppermute | solution.py:79
  160.3 1.8 collective-permute-start.23
  162.1 1.2 collective-permute-start.34
  163.4 1.2 collective-permute-done.23
  164.6 1.5 collective-permute-start.24
  167.0 1.5 collective-permute-start.35
  169.6 3.5 %collective-permute-done.35 = f32[448,128]{1,0:T(8,128)S(1)} collective-permute-done((f32[448,128]{1,0:T(8,128)S(1)}, f32[448,128]{1,0:T(8,128)S(1)}, u32[]{:S(2)}, u32[]{:S(2)}) %collective-permute-start.35) | collective-permute-done | bytes 229408 | tf_op jit(solution)/shard_map/ppermute | solution.py:79
  173.3 2.3 %collective-permute-done.25 = f32[448,128]{1,0:T(8,128)S(1)} collective-permute-done((f32[448,128]{1,0:T(8,128)S(1)}, f32[448,128]{1,0:T(8,128)S(1)}, u32[]{:S(2)}, u32[]{:S(2)}) %collective-permute-start.25) | collective-permute-done | bytes 229408 | tf_op jit(solution)/shard_map/ppermute | solution.py:79
  176.6 1.3 pad_maximum_fusion.3.direction_ref
  177.9 10.6 %shard_map.221 = bf16[8,200,1600]{2,1,0:T(8,128)(2,1)} custom-call(bf16[8,200,512]{2,1,0:T(8,128)(2,1)} %pad_maximum_fusion.3.direction_ref, bf16[1600,512]{1,0:T(8,128)(2,1)} %pad_maximum_fusion.4.basis_ref, bf16[8,200,1600]{2,1,0:T(8,128)(2,1)} %bitcast.72), custom_call_target="tpu_custom_call" | custom-call | tf_op jit(solution)/shard_map/pallas_call | solution.py:188
  188.6 1.1 broadcast_select_fusion.11
  191.4 1.5 fusion.8
  193.7 1.6 fusion.50
  196.2 1.6 fusion.51
  198.6 1.6 fusion.52
  201.1 1.6 fusion.53
  202.7 2.0 fusion
  (153 shorter events, 26.9 us)
Async XLA Ops:
  1.7 2.2 %copy-start.2 = (f32[400,128]{1,0:T(8,128)}, f32[400,128]{1,0:T(8,128)S(1)}, u32[]{:S(2)}) copy-start(f32[400,128]{1,0:T(8,128)S(1)} %reshape.183) | copy-start | bytes 614404
  8.1 0.9 slice-start
  8.2 4.6 %copy-start.10 = (bf16[1,4,1600]{2,1,0:T(4,128)(2,1)S(1)}, bf16[1,4,1600]{2,1,0:T(4,128)(2,1)}, u32[]{:S(2)}) copy-start(bf16[1,4,1600]{2,1,0:T(4,128)(2,1)} %param.15) | copy-start | bytes 38404
  9.9 14.1 %collective-permute-start = (f32[928,128]{1,0:T(8,128)}, f32[928,128]{1,0:T(8,128)}, u32[]{:S(2)}, u32[]{:S(2)}) collective-permute-start(f32[928,128]{1,0:T(8,128)} %constant_dynamic-slice_fusion.12), channel_id=1, source_target_pairs={{0,4},{4,0},{8,12},{12,8},{16,20},{20,16},{24,28},{28,24},{1,5},{5... | collective-permute-start | bytes 1425416 | tf_op jit(solution)/shard_map/ppermute | solution.py:79
  17.1 0.9 copy-start.3
  18.1 2.5 %copy-start = (f32[1600,256]{1,0:T(8,128)S(1)}, f32[1600,256]{1,0:T(8,128)}, u32[]{:S(2)}) copy-start(f32[1600,256]{1,0:T(8,128)} %param.18) | copy-start | bytes 4915204
  19.0 14.1 %collective-permute-start.6 = (f32[928,128]{1,0:T(8,128)}, f32[928,128]{1,0:T(8,128)}, u32[]{:S(2)}, u32[]{:S(2)}) collective-permute-start(f32[928,128]{1,0:T(8,128)} %pad_dynamic-slice_fusion.6), channel_id=1, source_target_pairs={{0,8},{4,12},{8,0},{12,4},{16,24},{20,28},{24,16},{28,20},{1,9},{5... | collective-permute-start | bytes 1425416 | tf_op jit(solution)/shard_map/ppermute | solution.py:79
  25.1 11.5 %collective-permute-start.1 = (f32[464,128]{1,0:T(8,128)S(1)}, f32[464,128]{1,0:T(8,128)S(1)}, u32[]{:S(2)}, u32[]{:S(2)}) collective-permute-start(f32[464,128]{1,0:T(8,128)S(1)} %constant_dynamic-slice_fusion.11), channel_id=1, source_target_pairs={{0,8},{4,12},{8,0},{12,4},{16,24},{20,28},{24,16},{28,20},{1,9},{5... | collective-permute-start | bytes 712712 | tf_op jit(solution)/shard_map/ppermute | solution.py:79
  34.2 6.2 %collective-permute-start.7 = (f32[464,128]{1,0:T(8,128)S(1)}, f32[464,128]{1,0:T(8,128)S(1)}, u32[]{:S(2)}, u32[]{:S(2)}) collective-permute-start(f32[464,128]{1,0:T(8,128)S(1)} %constant_dynamic-slice_fusion.9), channel_id=1, source_target_pairs={{0,4},{4,0},{8,12},{12,8},{16,20},{20,16},{24,28},{28,24},{1,5},{5... | collective-permute-start | bytes 712712 | tf_op jit(solution)/shard_map/ppermute | solution.py:79
  36.7 11.0 %collective-permute-start.2 = (f32[232,128]{1,0:T(8,128)S(1)}, f32[232,128]{1,0:T(8,128)S(1)}, u32[]{:S(2)}, u32[]{:S(2)}) collective-permute-start(f32[232,128]{1,0:T(8,128)S(1)} %constant_dynamic-slice_fusion.10), channel_id=1, source_target_pairs={{0,16},{4,20},{8,24},{12,28},{16,0},{20,4},{24,8},{28,12},{1,17},{... | collective-permute-start | bytes 356360 | tf_op jit(solution)/shard_map/ppermute | solution.py:79
  40.5 9.8 %collective-permute-start.8 = (f32[232,128]{1,0:T(8,128)S(1)}, f32[232,128]{1,0:T(8,128)S(1)}, u32[]{:S(2)}, u32[]{:S(2)}) collective-permute-start(f32[232,128]{1,0:T(8,128)S(1)} %constant_dynamic-slice_fusion.8), channel_id=1, source_target_pairs={{0,16},{4,20},{8,24},{12,28},{16,0},{20,4},{24,8},{28,12},{1,17},{... | collective-permute-start | bytes 356360 | tf_op jit(solution)/shard_map/ppermute | solution.py:79
  47.7 9.0 %collective-permute-start.3 = (f32[232,128]{1,0:T(8,128)S(1)}, f32[232,128]{1,0:T(8,128)S(1)}, u32[]{:S(2)}, u32[]{:S(2)}) collective-permute-start(f32[232,128]{1,0:T(8,128)S(1)} %dynamic-slice_add_fusion.6), channel_id=1, source_target_pairs={{0,16},{4,20},{8,24},{12,28},{16,0},{20,4},{24,8},{28,12},{1,17},{... | collective-permute-start | bytes 356360 | tf_op jit(solution)/shard_map/ppermute | solution.py:79
  50.2 9.1 %collective-permute-start.9 = (f32[232,128]{1,0:T(8,128)S(1)}, f32[232,128]{1,0:T(8,128)S(1)}, u32[]{:S(2)}, u32[]{:S(2)}) collective-permute-start(f32[232,128]{1,0:T(8,128)S(1)} %dynamic-slice_add_fusion.5), channel_id=1, source_target_pairs={{0,16},{4,20},{8,24},{12,28},{16,0},{20,4},{24,8},{28,12},{1,17},{... | collective-permute-start | bytes 356360 | tf_op jit(solution)/shard_map/ppermute | solution.py:79
  56.7 7.2 %collective-permute-start.4 = (f32[464,128]{1,0:T(8,128)S(1)}, f32[464,128]{1,0:T(8,128)S(1)}, u32[]{:S(2)}, u32[]{:S(2)}) collective-permute-start(f32[464,128]{1,0:T(8,128)S(1)} %pad_maximum_fusion.15), channel_id=1, source_target_pairs={{0,8},{4,12},{8,0},{12,4},{16,24},{20,28},{24,16},{28,20},{1,9},{5... | collective-permute-start | bytes 712712 | tf_op jit(solution)/shard_map/ppermute | solution.py:79
  59.3 6.4 %collective-permute-start.10 = (f32[464,128]{1,0:T(8,128)S(1)}, f32[464,128]{1,0:T(8,128)S(1)}, u32[]{:S(2)}, u32[]{:S(2)}) collective-permute-start(f32[464,128]{1,0:T(8,128)S(1)} %pad_maximum_fusion.16), channel_id=1, source_target_pairs={{0,4},{4,0},{8,12},{12,8},{16,20},{20,16},{24,28},{28,24},{1,5},{5... | collective-permute-start | bytes 712712 | tf_op jit(solution)/shard_map/ppermute | solution.py:79
  64.0 11.7 %collective-permute-start.5 = (f32[928,128]{1,0:T(8,128)S(1)}, f32[928,128]{1,0:T(8,128)S(1)}, u32[]{:S(2)}, u32[]{:S(2)}) collective-permute-start(f32[928,128]{1,0:T(8,128)S(1)} %pad_maximum_fusion.10), channel_id=1, source_target_pairs={{0,4},{4,0},{8,12},{12,8},{16,20},{20,16},{24,28},{28,24},{1,5},{5... | collective-permute-start | bytes 1425416 | tf_op jit(solution)/shard_map/ppermute | solution.py:79
  65.8 10.3 %collective-permute-start.11 = (f32[928,128]{1,0:T(8,128)S(1)}, f32[928,128]{1,0:T(8,128)S(1)}, u32[]{:S(2)}, u32[]{:S(2)}) collective-permute-start(f32[928,128]{1,0:T(8,128)S(1)} %pad_maximum_fusion.11), channel_id=1, source_target_pairs={{0,8},{4,12},{8,0},{12,4},{16,24},{20,28},{24,16},{28,20},{1,9},{5... | collective-permute-start | bytes 1425416 | tf_op jit(solution)/shard_map/ppermute | solution.py:79
  76.2 1.0 copy-start.1
  79.6 13.7 %collective-permute-start.12 = (f32[8,128]{1,0:T(8,128)S(1)}, f32[8,128]{1,0:T(8,128)S(1)}, u32[]{:S(2)}, u32[]{:S(2)}) collective-permute-start(f32[8,128]{1,0:T(8,128)S(1)} %broadcast_in_dim.6), channel_id=1, source_target_pairs={{0,1},{1,0},{2,3},{3,2},{4,5},{5,4},{6,7},{7,6},{8,9},{9,8},{10,11... | collective-permute-start | bytes 12296 | tf_op jit(solution)/shard_map/ppermute | solution.py:79
  85.4 35.9 %collective-permute-start.27 = (f32[896,128]{1,0:T(8,128)}, f32[896,128]{1,0:T(8,128)}, u32[]{:S(2)}, u32[]{:S(2)}) collective-permute-start(f32[896,128]{1,0:T(8,128)} %pad_dynamic-slice_fusion.2), channel_id=1, source_target_pairs={{0,1},{1,0},{2,3},{3,2},{4,5},{5,4},{6,7},{7,6},{8,9},{9,8},{10,11... | collective-permute-start | bytes 1376264 | tf_op jit(solution)/shard_map/ppermute | solution.py:79
  90.7 8.0 %copy-start.5 = (f32[1,1,4,1600]{3,2,1,0:T(4,128)S(1)}, f32[1,1,4,1600]{3,2,1,0:T(4,128)}, u32[]{:S(2)}) copy-start(f32[1,1,4,1600]{3,2,1,0:T(4,128)} %param.26) | copy-start | bytes 76804
  90.8 8.0 %copy-start.6 = (f32[1,1,4,1600]{3,2,1,0:T(4,128)S(1)}, f32[1,1,4,1600]{3,2,1,0:T(4,128)}, u32[]{:S(2)}) copy-start(f32[1,1,4,1600]{3,2,1,0:T(4,128)} %param.25) | copy-start | bytes 76804
  93.3 3.6 %collective-permute-start.13 = (f32[8,128]{1,0:T(8,128)S(1)}, f32[8,128]{1,0:T(8,128)S(1)}, u32[]{:S(2)}, u32[]{:S(2)}) collective-permute-start(f32[8,128]{1,0:T(8,128)S(1)} %broadcast_add_fusion), channel_id=1, source_target_pairs={{0,2},{1,3},{2,0},{3,1},{4,6},{5,7},{6,4},{7,5},{8,10},{9,11},{10,... | collective-permute-start | bytes 12296 | tf_op jit(solution)/shard_map/ppermute | solution.py:79
  95.6 27.4 %collective-permute-start.17 = (f32[896,128]{1,0:T(8,128)}, f32[896,128]{1,0:T(8,128)}, u32[]{:S(2)}, u32[]{:S(2)}) collective-permute-start(f32[896,128]{1,0:T(8,128)} %pad_dynamic-slice_fusion.4), channel_id=1, source_target_pairs={{0,1},{1,0},{2,3},{3,2},{4,5},{5,4},{6,7},{7,6},{8,9},{9,8},{10,11... | collective-permute-start | bytes 1376264 | tf_op jit(solution)/shard_map/ppermute | solution.py:79
  100.3 13.0 %copy-start.7 = (f32[4,1600]{1,0:T(4,128)S(1)}, f32[4,1600]{1,0:T(4,128)}, u32[]{:S(2)}) copy-start(f32[4,1600]{1,0:T(4,128)} %param.21) | copy-start | bytes 76804
  100.3 13.0 %copy-start.8 = (f32[4,1600]{1,0:T(4,128)S(1)}, f32[4,1600]{1,0:T(4,128)}, u32[]{:S(2)}) copy-start(f32[4,1600]{1,0:T(4,128)} %param.23) | copy-start | bytes 76804
  100.3 13.0 %copy-start.9 = (f32[4,1600]{1,0:T(4,128)S(1)}, f32[4,1600]{1,0:T(4,128)}, u32[]{:S(2)}) copy-start(f32[4,1600]{1,0:T(4,128)} %param.22) | copy-start | bytes 76804
  102.3 10.2 %collective-permute-start.14 = (bf16[1,250,256]{2,1,0:T(8,128)(2,1)S(1)}, bf16[1,250,256]{2,1,0:T(8,128)(2,1)S(1)}, u32[]{:S(2)}, u32[]{:S(2)}) collective-permute-start(bf16[1,250,256]{2,1,0:T(8,128)(2,1)S(1)} %maximum_bitcast_fusion), channel_id=1, source_target_pairs={{0,16},{4,20},{8,24},{12,28},{16,0},{20,4},{24,8},{28,12},{1,17},{... | collective-permute-start | bytes 384008 | tf_op jit(solution)/shard_map/ppermute | solution.py:79
  112.5 7.0 %collective-permute-start.15 = (bf16[2,250,256]{2,1,0:T(8,128)(2,1)S(1)}, bf16[2,250,256]{2,1,0:T(8,128)(2,1)S(1)}, u32[]{:S(2)}, u32[]{:S(2)}) collective-permute-start(bf16[2,250,256]{2,1,0:T(8,128)(2,1)S(1)} %pad_maximum_fusion.14), channel_id=1, source_target_pairs={{0,8},{4,12},{8,0},{12,4},{16,24},{20,28},{24,16},{28,20},{1,9},{5... | collective-permute-start | bytes 768008 | tf_op jit(solution)/shard_map/ppermute | solution.py:79
  119.7 37.2 %collective-permute-start.16 = (bf16[4,250,256]{2,1,0:T(8,128)(2,1)S(1)}, bf16[4,250,256]{2,1,0:T(8,128)(2,1)S(1)}, u32[]{:S(2)}, u32[]{:S(2)}) collective-permute-start(bf16[4,250,256]{2,1,0:T(8,128)(2,1)S(1)} %pad_maximum_fusion.9), channel_id=1, source_target_pairs={{0,4},{4,0},{8,12},{12,8},{16,20},{20,16},{24,28},{28,24},{1,5},{5... | collective-permute-start | bytes 1536008 | tf_op jit(solution)/shard_map/ppermute | solution.py:79
  122.4 14.3 %collective-permute-start.28 = (f32[448,128]{1,0:T(8,128)S(1)}, f32[448,128]{1,0:T(8,128)S(1)}, u32[]{:S(2)}, u32[]{:S(2)}) collective-permute-start(f32[448,128]{1,0:T(8,128)S(1)} %constant_dynamic-slice_fusion.3), channel_id=1, source_target_pairs={{0,4},{4,0},{8,12},{12,8},{16,20},{20,16},{24,28},{28,24},{1,5},{5... | collective-permute-start | bytes 688136 | tf_op jit(solution)/shard_map/ppermute | solution.py:79
  124.1 15.2 %collective-permute-start.18 = (f32[448,128]{1,0:T(8,128)S(1)}, f32[448,128]{1,0:T(8,128)S(1)}, u32[]{:S(2)}, u32[]{:S(2)}) collective-permute-start(f32[448,128]{1,0:T(8,128)S(1)} %constant_dynamic-slice_fusion.7), channel_id=1, source_target_pairs={{0,2},{1,3},{2,0},{3,1},{4,6},{5,7},{6,4},{7,5},{8,10},{9,11},{10,... | collective-permute-start | bytes 688136 | tf_op jit(solution)/shard_map/ppermute | solution.py:79
  136.7 5.3 %collective-permute-start.29 = (f32[224,128]{1,0:T(8,128)S(1)}, f32[224,128]{1,0:T(8,128)S(1)}, u32[]{:S(2)}, u32[]{:S(2)}) collective-permute-start(f32[224,128]{1,0:T(8,128)S(1)} %constant_dynamic-slice_fusion.2), channel_id=1, source_target_pairs={{0,8},{4,12},{8,0},{12,4},{16,24},{20,28},{24,16},{28,20},{1,9},{5... | collective-permute-start | bytes 344072 | tf_op jit(solution)/shard_map/ppermute | solution.py:79
  139.3 4.9 %collective-permute-start.19 = (f32[224,128]{1,0:T(8,128)S(1)}, f32[224,128]{1,0:T(8,128)S(1)}, u32[]{:S(2)}, u32[]{:S(2)}) collective-permute-start(f32[224,128]{1,0:T(8,128)S(1)} %constant_dynamic-slice_fusion.6), channel_id=1, source_target_pairs={{0,4},{4,0},{8,12},{12,8},{16,20},{20,16},{24,28},{28,24},{1,5},{5... | collective-permute-start | bytes 344072 | tf_op jit(solution)/shard_map/ppermute | solution.py:79
  142.1 4.2 %collective-permute-start.30 = (f32[112,128]{1,0:T(8,128)S(1)}, f32[112,128]{1,0:T(8,128)S(1)}, u32[]{:S(2)}, u32[]{:S(2)}) collective-permute-start(f32[112,128]{1,0:T(8,128)S(1)} %constant_dynamic-slice_fusion.1), channel_id=1, source_target_pairs={{0,2},{1,3},{2,0},{3,1},{4,6},{5,7},{6,4},{7,5},{8,10},{9,11},{10,... | collective-permute-start | bytes 172040 | tf_op jit(solution)/shard_map/ppermute | solution.py:79
  144.2 6.2 %collective-permute-start.20 = (f32[112,128]{1,0:T(8,128)S(1)}, f32[112,128]{1,0:T(8,128)S(1)}, u32[]{:S(2)}, u32[]{:S(2)}) collective-permute-start(f32[112,128]{1,0:T(8,128)S(1)} %constant_dynamic-slice_fusion.5), channel_id=1, source_target_pairs={{0,8},{4,12},{8,0},{12,4},{16,24},{20,28},{24,16},{28,20},{1,9},{5... | collective-permute-start | bytes 172040 | tf_op jit(solution)/shard_map/ppermute | solution.py:79
  146.4 6.0 %collective-permute-start.31 = (f32[56,128]{1,0:T(8,128)S(1)}, f32[56,128]{1,0:T(8,128)S(1)}, u32[]{:S(2)}, u32[]{:S(2)}) collective-permute-start(f32[56,128]{1,0:T(8,128)S(1)} %constant_dynamic-slice_fusion), channel_id=1, source_target_pairs={{0,16},{4,20},{8,24},{12,28},{16,0},{20,4},{24,8},{28,12},{1,17},{... | collective-permute-start | bytes 86024 | tf_op jit(solution)/shard_map/ppermute | solution.py:79
  150.4 5.0 %collective-permute-start.21 = (f32[56,128]{1,0:T(8,128)S(1)}, f32[56,128]{1,0:T(8,128)S(1)}, u32[]{:S(2)}, u32[]{:S(2)}) collective-permute-start(f32[56,128]{1,0:T(8,128)S(1)} %constant_dynamic-slice_fusion.4), channel_id=1, source_target_pairs={{0,16},{4,20},{8,24},{12,28},{16,0},{20,4},{24,8},{28,12},{1,17},{... | collective-permute-start | bytes 86024 | tf_op jit(solution)/shard_map/ppermute | solution.py:79
  152.4 5.1 %collective-permute-start.32 = (f32[56,128]{1,0:T(8,128)S(1)}, f32[56,128]{1,0:T(8,128)S(1)}, u32[]{:S(2)}, u32[]{:S(2)}) collective-permute-start(f32[56,128]{1,0:T(8,128)S(1)} %dynamic-slice_add_fusion.11), channel_id=1, source_target_pairs={{0,16},{4,20},{8,24},{12,28},{16,0},{20,4},{24,8},{28,12},{1,17},{... | collective-permute-start | bytes 86024 | tf_op jit(solution)/shard_map/ppermute | solution.py:79
  155.5 4.8 %collective-permute-start.22 = (f32[56,128]{1,0:T(8,128)S(1)}, f32[56,128]{1,0:T(8,128)S(1)}, u32[]{:S(2)}, u32[]{:S(2)}) collective-permute-start(f32[56,128]{1,0:T(8,128)S(1)} %dynamic-slice_add_fusion.12), channel_id=1, source_target_pairs={{0,16},{4,20},{8,24},{12,28},{16,0},{20,4},{24,8},{28,12},{1,17},{... | collective-permute-start | bytes 86024 | tf_op jit(solution)/shard_map/ppermute | solution.py:79
  157.5 4.6 %collective-permute-start.33 = (f32[112,128]{1,0:T(8,128)S(1)}, f32[112,128]{1,0:T(8,128)S(1)}, u32[]{:S(2)}, u32[]{:S(2)}) collective-permute-start(f32[112,128]{1,0:T(8,128)S(1)} %pad_maximum_fusion.23), channel_id=1, source_target_pairs={{0,2},{1,3},{2,0},{3,1},{4,6},{5,7},{6,4},{7,5},{8,10},{9,11},{10,... | collective-permute-start | bytes 172040 | tf_op jit(solution)/shard_map/ppermute | solution.py:79
  160.3 4.2 %collective-permute-start.23 = (f32[112,128]{1,0:T(8,128)S(1)}, f32[112,128]{1,0:T(8,128)S(1)}, u32[]{:S(2)}, u32[]{:S(2)}) collective-permute-start(f32[112,128]{1,0:T(8,128)S(1)} %pad_maximum_fusion.22), channel_id=1, source_target_pairs={{0,8},{4,12},{8,0},{12,4},{16,24},{20,28},{24,16},{28,20},{1,9},{5... | collective-permute-start | bytes 172040 | tf_op jit(solution)/shard_map/ppermute | solution.py:79
  162.1 4.9 %collective-permute-start.34 = (f32[224,128]{1,0:T(8,128)S(1)}, f32[224,128]{1,0:T(8,128)S(1)}, u32[]{:S(2)}, u32[]{:S(2)}) collective-permute-start(f32[224,128]{1,0:T(8,128)S(1)} %pad_maximum_fusion.21), channel_id=1, source_target_pairs={{0,8},{4,12},{8,0},{12,4},{16,24},{20,28},{24,16},{28,20},{1,9},{5... | collective-permute-start | bytes 344072 | tf_op jit(solution)/shard_map/ppermute | solution.py:79
  164.6 4.9 %collective-permute-start.24 = (f32[224,128]{1,0:T(8,128)S(1)}, f32[224,128]{1,0:T(8,128)S(1)}, u32[]{:S(2)}, u32[]{:S(2)}) collective-permute-start(f32[224,128]{1,0:T(8,128)S(1)} %pad_maximum_fusion.20), channel_id=1, source_target_pairs={{0,4},{4,0},{8,12},{12,8},{16,20},{20,16},{24,28},{28,24},{1,5},{5... | collective-permute-start | bytes 344072 | tf_op jit(solution)/shard_map/ppermute | solution.py:79
  167.0 6.1 %collective-permute-start.35 = (f32[448,128]{1,0:T(8,128)S(1)}, f32[448,128]{1,0:T(8,128)S(1)}, u32[]{:S(2)}, u32[]{:S(2)}) collective-permute-start(f32[448,128]{1,0:T(8,128)S(1)} %pad_maximum_fusion.18), channel_id=1, source_target_pairs={{0,4},{4,0},{8,12},{12,8},{16,20},{20,16},{24,28},{28,24},{1,5},{5... | collective-permute-start | bytes 688136 | tf_op jit(solution)/shard_map/ppermute | solution.py:79
  169.5 6.3 %copy-start.4 = (bf16[1,8,4,1600]{3,2,1,0:T(4,128)(2,1)S(1)}, bf16[1,8,4,1600]{3,2,1,0:T(4,128)(2,1)}, u32[]{:S(2)}) copy-start(bf16[1,8,4,1600]{3,2,1,0:T(4,128)(2,1)} %param.24) | copy-start | bytes 307204
  169.5 6.1 %collective-permute-start.25 = (f32[448,128]{1,0:T(8,128)S(1)}, f32[448,128]{1,0:T(8,128)S(1)}, u32[]{:S(2)}, u32[]{:S(2)}) collective-permute-start(f32[448,128]{1,0:T(8,128)S(1)} %pad_maximum_fusion.17), channel_id=1, source_target_pairs={{0,2},{1,3},{2,0},{3,1},{4,6},{5,7},{6,4},{7,5},{8,10},{9,11},{10,... | collective-permute-start | bytes 688136 | tf_op jit(solution)/shard_map/ppermute | solution.py:79
  173.2 15.3 %collective-permute-start.36 = (f32[896,128]{1,0:T(8,128)S(1)}, f32[896,128]{1,0:T(8,128)S(1)}, u32[]{:S(2)}, u32[]{:S(2)}) collective-permute-start(f32[896,128]{1,0:T(8,128)S(1)} %pad_maximum_fusion.13), channel_id=1, source_target_pairs={{0,1},{1,0},{2,3},{3,2},{4,5},{5,4},{6,7},{7,6},{8,9},{9,8},{10,11... | collective-permute-start | bytes 1376264 | tf_op jit(solution)/shard_map/ppermute | solution.py:79
  175.7 12.9 %collective-permute-start.26 = (f32[896,128]{1,0:T(8,128)S(1)}, f32[896,128]{1,0:T(8,128)}, u32[]{:S(2)}, u32[]{:S(2)}) collective-permute-start(f32[896,128]{1,0:T(8,128)S(1)} %pad_maximum_fusion.12), channel_id=1, source_target_pairs={{0,1},{1,0},{2,3},{3,2},{4,5},{5,4},{6,7},{7,6},{8,9},{9,8},{10,11... | collective-permute-start | bytes 1376264 | tf_op jit(solution)/shard_map/ppermute | solution.py:79

commit v3 on v2

--- a/solution.py
+++ b/solution.py
@@ -172,7 +172,7 @@
     update = lax.dot_general(
         direction_ref[0],
         basis_ref[...],
-        (((1,), (1,)), ((), ())),
+        (((1,), (0,)), ((), ())),
         preferred_element_type=jnp.float32,
     )
     out_ref[0] = (
@@ -182,8 +182,8 @@
 
 def updated_weights(direction_bf16, basis, weights):
     blocks, rows, width = weights.shape
-    pieces = split2(basis)
-    depth = pieces.shape[1]
+    pieces = split2(basis).T
+    depth = pieces.shape[0]
     doubled = jnp.concatenate([direction_bf16] * 2, axis=1).reshape(blocks, rows, depth)
     return pl.pallas_call(
         update_kernel,
@@ -191,7 +191,7 @@
         grid=(blocks,),
         in_specs=[
             pl.BlockSpec((1, rows, depth), lambda index: (index, 0, 0)),
-            pl.BlockSpec((width, depth), lambda index: (0, 0)),
+            pl.BlockSpec((depth, width), lambda index: (0, 0)),
             pl.BlockSpec((1, rows, width), lambda index: (index, 0, 0)),
         ],
         out_specs=pl.BlockSpec((1, rows, width), lambda index: (index, 0, 0)),

time: 206 us -> 206 us (level)
  waiting for transfers between devices: 75.1 us -> 70 us
  other arithmetic: 22 us -> 26.5 us
  local copies, waits for them, and re-layouts: 8.5 us -> 12 us
    ppermute x37, waiting for transfers between devices: 75.1 us -> 70 us  [swap_with(): lax.ppermute(values, name, [(index, index ^ bit) for index in range(size)])]
    convert_element_type x3, other arithmetic: 2.72 us -> 5.11 us  [split2(): second = (values - first.astype(jnp.float32)).astype(jnp.bfloat16)]
  transfers between devices with their start and end apart: 37 -> 37, of which waited for: 26 -> 24; matrix products, arithmetic and copies ran while one was open for 17% -> 21% of each run, Pallas kernels for 5% -> 5%
where the time goes in v3:
time: 206 us; the launch traced here: 205 us
  waiting for transfers between devices  70 us (34%)
  starting transfers between devices  49.7 us (24%)
  matrix products  31.3 us (15%)
  other arithmetic  26.5 us (13%)
  local copies, waits for them, and re-layouts  12 us (6%)
  Pallas kernels  9.91 us (5%)
  between operations  5.67 us (3%)
    ppermute x37, waiting for transfers between devices, swap_with(): lax.ppermute(values, name, [(index, index ^ bit) for index in range(size)])  70 us
    ppermute x37, starting transfers between devices, swap_with(): lax.ppermute(values, name, [(index, index ^ bit) for index in range(size)])  49.7 us
    dot_general x4, matrix products, exact_dot(): lax.dot_general(lhs_bf16, split2(rhs_f32), ((contract, (0,)), ((), ())),...  18 us
    pallas_call x1, Pallas kernels, updated_weights(): pl.pallas_call(update_kernel, out_shape=jax.ShapeDtypeStruct(weights.shap...  9.91 us
    dot_general x5, matrix products, orthogonalize(): gram_matrix = jnp.dot(iterate.T, iterate, precision=highest)  7.84 us
    dot_general x5, matrix products, orthogonalize(): jnp.dot(iterate, gram_matrix, precision=highest)  5.38 us
    convert_element_type x3, other arithmetic, split2(): second = (values - first.astype(jnp.float32)).astype(jnp.bfloat16)  5.11 us
    add x16, other arithmetic, run_steps(): parts = keep + swap_with(send, name, bit, size)  4.52 us
  transfers between devices with their start and end apart: 37, of which 24 were waited for; matrix products, arithmetic and copies ran while one was open for 21% of the time, Pallas kernels for 5%

profile of v3, /device:TPU:0, one launch (start us, length us, event | category | flops | bytes accessed | tf_op | source)
XLA Modules:
  0.0 205.1 jit_solution(11278270058856433314)
XLA Ops:
  1.7 2.2 %subtract_convert_fusion.4 = (bf16[1600,128]{1,0:T(8,128)(2,1)S(1)}, bf16[1600,128]{1,0:T(8,128)(2,1)S(1)}, bf16[1600,128]{1,0:T(8,128)(2,1)S(1)}, bf16[1600,128]{1,0:T(8,128)(2,1)S(1)}) fusion(f32[1600,256]{1,0:T(8,128)} %param.18), kind=kLoop, calls=%fused_computation.64 | loop fusion | flops 1228800 | bytes 4096000 | tf_op jit(solution)/shard_map/convert_element_type | solution.py:203
  3.9 4.2 %convolution_bitcast_fusion.1 = f32[1600,256]{1,0:T(8,128)S(1)} fusion(bf16[1600,1600]{1,0:T(8,128)(2,1)} %bitcast.79, bf16[1600,128]{1,0:T(8,128)(2,1)S(1)} %get-tuple-element.31, bf16[1600,128]{1,0:T(8,128)(2,1)S(1)} %get-tuple-element.32), kind=kOutput, calls=%fused_computation.11 | convolution fusion | flops 1312358400 | bytes 7577600 | tf_op jit(solution)/shard_map/dot_general | solution.py:209
  10.8 2.9 %collective-permute-start = (f32[928,128]{1,0:T(8,128)}, f32[928,128]{1,0:T(8,128)}, u32[]{:S(2)}, u32[]{:S(2)}) collective-permute-start(f32[928,128]{1,0:T(8,128)} %constant_dynamic-slice_fusion.12), channel_id=1, source_target_pairs={{0,4},{4,0},{8,12},{12,8},{16,20},{20,16},{24,28},{28,24},{1,5},{5... | collective-permute-start | bytes 1425416 | tf_op jit(solution)/shard_map/ppermute | solution.py:79
  13.9 4.2 %convolution_bitcast_fusion = f32[1600,256]{1,0:T(8,128)S(1)} fusion(bf16[1600,1600]{1,0:T(8,128)(2,1)} %bitcast.80, bf16[1600,128]{1,0:T(8,128)(2,1)S(1)} %get-tuple-element.35, bf16[1600,128]{1,0:T(8,128)(2,1)S(1)} %get-tuple-element.36), kind=kOutput, calls=%fused_computation.10 | convolution fusion | flops 1312358400 | bytes 7577600 | tf_op jit(solution)/shard_map/dot_general | solution.py:209
  18.2 1.1 fusion.11
  20.2 1.6 collective-permute-start.6
  22.8 1.6 copy.35
  24.4 1.7 copy.36
  26.1 2.6 %subtract_convert_fusion = bf16[1600,256]{0,1:T(8,128)(2,1)} fusion(f32[1600,256]{0,1:T(8,128)} %copy.35, bf16[1600,256]{0,1:T(8,128)(2,1)S(1)} %copy.36), kind=kLoop, calls=%fused_computation.18 | loop fusion | flops 1228800 | bytes 3276800 | tf_op jit(solution)/shard_map/convert_element_type | solution.py:203
  29.6 1.1 dynamic-slice_add_fusion
  31.2 1.9 collective-permute-done.6
  33.1 1.1 fusion.26
  35.0 2.8 %collective-permute-done.1 = f32[464,128]{1,0:T(8,128)S(1)} collective-permute-done((f32[464,128]{1,0:T(8,128)S(1)}, f32[464,128]{1,0:T(8,128)S(1)}, u32[]{:S(2)}, u32[]{:S(2)}) %collective-permute-start.1) | collective-permute-done | bytes 237600 | tf_op jit(solution)/shard_map/ppermute | solution.py:79
  37.9 2.7 %collective-permute-start.2 = (f32[232,128]{1,0:T(8,128)S(1)}, f32[232,128]{1,0:T(8,128)S(1)}, u32[]{:S(2)}, u32[]{:S(2)}) collective-permute-start(f32[232,128]{1,0:T(8,128)S(1)} %constant_dynamic-slice_fusion.10), channel_id=1, source_target_pairs={{0,16},{4,20},{8,24},{12,28},{16,0},{20,4},{24,8},{28,12},{1,17},{... | collective-permute-start | bytes 356360 | tf_op jit(solution)/shard_map/ppermute | solution.py:79
  40.6 2.5 %collective-permute-start.8 = (f32[232,128]{1,0:T(8,128)S(1)}, f32[232,128]{1,0:T(8,128)S(1)}, u32[]{:S(2)}, u32[]{:S(2)}) collective-permute-start(f32[232,128]{1,0:T(8,128)S(1)} %constant_dynamic-slice_fusion.8), channel_id=1, source_target_pairs={{0,16},{4,20},{8,24},{12,28},{16,0},{20,4},{24,8},{28,12},{1,17},{... | collective-permute-start | bytes 356360 | tf_op jit(solution)/shard_map/ppermute | solution.py:79
  43.1 5.9 %collective-permute-done.2 = f32[232,128]{1,0:T(8,128)S(1)} collective-permute-done((f32[232,128]{1,0:T(8,128)S(1)}, f32[232,128]{1,0:T(8,128)S(1)}, u32[]{:S(2)}, u32[]{:S(2)}) %collective-permute-start.2) | collective-permute-done | bytes 118816 | tf_op jit(solution)/shard_map/ppermute | solution.py:79
  49.1 2.4 %collective-permute-done.8 = f32[232,128]{1,0:T(8,128)S(1)} collective-permute-done((f32[232,128]{1,0:T(8,128)S(1)}, f32[232,128]{1,0:T(8,128)S(1)}, u32[]{:S(2)}, u32[]{:S(2)}) %collective-permute-start.8) | collective-permute-done | bytes 118816 | tf_op jit(solution)/shard_map/ppermute | solution.py:79
  52.1 5.7 %collective-permute-done.3 = f32[232,128]{1,0:T(8,128)S(1)} collective-permute-done((f32[232,128]{1,0:T(8,128)S(1)}, f32[232,128]{1,0:T(8,128)S(1)}, u32[]{:S(2)}, u32[]{:S(2)}) %collective-permute-start.3) | collective-permute-done | bytes 118816 | tf_op jit(solution)/shard_map/ppermute | solution.py:79
  57.9 2.0 collective-permute-start.4
  61.1 4.1 %collective-permute-done.4 = f32[464,128]{1,0:T(8,128)S(1)} collective-permute-done((f32[464,128]{1,0:T(8,128)S(1)}, f32[464,128]{1,0:T(8,128)S(1)}, u32[]{:S(2)}, u32[]{:S(2)}) %collective-permute-start.4) | collective-permute-done | bytes 237600 | tf_op jit(solution)/shard_map/ppermute | solution.py:79
  65.7 1.1 collective-permute-done.10
  67.0 4.6 %collective-permute-start.11 = (f32[928,128]{1,0:T(8,128)S(1)}, f32[928,128]{1,0:T(8,128)S(1)}, u32[]{:S(2)}, u32[]{:S(2)}) collective-permute-start(f32[928,128]{1,0:T(8,128)S(1)} %pad_maximum_fusion.10), channel_id=1, source_target_pairs={{0,8},{4,12},{8,0},{12,4},{16,24},{20,28},{24,16},{28,20},{1,9},{5... | collective-permute-start | bytes 1425416 | tf_op jit(solution)/shard_map/ppermute | solution.py:79
  71.6 1.4 maximum_bitcast_fusion.basis_ref
  72.9 3.9 %collective-permute-done.5 = f32[928,128]{1,0:T(8,128)S(1)} collective-permute-done((f32[928,128]{1,0:T(8,128)S(1)}, f32[928,128]{1,0:T(8,128)S(1)}, u32[]{:S(2)}, u32[]{:S(2)}) %collective-permute-start.5) | collective-permute-done | bytes 475168 | tf_op jit(solution)/shard_map/ppermute | solution.py:79
  76.9 1.2 collective-permute-done.11
  81.7 4.8 %convolution_bitcast_fusion.2 = f32[1600,256]{1,0:T(8,128)S(1)} fusion(bf16[1600,1600]{1,0:T(8,128)(2,1)} %bitcast.81, bf16[1600,128]{1,0:T(8,128)(2,1)S(1)} %get-tuple-element.17, bf16[1600,128]{1,0:T(8,128)(2,1)S(1)} %get-tuple-element.18), kind=kOutput, calls=%fused_computation.12 | convolution fusion | flops 1312358400 | bytes 7577600 | tf_op jit(solution)/shard_map/dot_general | solution.py:209
  87.9 4.8 %convolution_bitcast_fusion.3 = f32[1600,256]{1,0:T(8,128)S(1)} fusion(bf16[1600,1600]{1,0:T(8,128)(2,1)} %bitcast.82, bf16[1600,128]{1,0:T(8,128)(2,1)S(1)} %get-tuple-element.75, bf16[1600,128]{1,0:T(8,128)(2,1)S(1)} %get-tuple-element.76), kind=kOutput, calls=%fused_computation.13 | convolution fusion | flops 1312358400 | bytes 7577600 | tf_op jit(solution)/shard_map/dot_general | solution.py:209
  92.9 1.4 multiply_reduce_fusion.2
  95.1 1.5 collective-permute-start.13
  97.5 1.3 collective-permute-done.13
  100.6 1.4 multiply_divide_fusion.2
  102.2 1.9 convert_bitcast_fusion
  104.2 3.5 %collective-permute-start.14 = (bf16[1,250,256]{2,1,0:T(8,128)(2,1)S(1)}, bf16[1,250,256]{2,1,0:T(8,128)(2,1)S(1)}, u32[]{:S(2)}, u32[]{:S(2)}) collective-permute-start(bf16[1,250,256]{2,1,0:T(8,128)(2,1)S(1)} %maximum_bitcast_fusion.1), channel_id=1, source_target_pairs={{0,16},{4,20},{8,24},{12,28},{16,0},{20,4},{24,8},{28,12},{1,17},{... | collective-permute-start | bytes 384008 | tf_op jit(solution)/shard_map/ppermute | solution.py:79
  108.5 4.9 %collective-permute-done.14 = bf16[1,250,256]{2,1,0:T(8,128)(2,1)S(1)} collective-permute-done((bf16[1,250,256]{2,1,0:T(8,128)(2,1)S(1)}, bf16[1,250,256]{2,1,0:T(8,128)(2,1)S(1)}, u32[]{:S(2)}, u32[]{:S(2)}) %collective-permute-start.14) | collective-permute-done | bytes 128032 | tf_op jit(solution)/shard_map/ppermute | solution.py:79
  114.9 5.6 %collective-permute-done.15 = bf16[2,250,256]{2,1,0:T(8,128)(2,1)S(1)} collective-permute-done((bf16[2,250,256]{2,1,0:T(8,128)(2,1)S(1)}, bf16[2,250,256]{2,1,0:T(8,128)(2,1)S(1)}, u32[]{:S(2)}, u32[]{:S(2)}) %collective-permute-start.15) | collective-permute-done | bytes 256032 | tf_op jit(solution)/shard_map/ppermute | solution.py:79
  120.6 1.6 collective-permute-start.16
  122.2 1.1 fusion.28
  125.6 12.0 %collective-permute-done.28 = f32[448,128]{1,0:T(8,128)S(1)} collective-permute-done((f32[448,128]{1,0:T(8,128)S(1)}, f32[448,128]{1,0:T(8,128)S(1)}, u32[]{:S(2)}, u32[]{:S(2)}) %collective-permute-start.28) | collective-permute-done | bytes 229408 | tf_op jit(solution)/shard_map/ppermute | solution.py:79
  137.7 2.5 %collective-permute-start.29 = (f32[224,128]{1,0:T(8,128)S(1)}, f32[224,128]{1,0:T(8,128)S(1)}, u32[]{:S(2)}, u32[]{:S(2)}) collective-permute-start(f32[224,128]{1,0:T(8,128)S(1)} %constant_dynamic-slice_fusion.2), channel_id=1, source_target_pairs={{0,8},{4,12},{8,0},{12,4},{16,24},{20,28},{24,16},{28,20},{1,9},{5... | collective-permute-start | bytes 344072 | tf_op jit(solution)/shard_map/ppermute | solution.py:79
  140.3 1.5 collective-permute-start.19
  141.8 1.2 collective-permute-done.29
  143.1 2.0 collective-permute-done.19
  145.3 2.0 collective-permute-done.30
  147.3 4.0 %collective-permute-start.31 = (f32[56,128]{1,0:T(8,128)S(1)}, f32[56,128]{1,0:T(8,128)S(1)}, u32[]{:S(2)}, u32[]{:S(2)}) collective-permute-start(f32[56,128]{1,0:T(8,128)S(1)} %constant_dynamic-slice_fusion), channel_id=1, source_target_pairs={{0,16},{4,20},{8,24},{12,28},{16,0},{20,4},{24,8},{28,12},{1,17},{... | collective-permute-start | bytes 86024 | tf_op jit(solution)/shard_map/ppermute | solution.py:79
  151.4 1.7 collective-permute-start.21
  153.3 3.1 %collective-permute-start.32 = (f32[56,128]{1,0:T(8,128)S(1)}, f32[56,128]{1,0:T(8,128)S(1)}, u32[]{:S(2)}, u32[]{:S(2)}) collective-permute-start(f32[56,128]{1,0:T(8,128)S(1)} %dynamic-slice_add_fusion.11), channel_id=1, source_target_pairs={{0,16},{4,20},{8,24},{12,28},{16,0},{20,4},{24,8},{28,12},{1,17},{... | collective-permute-start | bytes 86024 | tf_op jit(solution)/shard_map/ppermute | solution.py:79
  156.4 1.5 collective-permute-start.22
  159.0 2.2 %collective-permute-done.22 = f32[56,128]{1,0:T(8,128)S(1)} collective-permute-done((f32[56,128]{1,0:T(8,128)S(1)}, f32[56,128]{1,0:T(8,128)S(1)}, u32[]{:S(2)}, u32[]{:S(2)}) %collective-permute-start.22) | collective-permute-done | bytes 28704 | tf_op jit(solution)/shard_map/ppermute | solution.py:79
  161.3 1.8 collective-permute-start.23
  163.1 1.3 collective-permute-start.34
  164.4 1.2 collective-permute-done.23
  165.6 1.5 collective-permute-start.24
  168.0 1.5 collective-permute-start.35
  170.6 3.5 %collective-permute-done.35 = f32[448,128]{1,0:T(8,128)S(1)} collective-permute-done((f32[448,128]{1,0:T(8,128)S(1)}, f32[448,128]{1,0:T(8,128)S(1)}, u32[]{:S(2)}, u32[]{:S(2)}) %collective-permute-start.35) | collective-permute-done | bytes 229408 | tf_op jit(solution)/shard_map/ppermute | solution.py:79
  174.2 2.3 %collective-permute-done.25 = f32[448,128]{1,0:T(8,128)S(1)} collective-permute-done((f32[448,128]{1,0:T(8,128)S(1)}, f32[448,128]{1,0:T(8,128)S(1)}, u32[]{:S(2)}, u32[]{:S(2)}) %collective-permute-start.25) | collective-permute-done | bytes 229408 | tf_op jit(solution)/shard_map/ppermute | solution.py:79
  177.8 1.3 pad_maximum_fusion.3.direction_ref
  179.1 9.9 %shard_map.221 = bf16[8,200,1600]{2,1,0:T(8,128)(2,1)} custom-call(bf16[8,200,512]{2,1,0:T(8,128)(2,1)} %pad_maximum_fusion.3.direction_ref, bf16[512,1600]{1,0:T(8,128)(2,1)} %maximum_bitcast_fusion.basis_ref, bf16[8,200,1600]{2,1,0:T(8,128)(2,1)} %bitcast.74), custom_call_target="tpu_custom_call" | custom-call | tf_op jit(solution)/shard_map/pallas_call | solution.py:188
  189.1 1.1 broadcast_select_fusion.11
  191.9 1.5 fusion.8
  194.2 1.6 fusion.50
  196.7 1.6 fusion.51
  199.1 1.6 fusion.52
  201.5 1.6 fusion.53
  203.1 2.0 fusion
  (160 shorter events, 30.2 us)
Async XLA Ops:
  1.7 2.2 %copy-start.5 = (f32[400,128]{1,0:T(8,128)}, f32[400,128]{1,0:T(8,128)S(1)}, u32[]{:S(2)}) copy-start(f32[400,128]{1,0:T(8,128)S(1)} %reshape.183) | copy-start | bytes 614404
  8.1 0.9 slice-start
  8.2 5.6 %copy-start.12 = (bf16[1,4,1600]{2,1,0:T(4,128)(2,1)S(1)}, bf16[1,4,1600]{2,1,0:T(4,128)(2,1)}, u32[]{:S(2)}) copy-start(bf16[1,4,1600]{2,1,0:T(4,128)(2,1)} %param.15) | copy-start | bytes 38404
  9.1 0.9 copy-start.1
  10.8 18.7 %collective-permute-start = (f32[928,128]{1,0:T(8,128)}, f32[928,128]{1,0:T(8,128)}, u32[]{:S(2)}, u32[]{:S(2)}) collective-permute-start(f32[928,128]{1,0:T(8,128)} %constant_dynamic-slice_fusion.12), channel_id=1, source_target_pairs={{0,4},{4,0},{8,12},{12,8},{16,20},{20,16},{24,28},{28,24},{1,5},{5... | collective-permute-start | bytes 1425416 | tf_op jit(solution)/shard_map/ppermute | solution.py:79
  18.2 3.6 %copy-start = (f32[1600,256]{1,0:T(8,128)S(1)}, f32[1600,256]{1,0:T(8,128)}, u32[]{:S(2)}) copy-start(f32[1600,256]{1,0:T(8,128)} %param.18) | copy-start | bytes 4915204
  20.2 12.9 %collective-permute-start.6 = (f32[928,128]{1,0:T(8,128)}, f32[928,128]{1,0:T(8,128)}, u32[]{:S(2)}, u32[]{:S(2)}) collective-permute-start(f32[928,128]{1,0:T(8,128)} %pad_dynamic-slice_fusion.6), channel_id=1, source_target_pairs={{0,8},{4,12},{8,0},{12,4},{16,24},{20,28},{24,16},{28,20},{1,9},{5... | collective-permute-start | bytes 1425416 | tf_op jit(solution)/shard_map/ppermute | solution.py:79
  26.1 3.5 %copy-start.2 = (f32[1856,128]{1,0:T(8,128)S(1)}, f32[1856,128]{1,0:T(8,128)}, u32[]{:S(2)}) copy-start(f32[1856,128]{1,0:T(8,128)} %copy-done.1) | copy-start | bytes 2850820
  30.7 7.1 %collective-permute-start.1 = (f32[464,128]{1,0:T(8,128)S(1)}, f32[464,128]{1,0:T(8,128)S(1)}, u32[]{:S(2)}, u32[]{:S(2)}) collective-permute-start(f32[464,128]{1,0:T(8,128)S(1)} %constant_dynamic-slice_fusion.11), channel_id=1, source_target_pairs={{0,8},{4,12},{8,0},{12,4},{16,24},{20,28},{24,16},{28,20},{1,9},{5... | collective-permute-start | bytes 712712 | tf_op jit(solution)/shard_map/ppermute | solution.py:79
  34.2 6.3 %collective-permute-start.7 = (f32[464,128]{1,0:T(8,128)S(1)}, f32[464,128]{1,0:T(8,128)S(1)}, u32[]{:S(2)}, u32[]{:S(2)}) collective-permute-start(f32[464,128]{1,0:T(8,128)S(1)} %constant_dynamic-slice_fusion.9), channel_id=1, source_target_pairs={{0,4},{4,0},{8,12},{12,8},{16,20},{20,16},{24,28},{28,24},{1,5},{5... | collective-permute-start | bytes 712712 | tf_op jit(solution)/shard_map/ppermute | solution.py:79
  37.9 11.2 %collective-permute-start.2 = (f32[232,128]{1,0:T(8,128)S(1)}, f32[232,128]{1,0:T(8,128)S(1)}, u32[]{:S(2)}, u32[]{:S(2)}) collective-permute-start(f32[232,128]{1,0:T(8,128)S(1)} %constant_dynamic-slice_fusion.10), channel_id=1, source_target_pairs={{0,16},{4,20},{8,24},{12,28},{16,0},{20,4},{24,8},{28,12},{1,17},{... | collective-permute-start | bytes 356360 | tf_op jit(solution)/shard_map/ppermute | solution.py:79
  40.6 11.0 %collective-permute-start.8 = (f32[232,128]{1,0:T(8,128)S(1)}, f32[232,128]{1,0:T(8,128)S(1)}, u32[]{:S(2)}, u32[]{:S(2)}) collective-permute-start(f32[232,128]{1,0:T(8,128)S(1)} %constant_dynamic-slice_fusion.8), channel_id=1, source_target_pairs={{0,16},{4,20},{8,24},{12,28},{16,0},{20,4},{24,8},{28,12},{1,17},{... | collective-permute-start | bytes 356360 | tf_op jit(solution)/shard_map/ppermute | solution.py:79
  49.0 8.8 %collective-permute-start.3 = (f32[232,128]{1,0:T(8,128)S(1)}, f32[232,128]{1,0:T(8,128)S(1)}, u32[]{:S(2)}, u32[]{:S(2)}) collective-permute-start(f32[232,128]{1,0:T(8,128)S(1)} %dynamic-slice_add_fusion.6), channel_id=1, source_target_pairs={{0,16},{4,20},{8,24},{12,28},{16,0},{20,4},{24,8},{28,12},{1,17},{... | collective-permute-start | bytes 356360 | tf_op jit(solution)/shard_map/ppermute | solution.py:79
  51.6 8.9 %collective-permute-start.9 = (f32[232,128]{1,0:T(8,128)S(1)}, f32[232,128]{1,0:T(8,128)S(1)}, u32[]{:S(2)}, u32[]{:S(2)}) collective-permute-start(f32[232,128]{1,0:T(8,128)S(1)} %dynamic-slice_add_fusion.5), channel_id=1, source_target_pairs={{0,16},{4,20},{8,24},{12,28},{16,0},{20,4},{24,8},{28,12},{1,17},{... | collective-permute-start | bytes 356360 | tf_op jit(solution)/shard_map/ppermute | solution.py:79
  57.9 7.2 %collective-permute-start.4 = (f32[464,128]{1,0:T(8,128)S(1)}, f32[464,128]{1,0:T(8,128)S(1)}, u32[]{:S(2)}, u32[]{:S(2)}) collective-permute-start(f32[464,128]{1,0:T(8,128)S(1)} %pad_maximum_fusion.14), channel_id=1, source_target_pairs={{0,8},{4,12},{8,0},{12,4},{16,24},{20,28},{24,16},{28,20},{1,9},{5... | collective-permute-start | bytes 712712 | tf_op jit(solution)/shard_map/ppermute | solution.py:79
  60.5 6.4 %collective-permute-start.10 = (f32[464,128]{1,0:T(8,128)S(1)}, f32[464,128]{1,0:T(8,128)S(1)}, u32[]{:S(2)}, u32[]{:S(2)}) collective-permute-start(f32[464,128]{1,0:T(8,128)S(1)} %pad_maximum_fusion.15), channel_id=1, source_target_pairs={{0,4},{4,0},{8,12},{12,8},{16,20},{20,16},{24,28},{28,24},{1,5},{5... | collective-permute-start | bytes 712712 | tf_op jit(solution)/shard_map/ppermute | solution.py:79
  65.1 6.4 %copy-start.3 = (bf16[1600,256]{0,1:T(8,128)(2,1)S(1)}, bf16[1600,256]{0,1:T(8,128)(2,1)}, u32[]{:S(2)}) copy-start(bf16[1600,256]{0,1:T(8,128)(2,1)} %subtract_convert_fusion) | copy-start | bytes 2457604
  65.2 11.7 %collective-permute-start.5 = (f32[928,128]{1,0:T(8,128)S(1)}, f32[928,128]{1,0:T(8,128)S(1)}, u32[]{:S(2)}, u32[]{:S(2)}) collective-permute-start(f32[928,128]{1,0:T(8,128)S(1)} %pad_maximum_fusion.9), channel_id=1, source_target_pairs={{0,4},{4,0},{8,12},{12,8},{16,20},{20,16},{24,28},{28,24},{1,5},{5... | collective-permute-start | bytes 1425416 | tf_op jit(solution)/shard_map/ppermute | solution.py:79
  67.0 11.2 %collective-permute-start.11 = (f32[928,128]{1,0:T(8,128)S(1)}, f32[928,128]{1,0:T(8,128)S(1)}, u32[]{:S(2)}, u32[]{:S(2)}) collective-permute-start(f32[928,128]{1,0:T(8,128)S(1)} %pad_maximum_fusion.10), channel_id=1, source_target_pairs={{0,8},{4,12},{8,0},{12,4},{16,24},{20,28},{24,16},{28,20},{1,9},{5... | collective-permute-start | bytes 1425416 | tf_op jit(solution)/shard_map/ppermute | solution.py:79
  78.3 1.0 copy-start.4
  81.6 13.5 %collective-permute-start.12 = (f32[8,128]{1,0:T(8,128)S(1)}, f32[8,128]{1,0:T(8,128)S(1)}, u32[]{:S(2)}, u32[]{:S(2)}) collective-permute-start(f32[8,128]{1,0:T(8,128)S(1)} %broadcast_in_dim.6), channel_id=1, source_target_pairs={{0,1},{1,0},{2,3},{3,2},{4,5},{5,4},{6,7},{7,6},{8,9},{9,8},{10,11... | collective-permute-start | bytes 12296 | tf_op jit(solution)/shard_map/ppermute | solution.py:79
  87.4 34.7 %collective-permute-start.27 = (f32[896,128]{1,0:T(8,128)}, f32[896,128]{1,0:T(8,128)}, u32[]{:S(2)}, u32[]{:S(2)}) collective-permute-start(f32[896,128]{1,0:T(8,128)} %pad_dynamic-slice_fusion.2), channel_id=1, source_target_pairs={{0,1},{1,0},{2,3},{3,2},{4,5},{5,4},{6,7},{7,6},{8,9},{9,8},{10,11... | collective-permute-start | bytes 1376264 | tf_op jit(solution)/shard_map/ppermute | solution.py:79
  92.8 7.8 %copy-start.7 = (f32[1,1,4,1600]{3,2,1,0:T(4,128)S(1)}, f32[1,1,4,1600]{3,2,1,0:T(4,128)}, u32[]{:S(2)}) copy-start(f32[1,1,4,1600]{3,2,1,0:T(4,128)} %param.26) | copy-start | bytes 76804
  92.8 7.8 %copy-start.8 = (f32[1,1,4,1600]{3,2,1,0:T(4,128)S(1)}, f32[1,1,4,1600]{3,2,1,0:T(4,128)}, u32[]{:S(2)}) copy-start(f32[1,1,4,1600]{3,2,1,0:T(4,128)} %param.25) | copy-start | bytes 76804
  95.1 3.6 %collective-permute-start.13 = (f32[8,128]{1,0:T(8,128)S(1)}, f32[8,128]{1,0:T(8,128)S(1)}, u32[]{:S(2)}, u32[]{:S(2)}) collective-permute-start(f32[8,128]{1,0:T(8,128)S(1)} %broadcast_add_fusion), channel_id=1, source_target_pairs={{0,2},{1,3},{2,0},{3,1},{4,6},{5,7},{6,4},{7,5},{8,10},{9,11},{10,... | collective-permute-start | bytes 12296 | tf_op jit(solution)/shard_map/ppermute | solution.py:79
  97.5 26.4 %collective-permute-start.17 = (f32[896,128]{1,0:T(8,128)}, f32[896,128]{1,0:T(8,128)}, u32[]{:S(2)}, u32[]{:S(2)}) collective-permute-start(f32[896,128]{1,0:T(8,128)} %pad_dynamic-slice_fusion.4), channel_id=1, source_target_pairs={{0,1},{1,0},{2,3},{3,2},{4,5},{5,4},{6,7},{7,6},{8,9},{9,8},{10,11... | collective-permute-start | bytes 1376264 | tf_op jit(solution)/shard_map/ppermute | solution.py:79
  102.2 12.0 %copy-start.9 = (f32[4,1600]{1,0:T(4,128)S(1)}, f32[4,1600]{1,0:T(4,128)}, u32[]{:S(2)}) copy-start(f32[4,1600]{1,0:T(4,128)} %param.21) | copy-start | bytes 76804
  102.2 12.0 %copy-start.10 = (f32[4,1600]{1,0:T(4,128)S(1)}, f32[4,1600]{1,0:T(4,128)}, u32[]{:S(2)}) copy-start(f32[4,1600]{1,0:T(4,128)} %param.23) | copy-start | bytes 76804
  102.2 12.0 %copy-start.11 = (f32[4,1600]{1,0:T(4,128)S(1)}, f32[4,1600]{1,0:T(4,128)}, u32[]{:S(2)}) copy-start(f32[4,1600]{1,0:T(4,128)} %param.22) | copy-start | bytes 76804
  104.2 9.2 %collective-permute-start.14 = (bf16[1,250,256]{2,1,0:T(8,128)(2,1)S(1)}, bf16[1,250,256]{2,1,0:T(8,128)(2,1)S(1)}, u32[]{:S(2)}, u32[]{:S(2)}) collective-permute-start(bf16[1,250,256]{2,1,0:T(8,128)(2,1)S(1)} %maximum_bitcast_fusion.1), channel_id=1, source_target_pairs={{0,16},{4,20},{8,24},{12,28},{16,0},{20,4},{24,8},{28,12},{1,17},{... | collective-permute-start | bytes 384008 | tf_op jit(solution)/shard_map/ppermute | solution.py:79
  113.4 7.1 %collective-permute-start.15 = (bf16[2,250,256]{2,1,0:T(8,128)(2,1)S(1)}, bf16[2,250,256]{2,1,0:T(8,128)(2,1)S(1)}, u32[]{:S(2)}, u32[]{:S(2)}) collective-permute-start(bf16[2,250,256]{2,1,0:T(8,128)(2,1)S(1)} %pad_maximum_fusion.13), channel_id=1, source_target_pairs={{0,8},{4,12},{8,0},{12,4},{16,24},{20,28},{24,16},{28,20},{1,9},{5... | collective-permute-start | bytes 768008 | tf_op jit(solution)/shard_map/ppermute | solution.py:79
  120.6 37.3 %collective-permute-start.16 = (bf16[4,250,256]{2,1,0:T(8,128)(2,1)S(1)}, bf16[4,250,256]{2,1,0:T(8,128)(2,1)S(1)}, u32[]{:S(2)}, u32[]{:S(2)}) collective-permute-start(bf16[4,250,256]{2,1,0:T(8,128)(2,1)S(1)} %pad_maximum_fusion.8), channel_id=1, source_target_pairs={{0,4},{4,0},{8,12},{12,8},{16,20},{20,16},{24,28},{28,24},{1,5},{5... | collective-permute-start | bytes 1536008 | tf_op jit(solution)/shard_map/ppermute | solution.py:79
  123.3 14.3 %collective-permute-start.28 = (f32[448,128]{1,0:T(8,128)S(1)}, f32[448,128]{1,0:T(8,128)S(1)}, u32[]{:S(2)}, u32[]{:S(2)}) collective-permute-start(f32[448,128]{1,0:T(8,128)S(1)} %constant_dynamic-slice_fusion.3), channel_id=1, source_target_pairs={{0,4},{4,0},{8,12},{12,8},{16,20},{20,16},{24,28},{28,24},{1,5},{5... | collective-permute-start | bytes 688136 | tf_op jit(solution)/shard_map/ppermute | solution.py:79
  125.0 15.2 %collective-permute-start.18 = (f32[448,128]{1,0:T(8,128)S(1)}, f32[448,128]{1,0:T(8,128)S(1)}, u32[]{:S(2)}, u32[]{:S(2)}) collective-permute-start(f32[448,128]{1,0:T(8,128)S(1)} %constant_dynamic-slice_fusion.7), channel_id=1, source_target_pairs={{0,2},{1,3},{2,0},{3,1},{4,6},{5,7},{6,4},{7,5},{8,10},{9,11},{10,... | collective-permute-start | bytes 688136 | tf_op jit(solution)/shard_map/ppermute | solution.py:79
  137.7 5.3 %collective-permute-start.29 = (f32[224,128]{1,0:T(8,128)S(1)}, f32[224,128]{1,0:T(8,128)S(1)}, u32[]{:S(2)}, u32[]{:S(2)}) collective-permute-start(f32[224,128]{1,0:T(8,128)S(1)} %constant_dynamic-slice_fusion.2), channel_id=1, source_target_pairs={{0,8},{4,12},{8,0},{12,4},{16,24},{20,28},{24,16},{28,20},{1,9},{5... | collective-permute-start | bytes 344072 | tf_op jit(solution)/shard_map/ppermute | solution.py:79
  140.3 4.9 %collective-permute-start.19 = (f32[224,128]{1,0:T(8,128)S(1)}, f32[224,128]{1,0:T(8,128)S(1)}, u32[]{:S(2)}, u32[]{:S(2)}) collective-permute-start(f32[224,128]{1,0:T(8,128)S(1)} %constant_dynamic-slice_fusion.6), channel_id=1, source_target_pairs={{0,4},{4,0},{8,12},{12,8},{16,20},{20,16},{24,28},{28,24},{1,5},{5... | collective-permute-start | bytes 344072 | tf_op jit(solution)/shard_map/ppermute | solution.py:79
  143.0 4.2 %collective-permute-start.30 = (f32[112,128]{1,0:T(8,128)S(1)}, f32[112,128]{1,0:T(8,128)S(1)}, u32[]{:S(2)}, u32[]{:S(2)}) collective-permute-start(f32[112,128]{1,0:T(8,128)S(1)} %constant_dynamic-slice_fusion.1), channel_id=1, source_target_pairs={{0,2},{1,3},{2,0},{3,1},{4,6},{5,7},{6,4},{7,5},{8,10},{9,11},{10,... | collective-permute-start | bytes 172040 | tf_op jit(solution)/shard_map/ppermute | solution.py:79
  145.2 6.2 %collective-permute-start.20 = (f32[112,128]{1,0:T(8,128)S(1)}, f32[112,128]{1,0:T(8,128)S(1)}, u32[]{:S(2)}, u32[]{:S(2)}) collective-permute-start(f32[112,128]{1,0:T(8,128)S(1)} %constant_dynamic-slice_fusion.5), channel_id=1, source_target_pairs={{0,8},{4,12},{8,0},{12,4},{16,24},{20,28},{24,16},{28,20},{1,9},{5... | collective-permute-start | bytes 172040 | tf_op jit(solution)/shard_map/ppermute | solution.py:79
  147.3 6.0 %collective-permute-start.31 = (f32[56,128]{1,0:T(8,128)S(1)}, f32[56,128]{1,0:T(8,128)S(1)}, u32[]{:S(2)}, u32[]{:S(2)}) collective-permute-start(f32[56,128]{1,0:T(8,128)S(1)} %constant_dynamic-slice_fusion), channel_id=1, source_target_pairs={{0,16},{4,20},{8,24},{12,28},{16,0},{20,4},{24,8},{28,12},{1,17},{... | collective-permute-start | bytes 86024 | tf_op jit(solution)/shard_map/ppermute | solution.py:79
  151.4 5.0 %collective-permute-start.21 = (f32[56,128]{1,0:T(8,128)S(1)}, f32[56,128]{1,0:T(8,128)S(1)}, u32[]{:S(2)}, u32[]{:S(2)}) collective-permute-start(f32[56,128]{1,0:T(8,128)S(1)} %constant_dynamic-slice_fusion.4), channel_id=1, source_target_pairs={{0,16},{4,20},{8,24},{12,28},{16,0},{20,4},{24,8},{28,12},{1,17},{... | collective-permute-start | bytes 86024 | tf_op jit(solution)/shard_map/ppermute | solution.py:79
  153.3 5.1 %collective-permute-start.32 = (f32[56,128]{1,0:T(8,128)S(1)}, f32[56,128]{1,0:T(8,128)S(1)}, u32[]{:S(2)}, u32[]{:S(2)}) collective-permute-start(f32[56,128]{1,0:T(8,128)S(1)} %dynamic-slice_add_fusion.11), channel_id=1, source_target_pairs={{0,16},{4,20},{8,24},{12,28},{16,0},{20,4},{24,8},{28,12},{1,17},{... | collective-permute-start | bytes 86024 | tf_op jit(solution)/shard_map/ppermute | solution.py:79
  156.4 4.8 %collective-permute-start.22 = (f32[56,128]{1,0:T(8,128)S(1)}, f32[56,128]{1,0:T(8,128)S(1)}, u32[]{:S(2)}, u32[]{:S(2)}) collective-permute-start(f32[56,128]{1,0:T(8,128)S(1)} %dynamic-slice_add_fusion.12), channel_id=1, source_target_pairs={{0,16},{4,20},{8,24},{12,28},{16,0},{20,4},{24,8},{28,12},{1,17},{... | collective-permute-start | bytes 86024 | tf_op jit(solution)/shard_map/ppermute | solution.py:79
  158.5 4.6 %collective-permute-start.33 = (f32[112,128]{1,0:T(8,128)S(1)}, f32[112,128]{1,0:T(8,128)S(1)}, u32[]{:S(2)}, u32[]{:S(2)}) collective-permute-start(f32[112,128]{1,0:T(8,128)S(1)} %pad_maximum_fusion.22), channel_id=1, source_target_pairs={{0,2},{1,3},{2,0},{3,1},{4,6},{5,7},{6,4},{7,5},{8,10},{9,11},{10,... | collective-permute-start | bytes 172040 | tf_op jit(solution)/shard_map/ppermute | solution.py:79
  161.3 4.2 %collective-permute-start.23 = (f32[112,128]{1,0:T(8,128)S(1)}, f32[112,128]{1,0:T(8,128)S(1)}, u32[]{:S(2)}, u32[]{:S(2)}) collective-permute-start(f32[112,128]{1,0:T(8,128)S(1)} %pad_maximum_fusion.21), channel_id=1, source_target_pairs={{0,8},{4,12},{8,0},{12,4},{16,24},{20,28},{24,16},{28,20},{1,9},{5... | collective-permute-start | bytes 172040 | tf_op jit(solution)/shard_map/ppermute | solution.py:79
  163.1 4.9 %collective-permute-start.34 = (f32[224,128]{1,0:T(8,128)S(1)}, f32[224,128]{1,0:T(8,128)S(1)}, u32[]{:S(2)}, u32[]{:S(2)}) collective-permute-start(f32[224,128]{1,0:T(8,128)S(1)} %pad_maximum_fusion.20), channel_id=1, source_target_pairs={{0,8},{4,12},{8,0},{12,4},{16,24},{20,28},{24,16},{28,20},{1,9},{5... | collective-permute-start | bytes 344072 | tf_op jit(solution)/shard_map/ppermute | solution.py:79
  165.6 4.9 %collective-permute-start.24 = (f32[224,128]{1,0:T(8,128)S(1)}, f32[224,128]{1,0:T(8,128)S(1)}, u32[]{:S(2)}, u32[]{:S(2)}) collective-permute-start(f32[224,128]{1,0:T(8,128)S(1)} %pad_maximum_fusion.19), channel_id=1, source_target_pairs={{0,4},{4,0},{8,12},{12,8},{16,20},{20,16},{24,28},{28,24},{1,5},{5... | collective-permute-start | bytes 344072 | tf_op jit(solution)/shard_map/ppermute | solution.py:79
  168.0 6.1 %collective-permute-start.35 = (f32[448,128]{1,0:T(8,128)S(1)}, f32[448,128]{1,0:T(8,128)S(1)}, u32[]{:S(2)}, u32[]{:S(2)}) collective-permute-start(f32[448,128]{1,0:T(8,128)S(1)} %pad_maximum_fusion.17), channel_id=1, source_target_pairs={{0,4},{4,0},{8,12},{12,8},{16,20},{20,16},{24,28},{28,24},{1,5},{5... | collective-permute-start | bytes 688136 | tf_op jit(solution)/shard_map/ppermute | solution.py:79
  170.5 6.3 %copy-start.6 = (bf16[1,8,4,1600]{3,2,1,0:T(4,128)(2,1)S(1)}, bf16[1,8,4,1600]{3,2,1,0:T(4,128)(2,1)}, u32[]{:S(2)}) copy-start(bf16[1,8,4,1600]{3,2,1,0:T(4,128)(2,1)} %param.24) | copy-start | bytes 307204
  170.5 6.1 %collective-permute-start.25 = (f32[448,128]{1,0:T(8,128)S(1)}, f32[448,128]{1,0:T(8,128)S(1)}, u32[]{:S(2)}, u32[]{:S(2)}) collective-permute-start(f32[448,128]{1,0:T(8,128)S(1)} %pad_maximum_fusion.16), channel_id=1, source_target_pairs={{0,2},{1,3},{2,0},{3,1},{4,6},{5,7},{6,4},{7,5},{8,10},{9,11},{10,... | collective-permute-start | bytes 688136 | tf_op jit(solution)/shard_map/ppermute | solution.py:79
  174.2 14.8 %collective-permute-start.36 = (f32[896,128]{1,0:T(8,128)S(1)}, f32[896,128]{1,0:T(8,128)S(1)}, u32[]{:S(2)}, u32[]{:S(2)}) collective-permute-start(f32[896,128]{1,0:T(8,128)S(1)} %pad_maximum_fusion.12), channel_id=1, source_target_pairs={{0,1},{1,0},{2,3},{3,2},{4,5},{5,4},{6,7},{7,6},{8,9},{9,8},{10,11... | collective-permute-start | bytes 1376264 | tf_op jit(solution)/shard_map/ppermute | solution.py:79
  176.7 12.4 %collective-permute-start.26 = (f32[896,128]{1,0:T(8,128)S(1)}, f32[896,128]{1,0:T(8,128)}, u32[]{:S(2)}, u32[]{:S(2)}) collective-permute-start(f32[896,128]{1,0:T(8,128)S(1)} %pad_maximum_fusion.11), channel_id=1, source_target_pairs={{0,1},{1,0},{2,3},{3,2},{4,5},{5,4},{6,7},{7,6},{8,9},{9,8},{10,11... | collective-permute-start | bytes 1376264 | tf_op jit(solution)/shard_map/ppermute | solution.py:79

commit v4 on v3

--- a/solution.py
+++ b/solution.py
@@ -26,12 +26,20 @@
 
 
 def orthogonalize(subspace):
-    highest = lax.Precision.HIGH
+    high = lax.Precision.HIGH
+    highest = lax.Precision.HIGHEST
     iterate = subspace * lax.rsqrt(jnp.sum(subspace * subspace) + 1e-06)
+    gram_matrix = jnp.dot(iterate.T, iterate, precision=highest)
+    identity = jnp.eye(gram_matrix.shape[0], dtype=gram_matrix.dtype)
+    product = None
     for sweep_index in range(NS_STEPS):
-        gram_matrix = jnp.dot(iterate.T, iterate, precision=highest)
-        iterate = 1.5 * iterate - 0.5 * jnp.dot(iterate, gram_matrix, precision=highest)
-    return iterate
+        step = 1.5 * identity - 0.5 * gram_matrix
+        product = step if product is None else jnp.dot(product, step, precision=highest)
+        if sweep_index + 1 < NS_STEPS:
+            gram_matrix = jnp.dot(
+                step, jnp.dot(gram_matrix, step, precision=highest), precision=highest
+            )
+    return jnp.dot(iterate, product, precision=high)
 
 
 def row_count_of(piece, cols):
@@ -169,15 +177,16 @@
 
 
 def update_kernel(direction_ref, basis_ref, weight_ref, out_ref):
-    update = lax.dot_general(
-        direction_ref[0],
-        basis_ref[...],
-        (((1,), (0,)), ((), ())),
-        preferred_element_type=jnp.float32,
-    )
-    out_ref[0] = (
-        weight_ref[0].astype(jnp.float32) - learn_rate * galore_scale * update
-    ).astype(out_ref.dtype)
+    for block in range(direction_ref.shape[0]):
+        update = lax.dot_general(
+            direction_ref[block],
+            basis_ref[...],
+            (((1,), (0,)), ((), ())),
+            preferred_element_type=jnp.float32,
+        )
+        out_ref[block] = (
+            weight_ref[block].astype(jnp.float32) - learn_rate * galore_scale * update
+        ).astype(out_ref.dtype)
 
 
 def updated_weights(direction_bf16, basis, weights):
@@ -185,16 +194,17 @@
     pieces = split2(basis).T
     depth = pieces.shape[0]
     doubled = jnp.concatenate([direction_bf16] * 2, axis=1).reshape(blocks, rows, depth)
+    group = 2 if blocks % 2 == 0 else 1
     return pl.pallas_call(
         update_kernel,
         out_shape=jax.ShapeDtypeStruct(weights.shape, jnp.bfloat16),
-        grid=(blocks,),
+        grid=(blocks // group,),
         in_specs=[
-            pl.BlockSpec((1, rows, depth), lambda index: (index, 0, 0)),
+            pl.BlockSpec((group, rows, depth), lambda index: (index, 0, 0)),
             pl.BlockSpec((depth, width), lambda index: (0, 0)),
-            pl.BlockSpec((1, rows, width), lambda index: (index, 0, 0)),
+            pl.BlockSpec((group, rows, width), lambda index: (index, 0, 0)),
         ],
-        out_specs=pl.BlockSpec((1, rows, width), lambda index: (index, 0, 0)),
+        out_specs=pl.BlockSpec((group, rows, width), lambda index: (index, 0, 0)),
     )(doubled, pieces, weights)
 
 

time: 206 us -> 202 us (0.981)
  matrix products: 31.3 us -> 27.7 us
    dot_general x5 -> x1, matrix products: 7.84 us -> 2.89 us  [orthogonalize(): gram_matrix = jnp.dot(iterate.T, iterate, precision=highest)]
    dot_general x5 -> x13, matrix products: 5.38 us -> 6.81 us  [the longest x1 1.98 us: orthogonalize(): return jnp.dot(iterate, product, precision=high)]
  transfers between devices with their start and end apart: 37 -> 37, of which waited for: 24 -> 24; matrix products, arithmetic and copies ran while one was open for 21% -> 22% of each run, Pallas kernels for 5% -> 4%
where the time goes in v4:
time: 202 us; the launch traced here: 201 us
  waiting for transfers between devices  70 us (35%)
  starting transfers between devices  49.7 us (25%)
  matrix products  27.7 us (14%)
  other arithmetic  27.6 us (14%)
  local copies, waits for them, and re-layouts  12 us (6%)
  Pallas kernels  8.16 us (4%)
  between operations  5.7 us (3%)
    ppermute x37, waiting for transfers between devices, swap_with(): lax.ppermute(values, name, [(index, index ^ bit) for index in range(size)])  70 us
    ppermute x37, starting transfers between devices, swap_with(): lax.ppermute(values, name, [(index, index ^ bit) for index in range(size)])  49.7 us
    dot_general x4, matrix products, exact_dot(): lax.dot_general(lhs_bf16, split2(rhs_f32), ((contract, (0,)), ((), ())),...  18 us
    pallas_call x1, Pallas kernels, updated_weights(): pl.pallas_call(update_kernel, out_shape=jax.ShapeDtypeStruct(weights.shap...  8.16 us
    convert_element_type x3, other arithmetic, split2(): second = (values - first.astype(jnp.float32)).astype(jnp.bfloat16)  5.11 us
    add x16, other arithmetic, run_steps(): parts = keep + swap_with(send, name, bit, size)  4.52 us
  transfers between devices with their start and end apart: 37, of which 24 were waited for; matrix products, arithmetic and copies ran while one was open for 22% of the time, Pallas kernels for 4%

profile of v4, /device:TPU:0, one launch (start us, length us, event | category | flops | bytes accessed | tf_op | source)
XLA Modules:
  0.0 200.9 jit_solution(9828686813635204712)
XLA Ops:
  0.7 1.0 reshape.183
  1.7 2.2 %subtract_convert_fusion.4 = (bf16[1600,128]{1,0:T(8,128)(2,1)S(1)}, bf16[1600,128]{1,0:T(8,128)(2,1)S(1)}, bf16[1600,128]{1,0:T(8,128)(2,1)S(1)}, bf16[1600,128]{1,0:T(8,128)(2,1)S(1)}) fusion(f32[1600,256]{1,0:T(8,128)} %param.18), kind=kLoop, calls=%fused_computation.57 | loop fusion | flops 1228800 | bytes 4096000 | tf_op jit(solution)/shard_map/convert_element_type | solution.py:213
  3.9 4.2 %convolution_bitcast_fusion.1 = f32[1600,256]{1,0:T(8,128)S(1)} fusion(bf16[1600,1600]{1,0:T(8,128)(2,1)} %bitcast.75, bf16[1600,128]{1,0:T(8,128)(2,1)S(1)} %get-tuple-element.31, bf16[1600,128]{1,0:T(8,128)(2,1)S(1)} %get-tuple-element.32), kind=kOutput, calls=%fused_computation.1 | convolution fusion | flops 1312358400 | bytes 7577600 | tf_op jit(solution)/shard_map/dot_general | solution.py:219
  10.8 2.9 %collective-permute-start = (f32[928,128]{1,0:T(8,128)}, f32[928,128]{1,0:T(8,128)}, u32[]{:S(2)}, u32[]{:S(2)}) collective-permute-start(f32[928,128]{1,0:T(8,128)} %constant_dynamic-slice_fusion.12), channel_id=1, source_target_pairs={{0,4},{4,0},{8,12},{12,8},{16,20},{20,16},{24,28},{28,24},{1,5},{5... | collective-permute-start | bytes 1425416 | tf_op jit(solution)/shard_map/ppermute | solution.py:87
  13.9 4.2 %convolution_bitcast_fusion = f32[1600,256]{1,0:T(8,128)S(1)} fusion(bf16[1600,1600]{1,0:T(8,128)(2,1)} %bitcast.76, bf16[1600,128]{1,0:T(8,128)(2,1)S(1)} %get-tuple-element.35, bf16[1600,128]{1,0:T(8,128)(2,1)S(1)} %get-tuple-element.36), kind=kOutput, calls=%fused_computation | convolution fusion | flops 1312358400 | bytes 7577600 | tf_op jit(solution)/shard_map/dot_general | solution.py:219
  18.2 1.1 fusion.8
  20.2 1.6 collective-permute-start.6
  22.8 1.6 copy.35
  24.4 1.7 copy.36
  26.1 2.6 %subtract_convert_fusion = bf16[1600,256]{0,1:T(8,128)(2,1)} fusion(f32[1600,256]{0,1:T(8,128)} %copy.35, bf16[1600,256]{0,1:T(8,128)(2,1)S(1)} %copy.36), kind=kLoop, calls=%fused_computation.8 | loop fusion | flops 1228800 | bytes 3276800 | tf_op jit(solution)/shard_map/convert_element_type | solution.py:213
  29.6 1.1 dynamic-slice_add_fusion
  31.2 1.9 collective-permute-done.6
  33.1 1.1 fusion.23
  35.0 2.8 %collective-permute-done.1 = f32[464,128]{1,0:T(8,128)S(1)} collective-permute-done((f32[464,128]{1,0:T(8,128)S(1)}, f32[464,128]{1,0:T(8,128)S(1)}, u32[]{:S(2)}, u32[]{:S(2)}) %collective-permute-start.1) | collective-permute-done | bytes 237600 | tf_op jit(solution)/shard_map/ppermute | solution.py:87
  37.9 2.7 %collective-permute-start.2 = (f32[232,128]{1,0:T(8,128)S(1)}, f32[232,128]{1,0:T(8,128)S(1)}, u32[]{:S(2)}, u32[]{:S(2)}) collective-permute-start(f32[232,128]{1,0:T(8,128)S(1)} %constant_dynamic-slice_fusion.10), channel_id=1, source_target_pairs={{0,16},{4,20},{8,24},{12,28},{16,0},{20,4},{24,8},{28,12},{1,17},{... | collective-permute-start | bytes 356360 | tf_op jit(solution)/shard_map/ppermute | solution.py:87
  40.6 2.5 %collective-permute-start.8 = (f32[232,128]{1,0:T(8,128)S(1)}, f32[232,128]{1,0:T(8,128)S(1)}, u32[]{:S(2)}, u32[]{:S(2)}) collective-permute-start(f32[232,128]{1,0:T(8,128)S(1)} %constant_dynamic-slice_fusion.8), channel_id=1, source_target_pairs={{0,16},{4,20},{8,24},{12,28},{16,0},{20,4},{24,8},{28,12},{1,17},{... | collective-permute-start | bytes 356360 | tf_op jit(solution)/shard_map/ppermute | solution.py:87
  43.1 5.9 %collective-permute-done.2 = f32[232,128]{1,0:T(8,128)S(1)} collective-permute-done((f32[232,128]{1,0:T(8,128)S(1)}, f32[232,128]{1,0:T(8,128)S(1)}, u32[]{:S(2)}, u32[]{:S(2)}) %collective-permute-start.2) | collective-permute-done | bytes 118816 | tf_op jit(solution)/shard_map/ppermute | solution.py:87
  49.1 2.4 %collective-permute-done.8 = f32[232,128]{1,0:T(8,128)S(1)} collective-permute-done((f32[232,128]{1,0:T(8,128)S(1)}, f32[232,128]{1,0:T(8,128)S(1)}, u32[]{:S(2)}, u32[]{:S(2)}) %collective-permute-start.8) | collective-permute-done | bytes 118816 | tf_op jit(solution)/shard_map/ppermute | solution.py:87
  52.1 5.7 %collective-permute-done.3 = f32[232,128]{1,0:T(8,128)S(1)} collective-permute-done((f32[232,128]{1,0:T(8,128)S(1)}, f32[232,128]{1,0:T(8,128)S(1)}, u32[]{:S(2)}, u32[]{:S(2)}) %collective-permute-start.3) | collective-permute-done | bytes 118816 | tf_op jit(solution)/shard_map/ppermute | solution.py:87
  57.9 2.0 collective-permute-start.4
  61.1 4.1 %collective-permute-done.4 = f32[464,128]{1,0:T(8,128)S(1)} collective-permute-done((f32[464,128]{1,0:T(8,128)S(1)}, f32[464,128]{1,0:T(8,128)S(1)}, u32[]{:S(2)}, u32[]{:S(2)}) %collective-permute-start.4) | collective-permute-done | bytes 237600 | tf_op jit(solution)/shard_map/ppermute | solution.py:87
  65.7 1.1 collective-permute-done.10
  67.0 4.6 %collective-permute-start.11 = (f32[928,128]{1,0:T(8,128)S(1)}, f32[928,128]{1,0:T(8,128)S(1)}, u32[]{:S(2)}, u32[]{:S(2)}) collective-permute-start(f32[928,128]{1,0:T(8,128)S(1)} %pad_maximum_fusion.10), channel_id=1, source_target_pairs={{0,8},{4,12},{8,0},{12,4},{16,24},{20,28},{24,16},{28,20},{1,9},{5... | collective-permute-start | bytes 1425416 | tf_op jit(solution)/shard_map/ppermute | solution.py:87
  71.6 1.4 maximum_bitcast_fusion.basis_ref
  72.9 3.9 %collective-permute-done.5 = f32[928,128]{1,0:T(8,128)S(1)} collective-permute-done((f32[928,128]{1,0:T(8,128)S(1)}, f32[928,128]{1,0:T(8,128)S(1)}, u32[]{:S(2)}, u32[]{:S(2)}) %collective-permute-start.5) | collective-permute-done | bytes 475168 | tf_op jit(solution)/shard_map/ppermute | solution.py:87
  76.9 1.2 collective-permute-done.11
  81.7 4.8 %convolution_bitcast_fusion.2 = f32[1600,256]{1,0:T(8,128)S(1)} fusion(bf16[1600,1600]{1,0:T(8,128)(2,1)} %bitcast.77, bf16[1600,128]{1,0:T(8,128)(2,1)S(1)} %get-tuple-element.17, bf16[1600,128]{1,0:T(8,128)(2,1)S(1)} %get-tuple-element.18), kind=kOutput, calls=%fused_computation.2 | convolution fusion | flops 1312358400 | bytes 7577600 | tf_op jit(solution)/shard_map/dot_general | solution.py:219
  87.9 4.8 %convolution_bitcast_fusion.3 = f32[1600,256]{1,0:T(8,128)S(1)} fusion(bf16[1600,1600]{1,0:T(8,128)(2,1)} %bitcast.78, bf16[1600,128]{1,0:T(8,128)(2,1)S(1)} %get-tuple-element.75, bf16[1600,128]{1,0:T(8,128)(2,1)S(1)} %get-tuple-element.76), kind=kOutput, calls=%fused_computation.3 | convolution fusion | flops 1312358400 | bytes 7577600 | tf_op jit(solution)/shard_map/dot_general | solution.py:219
  92.9 1.4 multiply_reduce_fusion.2
  95.1 1.5 collective-permute-start.13
  97.5 1.3 collective-permute-done.13
  100.6 1.4 multiply_divide_fusion.2
  102.2 1.9 convert_bitcast_fusion
  104.2 3.5 %collective-permute-start.14 = (bf16[1,250,256]{2,1,0:T(8,128)(2,1)S(1)}, bf16[1,250,256]{2,1,0:T(8,128)(2,1)S(1)}, u32[]{:S(2)}, u32[]{:S(2)}) collective-permute-start(bf16[1,250,256]{2,1,0:T(8,128)(2,1)S(1)} %maximum_bitcast_fusion.1), channel_id=1, source_target_pairs={{0,16},{4,20},{8,24},{12,28},{16,0},{20,4},{24,8},{28,12},{1,17},{... | collective-permute-start | bytes 384008 | tf_op jit(solution)/shard_map/ppermute | solution.py:87
  108.5 4.9 %collective-permute-done.14 = bf16[1,250,256]{2,1,0:T(8,128)(2,1)S(1)} collective-permute-done((bf16[1,250,256]{2,1,0:T(8,128)(2,1)S(1)}, bf16[1,250,256]{2,1,0:T(8,128)(2,1)S(1)}, u32[]{:S(2)}, u32[]{:S(2)}) %collective-permute-start.14) | collective-permute-done | bytes 128032 | tf_op jit(solution)/shard_map/ppermute | solution.py:87
  114.9 5.6 %collective-permute-done.15 = bf16[2,250,256]{2,1,0:T(8,128)(2,1)S(1)} collective-permute-done((bf16[2,250,256]{2,1,0:T(8,128)(2,1)S(1)}, bf16[2,250,256]{2,1,0:T(8,128)(2,1)S(1)}, u32[]{:S(2)}, u32[]{:S(2)}) %collective-permute-start.15) | collective-permute-done | bytes 256032 | tf_op jit(solution)/shard_map/ppermute | solution.py:87
  120.6 1.6 collective-permute-start.16
  122.2 1.1 fusion.25
  123.9 1.1 fusion.24
  125.6 12.0 %collective-permute-done.28 = f32[448,128]{1,0:T(8,128)S(1)} collective-permute-done((f32[448,128]{1,0:T(8,128)S(1)}, f32[448,128]{1,0:T(8,128)S(1)}, u32[]{:S(2)}, u32[]{:S(2)}) %collective-permute-start.28) | collective-permute-done | bytes 229408 | tf_op jit(solution)/shard_map/ppermute | solution.py:87
  137.7 2.5 %collective-permute-start.29 = (f32[224,128]{1,0:T(8,128)S(1)}, f32[224,128]{1,0:T(8,128)S(1)}, u32[]{:S(2)}, u32[]{:S(2)}) collective-permute-start(f32[224,128]{1,0:T(8,128)S(1)} %constant_dynamic-slice_fusion.2), channel_id=1, source_target_pairs={{0,8},{4,12},{8,0},{12,4},{16,24},{20,28},{24,16},{28,20},{1,9},{5... | collective-permute-start | bytes 344072 | tf_op jit(solution)/shard_map/ppermute | solution.py:87
  140.3 1.5 collective-permute-start.19
  141.8 1.2 collective-permute-done.29
  143.1 2.0 %collective-permute-done.19 = f32[224,128]{1,0:T(8,128)S(1)} collective-permute-done((f32[224,128]{1,0:T(8,128)S(1)}, f32[224,128]{1,0:T(8,128)S(1)}, u32[]{:S(2)}, u32[]{:S(2)}) %collective-permute-start.19) | collective-permute-done | bytes 114720 | tf_op jit(solution)/shard_map/ppermute | solution.py:87
  145.3 2.0 collective-permute-done.30
  147.3 4.0 %collective-permute-start.31 = (f32[56,128]{1,0:T(8,128)S(1)}, f32[56,128]{1,0:T(8,128)S(1)}, u32[]{:S(2)}, u32[]{:S(2)}) collective-permute-start(f32[56,128]{1,0:T(8,128)S(1)} %constant_dynamic-slice_fusion), channel_id=1, source_target_pairs={{0,16},{4,20},{8,24},{12,28},{16,0},{20,4},{24,8},{28,12},{1,17},{... | collective-permute-start | bytes 86024 | tf_op jit(solution)/shard_map/ppermute | solution.py:87
  151.4 1.7 collective-permute-start.21
  153.3 3.1 %collective-permute-start.32 = (f32[56,128]{1,0:T(8,128)S(1)}, f32[56,128]{1,0:T(8,128)S(1)}, u32[]{:S(2)}, u32[]{:S(2)}) collective-permute-start(f32[56,128]{1,0:T(8,128)S(1)} %dynamic-slice_add_fusion.11), channel_id=1, source_target_pairs={{0,16},{4,20},{8,24},{12,28},{16,0},{20,4},{24,8},{28,12},{1,17},{... | collective-permute-start | bytes 86024 | tf_op jit(solution)/shard_map/ppermute | solution.py:87
  156.4 1.5 collective-permute-start.22
  159.0 2.2 %collective-permute-done.22 = f32[56,128]{1,0:T(8,128)S(1)} collective-permute-done((f32[56,128]{1,0:T(8,128)S(1)}, f32[56,128]{1,0:T(8,128)S(1)}, u32[]{:S(2)}, u32[]{:S(2)}) %collective-permute-start.22) | collective-permute-done | bytes 28704 | tf_op jit(solution)/shard_map/ppermute | solution.py:87
  161.3 1.8 collective-permute-start.23
  163.1 1.3 collective-permute-start.34
  164.4 1.2 collective-permute-done.23
  165.6 1.5 collective-permute-start.24
  168.0 1.5 collective-permute-start.35
  170.6 3.5 %collective-permute-done.35 = f32[448,128]{1,0:T(8,128)S(1)} collective-permute-done((f32[448,128]{1,0:T(8,128)S(1)}, f32[448,128]{1,0:T(8,128)S(1)}, u32[]{:S(2)}, u32[]{:S(2)}) %collective-permute-start.35) | collective-permute-done | bytes 229408 | tf_op jit(solution)/shard_map/ppermute | solution.py:87
  174.2 2.3 %collective-permute-done.25 = f32[448,128]{1,0:T(8,128)S(1)} collective-permute-done((f32[448,128]{1,0:T(8,128)S(1)}, f32[448,128]{1,0:T(8,128)S(1)}, u32[]{:S(2)}, u32[]{:S(2)}) %collective-permute-start.25) | collective-permute-done | bytes 229408 | tf_op jit(solution)/shard_map/ppermute | solution.py:87
  177.8 1.3 pad_maximum_fusion.3.direction_ref
  179.1 8.2 %shard_map.221 = bf16[8,200,1600]{2,1,0:T(8,128)(2,1)} custom-call(bf16[8,200,512]{2,1,0:T(8,128)(2,1)} %pad_maximum_fusion.3.direction_ref, bf16[512,1600]{1,0:T(8,128)(2,1)} %maximum_bitcast_fusion.basis_ref, bf16[8,200,1600]{2,1,0:T(8,128)(2,1)} %bitcast.70), custom_call_target="tpu_custom_call" | custom-call | tf_op jit(solution)/shard_map/pallas_call | solution.py:198
  187.2 1.1 broadcast_select_fusion.9
  188.3 1.1 broadcast_select_fusion.11
  189.4 1.0 multiply_reduce_fusion
  191.1 2.9 %fusion.5 = f32[256,256]{1,0:T(8,128)S(1)} fusion(f32[]{:T(128)S(6)} %rsqrt.4, f32[896,128]{1,0:T(8,128)S(1)} %get-tuple-element.46, f32[896,128]{1,0:T(8,128)S(1)} %get-tuple-element.45, f32[896,128]{1,0:T(8,128)S(1)} %get-tuple-element.44, f32[896,128]{1,0:T(8,128)S(1)} %get-tuple-element.43), kind=kOutput, calls=%fused_computation.18 | convolution fusion | flops 1259929600 | bytes 2097156 | tf_op jit(solution)/shard_map/dot_general | solution.py:32
  198.9 2.0 fusion.3
  (164 shorter events, 28.5 us)
Async XLA Ops:
  1.7 2.2 %copy-start.5 = (f32[400,128]{1,0:T(8,128)}, f32[400,128]{1,0:T(8,128)S(1)}, u32[]{:S(2)}) copy-start(f32[400,128]{1,0:T(8,128)S(1)} %reshape.183) | copy-start | bytes 614404
  8.1 0.9 slice-start
  8.2 5.6 %copy-start.12 = (bf16[1,4,1600]{2,1,0:T(4,128)(2,1)S(1)}, bf16[1,4,1600]{2,1,0:T(4,128)(2,1)}, u32[]{:S(2)}) copy-start(bf16[1,4,1600]{2,1,0:T(4,128)(2,1)} %param.15) | copy-start | bytes 38404
  9.1 0.9 copy-start.1
  10.8 18.7 %collective-permute-start = (f32[928,128]{1,0:T(8,128)}, f32[928,128]{1,0:T(8,128)}, u32[]{:S(2)}, u32[]{:S(2)}) collective-permute-start(f32[928,128]{1,0:T(8,128)} %constant_dynamic-slice_fusion.12), channel_id=1, source_target_pairs={{0,4},{4,0},{8,12},{12,8},{16,20},{20,16},{24,28},{28,24},{1,5},{5... | collective-permute-start | bytes 1425416 | tf_op jit(solution)/shard_map/ppermute | solution.py:87
  18.2 3.6 %copy-start = (f32[1600,256]{1,0:T(8,128)S(1)}, f32[1600,256]{1,0:T(8,128)}, u32[]{:S(2)}) copy-start(f32[1600,256]{1,0:T(8,128)} %param.18) | copy-start | bytes 4915204
  20.2 12.9 %collective-permute-start.6 = (f32[928,128]{1,0:T(8,128)}, f32[928,128]{1,0:T(8,128)}, u32[]{:S(2)}, u32[]{:S(2)}) collective-permute-start(f32[928,128]{1,0:T(8,128)} %pad_dynamic-slice_fusion.6), channel_id=1, source_target_pairs={{0,8},{4,12},{8,0},{12,4},{16,24},{20,28},{24,16},{28,20},{1,9},{5... | collective-permute-start | bytes 1425416 | tf_op jit(solution)/shard_map/ppermute | solution.py:87
  26.1 3.5 %copy-start.2 = (f32[1856,128]{1,0:T(8,128)S(1)}, f32[1856,128]{1,0:T(8,128)}, u32[]{:S(2)}) copy-start(f32[1856,128]{1,0:T(8,128)} %copy-done.1) | copy-start | bytes 2850820
  30.7 7.1 %collective-permute-start.1 = (f32[464,128]{1,0:T(8,128)S(1)}, f32[464,128]{1,0:T(8,128)S(1)}, u32[]{:S(2)}, u32[]{:S(2)}) collective-permute-start(f32[464,128]{1,0:T(8,128)S(1)} %constant_dynamic-slice_fusion.11), channel_id=1, source_target_pairs={{0,8},{4,12},{8,0},{12,4},{16,24},{20,28},{24,16},{28,20},{1,9},{5... | collective-permute-start | bytes 712712 | tf_op jit(solution)/shard_map/ppermute | solution.py:87
  34.2 6.3 %collective-permute-start.7 = (f32[464,128]{1,0:T(8,128)S(1)}, f32[464,128]{1,0:T(8,128)S(1)}, u32[]{:S(2)}, u32[]{:S(2)}) collective-permute-start(f32[464,128]{1,0:T(8,128)S(1)} %constant_dynamic-slice_fusion.9), channel_id=1, source_target_pairs={{0,4},{4,0},{8,12},{12,8},{16,20},{20,16},{24,28},{28,24},{1,5},{5... | collective-permute-start | bytes 712712 | tf_op jit(solution)/shard_map/ppermute | solution.py:87
  37.9 11.2 %collective-permute-start.2 = (f32[232,128]{1,0:T(8,128)S(1)}, f32[232,128]{1,0:T(8,128)S(1)}, u32[]{:S(2)}, u32[]{:S(2)}) collective-permute-start(f32[232,128]{1,0:T(8,128)S(1)} %constant_dynamic-slice_fusion.10), channel_id=1, source_target_pairs={{0,16},{4,20},{8,24},{12,28},{16,0},{20,4},{24,8},{28,12},{1,17},{... | collective-permute-start | bytes 356360 | tf_op jit(solution)/shard_map/ppermute | solution.py:87
  40.6 11.0 %collective-permute-start.8 = (f32[232,128]{1,0:T(8,128)S(1)}, f32[232,128]{1,0:T(8,128)S(1)}, u32[]{:S(2)}, u32[]{:S(2)}) collective-permute-start(f32[232,128]{1,0:T(8,128)S(1)} %constant_dynamic-slice_fusion.8), channel_id=1, source_target_pairs={{0,16},{4,20},{8,24},{12,28},{16,0},{20,4},{24,8},{28,12},{1,17},{... | collective-permute-start | bytes 356360 | tf_op jit(solution)/shard_map/ppermute | solution.py:87
  49.0 8.8 %collective-permute-start.3 = (f32[232,128]{1,0:T(8,128)S(1)}, f32[232,128]{1,0:T(8,128)S(1)}, u32[]{:S(2)}, u32[]{:S(2)}) collective-permute-start(f32[232,128]{1,0:T(8,128)S(1)} %dynamic-slice_add_fusion.6), channel_id=1, source_target_pairs={{0,16},{4,20},{8,24},{12,28},{16,0},{20,4},{24,8},{28,12},{1,17},{... | collective-permute-start | bytes 356360 | tf_op jit(solution)/shard_map/ppermute | solution.py:87
  51.6 8.9 %collective-permute-start.9 = (f32[232,128]{1,0:T(8,128)S(1)}, f32[232,128]{1,0:T(8,128)S(1)}, u32[]{:S(2)}, u32[]{:S(2)}) collective-permute-start(f32[232,128]{1,0:T(8,128)S(1)} %dynamic-slice_add_fusion.5), channel_id=1, source_target_pairs={{0,16},{4,20},{8,24},{12,28},{16,0},{20,4},{24,8},{28,12},{1,17},{... | collective-permute-start | bytes 356360 | tf_op jit(solution)/shard_map/ppermute | solution.py:87
  57.9 7.2 %collective-permute-start.4 = (f32[464,128]{1,0:T(8,128)S(1)}, f32[464,128]{1,0:T(8,128)S(1)}, u32[]{:S(2)}, u32[]{:S(2)}) collective-permute-start(f32[464,128]{1,0:T(8,128)S(1)} %pad_maximum_fusion.14), channel_id=1, source_target_pairs={{0,8},{4,12},{8,0},{12,4},{16,24},{20,28},{24,16},{28,20},{1,9},{5... | collective-permute-start | bytes 712712 | tf_op jit(solution)/shard_map/ppermute | solution.py:87
  60.5 6.4 %collective-permute-start.10 = (f32[464,128]{1,0:T(8,128)S(1)}, f32[464,128]{1,0:T(8,128)S(1)}, u32[]{:S(2)}, u32[]{:S(2)}) collective-permute-start(f32[464,128]{1,0:T(8,128)S(1)} %pad_maximum_fusion.15), channel_id=1, source_target_pairs={{0,4},{4,0},{8,12},{12,8},{16,20},{20,16},{24,28},{28,24},{1,5},{5... | collective-permute-start | bytes 712712 | tf_op jit(solution)/shard_map/ppermute | solution.py:87
  65.1 6.4 %copy-start.3 = (bf16[1600,256]{0,1:T(8,128)(2,1)S(1)}, bf16[1600,256]{0,1:T(8,128)(2,1)}, u32[]{:S(2)}) copy-start(bf16[1600,256]{0,1:T(8,128)(2,1)} %subtract_convert_fusion) | copy-start | bytes 2457604
  65.2 11.7 %collective-permute-start.5 = (f32[928,128]{1,0:T(8,128)S(1)}, f32[928,128]{1,0:T(8,128)S(1)}, u32[]{:S(2)}, u32[]{:S(2)}) collective-permute-start(f32[928,128]{1,0:T(8,128)S(1)} %pad_maximum_fusion.9), channel_id=1, source_target_pairs={{0,4},{4,0},{8,12},{12,8},{16,20},{20,16},{24,28},{28,24},{1,5},{5... | collective-permute-start | bytes 1425416 | tf_op jit(solution)/shard_map/ppermute | solution.py:87
  67.0 11.2 %collective-permute-start.11 = (f32[928,128]{1,0:T(8,128)S(1)}, f32[928,128]{1,0:T(8,128)S(1)}, u32[]{:S(2)}, u32[]{:S(2)}) collective-permute-start(f32[928,128]{1,0:T(8,128)S(1)} %pad_maximum_fusion.10), channel_id=1, source_target_pairs={{0,8},{4,12},{8,0},{12,4},{16,24},{20,28},{24,16},{28,20},{1,9},{5... | collective-permute-start | bytes 1425416 | tf_op jit(solution)/shard_map/ppermute | solution.py:87
  78.3 1.0 copy-start.4
  81.6 13.5 %collective-permute-start.12 = (f32[8,128]{1,0:T(8,128)S(1)}, f32[8,128]{1,0:T(8,128)S(1)}, u32[]{:S(2)}, u32[]{:S(2)}) collective-permute-start(f32[8,128]{1,0:T(8,128)S(1)} %broadcast_in_dim.6), channel_id=1, source_target_pairs={{0,1},{1,0},{2,3},{3,2},{4,5},{5,4},{6,7},{7,6},{8,9},{9,8},{10,11... | collective-permute-start | bytes 12296 | tf_op jit(solution)/shard_map/ppermute | solution.py:87
  87.4 34.7 %collective-permute-start.27 = (f32[896,128]{1,0:T(8,128)}, f32[896,128]{1,0:T(8,128)}, u32[]{:S(2)}, u32[]{:S(2)}) collective-permute-start(f32[896,128]{1,0:T(8,128)} %pad_dynamic-slice_fusion.2), channel_id=1, source_target_pairs={{0,1},{1,0},{2,3},{3,2},{4,5},{5,4},{6,7},{7,6},{8,9},{9,8},{10,11... | collective-permute-start | bytes 1376264 | tf_op jit(solution)/shard_map/ppermute | solution.py:87
  92.8 7.8 %copy-start.7 = (f32[1,1,4,1600]{3,2,1,0:T(4,128)S(1)}, f32[1,1,4,1600]{3,2,1,0:T(4,128)}, u32[]{:S(2)}) copy-start(f32[1,1,4,1600]{3,2,1,0:T(4,128)} %param.26) | copy-start | bytes 76804
  92.8 7.8 %copy-start.8 = (f32[1,1,4,1600]{3,2,1,0:T(4,128)S(1)}, f32[1,1,4,1600]{3,2,1,0:T(4,128)}, u32[]{:S(2)}) copy-start(f32[1,1,4,1600]{3,2,1,0:T(4,128)} %param.25) | copy-start | bytes 76804
  95.1 3.6 %collective-permute-start.13 = (f32[8,128]{1,0:T(8,128)S(1)}, f32[8,128]{1,0:T(8,128)S(1)}, u32[]{:S(2)}, u32[]{:S(2)}) collective-permute-start(f32[8,128]{1,0:T(8,128)S(1)} %broadcast_add_fusion), channel_id=1, source_target_pairs={{0,2},{1,3},{2,0},{3,1},{4,6},{5,7},{6,4},{7,5},{8,10},{9,11},{10,... | collective-permute-start | bytes 12296 | tf_op jit(solution)/shard_map/ppermute | solution.py:87
  97.5 26.4 %collective-permute-start.17 = (f32[896,128]{1,0:T(8,128)}, f32[896,128]{1,0:T(8,128)}, u32[]{:S(2)}, u32[]{:S(2)}) collective-permute-start(f32[896,128]{1,0:T(8,128)} %pad_dynamic-slice_fusion.4), channel_id=1, source_target_pairs={{0,1},{1,0},{2,3},{3,2},{4,5},{5,4},{6,7},{7,6},{8,9},{9,8},{10,11... | collective-permute-start | bytes 1376264 | tf_op jit(solution)/shard_map/ppermute | solution.py:87
  102.2 12.0 %copy-start.9 = (f32[4,1600]{1,0:T(4,128)S(1)}, f32[4,1600]{1,0:T(4,128)}, u32[]{:S(2)}) copy-start(f32[4,1600]{1,0:T(4,128)} %param.21) | copy-start | bytes 76804
  102.2 12.0 %copy-start.10 = (f32[4,1600]{1,0:T(4,128)S(1)}, f32[4,1600]{1,0:T(4,128)}, u32[]{:S(2)}) copy-start(f32[4,1600]{1,0:T(4,128)} %param.23) | copy-start | bytes 76804
  102.2 12.0 %copy-start.11 = (f32[4,1600]{1,0:T(4,128)S(1)}, f32[4,1600]{1,0:T(4,128)}, u32[]{:S(2)}) copy-start(f32[4,1600]{1,0:T(4,128)} %param.22) | copy-start | bytes 76804
  104.2 9.2 %collective-permute-start.14 = (bf16[1,250,256]{2,1,0:T(8,128)(2,1)S(1)}, bf16[1,250,256]{2,1,0:T(8,128)(2,1)S(1)}, u32[]{:S(2)}, u32[]{:S(2)}) collective-permute-start(bf16[1,250,256]{2,1,0:T(8,128)(2,1)S(1)} %maximum_bitcast_fusion.1), channel_id=1, source_target_pairs={{0,16},{4,20},{8,24},{12,28},{16,0},{20,4},{24,8},{28,12},{1,17},{... | collective-permute-start | bytes 384008 | tf_op jit(solution)/shard_map/ppermute | solution.py:87
  113.4 7.1 %collective-permute-start.15 = (bf16[2,250,256]{2,1,0:T(8,128)(2,1)S(1)}, bf16[2,250,256]{2,1,0:T(8,128)(2,1)S(1)}, u32[]{:S(2)}, u32[]{:S(2)}) collective-permute-start(bf16[2,250,256]{2,1,0:T(8,128)(2,1)S(1)} %pad_maximum_fusion.13), channel_id=1, source_target_pairs={{0,8},{4,12},{8,0},{12,4},{16,24},{20,28},{24,16},{28,20},{1,9},{5... | collective-permute-start | bytes 768008 | tf_op jit(solution)/shard_map/ppermute | solution.py:87
  120.6 37.3 %collective-permute-start.16 = (bf16[4,250,256]{2,1,0:T(8,128)(2,1)S(1)}, bf16[4,250,256]{2,1,0:T(8,128)(2,1)S(1)}, u32[]{:S(2)}, u32[]{:S(2)}) collective-permute-start(bf16[4,250,256]{2,1,0:T(8,128)(2,1)S(1)} %pad_maximum_fusion.8), channel_id=1, source_target_pairs={{0,4},{4,0},{8,12},{12,8},{16,20},{20,16},{24,28},{28,24},{1,5},{5... | collective-permute-start | bytes 1536008 | tf_op jit(solution)/shard_map/ppermute | solution.py:87
  123.3 14.3 %collective-permute-start.28 = (f32[448,128]{1,0:T(8,128)S(1)}, f32[448,128]{1,0:T(8,128)S(1)}, u32[]{:S(2)}, u32[]{:S(2)}) collective-permute-start(f32[448,128]{1,0:T(8,128)S(1)} %constant_dynamic-slice_fusion.3), channel_id=1, source_target_pairs={{0,4},{4,0},{8,12},{12,8},{16,20},{20,16},{24,28},{28,24},{1,5},{5... | collective-permute-start | bytes 688136 | tf_op jit(solution)/shard_map/ppermute | solution.py:87
  125.0 15.2 %collective-permute-start.18 = (f32[448,128]{1,0:T(8,128)S(1)}, f32[448,128]{1,0:T(8,128)S(1)}, u32[]{:S(2)}, u32[]{:S(2)}) collective-permute-start(f32[448,128]{1,0:T(8,128)S(1)} %constant_dynamic-slice_fusion.7), channel_id=1, source_target_pairs={{0,2},{1,3},{2,0},{3,1},{4,6},{5,7},{6,4},{7,5},{8,10},{9,11},{10,... | collective-permute-start | bytes 688136 | tf_op jit(solution)/shard_map/ppermute | solution.py:87
  137.7 5.3 %collective-permute-start.29 = (f32[224,128]{1,0:T(8,128)S(1)}, f32[224,128]{1,0:T(8,128)S(1)}, u32[]{:S(2)}, u32[]{:S(2)}) collective-permute-start(f32[224,128]{1,0:T(8,128)S(1)} %constant_dynamic-slice_fusion.2), channel_id=1, source_target_pairs={{0,8},{4,12},{8,0},{12,4},{16,24},{20,28},{24,16},{28,20},{1,9},{5... | collective-permute-start | bytes 344072 | tf_op jit(solution)/shard_map/ppermute | solution.py:87
  140.3 4.9 %collective-permute-start.19 = (f32[224,128]{1,0:T(8,128)S(1)}, f32[224,128]{1,0:T(8,128)S(1)}, u32[]{:S(2)}, u32[]{:S(2)}) collective-permute-start(f32[224,128]{1,0:T(8,128)S(1)} %constant_dynamic-slice_fusion.6), channel_id=1, source_target_pairs={{0,4},{4,0},{8,12},{12,8},{16,20},{20,16},{24,28},{28,24},{1,5},{5... | collective-permute-start | bytes 344072 | tf_op jit(solution)/shard_map/ppermute | solution.py:87
  143.0 4.2 %collective-permute-start.30 = (f32[112,128]{1,0:T(8,128)S(1)}, f32[112,128]{1,0:T(8,128)S(1)}, u32[]{:S(2)}, u32[]{:S(2)}) collective-permute-start(f32[112,128]{1,0:T(8,128)S(1)} %constant_dynamic-slice_fusion.1), channel_id=1, source_target_pairs={{0,2},{1,3},{2,0},{3,1},{4,6},{5,7},{6,4},{7,5},{8,10},{9,11},{10,... | collective-permute-start | bytes 172040 | tf_op jit(solution)/shard_map/ppermute | solution.py:87
  145.2 6.2 %collective-permute-start.20 = (f32[112,128]{1,0:T(8,128)S(1)}, f32[112,128]{1,0:T(8,128)S(1)}, u32[]{:S(2)}, u32[]{:S(2)}) collective-permute-start(f32[112,128]{1,0:T(8,128)S(1)} %constant_dynamic-slice_fusion.5), channel_id=1, source_target_pairs={{0,8},{4,12},{8,0},{12,4},{16,24},{20,28},{24,16},{28,20},{1,9},{5... | collective-permute-start | bytes 172040 | tf_op jit(solution)/shard_map/ppermute | solution.py:87
  147.3 6.0 %collective-permute-start.31 = (f32[56,128]{1,0:T(8,128)S(1)}, f32[56,128]{1,0:T(8,128)S(1)}, u32[]{:S(2)}, u32[]{:S(2)}) collective-permute-start(f32[56,128]{1,0:T(8,128)S(1)} %constant_dynamic-slice_fusion), channel_id=1, source_target_pairs={{0,16},{4,20},{8,24},{12,28},{16,0},{20,4},{24,8},{28,12},{1,17},{... | collective-permute-start | bytes 86024 | tf_op jit(solution)/shard_map/ppermute | solution.py:87
  151.4 5.0 %collective-permute-start.21 = (f32[56,128]{1,0:T(8,128)S(1)}, f32[56,128]{1,0:T(8,128)S(1)}, u32[]{:S(2)}, u32[]{:S(2)}) collective-permute-start(f32[56,128]{1,0:T(8,128)S(1)} %constant_dynamic-slice_fusion.4), channel_id=1, source_target_pairs={{0,16},{4,20},{8,24},{12,28},{16,0},{20,4},{24,8},{28,12},{1,17},{... | collective-permute-start | bytes 86024 | tf_op jit(solution)/shard_map/ppermute | solution.py:87
  153.3 5.1 %collective-permute-start.32 = (f32[56,128]{1,0:T(8,128)S(1)}, f32[56,128]{1,0:T(8,128)S(1)}, u32[]{:S(2)}, u32[]{:S(2)}) collective-permute-start(f32[56,128]{1,0:T(8,128)S(1)} %dynamic-slice_add_fusion.11), channel_id=1, source_target_pairs={{0,16},{4,20},{8,24},{12,28},{16,0},{20,4},{24,8},{28,12},{1,17},{... | collective-permute-start | bytes 86024 | tf_op jit(solution)/shard_map/ppermute | solution.py:87
  156.4 4.8 %collective-permute-start.22 = (f32[56,128]{1,0:T(8,128)S(1)}, f32[56,128]{1,0:T(8,128)S(1)}, u32[]{:S(2)}, u32[]{:S(2)}) collective-permute-start(f32[56,128]{1,0:T(8,128)S(1)} %dynamic-slice_add_fusion.12), channel_id=1, source_target_pairs={{0,16},{4,20},{8,24},{12,28},{16,0},{20,4},{24,8},{28,12},{1,17},{... | collective-permute-start | bytes 86024 | tf_op jit(solution)/shard_map/ppermute | solution.py:87
  158.5 4.6 %collective-permute-start.33 = (f32[112,128]{1,0:T(8,128)S(1)}, f32[112,128]{1,0:T(8,128)S(1)}, u32[]{:S(2)}, u32[]{:S(2)}) collective-permute-start(f32[112,128]{1,0:T(8,128)S(1)} %pad_maximum_fusion.22), channel_id=1, source_target_pairs={{0,2},{1,3},{2,0},{3,1},{4,6},{5,7},{6,4},{7,5},{8,10},{9,11},{10,... | collective-permute-start | bytes 172040 | tf_op jit(solution)/shard_map/ppermute | solution.py:87
  161.3 4.2 %collective-permute-start.23 = (f32[112,128]{1,0:T(8,128)S(1)}, f32[112,128]{1,0:T(8,128)S(1)}, u32[]{:S(2)}, u32[]{:S(2)}) collective-permute-start(f32[112,128]{1,0:T(8,128)S(1)} %pad_maximum_fusion.21), channel_id=1, source_target_pairs={{0,8},{4,12},{8,0},{12,4},{16,24},{20,28},{24,16},{28,20},{1,9},{5... | collective-permute-start | bytes 172040 | tf_op jit(solution)/shard_map/ppermute | solution.py:87
  163.1 4.9 %collective-permute-start.34 = (f32[224,128]{1,0:T(8,128)S(1)}, f32[224,128]{1,0:T(8,128)S(1)}, u32[]{:S(2)}, u32[]{:S(2)}) collective-permute-start(f32[224,128]{1,0:T(8,128)S(1)} %pad_maximum_fusion.20), channel_id=1, source_target_pairs={{0,8},{4,12},{8,0},{12,4},{16,24},{20,28},{24,16},{28,20},{1,9},{5... | collective-permute-start | bytes 344072 | tf_op jit(solution)/shard_map/ppermute | solution.py:87
  165.6 4.9 %collective-permute-start.24 = (f32[224,128]{1,0:T(8,128)S(1)}, f32[224,128]{1,0:T(8,128)S(1)}, u32[]{:S(2)}, u32[]{:S(2)}) collective-permute-start(f32[224,128]{1,0:T(8,128)S(1)} %pad_maximum_fusion.19), channel_id=1, source_target_pairs={{0,4},{4,0},{8,12},{12,8},{16,20},{20,16},{24,28},{28,24},{1,5},{5... | collective-permute-start | bytes 344072 | tf_op jit(solution)/shard_map/ppermute | solution.py:87
  168.0 6.1 %collective-permute-start.35 = (f32[448,128]{1,0:T(8,128)S(1)}, f32[448,128]{1,0:T(8,128)S(1)}, u32[]{:S(2)}, u32[]{:S(2)}) collective-permute-start(f32[448,128]{1,0:T(8,128)S(1)} %pad_maximum_fusion.17), channel_id=1, source_target_pairs={{0,4},{4,0},{8,12},{12,8},{16,20},{20,16},{24,28},{28,24},{1,5},{5... | collective-permute-start | bytes 688136 | tf_op jit(solution)/shard_map/ppermute | solution.py:87
  170.5 6.3 %copy-start.6 = (bf16[1,8,4,1600]{3,2,1,0:T(4,128)(2,1)S(1)}, bf16[1,8,4,1600]{3,2,1,0:T(4,128)(2,1)}, u32[]{:S(2)}) copy-start(bf16[1,8,4,1600]{3,2,1,0:T(4,128)(2,1)} %param.24) | copy-start | bytes 307204
  170.5 6.1 %collective-permute-start.25 = (f32[448,128]{1,0:T(8,128)S(1)}, f32[448,128]{1,0:T(8,128)S(1)}, u32[]{:S(2)}, u32[]{:S(2)}) collective-permute-start(f32[448,128]{1,0:T(8,128)S(1)} %pad_maximum_fusion.16), channel_id=1, source_target_pairs={{0,2},{1,3},{2,0},{3,1},{4,6},{5,7},{6,4},{7,5},{8,10},{9,11},{10,... | collective-permute-start | bytes 688136 | tf_op jit(solution)/shard_map/ppermute | solution.py:87
  174.2 13.1 %collective-permute-start.36 = (f32[896,128]{1,0:T(8,128)S(1)}, f32[896,128]{1,0:T(8,128)}, u32[]{:S(2)}, u32[]{:S(2)}) collective-permute-start(f32[896,128]{1,0:T(8,128)S(1)} %pad_maximum_fusion.12), channel_id=1, source_target_pairs={{0,1},{1,0},{2,3},{3,2},{4,5},{5,4},{6,7},{7,6},{8,9},{9,8},{10,11... | collective-permute-start | bytes 1376264 | tf_op jit(solution)/shard_map/ppermute | solution.py:87
  176.7 11.7 %collective-permute-start.26 = (f32[896,128]{1,0:T(8,128)S(1)}, f32[896,128]{1,0:T(8,128)}, u32[]{:S(2)}, u32[]{:S(2)}) collective-permute-start(f32[896,128]{1,0:T(8,128)S(1)} %pad_maximum_fusion.11), channel_id=1, source_target_pairs={{0,1},{1,0},{2,3},{3,2},{4,5},{5,4},{6,7},{7,6},{8,9},{9,8},{10,11... | collective-permute-start | bytes 1376264 | tf_op jit(solution)/shard_map/ppermute | solution.py:87

commit v5 on v4

--- a/solution.py
+++ b/solution.py
@@ -87,20 +87,25 @@
     return lax.ppermute(values, name, [(index, index ^ bit) for index in range(size)])
 
 
-def run_steps(parts, steps):
+def run_steps(parts, steps, tied=None, tie_at=0):
     sides = []
-    for name, bit, size in steps:
+    for position, (name, bit, size) in enumerate(steps):
         side = (lax.axis_index(name) // bit) % 2
         half = parts.shape[0] // 2
         keep = lax.dynamic_slice_in_dim(parts, side * half, half, 0)
         send = lax.dynamic_slice_in_dim(parts, (1 - side) * half, half, 0)
-        parts = keep + swap_with(send, name, bit, size)
+        received = swap_with(send, name, bit, size)
+        if tied is not None and position == min(tie_at, len(steps) - 1):
+            received, tied = lax.optimization_barrier((received, tied))
+        parts = keep + received
         sides.append(side)
     for (name, bit, size), side in zip(reversed(steps), reversed(sides)):
         other = swap_with(parts, name, bit, size)
         first = jnp.where(side == 0, parts, other)
         second = jnp.where(side == 0, other, parts)
         parts = jnp.concatenate([first, second], axis=0)
+    if tied is not None:
+        return parts, tied
     return parts
 
 
@@ -116,15 +121,19 @@
     return steps, steps[:low] + middle[1:] + middle[:1] + steps[high:]
 
 
-def half_sum(piece, axes, which):
+def half_sum(piece, axes, which, tied=None, tie_at=0):
     orders = half_orders(axes)
     if orders is None:
-        return lax.psum(piece, axes)
+        summed = lax.psum(piece, axes)
+        return summed if tied is None else (summed, tied)
     steps = orders[which]
     count = 2 ** len(steps)
     rows = piece.shape[0]
     padded = -(-rows // (8 * count)) * 8 * count
-    return run_steps(jnp.pad(piece, ((0, padded - rows), (0, 0))), steps)[:rows]
+    out = run_steps(jnp.pad(piece, ((0, padded - rows), (0, 0))), steps, tied, tie_at)
+    if tied is None:
+        return out[:rows]
+    return out[0][:rows], out[1]
 
 
 def butterfly_sum(packed, axes):
@@ -306,9 +315,9 @@
     emb_next = (
         emb_weights.astype(jnp.float32) - learn_rate * emb_dir_all.reshape(emb_weights.shape)
     ).astype(jnp.bfloat16)
-    subspace = jnp.concatenate(
-        [half_sum(value_halves[which], ("own", "dp"), which) for which in range(2)], axis=1
-    )
+    first_half = half_sum(value_halves[0], ("own", "dp"), 0)
+    second_half, weights_next = half_sum(value_halves[1], ("own", "dp"), 1, weights_next, 1)
+    subspace = jnp.concatenate([first_half, second_half], axis=1)
     basis_next = orthogonalize(subspace)
     return (
         fc_m_next,

time: 202 us -> 202 us (level)
  waiting for transfers between devices: 70 us -> 73.5 us
    ppermute x37, waiting for transfers between devices: 70 us -> 73.5 us  [swap_with(): lax.ppermute(values, name, [(index, index ^ bit) for index in range(size)])]
    select_n x16, other arithmetic: 2.58 us -> 0.51 us  [run_steps(): first = jnp.where(side == 0, parts, other)]
  transfers between devices with their start and end apart: 37 -> 37, of which waited for: 24 -> 27; matrix products, arithmetic and copies ran while one was open for 22% -> 21% of each run, Pallas kernels for 4% -> 4%
where the time goes in v5:
time: 202 us; the launch traced here: 201 us
  waiting for transfers between devices  73.5 us (36%)
  starting transfers between devices  48 us (24%)
  matrix products  27.7 us (14%)
  other arithmetic  26 us (13%)
  local copies, waits for them, and re-layouts  12.4 us (6%)
  Pallas kernels  8.17 us (4%)
  between operations  5.61 us (3%)
    ppermute x37, waiting for transfers between devices, swap_with(): lax.ppermute(values, name, [(index, index ^ bit) for index in range(size)])  73.5 us
    ppermute x37, starting transfers between devices, swap_with(): lax.ppermute(values, name, [(index, index ^ bit) for index in range(size)])  48 us
    dot_general x4, matrix products, exact_dot(): lax.dot_general(lhs_bf16, split2(rhs_f32), ((contract, (0,)), ((), ())),...  18 us
    pallas_call x1, Pallas kernels, updated_weights(): pl.pallas_call(update_kernel, out_shape=jax.ShapeDtypeStruct(weights.shap...  8.17 us
    convert_element_type x3, other arithmetic, split2(): second = (values - first.astype(jnp.float32)).astype(jnp.bfloat16)  5.11 us
    add x16, other arithmetic, run_steps(): parts = keep + received  4.52 us
  transfers between devices with their start and end apart: 37, of which 27 were waited for; matrix products, arithmetic and copies ran while one was open for 21% of the time, Pallas kernels for 4%

profile of v5, /device:TPU:0, one launch (start us, length us, event | category | flops | bytes accessed | tf_op | source)
XLA Modules:
  0.0 201.5 jit_solution(10859918075180835146)
XLA Ops:
  0.7 1.0 reshape.183
  1.7 2.2 %subtract_convert_fusion.4 = (bf16[1600,128]{1,0:T(8,128)(2,1)S(1)}, bf16[1600,128]{1,0:T(8,128)(2,1)S(1)}, bf16[1600,128]{1,0:T(8,128)(2,1)S(1)}, bf16[1600,128]{1,0:T(8,128)(2,1)S(1)}) fusion(f32[1600,256]{1,0:T(8,128)} %param.18), kind=kLoop, calls=%fused_computation.57 | loop fusion | flops 1228800 | bytes 4096000 | tf_op jit(solution)/shard_map/convert_element_type | solution.py:222
  3.9 4.2 %convolution_bitcast_fusion.1 = f32[1600,256]{1,0:T(8,128)S(1)} fusion(bf16[1600,1600]{1,0:T(8,128)(2,1)} %bitcast.75, bf16[1600,128]{1,0:T(8,128)(2,1)S(1)} %get-tuple-element.35, bf16[1600,128]{1,0:T(8,128)(2,1)S(1)} %get-tuple-element.36), kind=kOutput, calls=%fused_computation.1 | convolution fusion | flops 1312358400 | bytes 7577600 | tf_op jit(solution)/shard_map/dot_general | solution.py:228
  10.8 2.9 %collective-permute-start = (f32[928,128]{1,0:T(8,128)}, f32[928,128]{1,0:T(8,128)}, u32[]{:S(2)}, u32[]{:S(2)}) collective-permute-start(f32[928,128]{1,0:T(8,128)} %constant_dynamic-slice_fusion.12), channel_id=1, source_target_pairs={{0,4},{4,0},{8,12},{12,8},{16,20},{20,16},{24,28},{28,24},{1,5},{5... | collective-permute-start | bytes 1425416 | tf_op jit(solution)/shard_map/ppermute | solution.py:87
  13.9 4.2 %convolution_bitcast_fusion = f32[1600,256]{1,0:T(8,128)S(1)} fusion(bf16[1600,1600]{1,0:T(8,128)(2,1)} %bitcast.76, bf16[1600,128]{1,0:T(8,128)(2,1)S(1)} %get-tuple-element.39, bf16[1600,128]{1,0:T(8,128)(2,1)S(1)} %get-tuple-element.40), kind=kOutput, calls=%fused_computation | convolution fusion | flops 1312358400 | bytes 7577600 | tf_op jit(solution)/shard_map/dot_general | solution.py:228
  18.2 1.1 fusion.8
  20.2 1.6 collective-permute-start.6
  21.7 1.0 convert_element_type.157
  22.7 1.6 copy.35
  24.4 1.5 copy.36
  25.9 2.6 %subtract_convert_fusion = bf16[1600,256]{0,1:T(8,128)(2,1)} fusion(f32[1600,256]{0,1:T(8,128)} %copy.35, bf16[1600,256]{0,1:T(8,128)(2,1)S(1)} %copy.36), kind=kLoop, calls=%fused_computation.8 | loop fusion | flops 1228800 | bytes 3276800 | tf_op jit(solution)/shard_map/convert_element_type | solution.py:222
  29.4 1.1 dynamic-slice_add_fusion
  31.0 2.2 %collective-permute-done.6 = f32[928,128]{1,0:T(8,128)} collective-permute-done((f32[928,128]{1,0:T(8,128)}, f32[928,128]{1,0:T(8,128)}, u32[]{:S(2)}, u32[]{:S(2)}) %collective-permute-start.6) | collective-permute-done | bytes 475168 | tf_op jit(solution)/shard_map/ppermute | solution.py:87
  33.3 1.1 fusion.23
  35.1 2.7 %collective-permute-done.1 = f32[464,128]{1,0:T(8,128)S(1)} collective-permute-done((f32[464,128]{1,0:T(8,128)S(1)}, f32[464,128]{1,0:T(8,128)S(1)}, u32[]{:S(2)}, u32[]{:S(2)}) %collective-permute-start.1) | collective-permute-done | bytes 237600 | tf_op jit(solution)/shard_map/ppermute | solution.py:87
  37.9 2.7 %collective-permute-start.2 = (f32[232,128]{1,0:T(8,128)S(1)}, f32[232,128]{1,0:T(8,128)S(1)}, u32[]{:S(2)}, u32[]{:S(2)}) collective-permute-start(f32[232,128]{1,0:T(8,128)S(1)} %constant_dynamic-slice_fusion.10), channel_id=1, source_target_pairs={{0,16},{4,20},{8,24},{12,28},{16,0},{20,4},{24,8},{28,12},{1,17},{... | collective-permute-start | bytes 356360 | tf_op jit(solution)/shard_map/ppermute | solution.py:87
  40.6 2.7 %collective-permute-start.8 = (f32[232,128]{1,0:T(8,128)S(1)}, f32[232,128]{1,0:T(8,128)S(1)}, u32[]{:S(2)}, u32[]{:S(2)}) collective-permute-start(f32[232,128]{1,0:T(8,128)S(1)} %constant_dynamic-slice_fusion.8), channel_id=1, source_target_pairs={{0,16},{4,20},{8,24},{12,28},{16,0},{20,4},{24,8},{28,12},{1,17},{... | collective-permute-start | bytes 356360 | tf_op jit(solution)/shard_map/ppermute | solution.py:87
  43.3 5.7 %collective-permute-done.2 = f32[232,128]{1,0:T(8,128)S(1)} collective-permute-done((f32[232,128]{1,0:T(8,128)S(1)}, f32[232,128]{1,0:T(8,128)S(1)}, u32[]{:S(2)}, u32[]{:S(2)}) %collective-permute-start.2) | collective-permute-done | bytes 118816 | tf_op jit(solution)/shard_map/ppermute | solution.py:87
  49.1 2.4 %collective-permute-done.8 = f32[232,128]{1,0:T(8,128)S(1)} collective-permute-done((f32[232,128]{1,0:T(8,128)S(1)}, f32[232,128]{1,0:T(8,128)S(1)}, u32[]{:S(2)}, u32[]{:S(2)}) %collective-permute-start.8) | collective-permute-done | bytes 118816 | tf_op jit(solution)/shard_map/ppermute | solution.py:87
  52.1 5.6 %collective-permute-done.3 = f32[232,128]{1,0:T(8,128)S(1)} collective-permute-done((f32[232,128]{1,0:T(8,128)S(1)}, f32[232,128]{1,0:T(8,128)S(1)}, u32[]{:S(2)}, u32[]{:S(2)}) %collective-permute-start.3) | collective-permute-done | bytes 118816 | tf_op jit(solution)/shard_map/ppermute | solution.py:87
  57.8 2.0 %collective-permute-start.4 = (f32[464,128]{1,0:T(8,128)S(1)}, f32[464,128]{1,0:T(8,128)S(1)}, u32[]{:S(2)}, u32[]{:S(2)}) collective-permute-start(f32[464,128]{1,0:T(8,128)S(1)} %pad_maximum_fusion.14), channel_id=1, source_target_pairs={{0,8},{4,12},{8,0},{12,4},{16,24},{20,28},{24,16},{28,20},{1,9},{5... | collective-permute-start | bytes 712712 | tf_op jit(solution)/shard_map/ppermute | solution.py:87
  60.9 4.1 %collective-permute-done.4 = f32[464,128]{1,0:T(8,128)S(1)} collective-permute-done((f32[464,128]{1,0:T(8,128)S(1)}, f32[464,128]{1,0:T(8,128)S(1)}, u32[]{:S(2)}, u32[]{:S(2)}) %collective-permute-start.4) | collective-permute-done | bytes 237600 | tf_op jit(solution)/shard_map/ppermute | solution.py:87
  65.6 1.1 collective-permute-done.10
  66.9 3.9 %collective-permute-start.11 = (f32[928,128]{1,0:T(8,128)S(1)}, f32[928,128]{1,0:T(8,128)S(1)}, u32[]{:S(2)}, u32[]{:S(2)}) collective-permute-start(f32[928,128]{1,0:T(8,128)S(1)} %pad_maximum_fusion.10), channel_id=1, source_target_pairs={{0,8},{4,12},{8,0},{12,4},{16,24},{20,28},{24,16},{28,20},{1,9},{5... | collective-permute-start | bytes 1425416 | tf_op jit(solution)/shard_map/ppermute | solution.py:87
  70.7 1.4 maximum_bitcast_fusion.basis_ref
  72.1 4.7 %collective-permute-done.5 = f32[928,128]{1,0:T(8,128)S(1)} collective-permute-done((f32[928,128]{1,0:T(8,128)S(1)}, f32[928,128]{1,0:T(8,128)S(1)}, u32[]{:S(2)}, u32[]{:S(2)}) %collective-permute-start.5) | collective-permute-done | bytes 475168 | tf_op jit(solution)/shard_map/ppermute | solution.py:87
  78.5 1.0 fusion.1
  80.9 4.8 %convolution_bitcast_fusion.2 = f32[1600,256]{1,0:T(8,128)S(1)} fusion(bf16[1600,1600]{1,0:T(8,128)(2,1)} %bitcast.77, bf16[1600,128]{1,0:T(8,128)(2,1)S(1)} %get-tuple-element.18, bf16[1600,128]{1,0:T(8,128)(2,1)S(1)} %get-tuple-element.19), kind=kOutput, calls=%fused_computation.2 | convolution fusion | flops 1312358400 | bytes 7577600 | tf_op jit(solution)/shard_map/dot_general | solution.py:228
  87.1 4.8 %convolution_bitcast_fusion.3 = f32[1600,256]{1,0:T(8,128)S(1)} fusion(bf16[1600,1600]{1,0:T(8,128)(2,1)} %bitcast.78, bf16[1600,128]{1,0:T(8,128)(2,1)S(1)} %get-tuple-element.79, bf16[1600,128]{1,0:T(8,128)(2,1)S(1)} %get-tuple-element.80), kind=kOutput, calls=%fused_computation.3 | convolution fusion | flops 1312358400 | bytes 7577600 | tf_op jit(solution)/shard_map/dot_general | solution.py:228
  92.1 1.4 multiply_reduce_fusion.2
  94.3 1.6 collective-permute-start.13
  96.7 1.3 collective-permute-done.13
  100.7 1.4 multiply_divide_fusion.2
  103.7 1.8 convert_bitcast_fusion
  105.5 4.4 %collective-permute-start.16 = (bf16[1,250,256]{2,1,0:T(8,128)(2,1)S(1)}, bf16[1,250,256]{2,1,0:T(8,128)(2,1)S(1)}, u32[]{:S(2)}, u32[]{:S(2)}) collective-permute-start(bf16[1,250,256]{2,1,0:T(8,128)(2,1)S(1)} %maximum_bitcast_fusion.1), channel_id=1, source_target_pairs={{0,16},{4,20},{8,24},{12,28},{16,0},{20,4},{24,8},{28,12},{1,17},{... | collective-permute-start | bytes 384008 | tf_op jit(solution)/shard_map/ppermute | solution.py:87
  110.6 5.0 %collective-permute-done.16 = bf16[1,250,256]{2,1,0:T(8,128)(2,1)S(1)} collective-permute-done((bf16[1,250,256]{2,1,0:T(8,128)(2,1)S(1)}, bf16[1,250,256]{2,1,0:T(8,128)(2,1)S(1)}, u32[]{:S(2)}, u32[]{:S(2)}) %collective-permute-start.16) | collective-permute-done | bytes 128032 | tf_op jit(solution)/shard_map/ppermute | solution.py:87
  116.6 1.1 fusion.25
  117.7 1.2 collective-permute-start.20
  118.9 3.9 %collective-permute-done.17 = bf16[2,250,256]{2,1,0:T(8,128)(2,1)S(1)} collective-permute-done((bf16[2,250,256]{2,1,0:T(8,128)(2,1)S(1)}, bf16[2,250,256]{2,1,0:T(8,128)(2,1)S(1)}, u32[]{:S(2)}, u32[]{:S(2)}) %collective-permute-start.17) | collective-permute-done | bytes 256032 | tf_op jit(solution)/shard_map/ppermute | solution.py:87
  122.9 1.9 collective-permute-done.20
  124.8 1.5 collective-permute-start.21
  127.0 3.9 %collective-permute-done.21 = f32[224,128]{1,0:T(8,128)S(1)} collective-permute-done((f32[224,128]{1,0:T(8,128)S(1)}, f32[224,128]{1,0:T(8,128)S(1)}, u32[]{:S(2)}, u32[]{:S(2)}) %collective-permute-start.21) | collective-permute-done | bytes 114720 | tf_op jit(solution)/shard_map/ppermute | solution.py:87
  131.3 1.1 fusion.24
  132.4 3.0 %collective-permute-done.22 = f32[112,128]{1,0:T(8,128)S(1)} collective-permute-done((f32[112,128]{1,0:T(8,128)S(1)}, f32[112,128]{1,0:T(8,128)S(1)}, u32[]{:S(2)}, u32[]{:S(2)}) %collective-permute-start.22) | collective-permute-done | bytes 57376 | tf_op jit(solution)/shard_map/ppermute | solution.py:87
  135.4 3.3 %collective-permute-start.23 = (f32[56,128]{1,0:T(8,128)S(1)}, f32[56,128]{1,0:T(8,128)S(1)}, u32[]{:S(2)}, u32[]{:S(2)}) collective-permute-start(f32[56,128]{1,0:T(8,128)S(1)} %constant_dynamic-slice_fusion.3), channel_id=1, source_target_pairs={{0,16},{4,20},{8,24},{12,28},{16,0},{20,4},{24,8},{28,12},{1,17},{... | collective-permute-start | bytes 86024 | tf_op jit(solution)/shard_map/ppermute | solution.py:87
  138.7 1.6 collective-permute-start.15
  140.8 2.7 %collective-permute-start.24 = (f32[56,128]{1,0:T(8,128)S(1)}, f32[56,128]{1,0:T(8,128)S(1)}, u32[]{:S(2)}, u32[]{:S(2)}) collective-permute-start(f32[56,128]{1,0:T(8,128)S(1)} %dynamic-slice_add_fusion.12), channel_id=1, source_target_pairs={{0,16},{4,20},{8,24},{12,28},{16,0},{20,4},{24,8},{28,12},{1,17},{... | collective-permute-start | bytes 86024 | tf_op jit(solution)/shard_map/ppermute | solution.py:87
  143.8 1.3 pad_maximum_fusion.3.direction_ref
  145.1 8.2 %shard_map.221 = bf16[8,200,1600]{2,1,0:T(8,128)(2,1)} custom-call(bf16[8,200,512]{2,1,0:T(8,128)(2,1)} %pad_maximum_fusion.3.direction_ref, bf16[512,1600]{1,0:T(8,128)(2,1)} %maximum_bitcast_fusion.basis_ref, bf16[8,200,1600]{2,1,0:T(8,128)(2,1)} %bitcast.70), custom_call_target="tpu_custom_call" | custom-call | tf_op jit(solution)/shard_map/pallas_call | solution.py:207
  154.2 4.3 %collective-permute-done.29 = f32[224,128]{1,0:T(8,128)S(1)} collective-permute-done((f32[224,128]{1,0:T(8,128)S(1)}, f32[224,128]{1,0:T(8,128)S(1)}, u32[]{:S(2)}, u32[]{:S(2)}) %collective-permute-start.29) | collective-permute-done | bytes 114720 | tf_op jit(solution)/shard_map/ppermute | solution.py:87
  159.5 3.2 %collective-permute-done.30 = f32[112,128]{1,0:T(8,128)S(1)} collective-permute-done((f32[112,128]{1,0:T(8,128)S(1)}, f32[112,128]{1,0:T(8,128)S(1)}, u32[]{:S(2)}, u32[]{:S(2)}) %collective-permute-start.30) | collective-permute-done | bytes 57376 | tf_op jit(solution)/shard_map/ppermute | solution.py:87
  162.8 2.4 %collective-permute-start.31 = (f32[56,128]{1,0:T(8,128)S(1)}, f32[56,128]{1,0:T(8,128)S(1)}, u32[]{:S(2)}, u32[]{:S(2)}) collective-permute-start(f32[56,128]{1,0:T(8,128)S(1)} %constant_dynamic-slice_fusion), channel_id=1, source_target_pairs={{0,16},{4,20},{8,24},{12,28},{16,0},{20,4},{24,8},{28,12},{1,17},{... | collective-permute-start | bytes 86024 | tf_op jit(solution)/shard_map/ppermute | solution.py:87
  165.2 2.6 %collective-permute-done.31 = f32[56,128]{1,0:T(8,128)S(1)} collective-permute-done((f32[56,128]{1,0:T(8,128)S(1)}, f32[56,128]{1,0:T(8,128)S(1)}, u32[]{:S(2)}, u32[]{:S(2)}) %collective-permute-start.31) | collective-permute-done | bytes 28704 | tf_op jit(solution)/shard_map/ppermute | solution.py:87
  167.8 2.1 %collective-permute-start.32 = (f32[56,128]{1,0:T(8,128)S(1)}, f32[56,128]{1,0:T(8,128)S(1)}, u32[]{:S(2)}, u32[]{:S(2)}) collective-permute-start(f32[56,128]{1,0:T(8,128)S(1)} %dynamic-slice_add_fusion.11), channel_id=1, source_target_pairs={{0,16},{4,20},{8,24},{12,28},{16,0},{20,4},{24,8},{28,12},{1,17},{... | collective-permute-start | bytes 86024 | tf_op jit(solution)/shard_map/ppermute | solution.py:87
  170.0 1.6 collective-permute-start.26
  171.6 1.0 collective-permute-done.32
  173.1 2.8 %collective-permute-done.26 = f32[224,128]{1,0:T(8,128)S(1)} collective-permute-done((f32[224,128]{1,0:T(8,128)S(1)}, f32[224,128]{1,0:T(8,128)S(1)}, u32[]{:S(2)}, u32[]{:S(2)}) %collective-permute-start.26) | collective-permute-done | bytes 114720 | tf_op jit(solution)/shard_map/ppermute | solution.py:87
  177.7 4.0 %collective-permute-done.34 = f32[224,128]{1,0:T(8,128)S(1)} collective-permute-done((f32[224,128]{1,0:T(8,128)S(1)}, f32[224,128]{1,0:T(8,128)S(1)}, u32[]{:S(2)}, u32[]{:S(2)}) %collective-permute-start.34) | collective-permute-done | bytes 114720 | tf_op jit(solution)/shard_map/ppermute | solution.py:87
  181.8 1.5 collective-permute-start.35
  183.5 4.4 %collective-permute-done.35 = f32[448,128]{1,0:T(8,128)S(1)} collective-permute-done((f32[448,128]{1,0:T(8,128)S(1)}, f32[448,128]{1,0:T(8,128)S(1)}, u32[]{:S(2)}, u32[]{:S(2)}) %collective-permute-start.35) | collective-permute-done | bytes 229408 | tf_op jit(solution)/shard_map/ppermute | solution.py:87
  188.9 1.0 collective-permute-done.36
  189.9 1.0 multiply_reduce_fusion
  191.7 2.9 %fusion.5 = f32[256,256]{1,0:T(8,128)S(1)} fusion(f32[]{:T(128)S(6)} %rsqrt.4, f32[896,128]{1,0:T(8,128)S(1)} %get-tuple-element.50, f32[896,128]{1,0:T(8,128)S(1)} %get-tuple-element.49, f32[896,128]{1,0:T(8,128)S(1)} %get-tuple-element.48, f32[896,128]{1,0:T(8,128)S(1)} %get-tuple-element.47), kind=kOutput, calls=%fused_computation.18 | convolution fusion | flops 1259929600 | bytes 2097156 | tf_op jit(solution)/shard_map/dot_general | solution.py:32
  199.5 2.0 fusion.3
  (162 shorter events, 29.3 us)
Async XLA Ops:
  1.7 2.2 %copy-start.5 = (f32[400,128]{1,0:T(8,128)}, f32[400,128]{1,0:T(8,128)S(1)}, u32[]{:S(2)}) copy-start(f32[400,128]{1,0:T(8,128)S(1)} %reshape.183) | copy-start | bytes 614404
  8.1 0.9 slice-start
  8.2 5.6 %copy-start.11 = (bf16[1,4,1600]{2,1,0:T(4,128)(2,1)S(1)}, bf16[1,4,1600]{2,1,0:T(4,128)(2,1)}, u32[]{:S(2)}) copy-start(bf16[1,4,1600]{2,1,0:T(4,128)(2,1)} %param.15) | copy-start | bytes 38404
  9.1 0.9 copy-start.1
  10.8 18.5 %collective-permute-start = (f32[928,128]{1,0:T(8,128)}, f32[928,128]{1,0:T(8,128)}, u32[]{:S(2)}, u32[]{:S(2)}) collective-permute-start(f32[928,128]{1,0:T(8,128)} %constant_dynamic-slice_fusion.12), channel_id=1, source_target_pairs={{0,4},{4,0},{8,12},{12,8},{16,20},{20,16},{24,28},{28,24},{1,5},{5... | collective-permute-start | bytes 1425416 | tf_op jit(solution)/shard_map/ppermute | solution.py:87
  18.2 3.6 %copy-start = (f32[1600,256]{1,0:T(8,128)S(1)}, f32[1600,256]{1,0:T(8,128)}, u32[]{:S(2)}) copy-start(f32[1600,256]{1,0:T(8,128)} %param.18) | copy-start | bytes 4915204
  20.2 13.1 %collective-permute-start.6 = (f32[928,128]{1,0:T(8,128)}, f32[928,128]{1,0:T(8,128)}, u32[]{:S(2)}, u32[]{:S(2)}) collective-permute-start(f32[928,128]{1,0:T(8,128)} %pad_dynamic-slice_fusion.6), channel_id=1, source_target_pairs={{0,8},{4,12},{8,0},{12,4},{16,24},{20,28},{24,16},{28,20},{1,9},{5... | collective-permute-start | bytes 1425416 | tf_op jit(solution)/shard_map/ppermute | solution.py:87
  25.9 3.5 %copy-start.2 = (f32[1856,128]{1,0:T(8,128)S(1)}, f32[1856,128]{1,0:T(8,128)}, u32[]{:S(2)}) copy-start(f32[1856,128]{1,0:T(8,128)} %copy-done.1) | copy-start | bytes 2850820
  30.5 7.3 %collective-permute-start.1 = (f32[464,128]{1,0:T(8,128)S(1)}, f32[464,128]{1,0:T(8,128)S(1)}, u32[]{:S(2)}, u32[]{:S(2)}) collective-permute-start(f32[464,128]{1,0:T(8,128)S(1)} %constant_dynamic-slice_fusion.11), channel_id=1, source_target_pairs={{0,8},{4,12},{8,0},{12,4},{16,24},{20,28},{24,16},{28,20},{1,9},{5... | collective-permute-start | bytes 712712 | tf_op jit(solution)/shard_map/ppermute | solution.py:87
  34.4 6.2 %collective-permute-start.7 = (f32[464,128]{1,0:T(8,128)S(1)}, f32[464,128]{1,0:T(8,128)S(1)}, u32[]{:S(2)}, u32[]{:S(2)}) collective-permute-start(f32[464,128]{1,0:T(8,128)S(1)} %constant_dynamic-slice_fusion.9), channel_id=1, source_target_pairs={{0,4},{4,0},{8,12},{12,8},{16,20},{20,16},{24,28},{28,24},{1,5},{5... | collective-permute-start | bytes 712712 | tf_op jit(solution)/shard_map/ppermute | solution.py:87
  37.9 11.1 %collective-permute-start.2 = (f32[232,128]{1,0:T(8,128)S(1)}, f32[232,128]{1,0:T(8,128)S(1)}, u32[]{:S(2)}, u32[]{:S(2)}) collective-permute-start(f32[232,128]{1,0:T(8,128)S(1)} %constant_dynamic-slice_fusion.10), channel_id=1, source_target_pairs={{0,16},{4,20},{8,24},{12,28},{16,0},{20,4},{24,8},{28,12},{1,17},{... | collective-permute-start | bytes 356360 | tf_op jit(solution)/shard_map/ppermute | solution.py:87
  40.6 10.9 %collective-permute-start.8 = (f32[232,128]{1,0:T(8,128)S(1)}, f32[232,128]{1,0:T(8,128)S(1)}, u32[]{:S(2)}, u32[]{:S(2)}) collective-permute-start(f32[232,128]{1,0:T(8,128)S(1)} %constant_dynamic-slice_fusion.8), channel_id=1, source_target_pairs={{0,16},{4,20},{8,24},{12,28},{16,0},{20,4},{24,8},{28,12},{1,17},{... | collective-permute-start | bytes 356360 | tf_op jit(solution)/shard_map/ppermute | solution.py:87
  49.0 8.7 %collective-permute-start.3 = (f32[232,128]{1,0:T(8,128)S(1)}, f32[232,128]{1,0:T(8,128)S(1)}, u32[]{:S(2)}, u32[]{:S(2)}) collective-permute-start(f32[232,128]{1,0:T(8,128)S(1)} %dynamic-slice_add_fusion.6), channel_id=1, source_target_pairs={{0,16},{4,20},{8,24},{12,28},{16,0},{20,4},{24,8},{28,12},{1,17},{... | collective-permute-start | bytes 356360 | tf_op jit(solution)/shard_map/ppermute | solution.py:87
  51.5 8.8 %collective-permute-start.9 = (f32[232,128]{1,0:T(8,128)S(1)}, f32[232,128]{1,0:T(8,128)S(1)}, u32[]{:S(2)}, u32[]{:S(2)}) collective-permute-start(f32[232,128]{1,0:T(8,128)S(1)} %dynamic-slice_add_fusion.5), channel_id=1, source_target_pairs={{0,16},{4,20},{8,24},{12,28},{16,0},{20,4},{24,8},{28,12},{1,17},{... | collective-permute-start | bytes 356360 | tf_op jit(solution)/shard_map/ppermute | solution.py:87
  57.8 7.2 %collective-permute-start.4 = (f32[464,128]{1,0:T(8,128)S(1)}, f32[464,128]{1,0:T(8,128)S(1)}, u32[]{:S(2)}, u32[]{:S(2)}) collective-permute-start(f32[464,128]{1,0:T(8,128)S(1)} %pad_maximum_fusion.14), channel_id=1, source_target_pairs={{0,8},{4,12},{8,0},{12,4},{16,24},{20,28},{24,16},{28,20},{1,9},{5... | collective-permute-start | bytes 712712 | tf_op jit(solution)/shard_map/ppermute | solution.py:87
  60.4 6.4 %collective-permute-start.10 = (f32[464,128]{1,0:T(8,128)S(1)}, f32[464,128]{1,0:T(8,128)S(1)}, u32[]{:S(2)}, u32[]{:S(2)}) collective-permute-start(f32[464,128]{1,0:T(8,128)S(1)} %pad_maximum_fusion.15), channel_id=1, source_target_pairs={{0,4},{4,0},{8,12},{12,8},{16,20},{20,16},{24,28},{28,24},{1,5},{5... | collective-permute-start | bytes 712712 | tf_op jit(solution)/shard_map/ppermute | solution.py:87
  65.0 5.7 %copy-start.3 = (bf16[1600,256]{0,1:T(8,128)(2,1)S(1)}, bf16[1600,256]{0,1:T(8,128)(2,1)}, u32[]{:S(2)}) copy-start(bf16[1600,256]{0,1:T(8,128)(2,1)} %subtract_convert_fusion) | copy-start | bytes 2457604
  65.1 11.7 %collective-permute-start.5 = (f32[928,128]{1,0:T(8,128)S(1)}, f32[928,128]{1,0:T(8,128)S(1)}, u32[]{:S(2)}, u32[]{:S(2)}) collective-permute-start(f32[928,128]{1,0:T(8,128)S(1)} %pad_maximum_fusion.9), channel_id=1, source_target_pairs={{0,4},{4,0},{8,12},{12,8},{16,20},{20,16},{24,28},{28,24},{1,5},{5... | collective-permute-start | bytes 1425416 | tf_op jit(solution)/shard_map/ppermute | solution.py:87
  66.9 10.5 %collective-permute-start.11 = (f32[928,128]{1,0:T(8,128)S(1)}, f32[928,128]{1,0:T(8,128)S(1)}, u32[]{:S(2)}, u32[]{:S(2)}) collective-permute-start(f32[928,128]{1,0:T(8,128)S(1)} %pad_maximum_fusion.10), channel_id=1, source_target_pairs={{0,8},{4,12},{8,0},{12,4},{16,24},{20,28},{24,16},{28,20},{1,9},{5... | collective-permute-start | bytes 1425416 | tf_op jit(solution)/shard_map/ppermute | solution.py:87
  77.4 1.0 copy-start.4
  80.8 13.5 %collective-permute-start.12 = (f32[8,128]{1,0:T(8,128)S(1)}, f32[8,128]{1,0:T(8,128)S(1)}, u32[]{:S(2)}, u32[]{:S(2)}) collective-permute-start(f32[8,128]{1,0:T(8,128)S(1)} %broadcast_in_dim.6), channel_id=1, source_target_pairs={{0,1},{1,0},{2,3},{3,2},{4,5},{5,4},{6,7},{7,6},{8,9},{9,8},{10,11... | collective-permute-start | bytes 12296 | tf_op jit(solution)/shard_map/ppermute | solution.py:87
  86.6 29.9 %collective-permute-start.19 = (f32[896,128]{1,0:T(8,128)}, f32[896,128]{1,0:T(8,128)}, u32[]{:S(2)}, u32[]{:S(2)}) collective-permute-start(f32[896,128]{1,0:T(8,128)} %pad_dynamic-slice_fusion.2), channel_id=1, source_target_pairs={{0,1},{1,0},{2,3},{3,2},{4,5},{5,4},{6,7},{7,6},{8,9},{9,8},{10,11... | collective-permute-start | bytes 1376264 | tf_op jit(solution)/shard_map/ppermute | solution.py:87
  94.3 9.3 %copy-start.6 = (f32[1,1,200,256]{3,2,1,0:T(8,128)S(1)}, f32[1,1,200,256]{3,2,1,0:T(8,128)}, u32[]{:S(2)}) copy-start(f32[1,1,200,256]{3,2,1,0:T(8,128)} %param.20) | copy-start | bytes 614404
  94.3 3.7 %collective-permute-start.13 = (f32[8,128]{1,0:T(8,128)S(1)}, f32[8,128]{1,0:T(8,128)S(1)}, u32[]{:S(2)}, u32[]{:S(2)}) collective-permute-start(f32[8,128]{1,0:T(8,128)S(1)} %broadcast_add_fusion), channel_id=1, source_target_pairs={{0,2},{1,3},{2,0},{3,1},{4,6},{5,7},{6,4},{7,5},{8,10},{9,11},{10,... | collective-permute-start | bytes 12296 | tf_op jit(solution)/shard_map/ppermute | solution.py:87
  96.7 34.6 %collective-permute-start.14 = (f32[896,128]{1,0:T(8,128)}, f32[896,128]{1,0:T(8,128)}, u32[]{:S(2)}, u32[]{:S(2)}) collective-permute-start(f32[896,128]{1,0:T(8,128)} %pad_dynamic-slice_fusion.4), channel_id=1, source_target_pairs={{0,1},{1,0},{2,3},{3,2},{4,5},{5,4},{6,7},{7,6},{8,9},{9,8},{10,11... | collective-permute-start | bytes 1376264 | tf_op jit(solution)/shard_map/ppermute | solution.py:87
  103.6 6.3 %copy-start.8 = (f32[4,1600]{1,0:T(4,128)S(1)}, f32[4,1600]{1,0:T(4,128)}, u32[]{:S(2)}) copy-start(f32[4,1600]{1,0:T(4,128)} %param.21) | copy-start | bytes 76804
  103.6 6.3 %copy-start.9 = (f32[4,1600]{1,0:T(4,128)S(1)}, f32[4,1600]{1,0:T(4,128)}, u32[]{:S(2)}) copy-start(f32[4,1600]{1,0:T(4,128)} %param.23) | copy-start | bytes 76804
  103.7 6.3 %copy-start.10 = (f32[4,1600]{1,0:T(4,128)S(1)}, f32[4,1600]{1,0:T(4,128)}, u32[]{:S(2)}) copy-start(f32[4,1600]{1,0:T(4,128)} %param.22) | copy-start | bytes 76804
  105.5 10.2 %collective-permute-start.16 = (bf16[1,250,256]{2,1,0:T(8,128)(2,1)S(1)}, bf16[1,250,256]{2,1,0:T(8,128)(2,1)S(1)}, u32[]{:S(2)}, u32[]{:S(2)}) collective-permute-start(bf16[1,250,256]{2,1,0:T(8,128)(2,1)S(1)} %maximum_bitcast_fusion.1), channel_id=1, source_target_pairs={{0,16},{4,20},{8,24},{12,28},{16,0},{20,4},{24,8},{28,12},{1,17},{... | collective-permute-start | bytes 384008 | tf_op jit(solution)/shard_map/ppermute | solution.py:87
  115.8 7.1 %collective-permute-start.17 = (bf16[2,250,256]{2,1,0:T(8,128)(2,1)S(1)}, bf16[2,250,256]{2,1,0:T(8,128)(2,1)S(1)}, u32[]{:S(2)}, u32[]{:S(2)}) collective-permute-start(bf16[2,250,256]{2,1,0:T(8,128)(2,1)S(1)} %pad_maximum_fusion.13), channel_id=1, source_target_pairs={{0,8},{4,12},{8,0},{12,4},{16,24},{20,28},{24,16},{28,20},{1,9},{5... | collective-permute-start | bytes 768008 | tf_op jit(solution)/shard_map/ppermute | solution.py:87
  117.7 7.1 %collective-permute-start.20 = (f32[448,128]{1,0:T(8,128)S(1)}, f32[448,128]{1,0:T(8,128)S(1)}, u32[]{:S(2)}, u32[]{:S(2)}) collective-permute-start(f32[448,128]{1,0:T(8,128)S(1)} %constant_dynamic-slice_fusion.6), channel_id=1, source_target_pairs={{0,2},{1,3},{2,0},{3,1},{4,6},{5,7},{6,4},{7,5},{8,10},{9,11},{10,... | collective-permute-start | bytes 688136 | tf_op jit(solution)/shard_map/ppermute | solution.py:87
  124.8 6.1 %collective-permute-start.21 = (f32[224,128]{1,0:T(8,128)S(1)}, f32[224,128]{1,0:T(8,128)S(1)}, u32[]{:S(2)}, u32[]{:S(2)}) collective-permute-start(f32[224,128]{1,0:T(8,128)S(1)} %constant_dynamic-slice_fusion.5), channel_id=1, source_target_pairs={{0,4},{4,0},{8,12},{12,8},{16,20},{20,16},{24,28},{28,24},{1,5},{5... | collective-permute-start | bytes 344072 | tf_op jit(solution)/shard_map/ppermute | solution.py:87
  126.4 17.0 %collective-permute-start.18 = (bf16[4,250,256]{2,1,0:T(8,128)(2,1)S(1)}, bf16[4,250,256]{2,1,0:T(8,128)(2,1)S(1)}, u32[]{:S(2)}, u32[]{:S(2)}) collective-permute-start(bf16[4,250,256]{2,1,0:T(8,128)(2,1)S(1)} %pad_maximum_fusion.8), channel_id=1, source_target_pairs={{0,4},{4,0},{8,12},{12,8},{16,20},{20,16},{24,28},{28,24},{1,5},{5... | collective-permute-start | bytes 1536008 | tf_op jit(solution)/shard_map/ppermute | solution.py:87
  130.9 4.4 %collective-permute-start.22 = (f32[112,128]{1,0:T(8,128)S(1)}, f32[112,128]{1,0:T(8,128)S(1)}, u32[]{:S(2)}, u32[]{:S(2)}) collective-permute-start(f32[112,128]{1,0:T(8,128)S(1)} %constant_dynamic-slice_fusion.4), channel_id=1, source_target_pairs={{0,8},{4,12},{8,0},{12,4},{16,24},{20,28},{24,16},{28,20},{1,9},{5... | collective-permute-start | bytes 172040 | tf_op jit(solution)/shard_map/ppermute | solution.py:87
  135.4 5.4 %collective-permute-start.23 = (f32[56,128]{1,0:T(8,128)S(1)}, f32[56,128]{1,0:T(8,128)S(1)}, u32[]{:S(2)}, u32[]{:S(2)}) collective-permute-start(f32[56,128]{1,0:T(8,128)S(1)} %constant_dynamic-slice_fusion.3), channel_id=1, source_target_pairs={{0,16},{4,20},{8,24},{12,28},{16,0},{20,4},{24,8},{28,12},{1,17},{... | collective-permute-start | bytes 86024 | tf_op jit(solution)/shard_map/ppermute | solution.py:87
  138.7 14.5 %collective-permute-start.15 = (f32[448,128]{1,0:T(8,128)S(1)}, f32[448,128]{1,0:T(8,128)S(1)}, u32[]{:S(2)}, u32[]{:S(2)}) collective-permute-start(f32[448,128]{1,0:T(8,128)S(1)} %constant_dynamic-slice_fusion.7), channel_id=1, source_target_pairs={{0,4},{4,0},{8,12},{12,8},{16,20},{20,16},{24,28},{28,24},{1,5},{5... | collective-permute-start | bytes 688136 | tf_op jit(solution)/shard_map/ppermute | solution.py:87
  140.8 13.4 %collective-permute-start.24 = (f32[56,128]{1,0:T(8,128)S(1)}, f32[56,128]{1,0:T(8,128)S(1)}, u32[]{:S(2)}, u32[]{:S(2)}) collective-permute-start(f32[56,128]{1,0:T(8,128)S(1)} %dynamic-slice_add_fusion.12), channel_id=1, source_target_pairs={{0,16},{4,20},{8,24},{12,28},{16,0},{20,4},{24,8},{28,12},{1,17},{... | collective-permute-start | bytes 86024 | tf_op jit(solution)/shard_map/ppermute | solution.py:87
  153.6 4.9 %collective-permute-start.29 = (f32[224,128]{1,0:T(8,128)S(1)}, f32[224,128]{1,0:T(8,128)S(1)}, u32[]{:S(2)}, u32[]{:S(2)}) collective-permute-start(f32[224,128]{1,0:T(8,128)S(1)} %constant_dynamic-slice_fusion.2), channel_id=1, source_target_pairs={{0,8},{4,12},{8,0},{12,4},{16,24},{20,28},{24,16},{28,20},{1,9},{5... | collective-permute-start | bytes 344072 | tf_op jit(solution)/shard_map/ppermute | solution.py:87
  158.5 4.2 %collective-permute-start.30 = (f32[112,128]{1,0:T(8,128)S(1)}, f32[112,128]{1,0:T(8,128)S(1)}, u32[]{:S(2)}, u32[]{:S(2)}) collective-permute-start(f32[112,128]{1,0:T(8,128)S(1)} %constant_dynamic-slice_fusion.1), channel_id=1, source_target_pairs={{0,2},{1,3},{2,0},{3,1},{4,6},{5,7},{6,4},{7,5},{8,10},{9,11},{10,... | collective-permute-start | bytes 172040 | tf_op jit(solution)/shard_map/ppermute | solution.py:87
  159.2 6.0 %collective-permute-start.25 = (f32[112,128]{1,0:T(8,128)S(1)}, f32[112,128]{1,0:T(8,128)S(1)}, u32[]{:S(2)}, u32[]{:S(2)}) collective-permute-start(f32[112,128]{1,0:T(8,128)S(1)} %pad_maximum_fusion.21), channel_id=1, source_target_pairs={{0,8},{4,12},{8,0},{12,4},{16,24},{20,28},{24,16},{28,20},{1,9},{5... | collective-permute-start | bytes 172040 | tf_op jit(solution)/shard_map/ppermute | solution.py:87
  162.8 5.1 %collective-permute-start.31 = (f32[56,128]{1,0:T(8,128)S(1)}, f32[56,128]{1,0:T(8,128)S(1)}, u32[]{:S(2)}, u32[]{:S(2)}) collective-permute-start(f32[56,128]{1,0:T(8,128)S(1)} %constant_dynamic-slice_fusion), channel_id=1, source_target_pairs={{0,16},{4,20},{8,24},{12,28},{16,0},{20,4},{24,8},{28,12},{1,17},{... | collective-permute-start | bytes 86024 | tf_op jit(solution)/shard_map/ppermute | solution.py:87
  167.8 4.8 %collective-permute-start.32 = (f32[56,128]{1,0:T(8,128)S(1)}, f32[56,128]{1,0:T(8,128)S(1)}, u32[]{:S(2)}, u32[]{:S(2)}) collective-permute-start(f32[56,128]{1,0:T(8,128)S(1)} %dynamic-slice_add_fusion.11), channel_id=1, source_target_pairs={{0,16},{4,20},{8,24},{12,28},{16,0},{20,4},{24,8},{28,12},{1,17},{... | collective-permute-start | bytes 86024 | tf_op jit(solution)/shard_map/ppermute | solution.py:87
  170.0 6.0 %collective-permute-start.26 = (f32[224,128]{1,0:T(8,128)S(1)}, f32[224,128]{1,0:T(8,128)S(1)}, u32[]{:S(2)}, u32[]{:S(2)}) collective-permute-start(f32[224,128]{1,0:T(8,128)S(1)} %pad_maximum_fusion.19), channel_id=1, source_target_pairs={{0,4},{4,0},{8,12},{12,8},{16,20},{20,16},{24,28},{28,24},{1,5},{5... | collective-permute-start | bytes 344072 | tf_op jit(solution)/shard_map/ppermute | solution.py:87
  172.6 4.2 %collective-permute-start.33 = (f32[112,128]{1,0:T(8,128)S(1)}, f32[112,128]{1,0:T(8,128)S(1)}, u32[]{:S(2)}, u32[]{:S(2)}) collective-permute-start(f32[112,128]{1,0:T(8,128)S(1)} %pad_maximum_fusion.22), channel_id=1, source_target_pairs={{0,2},{1,3},{2,0},{3,1},{4,6},{5,7},{6,4},{7,5},{8,10},{9,11},{10,... | collective-permute-start | bytes 172040 | tf_op jit(solution)/shard_map/ppermute | solution.py:87
  176.9 4.9 %collective-permute-start.34 = (f32[224,128]{1,0:T(8,128)S(1)}, f32[224,128]{1,0:T(8,128)S(1)}, u32[]{:S(2)}, u32[]{:S(2)}) collective-permute-start(f32[224,128]{1,0:T(8,128)S(1)} %pad_maximum_fusion.20), channel_id=1, source_target_pairs={{0,8},{4,12},{8,0},{12,4},{16,24},{20,28},{24,16},{28,20},{1,9},{5... | collective-permute-start | bytes 344072 | tf_op jit(solution)/shard_map/ppermute | solution.py:87
  177.3 6.1 %collective-permute-start.27 = (f32[448,128]{1,0:T(8,128)S(1)}, f32[448,128]{1,0:T(8,128)S(1)}, u32[]{:S(2)}, u32[]{:S(2)}) collective-permute-start(f32[448,128]{1,0:T(8,128)S(1)} %pad_maximum_fusion.16), channel_id=1, source_target_pairs={{0,2},{1,3},{2,0},{3,1},{4,6},{5,7},{6,4},{7,5},{8,10},{9,11},{10,... | collective-permute-start | bytes 688136 | tf_op jit(solution)/shard_map/ppermute | solution.py:87
  181.8 6.3 %copy-start.7 = (bf16[1,8,4,1600]{3,2,1,0:T(4,128)(2,1)S(1)}, bf16[1,8,4,1600]{3,2,1,0:T(4,128)(2,1)}, u32[]{:S(2)}) copy-start(bf16[1,8,4,1600]{3,2,1,0:T(4,128)(2,1)} %param.24) | copy-start | bytes 307204
  181.8 6.1 %collective-permute-start.35 = (f32[448,128]{1,0:T(8,128)S(1)}, f32[448,128]{1,0:T(8,128)S(1)}, u32[]{:S(2)}, u32[]{:S(2)}) collective-permute-start(f32[448,128]{1,0:T(8,128)S(1)} %pad_maximum_fusion.17), channel_id=1, source_target_pairs={{0,4},{4,0},{8,12},{12,8},{16,20},{20,16},{24,28},{28,24},{1,5},{5... | collective-permute-start | bytes 688136 | tf_op jit(solution)/shard_map/ppermute | solution.py:87
  183.4 5.4 %collective-permute-start.28 = (f32[896,128]{1,0:T(8,128)S(1)}, f32[896,128]{1,0:T(8,128)S(1)}, u32[]{:S(2)}, u32[]{:S(2)}) collective-permute-start(f32[896,128]{1,0:T(8,128)S(1)} %pad_maximum_fusion.11), channel_id=1, source_target_pairs={{0,1},{1,0},{2,3},{3,2},{4,5},{5,4},{6,7},{7,6},{8,9},{9,8},{10,11... | collective-permute-start | bytes 1376264 | tf_op jit(solution)/shard_map/ppermute | solution.py:87
  188.0 1.9 collective-permute-start.36

commit v6 on v5

--- a/solution.py
+++ b/solution.py
@@ -107,6 +107,29 @@
     if tied is not None:
         return parts, tied
     return parts
+
+
+def direct_sum(packed, name):
+    size = lax.axis_size(name)
+    rows = packed.shape[0]
+    block = -(-rows // (8 * size)) * 8
+    parts = jnp.pad(packed, ((0, block * size - rows), (0, 0)))
+    index = lax.axis_index(name)
+    mine = lax.dynamic_slice_in_dim(parts, index * block, block, 0)
+    for shift in range(1, size):
+        target = (index + shift) % size
+        outgoing = lax.dynamic_slice_in_dim(parts, target * block, block, 0)
+        mine = mine + lax.ppermute(
+            outgoing, name, [(source, (source + shift) % size) for source in range(size)]
+        )
+    full = jnp.zeros_like(parts)
+    full = lax.dynamic_update_slice_in_dim(full, mine, index * block, 0)
+    for shift in range(1, size):
+        incoming = lax.ppermute(
+            mine, name, [(source, (source + shift) % size) for source in range(size)]
+        )
+        full = lax.dynamic_update_slice_in_dim(full, incoming, ((index - shift) % size) * block, 0)
+    return full[:rows]
 
 
 def half_orders(axes):
@@ -263,22 +286,15 @@
     emb_local = grads_emb.reshape(blocks, emb_count, width).astype(jnp.float32)
     ln_local = grads_ln.reshape(4, width).astype(jnp.float32)
     half = rank_cols // 2
-    small = pack_rows((emb_local, ln_local), half)
-    small_rows = -(-small.shape[0] // 2)
-    small = jnp.pad(small, ((0, 2 * small_rows - small.shape[0]), (0, 0)))
-    proj_halves, small_halves, value_halves = [], [], []
-    for which in range(2):
-        proj_half = exact_dot(local_rows, basis[:, which * half : (which + 1) * half], (1,))
-        summed = half_sum(
-            jnp.concatenate([proj_half, small[which * small_rows : (which + 1) * small_rows]]),
-            ("dp",),
-            which,
-        )
-        proj_halves.append(summed[: proj_half.shape[0]])
-        small_halves.append(summed[proj_half.shape[0] :])
-        value_halves.append(exact_dot(local_rows, proj_halves[-1], (0,)))
-    proj_own = jnp.concatenate(proj_halves, axis=1)
-    emb_own, ln_sum = unpack_rows(jnp.concatenate(small_halves), (emb_local, ln_local))
+    local_proj = exact_dot(local_rows, basis, (1,))
+    proj_own, emb_own, ln_sum = unpack_rows(
+        direct_sum(pack_rows((local_proj, emb_local, ln_local), rank_cols), "dp"),
+        (local_proj, emb_local, ln_local),
+    )
+    value_halves = [
+        exact_dot(local_rows, proj_own[:, which * half : (which + 1) * half], (0,))
+        for which in range(2)
+    ]
     own_square = jnp.sum(proj_own * proj_own) + jnp.sum(emb_own * emb_own)
     square_total = small_sum(jnp.full((8, 128), own_square), ("own",))[0, 0]
     grad_norm = jnp.sqrt(square_total + jnp.sum(ln_sum * ln_sum) + 1e-06)

time: 202 us -> 228 us (1.13)
  starting transfers between devices: 48 us -> 71.1 us
  waiting for transfers between devices: 73.5 us -> 87.7 us
  matrix products: 27.7 us -> 22.5 us
  other arithmetic: 26 us -> 21 us
    ppermute x0 -> x14, starting transfers between devices: none -> 46.1 us  [the longest x7 29.8 us: direct_sum(): lax.ppermute(mine, name, [(source, (source + shift) % size) for source in...]
    ppermute x0 -> x14, waiting for transfers between devices: none -> 40.3 us  [the longest x7 31.3 us: direct_sum(): lax.ppermute(outgoing, name, [(source, (source + shift) % size) for sourc...]
    ppermute x37 -> x25, waiting for transfers between devices: 73.5 us -> 47.4 us  [swap_with(): lax.ppermute(values, name, [(index, index ^ bit) for index in range(size)])]
    ppermute x37 -> x25, starting transfers between devices: 48 us -> 25.1 us  [swap_with(): lax.ppermute(values, name, [(index, index ^ bit) for index in range(size)])]
    dot_general x4 -> x3, matrix products: 18 us -> 12.8 us  [exact_dot(): lax.dot_general(lhs_bf16, split2(rhs_f32), ((contract, (0,)), ((), ())),...]
    convert_element_type x3 -> x2, other arithmetic: 5.11 us -> 0.36 us  [split2(): second = (values - first.astype(jnp.float32)).astype(jnp.bfloat16)]
  transfers between devices with their start and end apart: 37 -> 39, of which waited for: 27 -> 24; matrix products, arithmetic and copies ran while one was open for 21% -> 8% of each run, Pallas kernels for 4% -> 4%
where the time goes in v6:
time: 228 us; the launch traced here: 227 us
  waiting for transfers between devices  87.7 us (38%)
  starting transfers between devices  71.1 us (31%)
  matrix products  22.5 us (10%)
  other arithmetic  21 us (9%)
  local copies, waits for them, and re-layouts  11.3 us (5%)
  Pallas kernels  8.16 us (4%)
  between operations  5.54 us (2%)
    ppermute x25, waiting for transfers between devices, swap_with(): lax.ppermute(values, name, [(index, index ^ bit) for index in range(size)])  47.4 us
    ppermute x7, waiting for transfers between devices, direct_sum(): lax.ppermute(outgoing, name, [(source, (source + shift) % size) for sourc...  31.3 us
    ppermute x7, starting transfers between devices, direct_sum(): lax.ppermute(mine, name, [(source, (source + shift) % size) for source in...  29.8 us
    ppermute x25, starting transfers between devices, swap_with(): lax.ppermute(values, name, [(index, index ^ bit) for index in range(size)])  25.1 us
    ppermute x7, starting transfers between devices, direct_sum(): lax.ppermute(outgoing, name, [(source, (source + shift) % size) for sourc...  16.3 us
    dot_general x3, matrix products, exact_dot(): lax.dot_general(lhs_bf16, split2(rhs_f32), ((contract, (0,)), ((), ())),...  12.8 us
    ppermute x7, waiting for transfers between devices, direct_sum(): lax.ppermute(mine, name, [(source, (source + shift) % size) for source in...  9.05 us
    pallas_call x1, Pallas kernels, updated_weights(): pl.pallas_call(update_kernel, out_shape=jax.ShapeDtypeStruct(weights.shap...  8.16 us
  transfers between devices with their start and end apart: 39, of which 24 were waited for; matrix products, arithmetic and copies ran while one was open for 8% of the time, Pallas kernels for 4%

profile of v6, /device:TPU:0, one launch (start us, length us, event | category | flops | bytes accessed | tf_op | source)
XLA Modules:
  0.0 227.4 jit_solution(16481771683053275759)
XLA Ops:
  0.7 2.5 %convert_element_type.122 = bf16[1600,256]{1,0:T(8,128)(2,1)} convert(f32[1600,256]{1,0:T(8,128)} %param.18) | non-fusion elementwise | flops 409600 | bytes 2457600 | tf_op jit(solution)/shard_map/convert_element_type | solution.py:244
  4.3 1.5 copy.35
  6.0 5.5 %convolution_bitcast_fusion = f32[1600,512]{1,0:T(8,128)S(1)} fusion(bf16[1600,1600]{1,0:T(8,128)(2,1)} %bitcast.72, bf16[1600,256]{0,1:T(8,128)(2,1)S(1)} %subtract_convert_fusion, bf16[1600,256]{0,1:T(8,128)(2,1)S(1)} %copy.35), kind=kOutput, calls=%fused_computation | convolution fusion | flops 2624716800 | bytes 10035200 | tf_op jit(solution)/shard_map/dot_general | solution.py:251
  11.9 1.2 copy-done
  13.3 3.0 %collective-permute-start = (f32[232,256]{1,0:T(8,128)S(1)}, f32[232,256]{1,0:T(8,128)S(1)}, u32[]{:S(2)}, u32[]{:S(2)}) collective-permute-start(f32[232,256]{1,0:T(8,128)S(1)} %get-tuple-element.39), channel_id=1, source_target_pairs={{0,4},{4,8},{8,12},{12,16},{16,20},{20,24},{24,28},{28,0},{1,5},{5... | collective-permute-start | bytes 712712 | tf_op jit(solution)/shard_map/ppermute | solution.py:122
  16.3 3.6 %collective-permute-start.5 = (f32[232,256]{1,0:T(8,128)S(1)}, f32[232,256]{1,0:T(8,128)S(1)}, u32[]{:S(2)}, u32[]{:S(2)}) collective-permute-start(f32[232,256]{1,0:T(8,128)S(1)} %get-tuple-element.40), channel_id=1, source_target_pairs={{0,24},{4,28},{8,0},{12,4},{16,8},{20,12},{24,16},{28,20},{1,25},{... | collective-permute-start | bytes 712712 | tf_op jit(solution)/shard_map/ppermute | solution.py:122
  20.3 2.0 collective-permute-start.3
  22.8 3.2 %collective-permute-done = f32[232,256]{1,0:T(8,128)S(1)} collective-permute-done((f32[232,256]{1,0:T(8,128)S(1)}, f32[232,256]{1,0:T(8,128)S(1)}, u32[]{:S(2)}, u32[]{:S(2)}) %collective-permute-start) | collective-permute-done | bytes 237600 | tf_op jit(solution)/shard_map/ppermute | solution.py:122
  26.1 6.8 %collective-permute-start.6 = (f32[232,256]{1,0:T(8,128)S(1)}, f32[232,256]{1,0:T(8,128)}, u32[]{:S(2)}, u32[]{:S(2)}) collective-permute-start(f32[232,256]{1,0:T(8,128)S(1)} %get-tuple-element.45), channel_id=1, source_target_pairs={{0,28},{4,0},{8,4},{12,8},{16,12},{20,16},{24,20},{28,24},{1,29},{... | collective-permute-start | bytes 712712 | tf_op jit(solution)/shard_map/ppermute | solution.py:122
  32.9 1.9 collective-permute-done.4
  34.8 21.8 %collective-permute-done.3 = f32[232,256]{1,0:T(8,128)S(1)} collective-permute-done((f32[232,256]{1,0:T(8,128)S(1)}, f32[232,256]{1,0:T(8,128)S(1)}, u32[]{:S(2)}, u32[]{:S(2)}) %collective-permute-start.3) | collective-permute-done | bytes 237600 | tf_op jit(solution)/shard_map/ppermute | solution.py:122
  56.6 4.3 %collective-permute-done.2 = f32[232,256]{1,0:T(8,128)} collective-permute-done((f32[232,256]{1,0:T(8,128)S(1)}, f32[232,256]{1,0:T(8,128)}, u32[]{:S(2)}, u32[]{:S(2)}) %collective-permute-start.2) | collective-permute-done | bytes 237600 | tf_op jit(solution)/shard_map/ppermute | solution.py:122
  62.6 1.5 constant_dynamic-update-slice_fusion.7
  64.1 0.9 collective-permute-start.8
  65.0 1.4 fusion.6.basis_ref
  67.1 3.5 %collective-permute-start.9 = (f32[232,256]{1,0:T(8,128)S(1)}, f32[232,256]{1,0:T(8,128)S(1)}, u32[]{:S(2)}, u32[]{:S(2)}) collective-permute-start(f32[232,256]{1,0:T(8,128)S(1)} %get-tuple-element.32), channel_id=1, source_target_pairs={{0,12},{4,16},{8,20},{12,24},{16,28},{20,0},{24,4},{28,8},{1,13},{... | collective-permute-start | bytes 712712 | tf_op jit(solution)/shard_map/ppermute | solution.py:128
  70.6 3.8 %collective-permute-start.12 = (f32[232,256]{1,0:T(8,128)S(1)}, f32[232,256]{1,0:T(8,128)S(1)}, u32[]{:S(2)}, u32[]{:S(2)}) collective-permute-start(f32[232,256]{1,0:T(8,128)S(1)} %get-tuple-element.32), channel_id=1, source_target_pairs={{0,24},{4,28},{8,0},{12,4},{16,8},{20,12},{24,16},{28,20},{1,25},{... | collective-permute-start | bytes 712712 | tf_op jit(solution)/shard_map/ppermute | solution.py:128
  74.4 2.1 collective-permute-done.7
  76.5 21.1 %collective-permute-start.10 = (f32[232,256]{1,0:T(8,128)S(1)}, f32[232,256]{1,0:T(8,128)S(1)}, u32[]{:S(2)}, u32[]{:S(2)}) collective-permute-start(f32[232,256]{1,0:T(8,128)S(1)} %get-tuple-element.32), channel_id=1, source_target_pairs={{0,16},{4,20},{8,24},{12,28},{16,0},{20,4},{24,8},{28,12},{1,17},{... | collective-permute-start | bytes 712712 | tf_op jit(solution)/shard_map/ppermute | solution.py:128
  98.2 6.9 %collective-permute-done.10 = f32[232,256]{1,0:T(8,128)S(1)} collective-permute-done((f32[232,256]{1,0:T(8,128)S(1)}, f32[232,256]{1,0:T(8,128)S(1)}, u32[]{:S(2)}, u32[]{:S(2)}) %collective-permute-start.10) | collective-permute-done | bytes 237600 | tf_op jit(solution)/shard_map/ppermute | solution.py:128
  105.2 1.3 fusion.111
  106.8 2.1 multiply_reduce_fusion.1
  108.9 4.9 %convolution_bitcast_fusion.1 = f32[1600,256]{1,0:T(8,128)S(1)} fusion(bf16[1600,1600]{1,0:T(8,128)(2,1)} %bitcast.73, bf16[1600,128]{1,0:T(8,128)(2,1)S(1)} %get-tuple-element.18, bf16[1600,128]{1,0:T(8,128)(2,1)S(1)} %get-tuple-element.19), kind=kOutput, calls=%fused_computation.1 | convolution fusion | flops 1312358400 | bytes 7577600 | tf_op jit(solution)/shard_map/dot_general | solution.py:251
  113.9 0.8 pad_dynamic-slice_fusion
  114.8 2.4 %convolution_bitcast_fusion.2 = f32[1600,256]{1,0:T(8,128)S(1)} fusion(bf16[1600,1600]{1,0:T(8,128)(2,1)S(1)} %bitcast.76, bf16[1600,128]{1,0:T(8,128)(2,1)S(1)} %get-tuple-element.33, bf16[1600,128]{1,0:T(8,128)(2,1)S(1)} %get-tuple-element.34), kind=kOutput, calls=%fused_computation.2 | convolution fusion | flops 1312358400 | bytes 7577600 | tf_op jit(solution)/shard_map/dot_general | solution.py:251
  119.7 1.8 reshape_reshape.4
  121.6 1.5 collective-permute-start.15
  123.9 1.3 collective-permute-done.15
  127.6 0.9 mul.396
  128.5 1.4 multiply_divide_fusion.2
  130.1 2.0 convert_bitcast_fusion
  132.1 3.7 %collective-permute-start.18 = (bf16[1,250,256]{2,1,0:T(8,128)(2,1)S(1)}, bf16[1,250,256]{2,1,0:T(8,128)(2,1)S(1)}, u32[]{:S(2)}, u32[]{:S(2)}) collective-permute-start(bf16[1,250,256]{2,1,0:T(8,128)(2,1)S(1)} %maximum_bitcast_fusion), channel_id=1, source_target_pairs={{0,16},{4,20},{8,24},{12,28},{16,0},{20,4},{24,8},{28,12},{1,17},{... | collective-permute-start | bytes 384008 | tf_op jit(solution)/shard_map/ppermute | solution.py:87
  136.5 5.1 %collective-permute-done.18 = bf16[1,250,256]{2,1,0:T(8,128)(2,1)S(1)} collective-permute-done((bf16[1,250,256]{2,1,0:T(8,128)(2,1)S(1)}, bf16[1,250,256]{2,1,0:T(8,128)(2,1)S(1)}, u32[]{:S(2)}, u32[]{:S(2)}) %collective-permute-start.18) | collective-permute-done | bytes 128032 | tf_op jit(solution)/shard_map/ppermute | solution.py:87
  141.6 0.9 collective-permute-start.19
  142.5 1.1 fusion.16
  143.6 1.2 collective-permute-start.22
  144.8 3.9 %collective-permute-done.19 = bf16[2,250,256]{2,1,0:T(8,128)(2,1)S(1)} collective-permute-done((bf16[2,250,256]{2,1,0:T(8,128)(2,1)S(1)}, bf16[2,250,256]{2,1,0:T(8,128)(2,1)S(1)}, u32[]{:S(2)}, u32[]{:S(2)}) %collective-permute-start.19) | collective-permute-done | bytes 256032 | tf_op jit(solution)/shard_map/ppermute | solution.py:87
  148.8 1.9 collective-permute-done.22
  150.7 1.5 collective-permute-start.23
  153.0 3.9 %collective-permute-done.23 = f32[224,128]{1,0:T(8,128)S(1)} collective-permute-done((f32[224,128]{1,0:T(8,128)S(1)}, f32[224,128]{1,0:T(8,128)S(1)}, u32[]{:S(2)}, u32[]{:S(2)}) %collective-permute-start.23) | collective-permute-done | bytes 114720 | tf_op jit(solution)/shard_map/ppermute | solution.py:87
  157.3 1.1 fusion.15
  158.4 3.1 %collective-permute-done.24 = f32[112,128]{1,0:T(8,128)S(1)} collective-permute-done((f32[112,128]{1,0:T(8,128)S(1)}, f32[112,128]{1,0:T(8,128)S(1)}, u32[]{:S(2)}, u32[]{:S(2)}) %collective-permute-start.24) | collective-permute-done | bytes 57376 | tf_op jit(solution)/shard_map/ppermute | solution.py:87
  161.5 3.1 %collective-permute-start.25 = (f32[56,128]{1,0:T(8,128)S(1)}, f32[56,128]{1,0:T(8,128)S(1)}, u32[]{:S(2)}, u32[]{:S(2)}) collective-permute-start(f32[56,128]{1,0:T(8,128)S(1)} %constant_dynamic-slice_fusion.3), channel_id=1, source_target_pairs={{0,16},{4,20},{8,24},{12,28},{16,0},{20,4},{24,8},{28,12},{1,17},{... | collective-permute-start | bytes 86024 | tf_op jit(solution)/shard_map/ppermute | solution.py:87
  164.8 1.9 collective-permute-done.25
  166.7 2.8 %collective-permute-start.26 = (f32[56,128]{1,0:T(8,128)S(1)}, f32[56,128]{1,0:T(8,128)S(1)}, u32[]{:S(2)}, u32[]{:S(2)}) collective-permute-start(f32[56,128]{1,0:T(8,128)S(1)} %dynamic-slice_add_fusion.7), channel_id=1, source_target_pairs={{0,16},{4,20},{8,24},{12,28},{16,0},{20,4},{24,8},{28,12},{1,17},{... | collective-permute-start | bytes 86024 | tf_op jit(solution)/shard_map/ppermute | solution.py:87
  169.8 1.3 pad_maximum_fusion.3.direction_ref
  171.1 8.2 %shard_map.221 = bf16[8,200,1600]{2,1,0:T(8,128)(2,1)} custom-call(bf16[8,200,512]{2,1,0:T(8,128)(2,1)} %pad_maximum_fusion.3.direction_ref, bf16[512,1600]{1,0:T(8,128)(2,1)} %fusion.6.basis_ref, bf16[8,200,1600]{2,1,0:T(8,128)(2,1)} %bitcast.67), custom_call_target="tpu_custom_call" | custom-call | tf_op jit(solution)/shard_map/pallas_call | solution.py:230
  180.1 4.4 %collective-permute-done.31 = f32[224,128]{1,0:T(8,128)S(1)} collective-permute-done((f32[224,128]{1,0:T(8,128)S(1)}, f32[224,128]{1,0:T(8,128)S(1)}, u32[]{:S(2)}, u32[]{:S(2)}) %collective-permute-start.31) | collective-permute-done | bytes 114720 | tf_op jit(solution)/shard_map/ppermute | solution.py:87
  184.5 1.1 collective-permute-start.32
  185.6 3.1 %collective-permute-done.32 = f32[112,128]{1,0:T(8,128)S(1)} collective-permute-done((f32[112,128]{1,0:T(8,128)S(1)}, f32[112,128]{1,0:T(8,128)S(1)}, u32[]{:S(2)}, u32[]{:S(2)}) %collective-permute-start.32) | collective-permute-done | bytes 57376 | tf_op jit(solution)/shard_map/ppermute | solution.py:87
  188.7 2.5 %collective-permute-start.33 = (f32[56,128]{1,0:T(8,128)S(1)}, f32[56,128]{1,0:T(8,128)S(1)}, u32[]{:S(2)}, u32[]{:S(2)}) collective-permute-start(f32[56,128]{1,0:T(8,128)S(1)} %constant_dynamic-slice_fusion), channel_id=1, source_target_pairs={{0,16},{4,20},{8,24},{12,28},{16,0},{20,4},{24,8},{28,12},{1,17},{... | collective-permute-start | bytes 86024 | tf_op jit(solution)/shard_map/ppermute | solution.py:87
  191.2 2.5 %collective-permute-done.33 = f32[56,128]{1,0:T(8,128)S(1)} collective-permute-done((f32[56,128]{1,0:T(8,128)S(1)}, f32[56,128]{1,0:T(8,128)S(1)}, u32[]{:S(2)}, u32[]{:S(2)}) %collective-permute-start.33) | collective-permute-done | bytes 28704 | tf_op jit(solution)/shard_map/ppermute | solution.py:87
  193.7 2.2 collective-permute-start.34
  196.1 2.5 %collective-permute-done.34 = f32[56,128]{1,0:T(8,128)S(1)} collective-permute-done((f32[56,128]{1,0:T(8,128)S(1)}, f32[56,128]{1,0:T(8,128)S(1)}, u32[]{:S(2)}, u32[]{:S(2)}) %collective-permute-start.34) | collective-permute-done | bytes 28704 | tf_op jit(solution)/shard_map/ppermute | solution.py:87
  198.6 0.9 collective-permute-start.35
  199.5 2.4 %collective-permute-done.28 = f32[224,128]{1,0:T(8,128)S(1)} collective-permute-done((f32[224,128]{1,0:T(8,128)S(1)}, f32[224,128]{1,0:T(8,128)S(1)}, u32[]{:S(2)}, u32[]{:S(2)}) %collective-permute-start.28) | collective-permute-done | bytes 114720 | tf_op jit(solution)/shard_map/ppermute | solution.py:87
  201.9 0.9 collective-permute-done.35
  203.8 3.8 %collective-permute-done.36 = f32[224,128]{1,0:T(8,128)S(1)} collective-permute-done((f32[224,128]{1,0:T(8,128)S(1)}, f32[224,128]{1,0:T(8,128)S(1)}, u32[]{:S(2)}, u32[]{:S(2)}) %collective-permute-start.36) | collective-permute-done | bytes 114720 | tf_op jit(solution)/shard_map/ppermute | solution.py:87
  208.1 1.2 collective-permute-done.29
  209.4 4.4 %collective-permute-done.37 = f32[448,128]{1,0:T(8,128)S(1)} collective-permute-done((f32[448,128]{1,0:T(8,128)S(1)}, f32[448,128]{1,0:T(8,128)S(1)}, u32[]{:S(2)}, u32[]{:S(2)}) %collective-permute-start.37) | collective-permute-done | bytes 229408 | tf_op jit(solution)/shard_map/ppermute | solution.py:87
  214.8 1.0 collective-permute-done.38
  215.9 1.0 multiply_reduce_fusion
  217.6 2.9 %fusion.3 = f32[256,256]{1,0:T(8,128)S(1)} fusion(f32[]{:T(128)S(6)} %rsqrt.4, f32[896,128]{1,0:T(8,128)S(1)} %get-tuple-element.51, f32[896,128]{1,0:T(8,128)S(1)} %get-tuple-element.50, f32[896,128]{1,0:T(8,128)S(1)} %get-tuple-element.49, f32[896,128]{1,0:T(8,128)S(1)} %get-tuple-element.48), kind=kOutput, calls=%fused_computation.17 | convolution fusion | flops 1259929600 | bytes 2097156 | tf_op jit(solution)/shard_map/dot_general | solution.py:32
  225.4 2.0 fusion.1
  (157 shorter events, 19.7 us)
Async XLA Ops:
  0.6 2.6 %copy-start.1 = (f32[1600,256]{1,0:T(8,128)S(1)}, f32[1600,256]{1,0:T(8,128)}, u32[]{:S(2)}) copy-start(f32[1600,256]{1,0:T(8,128)} %param.18) | copy-start | bytes 4915204
  3.3 0.8 copy-start.14
  3.3 0.9 copy-start.9
  6.0 5.5 %copy-start.2 = (bf16[1600,256]{0,1:T(8,128)(2,1)}, bf16[1600,256]{0,1:T(8,128)(2,1)S(1)}, u32[]{:S(2)}) copy-start(bf16[1600,256]{0,1:T(8,128)(2,1)S(1)} %subtract_convert_fusion) | copy-start | bytes 2457604
  11.9 1.3 copy-start
  13.3 12.7 %collective-permute-start = (f32[232,256]{1,0:T(8,128)S(1)}, f32[232,256]{1,0:T(8,128)S(1)}, u32[]{:S(2)}, u32[]{:S(2)}) collective-permute-start(f32[232,256]{1,0:T(8,128)S(1)} %get-tuple-element.39), channel_id=1, source_target_pairs={{0,4},{4,8},{8,12},{12,16},{16,20},{20,24},{24,28},{28,0},{1,5},{5... | collective-permute-start | bytes 712712 | tf_op jit(solution)/shard_map/ppermute | solution.py:122
  16.3 9.9 %collective-permute-start.5 = (f32[232,256]{1,0:T(8,128)S(1)}, f32[232,256]{1,0:T(8,128)S(1)}, u32[]{:S(2)}, u32[]{:S(2)}) collective-permute-start(f32[232,256]{1,0:T(8,128)S(1)} %get-tuple-element.40), channel_id=1, source_target_pairs={{0,24},{4,28},{8,0},{12,4},{16,8},{20,12},{24,16},{28,20},{1,25},{... | collective-permute-start | bytes 712712 | tf_op jit(solution)/shard_map/ppermute | solution.py:122
  19.9 14.9 %collective-permute-start.4 = (f32[232,256]{1,0:T(8,128)S(1)}, f32[232,256]{1,0:T(8,128)S(1)}, u32[]{:S(2)}, u32[]{:S(2)}) collective-permute-start(f32[232,256]{1,0:T(8,128)S(1)} %get-tuple-element.41), channel_id=1, source_target_pairs={{0,20},{4,24},{8,28},{12,0},{16,4},{20,8},{24,12},{28,16},{1,21},{... | collective-permute-start | bytes 712712 | tf_op jit(solution)/shard_map/ppermute | solution.py:122
  20.3 36.3 %collective-permute-start.3 = (f32[232,256]{1,0:T(8,128)S(1)}, f32[232,256]{1,0:T(8,128)S(1)}, u32[]{:S(2)}, u32[]{:S(2)}) collective-permute-start(f32[232,256]{1,0:T(8,128)S(1)} %get-tuple-element.42), channel_id=1, source_target_pairs={{0,16},{4,20},{8,24},{12,28},{16,0},{20,4},{24,8},{28,12},{1,17},{... | collective-permute-start | bytes 712712 | tf_op jit(solution)/shard_map/ppermute | solution.py:122
  22.3 38.6 %collective-permute-start.2 = (f32[232,256]{1,0:T(8,128)S(1)}, f32[232,256]{1,0:T(8,128)}, u32[]{:S(2)}, u32[]{:S(2)}) collective-permute-start(f32[232,256]{1,0:T(8,128)S(1)} %get-tuple-element.43), channel_id=1, source_target_pairs={{0,12},{4,16},{8,20},{12,24},{16,28},{20,0},{24,4},{28,8},{1,13},{... | collective-permute-start | bytes 712712 | tf_op jit(solution)/shard_map/ppermute | solution.py:122
  25.9 34.9 %collective-permute-start.1 = (f32[232,256]{1,0:T(8,128)S(1)}, f32[232,256]{1,0:T(8,128)S(1)}, u32[]{:S(2)}, u32[]{:S(2)}) collective-permute-start(f32[232,256]{1,0:T(8,128)S(1)} %get-tuple-element.44), channel_id=1, source_target_pairs={{0,8},{4,12},{8,16},{12,20},{16,24},{20,28},{24,0},{28,4},{1,9},{5... | collective-permute-start | bytes 712712 | tf_op jit(solution)/shard_map/ppermute | solution.py:122
  26.1 35.5 %collective-permute-start.6 = (f32[232,256]{1,0:T(8,128)S(1)}, f32[232,256]{1,0:T(8,128)}, u32[]{:S(2)}, u32[]{:S(2)}) collective-permute-start(f32[232,256]{1,0:T(8,128)S(1)} %get-tuple-element.45), channel_id=1, source_target_pairs={{0,28},{4,0},{8,4},{12,8},{16,12},{20,16},{24,20},{28,24},{1,29},{... | collective-permute-start | bytes 712712 | tf_op jit(solution)/shard_map/ppermute | solution.py:122
  32.9 32.1 %copy-start.3 = (bf16[1600,256]{0,1:T(8,128)(2,1)S(1)}, bf16[1600,256]{0,1:T(8,128)(2,1)}, u32[]{:S(2)}) copy-start(bf16[1600,256]{0,1:T(8,128)(2,1)} %copy-done.2) | copy-start | bytes 2457604
  34.8 26.1 %copy-start.4 = (f32[232,256]{1,0:T(8,128)}, f32[232,256]{1,0:T(8,128)S(1)}, u32[]{:S(2)}) copy-start(f32[232,256]{1,0:T(8,128)S(1)} %collective-permute-done.4) | copy-start | bytes 712708
  56.6 5.0 %copy-start.6 = (f32[232,256]{1,0:T(8,128)}, f32[232,256]{1,0:T(8,128)S(1)}, u32[]{:S(2)}) copy-start(f32[232,256]{1,0:T(8,128)S(1)} %collective-permute-done.3) | copy-start | bytes 712708
  60.9 0.7 copy-start.7
  61.6 0.9 copy-start.5
  61.6 1.1 copy-start.8
  64.1 33.5 %collective-permute-start.8 = (f32[232,256]{1,0:T(8,128)S(1)}, f32[232,256]{1,0:T(8,128)S(1)}, u32[]{:S(2)}, u32[]{:S(2)}) collective-permute-start(f32[232,256]{1,0:T(8,128)S(1)} %get-tuple-element.32), channel_id=1, source_target_pairs={{0,8},{4,12},{8,16},{12,20},{16,24},{20,28},{24,0},{28,4},{1,9},{5... | collective-permute-start | bytes 712712 | tf_op jit(solution)/shard_map/ppermute | solution.py:128
  65.0 11.5 %collective-permute-start.7 = (f32[232,256]{1,0:T(8,128)S(1)}, f32[232,256]{1,0:T(8,128)S(1)}, u32[]{:S(2)}, u32[]{:S(2)}) collective-permute-start(f32[232,256]{1,0:T(8,128)S(1)} %get-tuple-element.32), channel_id=1, source_target_pairs={{0,4},{4,8},{8,12},{12,16},{16,20},{20,24},{24,28},{28,0},{1,5},{5... | collective-permute-start | bytes 712712 | tf_op jit(solution)/shard_map/ppermute | solution.py:128
  67.1 31.0 %collective-permute-start.9 = (f32[232,256]{1,0:T(8,128)S(1)}, f32[232,256]{1,0:T(8,128)S(1)}, u32[]{:S(2)}, u32[]{:S(2)}) collective-permute-start(f32[232,256]{1,0:T(8,128)S(1)} %get-tuple-element.32), channel_id=1, source_target_pairs={{0,12},{4,16},{8,20},{12,24},{16,28},{20,0},{24,4},{28,8},{1,13},{... | collective-permute-start | bytes 712712 | tf_op jit(solution)/shard_map/ppermute | solution.py:128
  70.6 34.6 %collective-permute-start.12 = (f32[232,256]{1,0:T(8,128)S(1)}, f32[232,256]{1,0:T(8,128)S(1)}, u32[]{:S(2)}, u32[]{:S(2)}) collective-permute-start(f32[232,256]{1,0:T(8,128)S(1)} %get-tuple-element.32), channel_id=1, source_target_pairs={{0,24},{4,28},{8,0},{12,4},{16,8},{20,12},{24,16},{28,20},{1,25},{... | collective-permute-start | bytes 712712 | tf_op jit(solution)/shard_map/ppermute | solution.py:128
  74.4 30.8 %collective-permute-start.11 = (f32[232,256]{1,0:T(8,128)S(1)}, f32[232,256]{1,0:T(8,128)S(1)}, u32[]{:S(2)}, u32[]{:S(2)}) collective-permute-start(f32[232,256]{1,0:T(8,128)S(1)} %get-tuple-element.32), channel_id=1, source_target_pairs={{0,20},{4,24},{8,28},{12,0},{16,4},{20,8},{24,12},{28,16},{1,21},{... | collective-permute-start | bytes 712712 | tf_op jit(solution)/shard_map/ppermute | solution.py:128
  76.5 28.6 %collective-permute-start.10 = (f32[232,256]{1,0:T(8,128)S(1)}, f32[232,256]{1,0:T(8,128)S(1)}, u32[]{:S(2)}, u32[]{:S(2)}) collective-permute-start(f32[232,256]{1,0:T(8,128)S(1)} %get-tuple-element.32), channel_id=1, source_target_pairs={{0,16},{4,20},{8,24},{12,28},{16,0},{20,4},{24,8},{28,12},{1,17},{... | collective-permute-start | bytes 712712 | tf_op jit(solution)/shard_map/ppermute | solution.py:128
  97.6 7.6 %collective-permute-start.13 = (f32[232,256]{1,0:T(8,128)S(1)}, f32[232,256]{1,0:T(8,128)S(1)}, u32[]{:S(2)}, u32[]{:S(2)}) collective-permute-start(f32[232,256]{1,0:T(8,128)S(1)} %get-tuple-element.32), channel_id=1, source_target_pairs={{0,28},{4,0},{8,4},{12,8},{16,12},{20,16},{24,20},{28,24},{1,29},{... | collective-permute-start | bytes 712712 | tf_op jit(solution)/shard_map/ppermute | solution.py:128
  106.8 8.0 %slice-start = ((s8[5324800]{0:T(1024)(128)(4,1)}), s8[4194304]{0:T(1024)(128)(4,1)S(1)}, s32[]{:S(2)}) async-start(s8[5324800]{0:T(1024)(128)(4,1)} %bitcast.74), calls=%async_computation | async-start | bytes 8388608
  108.9 5.9 %slice-start.1 = ((s8[5324800]{0:T(1024)(128)(4,1)}), s8[1130496]{0:T(1024)(128)(4,1)S(1)}, s32[]{:S(2)}) async-start(s8[5324800]{0:T(1024)(128)(4,1)} %bitcast.74), calls=%async_computation.1 | async-start | bytes 2260992
  114.8 27.8 %collective-permute-start.21 = (f32[896,128]{1,0:T(8,128)}, f32[896,128]{1,0:T(8,128)}, u32[]{:S(2)}, u32[]{:S(2)}) collective-permute-start(f32[896,128]{1,0:T(8,128)} %pad_dynamic-slice_fusion), channel_id=1, source_target_pairs={{0,1},{1,0},{2,3},{3,2},{4,5},{5,4},{6,7},{7,6},{8,9},{9,8},{10,11... | collective-permute-start | bytes 1376264 | tf_op jit(solution)/shard_map/ppermute | solution.py:87
  118.6 3.0 %collective-permute-start.14 = (f32[8,128]{1,0:T(8,128)S(1)}, f32[8,128]{1,0:T(8,128)S(1)}, u32[]{:S(2)}, u32[]{:S(2)}) collective-permute-start(f32[8,128]{1,0:T(8,128)S(1)} %broadcast_in_dim.10), channel_id=1, source_target_pairs={{0,1},{1,0},{2,3},{3,2},{4,5},{5,4},{6,7},{7,6},{8,9},{9,8},{10,11... | collective-permute-start | bytes 12296 | tf_op jit(solution)/shard_map/ppermute | solution.py:87
  121.6 3.6 %collective-permute-start.15 = (f32[8,128]{1,0:T(8,128)S(1)}, f32[8,128]{1,0:T(8,128)S(1)}, u32[]{:S(2)}, u32[]{:S(2)}) collective-permute-start(f32[8,128]{1,0:T(8,128)S(1)} %broadcast_add_fusion), channel_id=1, source_target_pairs={{0,2},{1,3},{2,0},{3,1},{4,6},{5,7},{6,4},{7,5},{8,10},{9,11},{10,... | collective-permute-start | bytes 12296 | tf_op jit(solution)/shard_map/ppermute | solution.py:87
  123.9 33.4 %collective-permute-start.16 = (f32[896,128]{1,0:T(8,128)}, f32[896,128]{1,0:T(8,128)}, u32[]{:S(2)}, u32[]{:S(2)}) collective-permute-start(f32[896,128]{1,0:T(8,128)} %pad_dynamic-slice_fusion.2), channel_id=1, source_target_pairs={{0,1},{1,0},{2,3},{3,2},{4,5},{5,4},{6,7},{7,6},{8,9},{9,8},{10,11... | collective-permute-start | bytes 1376264 | tf_op jit(solution)/shard_map/ppermute | solution.py:87
  127.6 8.2 %copy-start.11 = (f32[4,1600]{1,0:T(4,128)S(1)}, f32[4,1600]{1,0:T(4,128)}, u32[]{:S(2)}) copy-start(f32[4,1600]{1,0:T(4,128)} %param.21) | copy-start | bytes 76804
  127.6 8.2 %copy-start.12 = (f32[4,1600]{1,0:T(4,128)S(1)}, f32[4,1600]{1,0:T(4,128)}, u32[]{:S(2)}) copy-start(f32[4,1600]{1,0:T(4,128)} %param.23) | copy-start | bytes 76804
  127.6 8.2 %copy-start.13 = (f32[4,1600]{1,0:T(4,128)S(1)}, f32[4,1600]{1,0:T(4,128)}, u32[]{:S(2)}) copy-start(f32[4,1600]{1,0:T(4,128)} %param.22) | copy-start | bytes 76804
  132.1 9.4 %collective-permute-start.18 = (bf16[1,250,256]{2,1,0:T(8,128)(2,1)S(1)}, bf16[1,250,256]{2,1,0:T(8,128)(2,1)S(1)}, u32[]{:S(2)}, u32[]{:S(2)}) collective-permute-start(bf16[1,250,256]{2,1,0:T(8,128)(2,1)S(1)} %maximum_bitcast_fusion), channel_id=1, source_target_pairs={{0,16},{4,20},{8,24},{12,28},{16,0},{20,4},{24,8},{28,12},{1,17},{... | collective-permute-start | bytes 384008 | tf_op jit(solution)/shard_map/ppermute | solution.py:87
  141.6 7.1 %collective-permute-start.19 = (bf16[2,250,256]{2,1,0:T(8,128)(2,1)S(1)}, bf16[2,250,256]{2,1,0:T(8,128)(2,1)S(1)}, u32[]{:S(2)}, u32[]{:S(2)}) collective-permute-start(bf16[2,250,256]{2,1,0:T(8,128)(2,1)S(1)} %pad_maximum_fusion.9), channel_id=1, source_target_pairs={{0,8},{4,12},{8,0},{12,4},{16,24},{20,28},{24,16},{28,20},{1,9},{5... | collective-permute-start | bytes 768008 | tf_op jit(solution)/shard_map/ppermute | solution.py:87
  143.6 7.1 %collective-permute-start.22 = (f32[448,128]{1,0:T(8,128)S(1)}, f32[448,128]{1,0:T(8,128)S(1)}, u32[]{:S(2)}, u32[]{:S(2)}) collective-permute-start(f32[448,128]{1,0:T(8,128)S(1)} %constant_dynamic-slice_fusion.6), channel_id=1, source_target_pairs={{0,2},{1,3},{2,0},{3,1},{4,6},{5,7},{6,4},{7,5},{8,10},{9,11},{10,... | collective-permute-start | bytes 688136 | tf_op jit(solution)/shard_map/ppermute | solution.py:87
  150.7 6.1 %collective-permute-start.23 = (f32[224,128]{1,0:T(8,128)S(1)}, f32[224,128]{1,0:T(8,128)S(1)}, u32[]{:S(2)}, u32[]{:S(2)}) collective-permute-start(f32[224,128]{1,0:T(8,128)S(1)} %constant_dynamic-slice_fusion.5), channel_id=1, source_target_pairs={{0,4},{4,0},{8,12},{12,8},{16,20},{20,16},{24,28},{28,24},{1,5},{5... | collective-permute-start | bytes 344072 | tf_op jit(solution)/shard_map/ppermute | solution.py:87
  152.3 17.1 %collective-permute-start.20 = (bf16[4,250,256]{2,1,0:T(8,128)(2,1)S(1)}, bf16[4,250,256]{2,1,0:T(8,128)(2,1)S(1)}, u32[]{:S(2)}, u32[]{:S(2)}) collective-permute-start(bf16[4,250,256]{2,1,0:T(8,128)(2,1)S(1)} %pad_maximum_fusion.6), channel_id=1, source_target_pairs={{0,4},{4,0},{8,12},{12,8},{16,20},{20,16},{24,28},{28,24},{1,5},{5... | collective-permute-start | bytes 1536008 | tf_op jit(solution)/shard_map/ppermute | solution.py:87
  156.9 4.6 %collective-permute-start.24 = (f32[112,128]{1,0:T(8,128)S(1)}, f32[112,128]{1,0:T(8,128)S(1)}, u32[]{:S(2)}, u32[]{:S(2)}) collective-permute-start(f32[112,128]{1,0:T(8,128)S(1)} %constant_dynamic-slice_fusion.4), channel_id=1, source_target_pairs={{0,8},{4,12},{8,0},{12,4},{16,24},{20,28},{24,16},{28,20},{1,9},{5... | collective-permute-start | bytes 172040 | tf_op jit(solution)/shard_map/ppermute | solution.py:87
  161.5 5.1 %collective-permute-start.25 = (f32[56,128]{1,0:T(8,128)S(1)}, f32[56,128]{1,0:T(8,128)S(1)}, u32[]{:S(2)}, u32[]{:S(2)}) collective-permute-start(f32[56,128]{1,0:T(8,128)S(1)} %constant_dynamic-slice_fusion.3), channel_id=1, source_target_pairs={{0,16},{4,20},{8,24},{12,28},{16,0},{20,4},{24,8},{28,12},{1,17},{... | collective-permute-start | bytes 86024 | tf_op jit(solution)/shard_map/ppermute | solution.py:87
  164.7 14.5 %collective-permute-start.17 = (f32[448,128]{1,0:T(8,128)S(1)}, f32[448,128]{1,0:T(8,128)S(1)}, u32[]{:S(2)}, u32[]{:S(2)}) collective-permute-start(f32[448,128]{1,0:T(8,128)S(1)} %constant_dynamic-slice_fusion.7), channel_id=1, source_target_pairs={{0,4},{4,0},{8,12},{12,8},{16,20},{20,16},{24,28},{28,24},{1,5},{5... | collective-permute-start | bytes 688136 | tf_op jit(solution)/shard_map/ppermute | solution.py:87
  166.7 13.4 %collective-permute-start.26 = (f32[56,128]{1,0:T(8,128)S(1)}, f32[56,128]{1,0:T(8,128)S(1)}, u32[]{:S(2)}, u32[]{:S(2)}) collective-permute-start(f32[56,128]{1,0:T(8,128)S(1)} %dynamic-slice_add_fusion.7), channel_id=1, source_target_pairs={{0,16},{4,20},{8,24},{12,28},{16,0},{20,4},{24,8},{28,12},{1,17},{... | collective-permute-start | bytes 86024 | tf_op jit(solution)/shard_map/ppermute | solution.py:87
  179.6 4.9 %collective-permute-start.31 = (f32[224,128]{1,0:T(8,128)S(1)}, f32[224,128]{1,0:T(8,128)S(1)}, u32[]{:S(2)}, u32[]{:S(2)}) collective-permute-start(f32[224,128]{1,0:T(8,128)S(1)} %constant_dynamic-slice_fusion.2), channel_id=1, source_target_pairs={{0,8},{4,12},{8,0},{12,4},{16,24},{20,28},{24,16},{28,20},{1,9},{5... | collective-permute-start | bytes 344072 | tf_op jit(solution)/shard_map/ppermute | solution.py:87
  184.5 4.2 %collective-permute-start.32 = (f32[112,128]{1,0:T(8,128)S(1)}, f32[112,128]{1,0:T(8,128)S(1)}, u32[]{:S(2)}, u32[]{:S(2)}) collective-permute-start(f32[112,128]{1,0:T(8,128)S(1)} %constant_dynamic-slice_fusion.1), channel_id=1, source_target_pairs={{0,2},{1,3},{2,0},{3,1},{4,6},{5,7},{6,4},{7,5},{8,10},{9,11},{10,... | collective-permute-start | bytes 172040 | tf_op jit(solution)/shard_map/ppermute | solution.py:87
  185.6 5.6 %collective-permute-start.27 = (f32[112,128]{1,0:T(8,128)S(1)}, f32[112,128]{1,0:T(8,128)S(1)}, u32[]{:S(2)}, u32[]{:S(2)}) collective-permute-start(f32[112,128]{1,0:T(8,128)S(1)} %pad_maximum_fusion.14), channel_id=1, source_target_pairs={{0,8},{4,12},{8,0},{12,4},{16,24},{20,28},{24,16},{28,20},{1,9},{5... | collective-permute-start | bytes 172040 | tf_op jit(solution)/shard_map/ppermute | solution.py:87
  188.7 5.0 %collective-permute-start.33 = (f32[56,128]{1,0:T(8,128)S(1)}, f32[56,128]{1,0:T(8,128)S(1)}, u32[]{:S(2)}, u32[]{:S(2)}) collective-permute-start(f32[56,128]{1,0:T(8,128)S(1)} %constant_dynamic-slice_fusion), channel_id=1, source_target_pairs={{0,16},{4,20},{8,24},{12,28},{16,0},{20,4},{24,8},{28,12},{1,17},{... | collective-permute-start | bytes 86024 | tf_op jit(solution)/shard_map/ppermute | solution.py:87
  193.7 4.8 %collective-permute-start.34 = (f32[56,128]{1,0:T(8,128)S(1)}, f32[56,128]{1,0:T(8,128)S(1)}, u32[]{:S(2)}, u32[]{:S(2)}) collective-permute-start(f32[56,128]{1,0:T(8,128)S(1)} %dynamic-slice_add_fusion.6), channel_id=1, source_target_pairs={{0,16},{4,20},{8,24},{12,28},{16,0},{20,4},{24,8},{28,12},{1,17},{... | collective-permute-start | bytes 86024 | tf_op jit(solution)/shard_map/ppermute | solution.py:87
  196.0 5.9 %collective-permute-start.28 = (f32[224,128]{1,0:T(8,128)S(1)}, f32[224,128]{1,0:T(8,128)S(1)}, u32[]{:S(2)}, u32[]{:S(2)}) collective-permute-start(f32[224,128]{1,0:T(8,128)S(1)} %pad_maximum_fusion.12), channel_id=1, source_target_pairs={{0,4},{4,0},{8,12},{12,8},{16,20},{20,16},{24,28},{28,24},{1,5},{5... | collective-permute-start | bytes 344072 | tf_op jit(solution)/shard_map/ppermute | solution.py:87
  198.6 4.2 %collective-permute-start.35 = (f32[112,128]{1,0:T(8,128)S(1)}, f32[112,128]{1,0:T(8,128)S(1)}, u32[]{:S(2)}, u32[]{:S(2)}) collective-permute-start(f32[112,128]{1,0:T(8,128)S(1)} %pad_maximum_fusion.15), channel_id=1, source_target_pairs={{0,2},{1,3},{2,0},{3,1},{4,6},{5,7},{6,4},{7,5},{8,10},{9,11},{10,... | collective-permute-start | bytes 172040 | tf_op jit(solution)/shard_map/ppermute | solution.py:87
  202.8 4.9 %collective-permute-start.36 = (f32[224,128]{1,0:T(8,128)S(1)}, f32[224,128]{1,0:T(8,128)S(1)}, u32[]{:S(2)}, u32[]{:S(2)}) collective-permute-start(f32[224,128]{1,0:T(8,128)S(1)} %pad_maximum_fusion.13), channel_id=1, source_target_pairs={{0,8},{4,12},{8,0},{12,4},{16,24},{20,28},{24,16},{28,20},{1,9},{5... | collective-permute-start | bytes 344072 | tf_op jit(solution)/shard_map/ppermute | solution.py:87
  203.2 6.1 %collective-permute-start.29 = (f32[448,128]{1,0:T(8,128)S(1)}, f32[448,128]{1,0:T(8,128)S(1)}, u32[]{:S(2)}, u32[]{:S(2)}) collective-permute-start(f32[448,128]{1,0:T(8,128)S(1)} %pad_maximum_fusion.10), channel_id=1, source_target_pairs={{0,2},{1,3},{2,0},{3,1},{4,6},{5,7},{6,4},{7,5},{8,10},{9,11},{10,... | collective-permute-start | bytes 688136 | tf_op jit(solution)/shard_map/ppermute | solution.py:87
  207.7 6.3 %copy-start.10 = (bf16[1,8,4,1600]{3,2,1,0:T(4,128)(2,1)S(1)}, bf16[1,8,4,1600]{3,2,1,0:T(4,128)(2,1)}, u32[]{:S(2)}) copy-start(bf16[1,8,4,1600]{3,2,1,0:T(4,128)(2,1)} %param.24) | copy-start | bytes 307204
  207.7 6.1 %collective-permute-start.37 = (f32[448,128]{1,0:T(8,128)S(1)}, f32[448,128]{1,0:T(8,128)S(1)}, u32[]{:S(2)}, u32[]{:S(2)}) collective-permute-start(f32[448,128]{1,0:T(8,128)S(1)} %pad_maximum_fusion.11), channel_id=1, source_target_pairs={{0,4},{4,0},{8,12},{12,8},{16,20},{20,16},{24,28},{28,24},{1,5},{5... | collective-permute-start | bytes 688136 | tf_op jit(solution)/shard_map/ppermute | solution.py:87
  209.3 5.4 %collective-permute-start.30 = (f32[896,128]{1,0:T(8,128)S(1)}, f32[896,128]{1,0:T(8,128)S(1)}, u32[]{:S(2)}, u32[]{:S(2)}) collective-permute-start(f32[896,128]{1,0:T(8,128)S(1)} %pad_maximum_fusion.7), channel_id=1, source_target_pairs={{0,1},{1,0},{2,3},{3,2},{4,5},{5,4},{6,7},{7,6},{8,9},{9,8},{10,11... | collective-permute-start | bytes 1376264 | tf_op jit(solution)/shard_map/ppermute | solution.py:87
  213.9 1.9 collective-permute-start.38

commit v7 on v4

--- a/solution.py
+++ b/solution.py
@@ -87,6 +87,13 @@
     return lax.ppermute(values, name, [(index, index ^ bit) for index in range(size)])
 
 
+def place_pair(mine, other, side):
+    length = mine.shape[0]
+    full = jnp.zeros((2 * length,) + mine.shape[1:], mine.dtype)
+    full = lax.dynamic_update_slice_in_dim(full, mine, side * length, 0)
+    return lax.dynamic_update_slice_in_dim(full, other, (1 - side) * length, 0)
+
+
 def run_steps(parts, steps):
     sides = []
     for name, bit, size in steps:
@@ -98,9 +105,7 @@
         sides.append(side)
     for (name, bit, size), side in zip(reversed(steps), reversed(sides)):
         other = swap_with(parts, name, bit, size)
-        first = jnp.where(side == 0, parts, other)
-        second = jnp.where(side == 0, other, parts)
-        parts = jnp.concatenate([first, second], axis=0)
+        parts = place_pair(parts, other, side)
     return parts
 
 
@@ -166,9 +171,7 @@
     while bit >= 1:
         side = (lax.axis_index(name) // bit) % 2
         other = swap_with(parts, name, bit, size)
-        first = jnp.where(side == 0, parts, other)
-        second = jnp.where(side == 0, other, parts)
-        parts = jnp.concatenate([first, second], axis=0)
+        parts = place_pair(parts, other, side)
         bit //= 2
         levels += 1
     parts = parts.reshape((2,) * levels + piece.shape)

time: 202 us -> 198 us (0.980)
  waiting for transfers between devices: 70 us -> 75.8 us
  starting transfers between devices: 49.7 us -> 44 us
  other arithmetic: 27.6 us -> 24.8 us
  matrix products: 27.7 us -> 25.4 us
    ppermute x37, waiting for transfers between devices: 70 us -> 75.8 us  [swap_with(): lax.ppermute(values, name, [(index, index ^ bit) for index in range(size)])]
    ppermute x37, starting transfers between devices: 49.7 us -> 44 us  [swap_with(): lax.ppermute(values, name, [(index, index ^ bit) for index in range(size)])]
    select_n x19 -> x0, other arithmetic: 2.74 us -> none  [the longest x16 2.58 us: run_steps(): first = jnp.where(side == 0, parts, other)]
    dot_general x4, matrix products: 18 us -> 15.7 us  [exact_dot(): lax.dot_general(lhs_bf16, split2(rhs_f32), ((contract, (0,)), ((), ())),...]
    convert_element_type x3 -> x4, other arithmetic: 5.11 us -> 5.03 us  [split2(): second = (values - first.astype(jnp.float32)).astype(jnp.bfloat16)]
    add x16 -> x12, other arithmetic: 4.52 us -> 4.49 us  [run_steps(): parts = keep + swap_with(send, name, bit, size)]
  transfers between devices with their start and end apart: 37 -> 37, of which waited for: 24 -> 25; matrix products, arithmetic and copies ran while one was open for 22% -> 19% of each run, Pallas kernels for 4% -> 4%
where the time goes in v7:
time: 198 us; the launch traced here: 197 us
  waiting for transfers between devices  75.8 us (38%)
  starting transfers between devices  44 us (22%)
  matrix products  25.4 us (13%)
  other arithmetic  24.8 us (13%)
  local copies, waits for them, and re-layouts  12.8 us (6%)
  Pallas kernels  8.16 us (4%)
  between operations  5.82 us (3%)
    ppermute x37, waiting for transfers between devices, swap_with(): lax.ppermute(values, name, [(index, index ^ bit) for index in range(size)])  75.8 us
    ppermute x37, starting transfers between devices, swap_with(): lax.ppermute(values, name, [(index, index ^ bit) for index in range(size)])  44 us
    dot_general x4, matrix products, exact_dot(): lax.dot_general(lhs_bf16, split2(rhs_f32), ((contract, (0,)), ((), ())),...  15.7 us
    pallas_call x1, Pallas kernels, updated_weights(): pl.pallas_call(update_kernel, out_shape=jax.ShapeDtypeStruct(weights.shap...  8.16 us
    convert_element_type x4, other arithmetic, split2(): second = (values - first.astype(jnp.float32)).astype(jnp.bfloat16)  5.03 us
    add x12, other arithmetic, run_steps(): parts = keep + swap_with(send, name, bit, size)  4.49 us
  transfers between devices with their start and end apart: 37, of which 25 were waited for; matrix products, arithmetic and copies ran while one was open for 19% of the time, Pallas kernels for 4%

profile of v7, /device:TPU:0, one launch (start us, length us, event | category | flops | bytes accessed | tf_op | source)
XLA Modules:
  0.0 196.8 jit_solution(15749549606811193106)
XLA Ops:
  0.7 2.2 %subtract_convert_fusion.4 = (bf16[1600,128]{1,0:T(8,128)(2,1)S(1)}, bf16[1600,128]{1,0:T(8,128)(2,1)S(1)}, bf16[1600,128]{1,0:T(8,128)(2,1)S(1)}, bf16[1600,128]{1,0:T(8,128)(2,1)S(1)}) fusion(f32[1600,256]{1,0:T(8,128)} %param.18), kind=kLoop, calls=%fused_computation.52 | loop fusion | flops 1228800 | bytes 4096000 | tf_op jit(solution)/shard_map/convert_element_type | solution.py:216
  2.8 4.2 %convolution_bitcast_fusion.1 = f32[1600,256]{1,0:T(8,128)S(1)} fusion(bf16[1600,1600]{1,0:T(8,128)(2,1)} %bitcast.73, bf16[1600,128]{1,0:T(8,128)(2,1)S(1)} %get-tuple-element.35, bf16[1600,128]{1,0:T(8,128)(2,1)S(1)} %get-tuple-element.36), kind=kOutput, calls=%fused_computation.1 | convolution fusion | flops 1312358400 | bytes 7577600 | tf_op jit(solution)/shard_map/dot_general | solution.py:222
  9.6 2.9 %collective-permute-start = (f32[928,128]{1,0:T(8,128)}, f32[928,128]{1,0:T(8,128)}, u32[]{:S(2)}, u32[]{:S(2)}) collective-permute-start(f32[928,128]{1,0:T(8,128)} %constant_dynamic-slice_fusion.12), channel_id=1, source_target_pairs={{0,4},{4,0},{8,12},{12,8},{16,20},{20,16},{24,28},{28,24},{1,5},{5... | collective-permute-start | bytes 1425416 | tf_op jit(solution)/shard_map/ppermute | solution.py:87
  12.6 4.2 %convolution_bitcast_fusion = f32[1600,256]{1,0:T(8,128)S(1)} fusion(bf16[1600,1600]{1,0:T(8,128)(2,1)} %bitcast.74, bf16[1600,128]{1,0:T(8,128)(2,1)S(1)} %get-tuple-element.41, bf16[1600,128]{1,0:T(8,128)(2,1)S(1)} %get-tuple-element.42), kind=kOutput, calls=%fused_computation | convolution fusion | flops 1312358400 | bytes 7577600 | tf_op jit(solution)/shard_map/dot_general | solution.py:222
  16.8 1.0 slice_add_fusion.2
  17.9 1.4 fusion.7
  20.1 1.6 collective-permute-start.6
  21.7 1.0 convert_element_type.154
  22.7 1.6 copy.34
  24.3 1.7 copy.35
  26.0 1.6 subtract_convert_fusion
  27.7 1.4 maximum_bitcast_fusion.basis_ref
  29.0 1.1 dynamic-slice_add_fusion
  30.7 2.7 %collective-permute-done.6 = f32[928,128]{1,0:T(8,128)} collective-permute-done((f32[928,128]{1,0:T(8,128)}, f32[928,128]{1,0:T(8,128)}, u32[]{:S(2)}, u32[]{:S(2)}) %collective-permute-start.6) | collective-permute-done | bytes 475168 | tf_op jit(solution)/shard_map/ppermute | solution.py:87
  33.3 1.1 fusion.22
  35.1 2.7 %collective-permute-done.1 = f32[464,128]{1,0:T(8,128)S(1)} collective-permute-done((f32[464,128]{1,0:T(8,128)S(1)}, f32[464,128]{1,0:T(8,128)S(1)}, u32[]{:S(2)}, u32[]{:S(2)}) %collective-permute-start.1) | collective-permute-done | bytes 237600 | tf_op jit(solution)/shard_map/ppermute | solution.py:87
  37.8 2.7 %collective-permute-start.2 = (f32[232,128]{1,0:T(8,128)S(1)}, f32[232,128]{1,0:T(8,128)S(1)}, u32[]{:S(2)}, u32[]{:S(2)}) collective-permute-start(f32[232,128]{1,0:T(8,128)S(1)} %constant_dynamic-slice_fusion.10), channel_id=1, source_target_pairs={{0,16},{4,20},{8,24},{12,28},{16,0},{20,4},{24,8},{28,12},{1,17},{... | collective-permute-start | bytes 356360 | tf_op jit(solution)/shard_map/ppermute | solution.py:87
  40.7 2.7 %collective-permute-start.8 = (f32[232,128]{1,0:T(8,128)S(1)}, f32[232,128]{1,0:T(8,128)S(1)}, u32[]{:S(2)}, u32[]{:S(2)}) collective-permute-start(f32[232,128]{1,0:T(8,128)S(1)} %constant_dynamic-slice_fusion.8), channel_id=1, source_target_pairs={{0,16},{4,20},{8,24},{12,28},{16,0},{20,4},{24,8},{28,12},{1,17},{... | collective-permute-start | bytes 356360 | tf_op jit(solution)/shard_map/ppermute | solution.py:87
  43.4 5.5 %collective-permute-done.2 = f32[232,128]{1,0:T(8,128)S(1)} collective-permute-done((f32[232,128]{1,0:T(8,128)S(1)}, f32[232,128]{1,0:T(8,128)S(1)}, u32[]{:S(2)}, u32[]{:S(2)}) %collective-permute-start.2) | collective-permute-done | bytes 118816 | tf_op jit(solution)/shard_map/ppermute | solution.py:87
  49.0 2.4 %collective-permute-done.8 = f32[232,128]{1,0:T(8,128)S(1)} collective-permute-done((f32[232,128]{1,0:T(8,128)S(1)}, f32[232,128]{1,0:T(8,128)S(1)}, u32[]{:S(2)}, u32[]{:S(2)}) %collective-permute-start.8) | collective-permute-done | bytes 118816 | tf_op jit(solution)/shard_map/ppermute | solution.py:87
  52.0 6.4 %collective-permute-done.3 = f32[232,128]{1,0:T(8,128)S(1)} collective-permute-done((f32[232,128]{1,0:T(8,128)S(1)}, f32[232,128]{1,0:T(8,128)S(1)}, u32[]{:S(2)}, u32[]{:S(2)}) %collective-permute-start.3) | collective-permute-done | bytes 118816 | tf_op jit(solution)/shard_map/ppermute | solution.py:87
  58.4 1.5 collective-permute-start.4
  60.8 1.6 collective-permute-done.9
  62.6 3.1 %collective-permute-done.4 = f32[464,128]{1,0:T(8,128)S(1)} collective-permute-done((f32[464,128]{1,0:T(8,128)S(1)}, f32[464,128]{1,0:T(8,128)S(1)}, u32[]{:S(2)}, u32[]{:S(2)}) %collective-permute-start.4) | collective-permute-done | bytes 237600 | tf_op jit(solution)/shard_map/ppermute | solution.py:87
  66.2 4.2 %collective-permute-done.10 = f32[464,128]{1,0:T(8,128)S(1)} collective-permute-done((f32[464,128]{1,0:T(8,128)S(1)}, f32[464,128]{1,0:T(8,128)S(1)}, u32[]{:S(2)}, u32[]{:S(2)}) %collective-permute-start.10) | collective-permute-done | bytes 237600 | tf_op jit(solution)/shard_map/ppermute | solution.py:87
  70.4 1.0 collective-permute-start.11
  71.7 7.1 %collective-permute-done.5 = f32[928,128]{1,0:T(8,128)S(1)} collective-permute-done((f32[928,128]{1,0:T(8,128)S(1)}, f32[928,128]{1,0:T(8,128)S(1)}, u32[]{:S(2)}, u32[]{:S(2)}) %collective-permute-start.5) | collective-permute-done | bytes 475168 | tf_op jit(solution)/shard_map/ppermute | solution.py:87
  79.2 1.1 subtract_convert_fusion.1
  80.9 2.4 %convolution_bitcast_fusion.3 = f32[1600,256]{1,0:T(8,128)S(1)} fusion(bf16[1600,1600]{1,0:T(8,128)(2,1)S(1)} %bitcast.78, bf16[1600,128]{1,0:T(8,128)(2,1)S(1)} %get-tuple-element.16, bf16[1600,128]{1,0:T(8,128)(2,1)S(1)} %get-tuple-element.17), kind=kOutput, calls=%fused_computation.3 | convolution fusion | flops 1312358400 | bytes 7577600 | tf_op jit(solution)/shard_map/dot_general | solution.py:222
  84.9 1.0 fusion.1
  87.8 5.0 %convolution_bitcast_fusion.2 = f32[1600,256]{1,0:T(8,128)S(1)} fusion(bf16[1600,1600]{1,0:T(8,128)(2,1)} %bitcast.75, bf16[1600,128]{1,0:T(8,128)(2,1)S(1)} %get-tuple-element.20, bf16[1600,128]{1,0:T(8,128)(2,1)} %get-tuple-element.21), kind=kOutput, calls=%fused_computation.2 | convolution fusion | flops 1312358400 | bytes 7577600 | tf_op jit(solution)/shard_map/dot_general | solution.py:222
  92.9 1.6 collective-permute-start.13
  98.4 1.4 multiply_divide_fusion.2
  100.0 1.9 convert_bitcast_fusion
  102.0 2.9 %collective-permute-start.14 = (bf16[1,250,256]{2,1,0:T(8,128)(2,1)S(1)}, bf16[1,250,256]{2,1,0:T(8,128)(2,1)S(1)}, u32[]{:S(2)}, u32[]{:S(2)}) collective-permute-start(bf16[1,250,256]{2,1,0:T(8,128)(2,1)S(1)} %maximum_bitcast_fusion.1), channel_id=1, source_target_pairs={{0,16},{4,20},{8,24},{12,28},{16,0},{20,4},{24,8},{28,12},{1,17},{... | collective-permute-start | bytes 384008 | tf_op jit(solution)/shard_map/ppermute | solution.py:87
  105.8 5.7 %collective-permute-done.14 = bf16[1,250,256]{2,1,0:T(8,128)(2,1)S(1)} collective-permute-done((bf16[1,250,256]{2,1,0:T(8,128)(2,1)S(1)}, bf16[1,250,256]{2,1,0:T(8,128)(2,1)S(1)}, u32[]{:S(2)}, u32[]{:S(2)}) %collective-permute-start.14) | collective-permute-done | bytes 128032 | tf_op jit(solution)/shard_map/ppermute | solution.py:87
  113.0 6.3 %collective-permute-done.15 = bf16[2,250,256]{2,1,0:T(8,128)(2,1)S(1)} collective-permute-done((bf16[2,250,256]{2,1,0:T(8,128)(2,1)S(1)}, bf16[2,250,256]{2,1,0:T(8,128)(2,1)S(1)}, u32[]{:S(2)}, u32[]{:S(2)}) %collective-permute-start.15) | collective-permute-done | bytes 256032 | tf_op jit(solution)/shard_map/ppermute | solution.py:87
  119.3 1.6 collective-permute-start.16
  121.1 1.1 fusion.23
  122.3 1.1 fusion.24
  123.9 4.4 %collective-permute-done.18 = f32[448,128]{1,0:T(8,128)S(1)} collective-permute-done((f32[448,128]{1,0:T(8,128)S(1)}, f32[448,128]{1,0:T(8,128)S(1)}, u32[]{:S(2)}, u32[]{:S(2)}) %collective-permute-start.18) | collective-permute-done | bytes 229408 | tf_op jit(solution)/shard_map/ppermute | solution.py:87
  128.8 9.1 %collective-permute-done.28 = f32[448,128]{1,0:T(8,128)S(1)} collective-permute-done((f32[448,128]{1,0:T(8,128)S(1)}, f32[448,128]{1,0:T(8,128)S(1)}, u32[]{:S(2)}, u32[]{:S(2)}) %collective-permute-start.28) | collective-permute-done | bytes 229408 | tf_op jit(solution)/shard_map/ppermute | solution.py:87
  138.0 1.9 collective-permute-start.29
  139.9 1.2 collective-permute-start.20
  141.1 1.7 collective-permute-done.29
  143.0 1.2 collective-permute-done.20
  144.2 3.5 %collective-permute-start.21 = (f32[56,128]{1,0:T(8,128)S(1)}, f32[56,128]{1,0:T(8,128)S(1)}, u32[]{:S(2)}, u32[]{:S(2)}) collective-permute-start(f32[56,128]{1,0:T(8,128)S(1)} %constant_dynamic-slice_fusion.4), channel_id=1, source_target_pairs={{0,16},{4,20},{8,24},{12,28},{16,0},{20,4},{24,8},{28,12},{1,17},{... | collective-permute-start | bytes 86024 | tf_op jit(solution)/shard_map/ppermute | solution.py:87
  147.8 3.2 %collective-permute-start.31 = (f32[56,128]{1,0:T(8,128)S(1)}, f32[56,128]{1,0:T(8,128)S(1)}, u32[]{:S(2)}, u32[]{:S(2)}) collective-permute-start(f32[56,128]{1,0:T(8,128)S(1)} %constant_dynamic-slice_fusion), channel_id=1, source_target_pairs={{0,16},{4,20},{8,24},{12,28},{16,0},{20,4},{24,8},{28,12},{1,17},{... | collective-permute-start | bytes 86024 | tf_op jit(solution)/shard_map/ppermute | solution.py:87
  151.0 1.7 collective-permute-start.22
  152.9 3.0 %collective-permute-start.32 = (f32[56,128]{1,0:T(8,128)S(1)}, f32[56,128]{1,0:T(8,128)S(1)}, u32[]{:S(2)}, u32[]{:S(2)}) collective-permute-start(f32[56,128]{1,0:T(8,128)S(1)} %get-tuple-element.19), channel_id=1, source_target_pairs={{0,16},{4,20},{8,24},{12,28},{16,0},{20,4},{24,8},{28,12},{1,17},{... | collective-permute-start | bytes 86024 | tf_op jit(solution)/shard_map/ppermute | solution.py:87
  157.7 1.7 collective-permute-start.23
  159.6 2.4 %collective-permute-done.23 = f32[112,128]{1,0:T(8,128)S(1)} collective-permute-done((f32[112,128]{1,0:T(8,128)S(1)}, f32[112,128]{1,0:T(8,128)S(1)}, u32[]{:S(2)}, u32[]{:S(2)}) %collective-permute-start.23) | collective-permute-done | bytes 57376 | tf_op jit(solution)/shard_map/ppermute | solution.py:87
  162.0 1.6 collective-permute-start.24
  164.4 1.0 collective-permute-start.34
  165.4 1.5 collective-permute-done.24
  166.9 2.3 %collective-permute-done.34 = f32[224,128]{1,0:T(8,128)S(1)} collective-permute-done((f32[224,128]{1,0:T(8,128)S(1)}, f32[224,128]{1,0:T(8,128)S(1)}, u32[]{:S(2)}, u32[]{:S(2)}) %collective-permute-start.34) | collective-permute-done | bytes 114720 | tf_op jit(solution)/shard_map/ppermute | solution.py:87
  169.2 1.6 collective-permute-start.35
  171.1 1.8 collective-permute-done.25
  173.0 2.3 %collective-permute-done.35 = f32[448,128]{1,0:T(8,128)S(1)} collective-permute-done((f32[448,128]{1,0:T(8,128)S(1)}, f32[448,128]{1,0:T(8,128)S(1)}, u32[]{:S(2)}, u32[]{:S(2)}) %collective-permute-start.35) | collective-permute-done | bytes 229408 | tf_op jit(solution)/shard_map/ppermute | solution.py:87
  175.4 1.3 pad_maximum_fusion.1.direction_ref
  176.7 8.2 %shard_map.221 = bf16[8,200,1600]{2,1,0:T(8,128)(2,1)} custom-call(bf16[8,200,512]{2,1,0:T(8,128)(2,1)} %pad_maximum_fusion.1.direction_ref, bf16[512,1600]{1,0:T(8,128)(2,1)} %maximum_bitcast_fusion.basis_ref, bf16[8,200,1600]{2,1,0:T(8,128)(2,1)} %bitcast.68), custom_call_target="tpu_custom_call" | custom-call | tf_op jit(solution)/shard_map/pallas_call | solution.py:201
  185.3 1.0 multiply_reduce_fusion
  187.0 2.9 %fusion.4 = f32[256,256]{1,0:T(8,128)S(1)} fusion(f32[1600,128]{1,0:T(8,128)S(1)} %slice.124, f32[1600,128]{1,0:T(8,128)S(1)} %slice.121, f32[]{:T(128)S(6)} %rsqrt.4), kind=kOutput, calls=%fused_computation.16 | convolution fusion | flops 1259110400 | bytes 1900548 | tf_op jit(solution)/shard_map/dot_general | solution.py:32
  194.9 2.0 %fusion.2 = f32[1600,256]{1,0:T(8,128)} fusion(f32[256,256]{1,0:T(8,128)S(1)} %fusion.120, f32[1600,128]{1,0:T(8,128)S(1)} %slice.124, f32[1600,128]{1,0:T(8,128)S(1)} %slice.121, f32[]{:T(128)S(6)} %rsqrt.4), kind=kOutput, calls=%fused_computation.14 | convolution fusion | flops 629964800 | bytes 3538948 | tf_op jit(solution)/shard_map/dot_general | solution.py:42
  (186 shorter events, 25.4 us)
Async XLA Ops:
  7.0 0.9 copy-start.3
  8.1 0.7 copy-start.2
  9.6 19.4 %collective-permute-start = (f32[928,128]{1,0:T(8,128)}, f32[928,128]{1,0:T(8,128)}, u32[]{:S(2)}, u32[]{:S(2)}) collective-permute-start(f32[928,128]{1,0:T(8,128)} %constant_dynamic-slice_fusion.12), channel_id=1, source_target_pairs={{0,4},{4,0},{8,12},{12,8},{16,20},{20,16},{24,28},{28,24},{1,5},{5... | collective-permute-start | bytes 1425416 | tf_op jit(solution)/shard_map/ppermute | solution.py:87
  16.8 1.0 copy-start.10
  17.8 3.9 %copy-start = (f32[1600,256]{1,0:T(8,128)S(1)}, f32[1600,256]{1,0:T(8,128)}, u32[]{:S(2)}) copy-start(f32[1600,256]{1,0:T(8,128)} %param.18) | copy-start | bytes 4915204
  20.1 13.2 %collective-permute-start.6 = (f32[928,128]{1,0:T(8,128)}, f32[928,128]{1,0:T(8,128)}, u32[]{:S(2)}, u32[]{:S(2)}) collective-permute-start(f32[928,128]{1,0:T(8,128)} %pad_dynamic-slice_fusion.6), channel_id=1, source_target_pairs={{0,8},{4,12},{8,0},{12,4},{16,24},{20,28},{24,16},{28,20},{1,9},{5... | collective-permute-start | bytes 1425416 | tf_op jit(solution)/shard_map/ppermute | solution.py:87
  30.2 7.6 %collective-permute-start.1 = (f32[464,128]{1,0:T(8,128)S(1)}, f32[464,128]{1,0:T(8,128)S(1)}, u32[]{:S(2)}, u32[]{:S(2)}) collective-permute-start(f32[464,128]{1,0:T(8,128)S(1)} %constant_dynamic-slice_fusion.11), channel_id=1, source_target_pairs={{0,8},{4,12},{8,0},{12,4},{16,24},{20,28},{24,16},{28,20},{1,9},{5... | collective-permute-start | bytes 712712 | tf_op jit(solution)/shard_map/ppermute | solution.py:87
  34.5 6.2 %collective-permute-start.7 = (f32[464,128]{1,0:T(8,128)S(1)}, f32[464,128]{1,0:T(8,128)S(1)}, u32[]{:S(2)}, u32[]{:S(2)}) collective-permute-start(f32[464,128]{1,0:T(8,128)S(1)} %constant_dynamic-slice_fusion.9), channel_id=1, source_target_pairs={{0,4},{4,0},{8,12},{12,8},{16,20},{20,16},{24,28},{28,24},{1,5},{5... | collective-permute-start | bytes 712712 | tf_op jit(solution)/shard_map/ppermute | solution.py:87
  37.8 11.0 %collective-permute-start.2 = (f32[232,128]{1,0:T(8,128)S(1)}, f32[232,128]{1,0:T(8,128)S(1)}, u32[]{:S(2)}, u32[]{:S(2)}) collective-permute-start(f32[232,128]{1,0:T(8,128)S(1)} %constant_dynamic-slice_fusion.10), channel_id=1, source_target_pairs={{0,16},{4,20},{8,24},{12,28},{16,0},{20,4},{24,8},{28,12},{1,17},{... | collective-permute-start | bytes 356360 | tf_op jit(solution)/shard_map/ppermute | solution.py:87
  40.7 10.7 %collective-permute-start.8 = (f32[232,128]{1,0:T(8,128)S(1)}, f32[232,128]{1,0:T(8,128)S(1)}, u32[]{:S(2)}, u32[]{:S(2)}) collective-permute-start(f32[232,128]{1,0:T(8,128)S(1)} %constant_dynamic-slice_fusion.8), channel_id=1, source_target_pairs={{0,16},{4,20},{8,24},{12,28},{16,0},{20,4},{24,8},{28,12},{1,17},{... | collective-permute-start | bytes 356360 | tf_op jit(solution)/shard_map/ppermute | solution.py:87
  48.9 9.5 %collective-permute-start.3 = (f32[232,128]{1,0:T(8,128)S(1)}, f32[232,128]{1,0:T(8,128)S(1)}, u32[]{:S(2)}, u32[]{:S(2)}) collective-permute-start(f32[232,128]{1,0:T(8,128)S(1)} %get-tuple-element.34), channel_id=1, source_target_pairs={{0,16},{4,20},{8,24},{12,28},{16,0},{20,4},{24,8},{28,12},{1,17},{... | collective-permute-start | bytes 356360 | tf_op jit(solution)/shard_map/ppermute | solution.py:87
  51.4 11.0 %collective-permute-start.9 = (f32[232,128]{1,0:T(8,128)S(1)}, f32[232,128]{1,0:T(8,128)S(1)}, u32[]{:S(2)}, u32[]{:S(2)}) collective-permute-start(f32[232,128]{1,0:T(8,128)S(1)} %get-tuple-element.38), channel_id=1, source_target_pairs={{0,16},{4,20},{8,24},{12,28},{16,0},{20,4},{24,8},{28,12},{1,17},{... | collective-permute-start | bytes 356360 | tf_op jit(solution)/shard_map/ppermute | solution.py:87
  58.4 7.2 %collective-permute-start.4 = (f32[464,128]{1,0:T(8,128)S(1)}, f32[464,128]{1,0:T(8,128)S(1)}, u32[]{:S(2)}, u32[]{:S(2)}) collective-permute-start(f32[464,128]{1,0:T(8,128)S(1)} %constant_dynamic-update-slice_fusion.36), channel_id=1, source_target_pairs={{0,8},{4,12},{8,0},{12,4},{16,24},{20,28},{24,16},{28,20},{1,9},{5... | collective-permute-start | bytes 712712 | tf_op jit(solution)/shard_map/ppermute | solution.py:87
  62.4 8.0 %collective-permute-start.10 = (f32[464,128]{1,0:T(8,128)S(1)}, f32[464,128]{1,0:T(8,128)S(1)}, u32[]{:S(2)}, u32[]{:S(2)}) collective-permute-start(f32[464,128]{1,0:T(8,128)S(1)} %constant_dynamic-update-slice_fusion.30), channel_id=1, source_target_pairs={{0,4},{4,0},{8,12},{12,8},{16,20},{20,16},{24,28},{28,24},{1,5},{5... | collective-permute-start | bytes 712712 | tf_op jit(solution)/shard_map/ppermute | solution.py:87
  62.5 18.4 %slice-start = ((s8[5324800]{0:T(1024)(128)(4,1)}), s8[4194304]{0:T(1024)(128)(4,1)S(1)}, s32[]{:S(2)}) async-start(s8[5324800]{0:T(1024)(128)(4,1)} %bitcast.76), calls=%async_computation | async-start | bytes 8388608
  65.7 13.1 %collective-permute-start.5 = (f32[928,128]{1,0:T(8,128)S(1)}, f32[928,128]{1,0:T(8,128)S(1)}, u32[]{:S(2)}, u32[]{:S(2)}) collective-permute-start(f32[928,128]{1,0:T(8,128)S(1)} %constant_dynamic-update-slice_fusion.34), channel_id=1, source_target_pairs={{0,4},{4,0},{8,12},{12,8},{16,20},{20,16},{24,28},{28,24},{1,5},{5... | collective-permute-start | bytes 1425416 | tf_op jit(solution)/shard_map/ppermute | solution.py:87
  70.4 8.7 %collective-permute-start.11 = (f32[928,128]{1,0:T(8,128)S(1)}, f32[928,128]{1,0:T(8,128)S(1)}, u32[]{:S(2)}, u32[]{:S(2)}) collective-permute-start(f32[928,128]{1,0:T(8,128)S(1)} %constant_dynamic-update-slice_fusion.28), channel_id=1, source_target_pairs={{0,8},{4,12},{8,0},{12,4},{16,24},{20,28},{24,16},{28,20},{1,9},{5... | collective-permute-start | bytes 1425416 | tf_op jit(solution)/shard_map/ppermute | solution.py:87
  71.7 9.2 %slice-start.1 = ((s8[5324800]{0:T(1024)(128)(4,1)}), s8[1130496]{0:T(1024)(128)(4,1)S(1)}, s32[]{:S(2)}) async-start(s8[5324800]{0:T(1024)(128)(4,1)} %bitcast.76), calls=%async_computation.1 | async-start | bytes 2260992
  79.2 1.1 copy-start.1
  84.2 36.9 %collective-permute-start.17 = (f32[896,128]{1,0:T(8,128)}, f32[896,128]{1,0:T(8,128)}, u32[]{:S(2)}, u32[]{:S(2)}) collective-permute-start(f32[896,128]{1,0:T(8,128)} %pad_dynamic-slice_fusion.4), channel_id=1, source_target_pairs={{0,1},{1,0},{2,3},{3,2},{4,5},{5,4},{6,7},{7,6},{8,9},{9,8},{10,11... | collective-permute-start | bytes 1376264 | tf_op jit(solution)/shard_map/ppermute | solution.py:87
  87.2 5.7 %collective-permute-start.12 = (f32[8,128]{1,0:T(8,128)S(1)}, f32[8,128]{1,0:T(8,128)S(1)}, u32[]{:S(2)}, u32[]{:S(2)}) collective-permute-start(f32[8,128]{1,0:T(8,128)S(1)} %broadcast_in_dim.15), channel_id=1, source_target_pairs={{0,1},{1,0},{2,3},{3,2},{4,5},{5,4},{6,7},{7,6},{8,9},{9,8},{10,11... | collective-permute-start | bytes 12296 | tf_op jit(solution)/shard_map/ppermute | solution.py:87
  92.7 5.7 %copy-start.5 = (f32[1,1,4,1600]{3,2,1,0:T(4,128)S(1)}, f32[1,1,4,1600]{3,2,1,0:T(4,128)}, u32[]{:S(2)}) copy-start(f32[1,1,4,1600]{3,2,1,0:T(4,128)} %param.26) | copy-start | bytes 76804
  92.8 5.7 %copy-start.6 = (f32[1,1,4,1600]{3,2,1,0:T(4,128)S(1)}, f32[1,1,4,1600]{3,2,1,0:T(4,128)}, u32[]{:S(2)}) copy-start(f32[1,1,4,1600]{3,2,1,0:T(4,128)} %param.25) | copy-start | bytes 76804
  92.9 3.7 %collective-permute-start.13 = (f32[8,128]{1,0:T(8,128)S(1)}, f32[8,128]{1,0:T(8,128)S(1)}, u32[]{:S(2)}, u32[]{:S(2)}) collective-permute-start(f32[8,128]{1,0:T(8,128)S(1)} %broadcast_add_fusion), channel_id=1, source_target_pairs={{0,2},{1,3},{2,0},{3,1},{4,6},{5,7},{6,4},{7,5},{8,10},{9,11},{10,... | collective-permute-start | bytes 12296 | tf_op jit(solution)/shard_map/ppermute | solution.py:87
  95.3 27.0 %collective-permute-start.27 = (f32[896,128]{1,0:T(8,128)}, f32[896,128]{1,0:T(8,128)}, u32[]{:S(2)}, u32[]{:S(2)}) collective-permute-start(f32[896,128]{1,0:T(8,128)} %pad_dynamic-slice_fusion.2), channel_id=1, source_target_pairs={{0,1},{1,0},{2,3},{3,2},{4,5},{5,4},{6,7},{7,6},{8,9},{9,8},{10,11... | collective-permute-start | bytes 1376264 | tf_op jit(solution)/shard_map/ppermute | solution.py:87
  100.0 12.3 %copy-start.7 = (f32[4,1600]{1,0:T(4,128)S(1)}, f32[4,1600]{1,0:T(4,128)}, u32[]{:S(2)}) copy-start(f32[4,1600]{1,0:T(4,128)} %param.21) | copy-start | bytes 76804
  100.0 12.3 %copy-start.8 = (f32[4,1600]{1,0:T(4,128)S(1)}, f32[4,1600]{1,0:T(4,128)}, u32[]{:S(2)}) copy-start(f32[4,1600]{1,0:T(4,128)} %param.23) | copy-start | bytes 76804
  100.0 12.3 %copy-start.9 = (f32[4,1600]{1,0:T(4,128)S(1)}, f32[4,1600]{1,0:T(4,128)}, u32[]{:S(2)}) copy-start(f32[4,1600]{1,0:T(4,128)} %param.22) | copy-start | bytes 76804
  102.0 9.5 %collective-permute-start.14 = (bf16[1,250,256]{2,1,0:T(8,128)(2,1)S(1)}, bf16[1,250,256]{2,1,0:T(8,128)(2,1)S(1)}, u32[]{:S(2)}, u32[]{:S(2)}) collective-permute-start(bf16[1,250,256]{2,1,0:T(8,128)(2,1)S(1)} %maximum_bitcast_fusion.1), channel_id=1, source_target_pairs={{0,16},{4,20},{8,24},{12,28},{16,0},{20,4},{24,8},{28,12},{1,17},{... | collective-permute-start | bytes 384008 | tf_op jit(solution)/shard_map/ppermute | solution.py:87
  111.5 7.8 %collective-permute-start.15 = (bf16[2,250,256]{2,1,0:T(8,128)(2,1)S(1)}, bf16[2,250,256]{2,1,0:T(8,128)(2,1)S(1)}, u32[]{:S(2)}, u32[]{:S(2)}) collective-permute-start(bf16[2,250,256]{2,1,0:T(8,128)(2,1)S(1)} %constant_dynamic-update-slice_fusion.24), channel_id=1, source_target_pairs={{0,8},{4,12},{8,0},{12,4},{16,24},{20,28},{24,16},{28,20},{1,9},{5... | collective-permute-start | bytes 768008 | tf_op jit(solution)/shard_map/ppermute | solution.py:87
  119.3 36.7 %collective-permute-start.16 = (bf16[4,250,256]{2,1,0:T(8,128)(2,1)S(1)}, bf16[4,250,256]{2,1,0:T(8,128)(2,1)S(1)}, u32[]{:S(2)}, u32[]{:S(2)}) collective-permute-start(bf16[4,250,256]{2,1,0:T(8,128)(2,1)S(1)} %constant_dynamic-update-slice_fusion.22), channel_id=1, source_target_pairs={{0,4},{4,0},{8,12},{12,8},{16,20},{20,16},{24,28},{28,24},{1,5},{5... | collective-permute-start | bytes 1536008 | tf_op jit(solution)/shard_map/ppermute | solution.py:87
  122.2 6.1 %collective-permute-start.18 = (f32[448,128]{1,0:T(8,128)S(1)}, f32[448,128]{1,0:T(8,128)S(1)}, u32[]{:S(2)}, u32[]{:S(2)}) collective-permute-start(f32[448,128]{1,0:T(8,128)S(1)} %constant_dynamic-slice_fusion.7), channel_id=1, source_target_pairs={{0,2},{1,3},{2,0},{3,1},{4,6},{5,7},{6,4},{7,5},{8,10},{9,11},{10,... | collective-permute-start | bytes 688136 | tf_op jit(solution)/shard_map/ppermute | solution.py:87
  123.4 14.6 %collective-permute-start.28 = (f32[448,128]{1,0:T(8,128)S(1)}, f32[448,128]{1,0:T(8,128)S(1)}, u32[]{:S(2)}, u32[]{:S(2)}) collective-permute-start(f32[448,128]{1,0:T(8,128)S(1)} %constant_dynamic-slice_fusion.3), channel_id=1, source_target_pairs={{0,4},{4,0},{8,12},{12,8},{16,20},{20,16},{24,28},{28,24},{1,5},{5... | collective-permute-start | bytes 688136 | tf_op jit(solution)/shard_map/ppermute | solution.py:87
  128.3 11.6 %collective-permute-start.19 = (f32[224,128]{1,0:T(8,128)S(1)}, f32[224,128]{1,0:T(8,128)S(1)}, u32[]{:S(2)}, u32[]{:S(2)}) collective-permute-start(f32[224,128]{1,0:T(8,128)S(1)} %constant_dynamic-slice_fusion.6), channel_id=1, source_target_pairs={{0,4},{4,0},{8,12},{12,8},{16,20},{20,16},{24,28},{28,24},{1,5},{5... | collective-permute-start | bytes 344072 | tf_op jit(solution)/shard_map/ppermute | solution.py:87
  138.0 4.9 %collective-permute-start.29 = (f32[224,128]{1,0:T(8,128)S(1)}, f32[224,128]{1,0:T(8,128)S(1)}, u32[]{:S(2)}, u32[]{:S(2)}) collective-permute-start(f32[224,128]{1,0:T(8,128)S(1)} %constant_dynamic-slice_fusion.2), channel_id=1, source_target_pairs={{0,8},{4,12},{8,0},{12,4},{16,24},{20,28},{24,16},{28,20},{1,9},{5... | collective-permute-start | bytes 344072 | tf_op jit(solution)/shard_map/ppermute | solution.py:87
  139.9 4.2 %collective-permute-start.20 = (f32[112,128]{1,0:T(8,128)S(1)}, f32[112,128]{1,0:T(8,128)S(1)}, u32[]{:S(2)}, u32[]{:S(2)}) collective-permute-start(f32[112,128]{1,0:T(8,128)S(1)} %constant_dynamic-slice_fusion.5), channel_id=1, source_target_pairs={{0,8},{4,12},{8,0},{12,4},{16,24},{20,28},{24,16},{28,20},{1,9},{5... | collective-permute-start | bytes 172040 | tf_op jit(solution)/shard_map/ppermute | solution.py:87
  142.9 4.9 %collective-permute-start.30 = (f32[112,128]{1,0:T(8,128)S(1)}, f32[112,128]{1,0:T(8,128)S(1)}, u32[]{:S(2)}, u32[]{:S(2)}) collective-permute-start(f32[112,128]{1,0:T(8,128)S(1)} %constant_dynamic-slice_fusion.1), channel_id=1, source_target_pairs={{0,2},{1,3},{2,0},{3,1},{4,6},{5,7},{6,4},{7,5},{8,10},{9,11},{10,... | collective-permute-start | bytes 172040 | tf_op jit(solution)/shard_map/ppermute | solution.py:87
  144.2 6.8 %collective-permute-start.21 = (f32[56,128]{1,0:T(8,128)S(1)}, f32[56,128]{1,0:T(8,128)S(1)}, u32[]{:S(2)}, u32[]{:S(2)}) collective-permute-start(f32[56,128]{1,0:T(8,128)S(1)} %constant_dynamic-slice_fusion.4), channel_id=1, source_target_pairs={{0,16},{4,20},{8,24},{12,28},{16,0},{20,4},{24,8},{28,12},{1,17},{... | collective-permute-start | bytes 86024 | tf_op jit(solution)/shard_map/ppermute | solution.py:87
  147.8 5.2 %collective-permute-start.31 = (f32[56,128]{1,0:T(8,128)S(1)}, f32[56,128]{1,0:T(8,128)S(1)}, u32[]{:S(2)}, u32[]{:S(2)}) collective-permute-start(f32[56,128]{1,0:T(8,128)S(1)} %constant_dynamic-slice_fusion), channel_id=1, source_target_pairs={{0,16},{4,20},{8,24},{12,28},{16,0},{20,4},{24,8},{28,12},{1,17},{... | collective-permute-start | bytes 86024 | tf_op jit(solution)/shard_map/ppermute | solution.py:87
  151.0 6.7 %collective-permute-start.22 = (f32[56,128]{1,0:T(8,128)S(1)}, f32[56,128]{1,0:T(8,128)S(1)}, u32[]{:S(2)}, u32[]{:S(2)}) collective-permute-start(f32[56,128]{1,0:T(8,128)S(1)} %get-tuple-element.15), channel_id=1, source_target_pairs={{0,16},{4,20},{8,24},{12,28},{16,0},{20,4},{24,8},{28,12},{1,17},{... | collective-permute-start | bytes 86024 | tf_op jit(solution)/shard_map/ppermute | solution.py:87
  152.9 6.5 %collective-permute-start.32 = (f32[56,128]{1,0:T(8,128)S(1)}, f32[56,128]{1,0:T(8,128)S(1)}, u32[]{:S(2)}, u32[]{:S(2)}) collective-permute-start(f32[56,128]{1,0:T(8,128)S(1)} %get-tuple-element.19), channel_id=1, source_target_pairs={{0,16},{4,20},{8,24},{12,28},{16,0},{20,4},{24,8},{28,12},{1,17},{... | collective-permute-start | bytes 86024 | tf_op jit(solution)/shard_map/ppermute | solution.py:87
  156.0 0.9 copy-start.4
  157.7 4.2 %collective-permute-start.23 = (f32[112,128]{1,0:T(8,128)S(1)}, f32[112,128]{1,0:T(8,128)S(1)}, u32[]{:S(2)}, u32[]{:S(2)}) collective-permute-start(f32[112,128]{1,0:T(8,128)S(1)} %constant_dynamic-update-slice_fusion.18), channel_id=1, source_target_pairs={{0,8},{4,12},{8,0},{12,4},{16,24},{20,28},{24,16},{28,20},{1,9},{5... | collective-permute-start | bytes 172040 | tf_op jit(solution)/shard_map/ppermute | solution.py:87
  159.5 4.9 %collective-permute-start.33 = (f32[112,128]{1,0:T(8,128)S(1)}, f32[112,128]{1,0:T(8,128)S(1)}, u32[]{:S(2)}, u32[]{:S(2)}) collective-permute-start(f32[112,128]{1,0:T(8,128)S(1)} %constant_dynamic-update-slice_fusion.8), channel_id=1, source_target_pairs={{0,2},{1,3},{2,0},{3,1},{4,6},{5,7},{6,4},{7,5},{8,10},{9,11},{10,... | collective-permute-start | bytes 172040 | tf_op jit(solution)/shard_map/ppermute | solution.py:87
  162.0 4.9 %collective-permute-start.24 = (f32[224,128]{1,0:T(8,128)S(1)}, f32[224,128]{1,0:T(8,128)S(1)}, u32[]{:S(2)}, u32[]{:S(2)}) collective-permute-start(f32[224,128]{1,0:T(8,128)S(1)} %constant_dynamic-update-slice_fusion.16), channel_id=1, source_target_pairs={{0,4},{4,0},{8,12},{12,8},{16,20},{20,16},{24,28},{28,24},{1,5},{5... | collective-permute-start | bytes 344072 | tf_op jit(solution)/shard_map/ppermute | solution.py:87
  164.4 4.9 %collective-permute-start.34 = (f32[224,128]{1,0:T(8,128)S(1)}, f32[224,128]{1,0:T(8,128)S(1)}, u32[]{:S(2)}, u32[]{:S(2)}) collective-permute-start(f32[224,128]{1,0:T(8,128)S(1)} %constant_dynamic-update-slice_fusion.6), channel_id=1, source_target_pairs={{0,8},{4,12},{8,0},{12,4},{16,24},{20,28},{24,16},{28,20},{1,9},{5... | collective-permute-start | bytes 344072 | tf_op jit(solution)/shard_map/ppermute | solution.py:87
  166.9 6.1 %collective-permute-start.25 = (f32[448,128]{1,0:T(8,128)S(1)}, f32[448,128]{1,0:T(8,128)S(1)}, u32[]{:S(2)}, u32[]{:S(2)}) collective-permute-start(f32[448,128]{1,0:T(8,128)S(1)} %constant_dynamic-update-slice_fusion.14), channel_id=1, source_target_pairs={{0,2},{1,3},{2,0},{3,1},{4,6},{5,7},{6,4},{7,5},{8,10},{9,11},{10,... | collective-permute-start | bytes 688136 | tf_op jit(solution)/shard_map/ppermute | solution.py:87
  169.2 6.1 %collective-permute-start.35 = (f32[448,128]{1,0:T(8,128)S(1)}, f32[448,128]{1,0:T(8,128)S(1)}, u32[]{:S(2)}, u32[]{:S(2)}) collective-permute-start(f32[448,128]{1,0:T(8,128)S(1)} %constant_dynamic-update-slice_fusion.4), channel_id=1, source_target_pairs={{0,4},{4,0},{8,12},{12,8},{16,20},{20,16},{24,28},{28,24},{1,5},{5... | collective-permute-start | bytes 688136 | tf_op jit(solution)/shard_map/ppermute | solution.py:87
  173.0 12.1 %collective-permute-start.26 = (f32[896,128]{1,0:T(8,128)S(1)}, f32[896,128]{1,0:T(8,128)S(1)}, u32[]{:S(2)}, u32[]{:S(2)}) collective-permute-start(f32[896,128]{1,0:T(8,128)S(1)} %constant_dynamic-update-slice_fusion.12), channel_id=1, source_target_pairs={{0,1},{1,0},{2,3},{3,2},{4,5},{5,4},{6,7},{7,6},{8,9},{9,8},{10,11... | collective-permute-start | bytes 1376264 | tf_op jit(solution)/shard_map/ppermute | solution.py:87
  175.3 9.9 %collective-permute-start.36 = (f32[896,128]{1,0:T(8,128)S(1)}, f32[896,128]{1,0:T(8,128)S(1)}, u32[]{:S(2)}, u32[]{:S(2)}) collective-permute-start(f32[896,128]{1,0:T(8,128)S(1)} %constant_dynamic-update-slice_fusion.2), channel_id=1, source_target_pairs={{0,1},{1,0},{2,3},{3,2},{4,5},{5,4},{6,7},{7,6},{8,9},{9,8},{10,11... | collective-permute-start | bytes 1376264 | tf_op jit(solution)/shard_map/ppermute | solution.py:87

commit v8 on v7

--- a/solution.py
+++ b/solution.py
@@ -128,7 +128,7 @@
     steps = orders[which]
     count = 2 ** len(steps)
     rows = piece.shape[0]
-    padded = -(-rows // (8 * count)) * 8 * count
+    padded = -(-rows // count) * count
     return run_steps(jnp.pad(piece, ((0, padded - rows), (0, 0))), steps)[:rows]
 
 

time: 198 us -> 216 us (1.091)
  local copies, waits for them, and re-layouts: 12.8 us -> 41.7 us
  starting transfers between devices: 44 us -> 33.4 us
  matrix products: 25.4 us -> 28 us
    dynamic_update_slice x19, local copies, waits for them, and re-layouts: 0.37 us -> 14.5 us  [place_pair(): return lax.dynamic_update_slice_in_dim(full, other, (1 - side) * length, 0)]
    dynamic_update_slice x14 -> x18, local copies, waits for them, and re-layouts: 0.58 us -> 13.2 us  [place_pair(): full = lax.dynamic_update_slice_in_dim(full, mine, side * length, 0)]
    ppermute x37, starting transfers between devices: 44 us -> 33.4 us  [swap_with(): lax.ppermute(values, name, [(index, index ^ bit) for index in range(size)])]
    dot_general x4, matrix products: 15.7 us -> 18.3 us  [exact_dot(): lax.dot_general(lhs_bf16, split2(rhs_f32), ((contract, (0,)), ((), ())),...]
    add x12 -> x16, other arithmetic: 4.49 us -> 3.41 us  [run_steps(): parts = keep + swap_with(send, name, bit, size)]
  transfers between devices with their start and end apart: 37 -> 37, of which waited for: 25 -> 24; matrix products, arithmetic and copies ran while one was open for 19% -> 29% of each run, Pallas kernels for 4% -> 4%
where the time goes in v8:
time: 216 us; the launch traced here: 214 us
  waiting for transfers between devices  74.5 us (34%)
  local copies, waits for them, and re-layouts  41.7 us (19%)
  starting transfers between devices  33.4 us (15%)
  matrix products  28 us (13%)
  other arithmetic  22.8 us (11%)
  Pallas kernels  8.16 us (4%)
  between operations  5.93 us (3%)
    ppermute x37, waiting for transfers between devices, swap_with(): lax.ppermute(values, name, [(index, index ^ bit) for index in range(size)])  74.5 us
    ppermute x37, starting transfers between devices, swap_with(): lax.ppermute(values, name, [(index, index ^ bit) for index in range(size)])  33.4 us
    dot_general x4, matrix products, exact_dot(): lax.dot_general(lhs_bf16, split2(rhs_f32), ((contract, (0,)), ((), ())),...  18.3 us
    dynamic_update_slice x19, local copies, waits for them, and re-layouts, place_pair(): return lax.dynamic_update_slice_in_dim(full, other, (1 - side) * length, 0)  14.5 us
    dynamic_update_slice x18, local copies, waits for them, and re-layouts, place_pair(): full = lax.dynamic_update_slice_in_dim(full, mine, side * length, 0)  13.2 us
    pallas_call x1, Pallas kernels, updated_weights(): pl.pallas_call(update_kernel, out_shape=jax.ShapeDtypeStruct(weights.shap...  8.16 us
    convert_element_type x4, other arithmetic, split2(): second = (values - first.astype(jnp.float32)).astype(jnp.bfloat16)  4.44 us
  transfers between devices with their start and end apart: 37, of which 24 were waited for; matrix products, arithmetic and copies ran while one was open for 29% of the time, Pallas kernels for 4%

profile of v8, /device:TPU:0, one launch (start us, length us, event | category | flops | bytes accessed | tf_op | source)
XLA Modules:
  0.0 214.5 jit_solution(1176014095436775336)
XLA Ops:
  0.7 1.0 reshape.183
  1.7 2.2 %subtract_convert_fusion.4 = (bf16[1600,128]{1,0:T(8,128)(2,1)S(1)}, bf16[1600,128]{1,0:T(8,128)(2,1)S(1)}, bf16[1600,128]{1,0:T(8,128)(2,1)S(1)}, bf16[1600,128]{1,0:T(8,128)(2,1)S(1)}) fusion(f32[1600,256]{1,0:T(8,128)} %param.18), kind=kLoop, calls=%fused_computation.48 | loop fusion | flops 1228800 | bytes 4096000 | tf_op jit(solution)/shard_map/convert_element_type | solution.py:216
  3.9 4.2 %convolution_bitcast_fusion.1 = f32[1600,256]{1,0:T(8,128)S(1)} fusion(bf16[1600,1600]{1,0:T(8,128)(2,1)} %bitcast.73, bf16[1600,128]{1,0:T(8,128)(2,1)S(1)} %get-tuple-element.29, bf16[1600,128]{1,0:T(8,128)(2,1)S(1)} %get-tuple-element.30), kind=kOutput, calls=%fused_computation.1 | convolution fusion | flops 1312358400 | bytes 7577600 | tf_op jit(solution)/shard_map/dot_general | solution.py:222
  9.9 2.9 %collective-permute-start = (f32[916,128]{1,0:T(8,128)}, f32[916,128]{1,0:T(8,128)S(1)}, u32[]{:S(2)}, u32[]{:S(2)}) collective-permute-start(f32[916,128]{1,0:T(8,128)} %constant_dynamic-slice_fusion.14), channel_id=1, source_target_pairs={{0,4},{4,0},{8,12},{12,8},{16,20},{20,16},{24,28},{28,24},{1,5},{5... | collective-permute-start | bytes 1406984 | tf_op jit(solution)/shard_map/ppermute | solution.py:87
  12.9 4.2 %convolution_bitcast_fusion = f32[1600,256]{1,0:T(8,128)S(1)} fusion(bf16[1600,1600]{1,0:T(8,128)(2,1)} %bitcast.74, bf16[1600,128]{1,0:T(8,128)(2,1)S(1)} %get-tuple-element.33, bf16[1600,128]{1,0:T(8,128)(2,1)S(1)} %get-tuple-element.34), kind=kOutput, calls=%fused_computation | convolution fusion | flops 1312358400 | bytes 7577600 | tf_op jit(solution)/shard_map/dot_general | solution.py:222
  18.2 1.6 collective-permute-start.6
  19.9 4.0 %collective-permute-done = f32[916,128]{1,0:T(8,128)S(1)} collective-permute-done((f32[916,128]{1,0:T(8,128)}, f32[916,128]{1,0:T(8,128)S(1)}, u32[]{:S(2)}, u32[]{:S(2)}) %collective-permute-start) | collective-permute-done | bytes 469024 | tf_op jit(solution)/shard_map/ppermute | solution.py:87
  23.9 1.9 collective-permute-start.1
  25.8 6.2 %collective-permute-done.6 = f32[916,128]{1,0:T(8,128)S(1)} collective-permute-done((f32[916,128]{1,0:T(8,128)S(1)}, f32[916,128]{1,0:T(8,128)S(1)}, u32[]{:S(2)}, u32[]{:S(2)}) %collective-permute-start.6) | collective-permute-done | bytes 469024 | tf_op jit(solution)/shard_map/ppermute | solution.py:87
  32.3 3.3 %collective-permute-done.1 = f32[458,128]{1,0:T(8,128)S(1)} collective-permute-done((f32[458,128]{1,0:T(8,128)S(1)}, f32[458,128]{1,0:T(8,128)S(1)}, u32[]{:S(2)}, u32[]{:S(2)}) %collective-permute-start.1) | collective-permute-done | bytes 234528 | tf_op jit(solution)/shard_map/ppermute | solution.py:87
  35.7 2.7 %collective-permute-start.2 = (f32[229,128]{1,0:T(8,128)S(1)}, f32[229,128]{1,0:T(8,128)S(1)}, u32[]{:S(2)}, u32[]{:S(2)}) collective-permute-start(f32[229,128]{1,0:T(8,128)S(1)} %constant_dynamic-slice_fusion.12), channel_id=1, source_target_pairs={{0,16},{4,20},{8,24},{12,28},{16,0},{20,4},{24,8},{28,12},{1,17},{... | collective-permute-start | bytes 351752 | tf_op jit(solution)/shard_map/ppermute | solution.py:87
  38.4 4.6 %collective-permute-done.2 = f32[229,128]{1,0:T(8,128)S(1)} collective-permute-done((f32[229,128]{1,0:T(8,128)S(1)}, f32[229,128]{1,0:T(8,128)S(1)}, u32[]{:S(2)}, u32[]{:S(2)}) %collective-permute-start.2) | collective-permute-done | bytes 117280 | tf_op jit(solution)/shard_map/ppermute | solution.py:87
  43.0 1.3 collective-permute-start.3
  44.3 1.8 collective-permute-start.8
  46.8 1.7 dynamic_update_slice.114
  48.5 3.4 %collective-permute-done.3 = f32[229,128]{1,0:T(8,128)S(1)} collective-permute-done((f32[229,128]{1,0:T(8,128)S(1)}, f32[229,128]{1,0:T(8,128)S(1)}, u32[]{:S(2)}, u32[]{:S(2)}) %collective-permute-start.3) | collective-permute-done | bytes 117280 | tf_op jit(solution)/shard_map/ppermute | solution.py:87
  51.9 1.6 dynamic_update_slice.115
  55.9 1.6 copy.35
  58.4 3.5 %collective-permute-start.9 = (f32[229,128]{1,0:T(8,128)S(1)}, f32[229,128]{1,0:T(8,128)}, u32[]{:S(2)}, u32[]{:S(2)}) collective-permute-start(f32[229,128]{1,0:T(8,128)S(1)} %dynamic-slice_add_fusion.7), channel_id=1, source_target_pairs={{0,16},{4,20},{8,24},{12,28},{16,0},{20,4},{24,8},{28,12},{1,17},{... | collective-permute-start | bytes 351752 | tf_op jit(solution)/shard_map/ppermute | solution.py:87
  61.9 2.2 %dynamic_update_slice.116 = f32[916,128]{1,0:T(8,128)S(1)} dynamic-update-slice(f32[916,128]{1,0:T(8,128)S(1)} %broadcast.93.clone.1, f32[458,128]{1,0:T(8,128)} %dynamic_update_slice.115, s32[]{:T(128)S(6)} %select_n.223, s32[]{:T(128)} %constant.194.clone.1) | dynamic-update-slice | bytes 468996 | tf_op jit(solution)/shard_map/dynamic_update_slice | solution.py:93
  64.1 1.9 dynamic_update_slice.117
  66.9 1.0 subtract_convert_fusion
  69.7 1.4 dynamic_update_slice.121
  71.1 1.3 collective-permute-start.10
  72.4 2.5 %maximum_bitcast_fusion.basis_ref = bf16[512,1600]{1,0:T(8,128)(2,1)} fusion(bf16[1600,256]{0,1:T(8,128)(2,1)} %subtract_convert_fusion, bf16[1600,256]{0,1:T(8,128)(2,1)S(1)} %copy.35), kind=kLoop, calls=%fused_computation.7 | loop fusion | flops 3276800 | bytes 3276800 | tf_op jit(solution)/shard_map/transpose | solution.py:197
  75.7 1.8 dynamic_update_slice.122
  77.6 2.2 %dynamic_update_slice.118 = f32[1832,128]{1,0:T(8,128)S(1)} dynamic-update-slice(f32[1832,128]{1,0:T(8,128)S(1)} %broadcast.92.clone.1, f32[916,128]{1,0:T(8,128)S(1)} %dynamic_update_slice.117, s32[]{:T(128)S(6)} %select_n.219, s32[]{:T(128)} %constant.194.clone.1) | dynamic-update-slice | bytes 937988 | tf_op jit(solution)/shard_map/dynamic_update_slice | solution.py:93
  79.8 1.4 collective-permute-done.10
  81.2 1.7 dynamic_update_slice.123
  83.2 2.4 %dynamic_update_slice.124 = f32[1832,128]{1,0:T(8,128)S(1)} dynamic-update-slice(f32[1832,128]{1,0:T(8,128)S(1)} %broadcast.92.clone, f32[916,128]{1,0:T(8,128)} %dynamic_update_slice.123, s32[]{:T(128)S(6)} %select_n.229, s32[]{:T(128)} %constant.194.clone.1) | dynamic-update-slice | bytes 937988 | tf_op jit(solution)/shard_map/dynamic_update_slice | solution.py:93
  85.7 2.3 %dynamic_update_slice.119 = f32[1832,128]{1,0:T(8,128)S(1)} dynamic-update-slice(f32[1832,128]{1,0:T(8,128)S(1)} %dynamic_update_slice.118, f32[916,128]{1,0:T(8,128)} %collective-permute-done.5, s32[]{:T(128)S(6)} %select_n.220, s32[]{:T(128)} %constant.194.clone.1) | dynamic-update-slice | bytes 937988 | tf_op jit(solution)/shard_map/dynamic_update_slice | solution.py:94
  88.8 3.6 %collective-permute-done.11 = f32[916,128]{1,0:T(8,128)} collective-permute-done((f32[916,128]{1,0:T(8,128)}, f32[916,128]{1,0:T(8,128)}, u32[]{:S(2)}, u32[]{:S(2)}) %collective-permute-start.11) | collective-permute-done | bytes 469024 | tf_op jit(solution)/shard_map/ppermute | solution.py:87
  92.4 2.3 %dynamic_update_slice.125 = f32[1832,128]{1,0:T(8,128)S(1)} dynamic-update-slice(f32[1832,128]{1,0:T(8,128)S(1)} %dynamic_update_slice.124, f32[916,128]{1,0:T(8,128)} %collective-permute-done.11, s32[]{:T(128)S(6)} %select_n.230, s32[]{:T(128)} %constant.194.clone.1) | dynamic-update-slice | bytes 937988 | tf_op jit(solution)/shard_map/dynamic_update_slice | solution.py:94
  94.7 1.1 subtract_convert_fusion.1
  95.8 4.9 %convolution_bitcast_fusion.3 = f32[1600,256]{1,0:T(8,128)S(1)} fusion(bf16[1600,1600]{1,0:T(8,128)(2,1)} %bitcast.75, bf16[1600,128]{1,0:T(8,128)(2,1)S(1)} %get-tuple-element.14, bf16[1600,128]{1,0:T(8,128)(2,1)S(1)} %get-tuple-element.15), kind=kOutput, calls=%fused_computation.3 | convolution fusion | flops 1312358400 | bytes 7577600 | tf_op jit(solution)/shard_map/dot_general | solution.py:222
  101.6 1.3 multiply_reduce_fusion.1
  105.8 5.1 %convolution_bitcast_fusion.2 = f32[1600,256]{1,0:T(8,128)S(1)} fusion(bf16[1600,1600]{1,0:T(8,128)(2,1)} %bitcast.76, bf16[1600,128]{1,0:T(8,128)(2,1)} %get-tuple-element.16, bf16[1600,128]{1,0:T(8,128)(2,1)} %get-tuple-element.17), kind=kOutput, calls=%fused_computation.2 | convolution fusion | flops 1312358400 | bytes 7577600 | tf_op jit(solution)/shard_map/dot_general | solution.py:222
  111.9 1.5 collective-permute-start.13
  114.0 1.8 reshape_reshape.4
  117.7 1.4 multiply_divide_fusion.2
  119.2 2.0 convert_bitcast_fusion
  122.7 7.4 %collective-permute-done.14 = bf16[1,250,256]{2,1,0:T(8,128)(2,1)S(1)} collective-permute-done((bf16[1,250,256]{2,1,0:T(8,128)(2,1)S(1)}, bf16[1,250,256]{2,1,0:T(8,128)(2,1)S(1)}, u32[]{:S(2)}, u32[]{:S(2)}) %collective-permute-start.14) | collective-permute-done | bytes 128032 | tf_op jit(solution)/shard_map/ppermute | solution.py:87
  130.5 7.9 %collective-permute-done.15 = bf16[2,250,256]{2,1,0:T(8,128)(2,1)S(1)} collective-permute-done((bf16[2,250,256]{2,1,0:T(8,128)(2,1)S(1)}, bf16[2,250,256]{2,1,0:T(8,128)(2,1)S(1)}, u32[]{:S(2)}, u32[]{:S(2)}) %collective-permute-start.15) | collective-permute-done | bytes 256032 | tf_op jit(solution)/shard_map/ppermute | solution.py:87
  139.1 1.0 dynamic-slice_add_fusion.2
  140.2 1.1 collective-permute-start.18
  141.3 1.0 dynamic-slice_add_fusion.1
  142.9 3.1 %collective-permute-done.18 = f32[400,128]{1,0:T(8,128)S(1)} collective-permute-done((f32[400,128]{1,0:T(8,128)S(1)}, f32[400,128]{1,0:T(8,128)S(1)}, u32[]{:S(2)}, u32[]{:S(2)}) %collective-permute-start.18) | collective-permute-done | bytes 204832 | tf_op jit(solution)/shard_map/ppermute | solution.py:87
  146.1 1.4 collective-permute-start.19
  147.5 9.3 %collective-permute-done.28 = f32[400,128]{1,0:T(8,128)S(1)} collective-permute-done((f32[400,128]{1,0:T(8,128)S(1)}, f32[400,128]{1,0:T(8,128)S(1)}, u32[]{:S(2)}, u32[]{:S(2)}) %collective-permute-start.28) | collective-permute-done | bytes 204832 | tf_op jit(solution)/shard_map/ppermute | solution.py:87
  158.0 1.1 collective-permute-start.20
  159.1 2.5 %collective-permute-done.29 = f32[200,128]{1,0:T(8,128)S(1)} collective-permute-done((f32[200,128]{1,0:T(8,128)S(1)}, f32[200,128]{1,0:T(8,128)S(1)}, u32[]{:S(2)}, u32[]{:S(2)}) %collective-permute-start.29) | collective-permute-done | bytes 102432 | tf_op jit(solution)/shard_map/ppermute | solution.py:87
  162.3 3.6 %collective-permute-done.30 = f32[100,128]{1,0:T(8,128)S(1)} collective-permute-done((f32[100,128]{1,0:T(8,128)S(1)}, f32[100,128]{1,0:T(8,128)S(1)}, u32[]{:S(2)}, u32[]{:S(2)}) %collective-permute-start.30) | collective-permute-done | bytes 51232 | tf_op jit(solution)/shard_map/ppermute | solution.py:87
  166.0 1.7 collective-permute-done.21
  167.7 1.3 collective-permute-start.22
  169.0 2.1 collective-permute-done.31
  173.5 2.7 %collective-permute-done.32 = f32[50,128]{1,0:T(8,128)S(1)} collective-permute-done((f32[50,128]{1,0:T(8,128)S(1)}, f32[50,128]{1,0:T(8,128)S(1)}, u32[]{:S(2)}, u32[]{:S(2)}) %collective-permute-start.32) | collective-permute-done | bytes 25632 | tf_op jit(solution)/shard_map/ppermute | solution.py:87
  178.3 1.7 collective-permute-start.24
  179.9 1.4 collective-permute-done.33
  188.3 2.3 %collective-permute-done.25 = f32[400,128]{1,0:T(8,128)S(1)} collective-permute-done((f32[400,128]{1,0:T(8,128)S(1)}, f32[400,128]{1,0:T(8,128)S(1)}, u32[]{:S(2)}, u32[]{:S(2)}) %collective-permute-start.25) | collective-permute-done | bytes 204832 | tf_op jit(solution)/shard_map/ppermute | solution.py:87
  190.7 2.3 %collective-permute-done.35 = f32[400,128]{1,0:T(8,128)S(1)} collective-permute-done((f32[400,128]{1,0:T(8,128)S(1)}, f32[400,128]{1,0:T(8,128)S(1)}, u32[]{:S(2)}, u32[]{:S(2)}) %collective-permute-start.35) | collective-permute-done | bytes 204832 | tf_op jit(solution)/shard_map/ppermute | solution.py:87
  193.2 1.3 pad_maximum_fusion.1.direction_ref
  194.5 8.2 %shard_map.221 = bf16[8,200,1600]{2,1,0:T(8,128)(2,1)} custom-call(bf16[8,200,512]{2,1,0:T(8,128)(2,1)} %pad_maximum_fusion.1.direction_ref, bf16[512,1600]{1,0:T(8,128)(2,1)} %maximum_bitcast_fusion.basis_ref, bf16[8,200,1600]{2,1,0:T(8,128)(2,1)} %bitcast.68), custom_call_target="tpu_custom_call" | custom-call | tf_op jit(solution)/shard_map/pallas_call | solution.py:201
  204.7 2.9 %fusion.4 = f32[256,256]{1,0:T(8,128)S(1)} fusion(f32[1600,128]{1,0:T(8,128)S(1)} %constant_dynamic-update-slice_fusion, f32[1600,128]{1,0:T(8,128)S(1)} %constant_dynamic-update-slice_fusion.6, f32[]{:T(128)S(6)} %rsqrt.4), kind=kOutput, calls=%fused_computation.16 | convolution fusion | flops 1259110400 | bytes 1900548 | tf_op jit(solution)/shard_map/dot_general | solution.py:32
  212.5 2.0 fusion.2
  (192 shorter events, 38.6 us)
Async XLA Ops:
  1.7 2.2 %copy-start.3 = (f32[400,128]{1,0:T(8,128)}, f32[400,128]{1,0:T(8,128)S(1)}, u32[]{:S(2)}) copy-start(f32[400,128]{1,0:T(8,128)S(1)} %reshape.183) | copy-start | bytes 614404
  8.1 0.9 slice-start
  8.2 4.6 %copy-start.14 = (bf16[1,4,1600]{2,1,0:T(4,128)(2,1)S(1)}, bf16[1,4,1600]{2,1,0:T(4,128)(2,1)}, u32[]{:S(2)}) copy-start(bf16[1,4,1600]{2,1,0:T(4,128)(2,1)} %param.15) | copy-start | bytes 38404
  9.9 13.9 %collective-permute-start = (f32[916,128]{1,0:T(8,128)}, f32[916,128]{1,0:T(8,128)S(1)}, u32[]{:S(2)}, u32[]{:S(2)}) collective-permute-start(f32[916,128]{1,0:T(8,128)} %constant_dynamic-slice_fusion.14), channel_id=1, source_target_pairs={{0,4},{4,0},{8,12},{12,8},{16,20},{20,16},{24,28},{28,24},{1,5},{5... | collective-permute-start | bytes 1406984 | tf_op jit(solution)/shard_map/ppermute | solution.py:87
  17.1 0.9 copy-start.4
  18.2 13.8 %collective-permute-start.6 = (f32[916,128]{1,0:T(8,128)S(1)}, f32[916,128]{1,0:T(8,128)S(1)}, u32[]{:S(2)}, u32[]{:S(2)}) collective-permute-start(f32[916,128]{1,0:T(8,128)S(1)} %pad_dynamic-slice_fusion.2), channel_id=1, source_target_pairs={{0,8},{4,12},{8,0},{12,4},{16,24},{20,28},{24,16},{28,20},{1,9},{5... | collective-permute-start | bytes 1406984 | tf_op jit(solution)/shard_map/ppermute | solution.py:87
  23.9 11.7 %collective-permute-start.1 = (f32[458,128]{1,0:T(8,128)S(1)}, f32[458,128]{1,0:T(8,128)S(1)}, u32[]{:S(2)}, u32[]{:S(2)}) collective-permute-start(f32[458,128]{1,0:T(8,128)S(1)} %constant_dynamic-slice_fusion.13), channel_id=1, source_target_pairs={{0,8},{4,12},{8,0},{12,4},{16,24},{20,28},{24,16},{28,20},{1,9},{5... | collective-permute-start | bytes 703496 | tf_op jit(solution)/shard_map/ppermute | solution.py:87
  32.1 22.0 %copy-start = (f32[1600,256]{1,0:T(8,128)S(1)}, f32[1600,256]{1,0:T(8,128)}, u32[]{:S(2)}) copy-start(f32[1600,256]{1,0:T(8,128)} %param.18) | copy-start | bytes 4915204
  32.2 6.2 %collective-permute-start.7 = (f32[458,128]{1,0:T(8,128)S(1)}, f32[458,128]{1,0:T(8,128)S(1)}, u32[]{:S(2)}, u32[]{:S(2)}) collective-permute-start(f32[458,128]{1,0:T(8,128)S(1)} %constant_dynamic-slice_fusion.11), channel_id=1, source_target_pairs={{0,4},{4,0},{8,12},{12,8},{16,20},{20,16},{24,28},{28,24},{1,5},{5... | collective-permute-start | bytes 703496 | tf_op jit(solution)/shard_map/ppermute | solution.py:87
  35.7 7.3 %collective-permute-start.2 = (f32[229,128]{1,0:T(8,128)S(1)}, f32[229,128]{1,0:T(8,128)S(1)}, u32[]{:S(2)}, u32[]{:S(2)}) collective-permute-start(f32[229,128]{1,0:T(8,128)S(1)} %constant_dynamic-slice_fusion.12), channel_id=1, source_target_pairs={{0,16},{4,20},{8,24},{12,28},{16,0},{20,4},{24,8},{28,12},{1,17},{... | collective-permute-start | bytes 351752 | tf_op jit(solution)/shard_map/ppermute | solution.py:87
  38.4 5.9 %copy-start.5 = (f32[458,128]{1,0:T(8,128)}, f32[458,128]{1,0:T(8,128)S(1)}, u32[]{:S(2)}) copy-start(f32[458,128]{1,0:T(8,128)S(1)} %dynamic-slice_add_fusion.3) | copy-start | bytes 703492
  43.0 8.9 %collective-permute-start.3 = (f32[229,128]{1,0:T(8,128)S(1)}, f32[229,128]{1,0:T(8,128)S(1)}, u32[]{:S(2)}, u32[]{:S(2)}) collective-permute-start(f32[229,128]{1,0:T(8,128)S(1)} %dynamic-slice_add_fusion.8), channel_id=1, source_target_pairs={{0,16},{4,20},{8,24},{12,28},{16,0},{20,4},{24,8},{28,12},{1,17},{... | collective-permute-start | bytes 351752 | tf_op jit(solution)/shard_map/ppermute | solution.py:87
  44.3 13.1 %collective-permute-start.8 = (f32[229,128]{1,0:T(8,128)S(1)}, f32[229,128]{1,0:T(8,128)}, u32[]{:S(2)}, u32[]{:S(2)}) collective-permute-start(f32[229,128]{1,0:T(8,128)S(1)} %constant_dynamic-slice_fusion.10), channel_id=1, source_target_pairs={{0,16},{4,20},{8,24},{12,28},{16,0},{20,4},{24,8},{28,12},{1,17},{... | collective-permute-start | bytes 351752 | tf_op jit(solution)/shard_map/ppermute | solution.py:87
  53.5 10.7 %collective-permute-start.4 = (f32[458,128]{1,0:T(8,128)}, f32[458,128]{1,0:T(8,128)}, u32[]{:S(2)}, u32[]{:S(2)}) collective-permute-start(f32[458,128]{1,0:T(8,128)} %dynamic_update_slice.115), channel_id=1, source_target_pairs={{0,8},{4,12},{8,0},{12,4},{16,24},{20,28},{24,16},{28,20},{1,9},{5... | collective-permute-start | bytes 703496 | tf_op jit(solution)/shard_map/ppermute | solution.py:87
  55.8 1.6 copy-start.6
  58.4 11.3 %collective-permute-start.9 = (f32[229,128]{1,0:T(8,128)S(1)}, f32[229,128]{1,0:T(8,128)}, u32[]{:S(2)}, u32[]{:S(2)}) collective-permute-start(f32[229,128]{1,0:T(8,128)S(1)} %dynamic-slice_add_fusion.7), channel_id=1, source_target_pairs={{0,16},{4,20},{8,24},{12,28},{16,0},{20,4},{24,8},{28,12},{1,17},{... | collective-permute-start | bytes 351752 | tf_op jit(solution)/shard_map/ppermute | solution.py:87
  66.0 19.6 %collective-permute-start.5 = (f32[916,128]{1,0:T(8,128)S(1)}, f32[916,128]{1,0:T(8,128)}, u32[]{:S(2)}, u32[]{:S(2)}) collective-permute-start(f32[916,128]{1,0:T(8,128)S(1)} %dynamic_update_slice.117), channel_id=1, source_target_pairs={{0,4},{4,0},{8,12},{12,8},{16,20},{20,16},{24,28},{28,24},{1,5},{5... | collective-permute-start | bytes 1406984 | tf_op jit(solution)/shard_map/ppermute | solution.py:87
  71.1 10.1 %collective-permute-start.10 = (f32[458,128]{1,0:T(8,128)S(1)}, f32[458,128]{1,0:T(8,128)S(1)}, u32[]{:S(2)}, u32[]{:S(2)}) collective-permute-start(f32[458,128]{1,0:T(8,128)S(1)} %dynamic_update_slice.121), channel_id=1, source_target_pairs={{0,4},{4,0},{8,12},{12,8},{16,20},{20,16},{24,28},{28,24},{1,5},{5... | collective-permute-start | bytes 703496 | tf_op jit(solution)/shard_map/ppermute | solution.py:87
  82.9 9.5 %collective-permute-start.11 = (f32[916,128]{1,0:T(8,128)}, f32[916,128]{1,0:T(8,128)}, u32[]{:S(2)}, u32[]{:S(2)}) collective-permute-start(f32[916,128]{1,0:T(8,128)} %dynamic_update_slice.123), channel_id=1, source_target_pairs={{0,8},{4,12},{8,0},{12,4},{16,24},{20,28},{24,16},{28,20},{1,9},{5... | collective-permute-start | bytes 1406984 | tf_op jit(solution)/shard_map/ppermute | solution.py:87
  100.6 0.9 copy-start.7
  101.6 37.6 %collective-permute-start.17 = (f32[800,128]{1,0:T(8,128)}, f32[800,128]{1,0:T(8,128)}, u32[]{:S(2)}, u32[]{:S(2)}) collective-permute-start(f32[800,128]{1,0:T(8,128)} %constant_dynamic-slice_fusion.9), channel_id=1, source_target_pairs={{0,1},{1,0},{2,3},{3,2},{4,5},{5,4},{6,7},{7,6},{8,9},{9,8},{10,11... | collective-permute-start | bytes 1228808 | tf_op jit(solution)/shard_map/ppermute | solution.py:87
  105.2 6.7 %collective-permute-start.12 = (f32[8,128]{1,0:T(8,128)S(1)}, f32[8,128]{1,0:T(8,128)S(1)}, u32[]{:S(2)}, u32[]{:S(2)}) collective-permute-start(f32[8,128]{1,0:T(8,128)S(1)} %broadcast_in_dim.15), channel_id=1, source_target_pairs={{0,1},{1,0},{2,3},{3,2},{4,5},{5,4},{6,7},{7,6},{8,9},{9,8},{10,11... | collective-permute-start | bytes 12296 | tf_op jit(solution)/shard_map/ppermute | solution.py:87
  110.9 6.8 %copy-start.9 = (f32[1,1,4,1600]{3,2,1,0:T(4,128)S(1)}, f32[1,1,4,1600]{3,2,1,0:T(4,128)}, u32[]{:S(2)}) copy-start(f32[1,1,4,1600]{3,2,1,0:T(4,128)} %param.26) | copy-start | bytes 76804
  110.9 6.8 %copy-start.10 = (f32[1,1,4,1600]{3,2,1,0:T(4,128)S(1)}, f32[1,1,4,1600]{3,2,1,0:T(4,128)}, u32[]{:S(2)}) copy-start(f32[1,1,4,1600]{3,2,1,0:T(4,128)} %param.25) | copy-start | bytes 76804
  111.9 3.9 %collective-permute-start.13 = (f32[8,128]{1,0:T(8,128)S(1)}, f32[8,128]{1,0:T(8,128)S(1)}, u32[]{:S(2)}, u32[]{:S(2)}) collective-permute-start(f32[8,128]{1,0:T(8,128)S(1)} %broadcast_add_fusion), channel_id=1, source_target_pairs={{0,2},{1,3},{2,0},{3,1},{4,6},{5,7},{6,4},{7,5},{8,10},{9,11},{10,... | collective-permute-start | bytes 12296 | tf_op jit(solution)/shard_map/ppermute | solution.py:87
  119.2 2.7 %copy-start.1 = (f32[1600,128]{1,0:T(8,128)S(1)}, f32[1600,128]{1,0:T(8,128)}, u32[]{:S(2)}) copy-start(f32[1600,128]{1,0:T(8,128)} %slice_add_fusion) | copy-start | bytes 2457604
  121.3 8.9 %collective-permute-start.14 = (bf16[1,250,256]{2,1,0:T(8,128)(2,1)S(1)}, bf16[1,250,256]{2,1,0:T(8,128)(2,1)S(1)}, u32[]{:S(2)}, u32[]{:S(2)}) collective-permute-start(bf16[1,250,256]{2,1,0:T(8,128)(2,1)S(1)} %maximum_bitcast_fusion.1), channel_id=1, source_target_pairs={{0,16},{4,20},{8,24},{12,28},{16,0},{20,4},{24,8},{28,12},{1,17},{... | collective-permute-start | bytes 384008 | tf_op jit(solution)/shard_map/ppermute | solution.py:87
  122.7 18.6 %collective-permute-start.27 = (f32[800,128]{1,0:T(8,128)}, f32[800,128]{1,0:T(8,128)}, u32[]{:S(2)}, u32[]{:S(2)}) collective-permute-start(f32[800,128]{1,0:T(8,128)} %constant_dynamic-slice_fusion.4), channel_id=1, source_target_pairs={{0,1},{1,0},{2,3},{3,2},{4,5},{5,4},{6,7},{7,6},{8,9},{9,8},{10,11... | collective-permute-start | bytes 1228808 | tf_op jit(solution)/shard_map/ppermute | solution.py:87
  130.2 8.2 %collective-permute-start.15 = (bf16[2,250,256]{2,1,0:T(8,128)(2,1)S(1)}, bf16[2,250,256]{2,1,0:T(8,128)(2,1)S(1)}, u32[]{:S(2)}, u32[]{:S(2)}) collective-permute-start(bf16[2,250,256]{2,1,0:T(8,128)(2,1)S(1)} %constant_dynamic-update-slice_fusion.16), channel_id=1, source_target_pairs={{0,8},{4,12},{8,0},{12,4},{16,24},{20,28},{24,16},{28,20},{1,9},{5... | collective-permute-start | bytes 768008 | tf_op jit(solution)/shard_map/ppermute | solution.py:87
  130.3 11.0 %copy-start.2 = (f32[1600,128]{1,0:T(8,128)S(1)}, f32[1600,128]{1,0:T(8,128)}, u32[]{:S(2)}) copy-start(f32[1600,128]{1,0:T(8,128)} %slice_add_fusion) | copy-start | bytes 2457604
  138.4 43.6 %collective-permute-start.16 = (bf16[4,250,256]{2,1,0:T(8,128)(2,1)S(1)}, bf16[4,250,256]{2,1,0:T(8,128)(2,1)S(1)}, u32[]{:S(2)}, u32[]{:S(2)}) collective-permute-start(bf16[4,250,256]{2,1,0:T(8,128)(2,1)S(1)} %constant_dynamic-update-slice_fusion.14), channel_id=1, source_target_pairs={{0,4},{4,0},{8,12},{12,8},{16,20},{20,16},{24,28},{28,24},{1,5},{5... | collective-permute-start | bytes 1536008 | tf_op jit(solution)/shard_map/ppermute | solution.py:87
  140.2 5.9 %collective-permute-start.18 = (f32[400,128]{1,0:T(8,128)S(1)}, f32[400,128]{1,0:T(8,128)S(1)}, u32[]{:S(2)}, u32[]{:S(2)}) collective-permute-start(f32[400,128]{1,0:T(8,128)S(1)} %constant_dynamic-slice_fusion.8), channel_id=1, source_target_pairs={{0,2},{1,3},{2,0},{3,1},{4,6},{5,7},{6,4},{7,5},{8,10},{9,11},{10,... | collective-permute-start | bytes 614408 | tf_op jit(solution)/shard_map/ppermute | solution.py:87
  142.4 28.8 %copy-start.11 = (f32[4,1600]{1,0:T(4,128)S(1)}, f32[4,1600]{1,0:T(4,128)}, u32[]{:S(2)}) copy-start(f32[4,1600]{1,0:T(4,128)} %param.21) | copy-start | bytes 76804
  142.4 28.8 %copy-start.12 = (f32[4,1600]{1,0:T(4,128)S(1)}, f32[4,1600]{1,0:T(4,128)}, u32[]{:S(2)}) copy-start(f32[4,1600]{1,0:T(4,128)} %param.23) | copy-start | bytes 76804
  142.4 28.8 %copy-start.13 = (f32[4,1600]{1,0:T(4,128)S(1)}, f32[4,1600]{1,0:T(4,128)}, u32[]{:S(2)}) copy-start(f32[4,1600]{1,0:T(4,128)} %param.22) | copy-start | bytes 76804
  142.4 14.5 %collective-permute-start.28 = (f32[400,128]{1,0:T(8,128)S(1)}, f32[400,128]{1,0:T(8,128)S(1)}, u32[]{:S(2)}, u32[]{:S(2)}) collective-permute-start(f32[400,128]{1,0:T(8,128)S(1)} %constant_dynamic-slice_fusion.3), channel_id=1, source_target_pairs={{0,4},{4,0},{8,12},{12,8},{16,20},{20,16},{24,28},{28,24},{1,5},{5... | collective-permute-start | bytes 614408 | tf_op jit(solution)/shard_map/ppermute | solution.py:87
  146.1 11.8 %collective-permute-start.19 = (f32[200,128]{1,0:T(8,128)S(1)}, f32[200,128]{1,0:T(8,128)S(1)}, u32[]{:S(2)}, u32[]{:S(2)}) collective-permute-start(f32[200,128]{1,0:T(8,128)S(1)} %constant_dynamic-slice_fusion.7), channel_id=1, source_target_pairs={{0,4},{4,0},{8,12},{12,8},{16,20},{20,16},{24,28},{28,24},{1,5},{5... | collective-permute-start | bytes 307208 | tf_op jit(solution)/shard_map/ppermute | solution.py:87
  156.9 4.7 %collective-permute-start.29 = (f32[200,128]{1,0:T(8,128)S(1)}, f32[200,128]{1,0:T(8,128)S(1)}, u32[]{:S(2)}, u32[]{:S(2)}) collective-permute-start(f32[200,128]{1,0:T(8,128)S(1)} %constant_dynamic-slice_fusion.2), channel_id=1, source_target_pairs={{0,8},{4,12},{8,0},{12,4},{16,24},{20,28},{24,16},{28,20},{1,9},{5... | collective-permute-start | bytes 307208 | tf_op jit(solution)/shard_map/ppermute | solution.py:87
  158.0 4.2 %collective-permute-start.20 = (f32[100,128]{1,0:T(8,128)S(1)}, f32[100,128]{1,0:T(8,128)S(1)}, u32[]{:S(2)}, u32[]{:S(2)}) collective-permute-start(f32[100,128]{1,0:T(8,128)S(1)} %constant_dynamic-slice_fusion.6), channel_id=1, source_target_pairs={{0,8},{4,12},{8,0},{12,4},{16,24},{20,28},{24,16},{28,20},{1,9},{5... | collective-permute-start | bytes 153608 | tf_op jit(solution)/shard_map/ppermute | solution.py:87
  161.7 4.2 %collective-permute-start.30 = (f32[100,128]{1,0:T(8,128)S(1)}, f32[100,128]{1,0:T(8,128)S(1)}, u32[]{:S(2)}, u32[]{:S(2)}) collective-permute-start(f32[100,128]{1,0:T(8,128)S(1)} %constant_dynamic-slice_fusion.1), channel_id=1, source_target_pairs={{0,2},{1,3},{2,0},{3,1},{4,6},{5,7},{6,4},{7,5},{8,10},{9,11},{10,... | collective-permute-start | bytes 153608 | tf_op jit(solution)/shard_map/ppermute | solution.py:87
  162.2 5.5 %collective-permute-start.21 = (f32[50,128]{1,0:T(8,128)S(1)}, f32[50,128]{1,0:T(8,128)S(1)}, u32[]{:S(2)}, u32[]{:S(2)}) collective-permute-start(f32[50,128]{1,0:T(8,128)S(1)} %constant_dynamic-slice_fusion.5), channel_id=1, source_target_pairs={{0,16},{4,20},{8,24},{12,28},{16,0},{20,4},{24,8},{28,12},{1,17},{... | collective-permute-start | bytes 76808 | tf_op jit(solution)/shard_map/ppermute | solution.py:87
  165.9 5.1 %collective-permute-start.31 = (f32[50,128]{1,0:T(8,128)S(1)}, f32[50,128]{1,0:T(8,128)S(1)}, u32[]{:S(2)}, u32[]{:S(2)}) collective-permute-start(f32[50,128]{1,0:T(8,128)S(1)} %constant_dynamic-slice_fusion), channel_id=1, source_target_pairs={{0,16},{4,20},{8,24},{12,28},{16,0},{20,4},{24,8},{28,12},{1,17},{... | collective-permute-start | bytes 76808 | tf_op jit(solution)/shard_map/ppermute | solution.py:87
  167.7 5.0 %collective-permute-start.22 = (f32[50,128]{1,0:T(8,128)S(1)}, f32[50,128]{1,0:T(8,128)S(1)}, u32[]{:S(2)}, u32[]{:S(2)}) collective-permute-start(f32[50,128]{1,0:T(8,128)S(1)} %dynamic-slice_add_fusion.14), channel_id=1, source_target_pairs={{0,16},{4,20},{8,24},{12,28},{16,0},{20,4},{24,8},{28,12},{1,17},{... | collective-permute-start | bytes 76808 | tf_op jit(solution)/shard_map/ppermute | solution.py:87
  171.1 5.2 %collective-permute-start.32 = (f32[50,128]{1,0:T(8,128)S(1)}, f32[50,128]{1,0:T(8,128)S(1)}, u32[]{:S(2)}, u32[]{:S(2)}) collective-permute-start(f32[50,128]{1,0:T(8,128)S(1)} %dynamic-slice_add_fusion.13), channel_id=1, source_target_pairs={{0,16},{4,20},{8,24},{12,28},{16,0},{20,4},{24,8},{28,12},{1,17},{... | collective-permute-start | bytes 76808 | tf_op jit(solution)/shard_map/ppermute | solution.py:87
  173.0 4.9 %collective-permute-start.23 = (f32[100,128]{1,0:T(8,128)S(1)}, f32[100,128]{1,0:T(8,128)S(1)}, u32[]{:S(2)}, u32[]{:S(2)}) collective-permute-start(f32[100,128]{1,0:T(8,128)S(1)} %dynamic_update_slice.133), channel_id=1, source_target_pairs={{0,8},{4,12},{8,0},{12,4},{16,24},{20,28},{24,16},{28,20},{1,9},{5... | collective-permute-start | bytes 153608 | tf_op jit(solution)/shard_map/ppermute | solution.py:87
  176.7 4.6 %collective-permute-start.33 = (f32[100,128]{1,0:T(8,128)S(1)}, f32[100,128]{1,0:T(8,128)S(1)}, u32[]{:S(2)}, u32[]{:S(2)}) collective-permute-start(f32[100,128]{1,0:T(8,128)S(1)} %dynamic_update_slice.143), channel_id=1, source_target_pairs={{0,2},{1,3},{2,0},{3,1},{4,6},{5,7},{6,4},{7,5},{8,10},{9,11},{10,... | collective-permute-start | bytes 153608 | tf_op jit(solution)/shard_map/ppermute | solution.py:87
  178.3 5.7 %collective-permute-start.24 = (f32[200,128]{1,0:T(8,128)S(1)}, f32[200,128]{1,0:T(8,128)}, u32[]{:S(2)}, u32[]{:S(2)}) collective-permute-start(f32[200,128]{1,0:T(8,128)S(1)} %dynamic_update_slice.135), channel_id=1, source_target_pairs={{0,4},{4,0},{8,12},{12,8},{16,20},{20,16},{24,28},{28,24},{1,5},{5... | collective-permute-start | bytes 307208 | tf_op jit(solution)/shard_map/ppermute | solution.py:87
  181.6 4.8 %collective-permute-start.34 = (f32[200,128]{1,0:T(8,128)S(1)}, f32[200,128]{1,0:T(8,128)}, u32[]{:S(2)}, u32[]{:S(2)}) collective-permute-start(f32[200,128]{1,0:T(8,128)S(1)} %dynamic_update_slice.145), channel_id=1, source_target_pairs={{0,8},{4,12},{8,0},{12,4},{16,24},{20,28},{24,16},{28,20},{1,9},{5... | collective-permute-start | bytes 307208 | tf_op jit(solution)/shard_map/ppermute | solution.py:87
  182.1 0.9 copy-start.8
  184.9 5.8 %collective-permute-start.25 = (f32[400,128]{1,0:T(8,128)S(1)}, f32[400,128]{1,0:T(8,128)S(1)}, u32[]{:S(2)}, u32[]{:S(2)}) collective-permute-start(f32[400,128]{1,0:T(8,128)S(1)} %constant_dynamic-update-slice_fusion.10), channel_id=1, source_target_pairs={{0,2},{1,3},{2,0},{3,1},{4,6},{5,7},{6,4},{7,5},{8,10},{9,11},{10,... | collective-permute-start | bytes 614408 | tf_op jit(solution)/shard_map/ppermute | solution.py:87
  187.3 5.8 %collective-permute-start.35 = (f32[400,128]{1,0:T(8,128)S(1)}, f32[400,128]{1,0:T(8,128)S(1)}, u32[]{:S(2)}, u32[]{:S(2)}) collective-permute-start(f32[400,128]{1,0:T(8,128)S(1)} %constant_dynamic-update-slice_fusion.4), channel_id=1, source_target_pairs={{0,4},{4,0},{8,12},{12,8},{16,20},{20,16},{24,28},{28,24},{1,5},{5... | collective-permute-start | bytes 614408 | tf_op jit(solution)/shard_map/ppermute | solution.py:87
  190.7 12.2 %collective-permute-start.26 = (f32[800,128]{1,0:T(8,128)S(1)}, f32[800,128]{1,0:T(8,128)S(1)}, u32[]{:S(2)}, u32[]{:S(2)}) collective-permute-start(f32[800,128]{1,0:T(8,128)S(1)} %constant_dynamic-update-slice_fusion.8), channel_id=1, source_target_pairs={{0,1},{1,0},{2,3},{3,2},{4,5},{5,4},{6,7},{7,6},{8,9},{9,8},{10,11... | collective-permute-start | bytes 1228808 | tf_op jit(solution)/shard_map/ppermute | solution.py:87
  193.1 9.8 %collective-permute-start.36 = (f32[800,128]{1,0:T(8,128)S(1)}, f32[800,128]{1,0:T(8,128)S(1)}, u32[]{:S(2)}, u32[]{:S(2)}) collective-permute-start(f32[800,128]{1,0:T(8,128)S(1)} %constant_dynamic-update-slice_fusion.2), channel_id=1, source_target_pairs={{0,1},{1,0},{2,3},{3,2},{4,5},{5,4},{6,7},{7,6},{8,9},{9,8},{10,11... | collective-permute-start | bytes 1228808 | tf_op jit(solution)/shard_map/ppermute | solution.py:87

commit v9 on v7

--- a/solution.py
+++ b/solution.py
@@ -197,7 +197,7 @@
     pieces = split2(basis).T
     depth = pieces.shape[0]
     doubled = jnp.concatenate([direction_bf16] * 2, axis=1).reshape(blocks, rows, depth)
-    group = 2 if blocks % 2 == 0 else 1
+    group = 4 if blocks % 4 == 0 else 1
     return pl.pallas_call(
         update_kernel,
         out_shape=jax.ShapeDtypeStruct(weights.shape, jnp.bfloat16),

time: 198 us -> 197 us (level)
  no operation moved by 1% of the time
where the time goes in v9:
time: 197 us; the launch traced here: 196 us
  waiting for transfers between devices  75.8 us (38%)
  starting transfers between devices  44 us (22%)
  matrix products  25.4 us (13%)
  other arithmetic  24.8 us (13%)
  local copies, waits for them, and re-layouts  12.8 us (6%)
  Pallas kernels  7.5 us (4%)
  between operations  5.82 us (3%)
    ppermute x37, waiting for transfers between devices, swap_with(): lax.ppermute(values, name, [(index, index ^ bit) for index in range(size)])  75.8 us
    ppermute x37, starting transfers between devices, swap_with(): lax.ppermute(values, name, [(index, index ^ bit) for index in range(size)])  44 us
    dot_general x4, matrix products, exact_dot(): lax.dot_general(lhs_bf16, split2(rhs_f32), ((contract, (0,)), ((), ())),...  15.7 us
    pallas_call x1, Pallas kernels, updated_weights(): pl.pallas_call(update_kernel, out_shape=jax.ShapeDtypeStruct(weights.shap...  7.5 us
    convert_element_type x4, other arithmetic, split2(): second = (values - first.astype(jnp.float32)).astype(jnp.bfloat16)  5.03 us
    add x12, other arithmetic, run_steps(): parts = keep + swap_with(send, name, bit, size)  4.49 us
  transfers between devices with their start and end apart: 37, of which 25 were waited for; matrix products, arithmetic and copies ran while one was open for 19% of the time, Pallas kernels for 4%

profile of v9, /device:TPU:0, one launch (start us, length us, event | category | flops | bytes accessed | tf_op | source)
XLA Modules:
  0.0 196.2 jit_solution(6053056738757536592)
XLA Ops:
  0.7 2.2 %subtract_convert_fusion.4 = (bf16[1600,128]{1,0:T(8,128)(2,1)S(1)}, bf16[1600,128]{1,0:T(8,128)(2,1)S(1)}, bf16[1600,128]{1,0:T(8,128)(2,1)S(1)}, bf16[1600,128]{1,0:T(8,128)(2,1)S(1)}) fusion(f32[1600,256]{1,0:T(8,128)} %param.18), kind=kLoop, calls=%fused_computation.52 | loop fusion | flops 1228800 | bytes 4096000 | tf_op jit(solution)/shard_map/convert_element_type | solution.py:216
  2.8 4.2 %convolution_bitcast_fusion.1 = f32[1600,256]{1,0:T(8,128)S(1)} fusion(bf16[1600,1600]{1,0:T(8,128)(2,1)} %bitcast.73, bf16[1600,128]{1,0:T(8,128)(2,1)S(1)} %get-tuple-element.35, bf16[1600,128]{1,0:T(8,128)(2,1)S(1)} %get-tuple-element.36), kind=kOutput, calls=%fused_computation.1 | convolution fusion | flops 1312358400 | bytes 7577600 | tf_op jit(solution)/shard_map/dot_general | solution.py:222
  9.6 2.9 %collective-permute-start = (f32[928,128]{1,0:T(8,128)}, f32[928,128]{1,0:T(8,128)}, u32[]{:S(2)}, u32[]{:S(2)}) collective-permute-start(f32[928,128]{1,0:T(8,128)} %constant_dynamic-slice_fusion.12), channel_id=1, source_target_pairs={{0,4},{4,0},{8,12},{12,8},{16,20},{20,16},{24,28},{28,24},{1,5},{5... | collective-permute-start | bytes 1425416 | tf_op jit(solution)/shard_map/ppermute | solution.py:87
  12.6 4.2 %convolution_bitcast_fusion = f32[1600,256]{1,0:T(8,128)S(1)} fusion(bf16[1600,1600]{1,0:T(8,128)(2,1)} %bitcast.74, bf16[1600,128]{1,0:T(8,128)(2,1)S(1)} %get-tuple-element.41, bf16[1600,128]{1,0:T(8,128)(2,1)S(1)} %get-tuple-element.42), kind=kOutput, calls=%fused_computation | convolution fusion | flops 1312358400 | bytes 7577600 | tf_op jit(solution)/shard_map/dot_general | solution.py:222
  16.8 1.0 slice_add_fusion.2
  17.9 1.4 fusion.7
  20.1 1.6 collective-permute-start.6
  21.7 1.0 convert_element_type.154
  22.7 1.6 copy.34
  24.3 1.7 copy.35
  26.0 1.6 subtract_convert_fusion
  27.7 1.4 maximum_bitcast_fusion.basis_ref
  29.0 1.1 dynamic-slice_add_fusion
  30.7 2.7 %collective-permute-done.6 = f32[928,128]{1,0:T(8,128)} collective-permute-done((f32[928,128]{1,0:T(8,128)}, f32[928,128]{1,0:T(8,128)}, u32[]{:S(2)}, u32[]{:S(2)}) %collective-permute-start.6) | collective-permute-done | bytes 475168 | tf_op jit(solution)/shard_map/ppermute | solution.py:87
  33.3 1.1 fusion.22
  35.1 2.7 %collective-permute-done.1 = f32[464,128]{1,0:T(8,128)S(1)} collective-permute-done((f32[464,128]{1,0:T(8,128)S(1)}, f32[464,128]{1,0:T(8,128)S(1)}, u32[]{:S(2)}, u32[]{:S(2)}) %collective-permute-start.1) | collective-permute-done | bytes 237600 | tf_op jit(solution)/shard_map/ppermute | solution.py:87
  37.8 2.7 %collective-permute-start.2 = (f32[232,128]{1,0:T(8,128)S(1)}, f32[232,128]{1,0:T(8,128)S(1)}, u32[]{:S(2)}, u32[]{:S(2)}) collective-permute-start(f32[232,128]{1,0:T(8,128)S(1)} %constant_dynamic-slice_fusion.10), channel_id=1, source_target_pairs={{0,16},{4,20},{8,24},{12,28},{16,0},{20,4},{24,8},{28,12},{1,17},{... | collective-permute-start | bytes 356360 | tf_op jit(solution)/shard_map/ppermute | solution.py:87
  40.7 2.7 %collective-permute-start.8 = (f32[232,128]{1,0:T(8,128)S(1)}, f32[232,128]{1,0:T(8,128)S(1)}, u32[]{:S(2)}, u32[]{:S(2)}) collective-permute-start(f32[232,128]{1,0:T(8,128)S(1)} %constant_dynamic-slice_fusion.8), channel_id=1, source_target_pairs={{0,16},{4,20},{8,24},{12,28},{16,0},{20,4},{24,8},{28,12},{1,17},{... | collective-permute-start | bytes 356360 | tf_op jit(solution)/shard_map/ppermute | solution.py:87
  43.4 5.5 %collective-permute-done.2 = f32[232,128]{1,0:T(8,128)S(1)} collective-permute-done((f32[232,128]{1,0:T(8,128)S(1)}, f32[232,128]{1,0:T(8,128)S(1)}, u32[]{:S(2)}, u32[]{:S(2)}) %collective-permute-start.2) | collective-permute-done | bytes 118816 | tf_op jit(solution)/shard_map/ppermute | solution.py:87
  49.0 2.4 %collective-permute-done.8 = f32[232,128]{1,0:T(8,128)S(1)} collective-permute-done((f32[232,128]{1,0:T(8,128)S(1)}, f32[232,128]{1,0:T(8,128)S(1)}, u32[]{:S(2)}, u32[]{:S(2)}) %collective-permute-start.8) | collective-permute-done | bytes 118816 | tf_op jit(solution)/shard_map/ppermute | solution.py:87
  52.0 6.4 %collective-permute-done.3 = f32[232,128]{1,0:T(8,128)S(1)} collective-permute-done((f32[232,128]{1,0:T(8,128)S(1)}, f32[232,128]{1,0:T(8,128)S(1)}, u32[]{:S(2)}, u32[]{:S(2)}) %collective-permute-start.3) | collective-permute-done | bytes 118816 | tf_op jit(solution)/shard_map/ppermute | solution.py:87
  58.4 1.5 collective-permute-start.4
  60.8 1.6 collective-permute-done.9
  62.6 3.1 %collective-permute-done.4 = f32[464,128]{1,0:T(8,128)S(1)} collective-permute-done((f32[464,128]{1,0:T(8,128)S(1)}, f32[464,128]{1,0:T(8,128)S(1)}, u32[]{:S(2)}, u32[]{:S(2)}) %collective-permute-start.4) | collective-permute-done | bytes 237600 | tf_op jit(solution)/shard_map/ppermute | solution.py:87
  66.2 4.2 %collective-permute-done.10 = f32[464,128]{1,0:T(8,128)S(1)} collective-permute-done((f32[464,128]{1,0:T(8,128)S(1)}, f32[464,128]{1,0:T(8,128)S(1)}, u32[]{:S(2)}, u32[]{:S(2)}) %collective-permute-start.10) | collective-permute-done | bytes 237600 | tf_op jit(solution)/shard_map/ppermute | solution.py:87
  70.4 1.0 collective-permute-start.11
  71.7 7.1 %collective-permute-done.5 = f32[928,128]{1,0:T(8,128)S(1)} collective-permute-done((f32[928,128]{1,0:T(8,128)S(1)}, f32[928,128]{1,0:T(8,128)S(1)}, u32[]{:S(2)}, u32[]{:S(2)}) %collective-permute-start.5) | collective-permute-done | bytes 475168 | tf_op jit(solution)/shard_map/ppermute | solution.py:87
  79.2 1.1 subtract_convert_fusion.1
  80.9 2.4 %convolution_bitcast_fusion.3 = f32[1600,256]{1,0:T(8,128)S(1)} fusion(bf16[1600,1600]{1,0:T(8,128)(2,1)S(1)} %bitcast.78, bf16[1600,128]{1,0:T(8,128)(2,1)S(1)} %get-tuple-element.16, bf16[1600,128]{1,0:T(8,128)(2,1)S(1)} %get-tuple-element.17), kind=kOutput, calls=%fused_computation.3 | convolution fusion | flops 1312358400 | bytes 7577600 | tf_op jit(solution)/shard_map/dot_general | solution.py:222
  84.9 1.0 fusion.1
  87.8 5.0 %convolution_bitcast_fusion.2 = f32[1600,256]{1,0:T(8,128)S(1)} fusion(bf16[1600,1600]{1,0:T(8,128)(2,1)} %bitcast.75, bf16[1600,128]{1,0:T(8,128)(2,1)S(1)} %get-tuple-element.20, bf16[1600,128]{1,0:T(8,128)(2,1)} %get-tuple-element.21), kind=kOutput, calls=%fused_computation.2 | convolution fusion | flops 1312358400 | bytes 7577600 | tf_op jit(solution)/shard_map/dot_general | solution.py:222
  92.9 1.6 collective-permute-start.13
  98.4 1.4 multiply_divide_fusion.2
  100.0 1.9 convert_bitcast_fusion
  102.0 2.9 %collective-permute-start.14 = (bf16[1,250,256]{2,1,0:T(8,128)(2,1)S(1)}, bf16[1,250,256]{2,1,0:T(8,128)(2,1)S(1)}, u32[]{:S(2)}, u32[]{:S(2)}) collective-permute-start(bf16[1,250,256]{2,1,0:T(8,128)(2,1)S(1)} %maximum_bitcast_fusion.1), channel_id=1, source_target_pairs={{0,16},{4,20},{8,24},{12,28},{16,0},{20,4},{24,8},{28,12},{1,17},{... | collective-permute-start | bytes 384008 | tf_op jit(solution)/shard_map/ppermute | solution.py:87
  105.8 5.7 %collective-permute-done.14 = bf16[1,250,256]{2,1,0:T(8,128)(2,1)S(1)} collective-permute-done((bf16[1,250,256]{2,1,0:T(8,128)(2,1)S(1)}, bf16[1,250,256]{2,1,0:T(8,128)(2,1)S(1)}, u32[]{:S(2)}, u32[]{:S(2)}) %collective-permute-start.14) | collective-permute-done | bytes 128032 | tf_op jit(solution)/shard_map/ppermute | solution.py:87
  113.0 6.3 %collective-permute-done.15 = bf16[2,250,256]{2,1,0:T(8,128)(2,1)S(1)} collective-permute-done((bf16[2,250,256]{2,1,0:T(8,128)(2,1)S(1)}, bf16[2,250,256]{2,1,0:T(8,128)(2,1)S(1)}, u32[]{:S(2)}, u32[]{:S(2)}) %collective-permute-start.15) | collective-permute-done | bytes 256032 | tf_op jit(solution)/shard_map/ppermute | solution.py:87
  119.3 1.6 collective-permute-start.16
  121.1 1.1 fusion.23
  122.3 1.1 fusion.24
  123.9 4.4 %collective-permute-done.18 = f32[448,128]{1,0:T(8,128)S(1)} collective-permute-done((f32[448,128]{1,0:T(8,128)S(1)}, f32[448,128]{1,0:T(8,128)S(1)}, u32[]{:S(2)}, u32[]{:S(2)}) %collective-permute-start.18) | collective-permute-done | bytes 229408 | tf_op jit(solution)/shard_map/ppermute | solution.py:87
  128.8 9.1 %collective-permute-done.28 = f32[448,128]{1,0:T(8,128)S(1)} collective-permute-done((f32[448,128]{1,0:T(8,128)S(1)}, f32[448,128]{1,0:T(8,128)S(1)}, u32[]{:S(2)}, u32[]{:S(2)}) %collective-permute-start.28) | collective-permute-done | bytes 229408 | tf_op jit(solution)/shard_map/ppermute | solution.py:87
  138.0 1.9 collective-permute-start.29
  139.9 1.2 collective-permute-start.20
  141.1 1.7 collective-permute-done.29
  143.0 1.2 collective-permute-done.20
  144.2 3.5 %collective-permute-start.21 = (f32[56,128]{1,0:T(8,128)S(1)}, f32[56,128]{1,0:T(8,128)S(1)}, u32[]{:S(2)}, u32[]{:S(2)}) collective-permute-start(f32[56,128]{1,0:T(8,128)S(1)} %constant_dynamic-slice_fusion.4), channel_id=1, source_target_pairs={{0,16},{4,20},{8,24},{12,28},{16,0},{20,4},{24,8},{28,12},{1,17},{... | collective-permute-start | bytes 86024 | tf_op jit(solution)/shard_map/ppermute | solution.py:87
  147.8 3.2 %collective-permute-start.31 = (f32[56,128]{1,0:T(8,128)S(1)}, f32[56,128]{1,0:T(8,128)S(1)}, u32[]{:S(2)}, u32[]{:S(2)}) collective-permute-start(f32[56,128]{1,0:T(8,128)S(1)} %constant_dynamic-slice_fusion), channel_id=1, source_target_pairs={{0,16},{4,20},{8,24},{12,28},{16,0},{20,4},{24,8},{28,12},{1,17},{... | collective-permute-start | bytes 86024 | tf_op jit(solution)/shard_map/ppermute | solution.py:87
  151.0 1.7 collective-permute-start.22
  152.9 3.0 %collective-permute-start.32 = (f32[56,128]{1,0:T(8,128)S(1)}, f32[56,128]{1,0:T(8,128)S(1)}, u32[]{:S(2)}, u32[]{:S(2)}) collective-permute-start(f32[56,128]{1,0:T(8,128)S(1)} %get-tuple-element.19), channel_id=1, source_target_pairs={{0,16},{4,20},{8,24},{12,28},{16,0},{20,4},{24,8},{28,12},{1,17},{... | collective-permute-start | bytes 86024 | tf_op jit(solution)/shard_map/ppermute | solution.py:87
  157.7 1.7 collective-permute-start.23
  159.6 2.4 %collective-permute-done.23 = f32[112,128]{1,0:T(8,128)S(1)} collective-permute-done((f32[112,128]{1,0:T(8,128)S(1)}, f32[112,128]{1,0:T(8,128)S(1)}, u32[]{:S(2)}, u32[]{:S(2)}) %collective-permute-start.23) | collective-permute-done | bytes 57376 | tf_op jit(solution)/shard_map/ppermute | solution.py:87
  162.0 1.6 collective-permute-start.24
  164.4 1.0 collective-permute-start.34
  165.4 1.5 collective-permute-done.24
  166.9 2.3 %collective-permute-done.34 = f32[224,128]{1,0:T(8,128)S(1)} collective-permute-done((f32[224,128]{1,0:T(8,128)S(1)}, f32[224,128]{1,0:T(8,128)S(1)}, u32[]{:S(2)}, u32[]{:S(2)}) %collective-permute-start.34) | collective-permute-done | bytes 114720 | tf_op jit(solution)/shard_map/ppermute | solution.py:87
  169.2 1.6 collective-permute-start.35
  171.1 1.8 collective-permute-done.25
  173.0 2.3 %collective-permute-done.35 = f32[448,128]{1,0:T(8,128)S(1)} collective-permute-done((f32[448,128]{1,0:T(8,128)S(1)}, f32[448,128]{1,0:T(8,128)S(1)}, u32[]{:S(2)}, u32[]{:S(2)}) %collective-permute-start.35) | collective-permute-done | bytes 229408 | tf_op jit(solution)/shard_map/ppermute | solution.py:87
  175.4 1.3 pad_maximum_fusion.1.direction_ref
  176.7 7.5 %shard_map.221 = bf16[8,200,1600]{2,1,0:T(8,128)(2,1)} custom-call(bf16[8,200,512]{2,1,0:T(8,128)(2,1)} %pad_maximum_fusion.1.direction_ref, bf16[512,1600]{1,0:T(8,128)(2,1)} %maximum_bitcast_fusion.basis_ref, bf16[8,200,1600]{2,1,0:T(8,128)(2,1)} %bitcast.68), custom_call_target="tpu_custom_call" | custom-call | tf_op jit(solution)/shard_map/pallas_call | solution.py:201
  184.7 1.0 multiply_reduce_fusion
  186.4 2.9 %fusion.4 = f32[256,256]{1,0:T(8,128)S(1)} fusion(f32[1600,128]{1,0:T(8,128)S(1)} %slice.124, f32[1600,128]{1,0:T(8,128)S(1)} %slice.121, f32[]{:T(128)S(6)} %rsqrt.4), kind=kOutput, calls=%fused_computation.16 | convolution fusion | flops 1259110400 | bytes 1900548 | tf_op jit(solution)/shard_map/dot_general | solution.py:32
  194.2 2.0 %fusion.2 = f32[1600,256]{1,0:T(8,128)} fusion(f32[256,256]{1,0:T(8,128)S(1)} %fusion.120, f32[1600,128]{1,0:T(8,128)S(1)} %slice.124, f32[1600,128]{1,0:T(8,128)S(1)} %slice.121, f32[]{:T(128)S(6)} %rsqrt.4), kind=kOutput, calls=%fused_computation.14 | convolution fusion | flops 629964800 | bytes 3538948 | tf_op jit(solution)/shard_map/dot_general | solution.py:42
  (186 shorter events, 25.4 us)
Async XLA Ops:
  7.0 0.9 copy-start.3
  8.1 0.7 copy-start.2
  9.6 19.4 %collective-permute-start = (f32[928,128]{1,0:T(8,128)}, f32[928,128]{1,0:T(8,128)}, u32[]{:S(2)}, u32[]{:S(2)}) collective-permute-start(f32[928,128]{1,0:T(8,128)} %constant_dynamic-slice_fusion.12), channel_id=1, source_target_pairs={{0,4},{4,0},{8,12},{12,8},{16,20},{20,16},{24,28},{28,24},{1,5},{5... | collective-permute-start | bytes 1425416 | tf_op jit(solution)/shard_map/ppermute | solution.py:87
  16.8 1.0 copy-start.10
  17.8 3.9 %copy-start = (f32[1600,256]{1,0:T(8,128)S(1)}, f32[1600,256]{1,0:T(8,128)}, u32[]{:S(2)}) copy-start(f32[1600,256]{1,0:T(8,128)} %param.18) | copy-start | bytes 4915204
  20.1 13.2 %collective-permute-start.6 = (f32[928,128]{1,0:T(8,128)}, f32[928,128]{1,0:T(8,128)}, u32[]{:S(2)}, u32[]{:S(2)}) collective-permute-start(f32[928,128]{1,0:T(8,128)} %pad_dynamic-slice_fusion.6), channel_id=1, source_target_pairs={{0,8},{4,12},{8,0},{12,4},{16,24},{20,28},{24,16},{28,20},{1,9},{5... | collective-permute-start | bytes 1425416 | tf_op jit(solution)/shard_map/ppermute | solution.py:87
  30.2 7.6 %collective-permute-start.1 = (f32[464,128]{1,0:T(8,128)S(1)}, f32[464,128]{1,0:T(8,128)S(1)}, u32[]{:S(2)}, u32[]{:S(2)}) collective-permute-start(f32[464,128]{1,0:T(8,128)S(1)} %constant_dynamic-slice_fusion.11), channel_id=1, source_target_pairs={{0,8},{4,12},{8,0},{12,4},{16,24},{20,28},{24,16},{28,20},{1,9},{5... | collective-permute-start | bytes 712712 | tf_op jit(solution)/shard_map/ppermute | solution.py:87
  34.5 6.2 %collective-permute-start.7 = (f32[464,128]{1,0:T(8,128)S(1)}, f32[464,128]{1,0:T(8,128)S(1)}, u32[]{:S(2)}, u32[]{:S(2)}) collective-permute-start(f32[464,128]{1,0:T(8,128)S(1)} %constant_dynamic-slice_fusion.9), channel_id=1, source_target_pairs={{0,4},{4,0},{8,12},{12,8},{16,20},{20,16},{24,28},{28,24},{1,5},{5... | collective-permute-start | bytes 712712 | tf_op jit(solution)/shard_map/ppermute | solution.py:87
  37.8 11.0 %collective-permute-start.2 = (f32[232,128]{1,0:T(8,128)S(1)}, f32[232,128]{1,0:T(8,128)S(1)}, u32[]{:S(2)}, u32[]{:S(2)}) collective-permute-start(f32[232,128]{1,0:T(8,128)S(1)} %constant_dynamic-slice_fusion.10), channel_id=1, source_target_pairs={{0,16},{4,20},{8,24},{12,28},{16,0},{20,4},{24,8},{28,12},{1,17},{... | collective-permute-start | bytes 356360 | tf_op jit(solution)/shard_map/ppermute | solution.py:87
  40.7 10.7 %collective-permute-start.8 = (f32[232,128]{1,0:T(8,128)S(1)}, f32[232,128]{1,0:T(8,128)S(1)}, u32[]{:S(2)}, u32[]{:S(2)}) collective-permute-start(f32[232,128]{1,0:T(8,128)S(1)} %constant_dynamic-slice_fusion.8), channel_id=1, source_target_pairs={{0,16},{4,20},{8,24},{12,28},{16,0},{20,4},{24,8},{28,12},{1,17},{... | collective-permute-start | bytes 356360 | tf_op jit(solution)/shard_map/ppermute | solution.py:87
  48.9 9.5 %collective-permute-start.3 = (f32[232,128]{1,0:T(8,128)S(1)}, f32[232,128]{1,0:T(8,128)S(1)}, u32[]{:S(2)}, u32[]{:S(2)}) collective-permute-start(f32[232,128]{1,0:T(8,128)S(1)} %get-tuple-element.34), channel_id=1, source_target_pairs={{0,16},{4,20},{8,24},{12,28},{16,0},{20,4},{24,8},{28,12},{1,17},{... | collective-permute-start | bytes 356360 | tf_op jit(solution)/shard_map/ppermute | solution.py:87
  51.4 11.0 %collective-permute-start.9 = (f32[232,128]{1,0:T(8,128)S(1)}, f32[232,128]{1,0:T(8,128)S(1)}, u32[]{:S(2)}, u32[]{:S(2)}) collective-permute-start(f32[232,128]{1,0:T(8,128)S(1)} %get-tuple-element.38), channel_id=1, source_target_pairs={{0,16},{4,20},{8,24},{12,28},{16,0},{20,4},{24,8},{28,12},{1,17},{... | collective-permute-start | bytes 356360 | tf_op jit(solution)/shard_map/ppermute | solution.py:87
  58.4 7.2 %collective-permute-start.4 = (f32[464,128]{1,0:T(8,128)S(1)}, f32[464,128]{1,0:T(8,128)S(1)}, u32[]{:S(2)}, u32[]{:S(2)}) collective-permute-start(f32[464,128]{1,0:T(8,128)S(1)} %constant_dynamic-update-slice_fusion.36), channel_id=1, source_target_pairs={{0,8},{4,12},{8,0},{12,4},{16,24},{20,28},{24,16},{28,20},{1,9},{5... | collective-permute-start | bytes 712712 | tf_op jit(solution)/shard_map/ppermute | solution.py:87
  62.4 8.0 %collective-permute-start.10 = (f32[464,128]{1,0:T(8,128)S(1)}, f32[464,128]{1,0:T(8,128)S(1)}, u32[]{:S(2)}, u32[]{:S(2)}) collective-permute-start(f32[464,128]{1,0:T(8,128)S(1)} %constant_dynamic-update-slice_fusion.30), channel_id=1, source_target_pairs={{0,4},{4,0},{8,12},{12,8},{16,20},{20,16},{24,28},{28,24},{1,5},{5... | collective-permute-start | bytes 712712 | tf_op jit(solution)/shard_map/ppermute | solution.py:87
  62.5 18.4 %slice-start = ((s8[5324800]{0:T(1024)(128)(4,1)}), s8[4194304]{0:T(1024)(128)(4,1)S(1)}, s32[]{:S(2)}) async-start(s8[5324800]{0:T(1024)(128)(4,1)} %bitcast.76), calls=%async_computation | async-start | bytes 8388608
  65.7 13.1 %collective-permute-start.5 = (f32[928,128]{1,0:T(8,128)S(1)}, f32[928,128]{1,0:T(8,128)S(1)}, u32[]{:S(2)}, u32[]{:S(2)}) collective-permute-start(f32[928,128]{1,0:T(8,128)S(1)} %constant_dynamic-update-slice_fusion.34), channel_id=1, source_target_pairs={{0,4},{4,0},{8,12},{12,8},{16,20},{20,16},{24,28},{28,24},{1,5},{5... | collective-permute-start | bytes 1425416 | tf_op jit(solution)/shard_map/ppermute | solution.py:87
  70.4 8.7 %collective-permute-start.11 = (f32[928,128]{1,0:T(8,128)S(1)}, f32[928,128]{1,0:T(8,128)S(1)}, u32[]{:S(2)}, u32[]{:S(2)}) collective-permute-start(f32[928,128]{1,0:T(8,128)S(1)} %constant_dynamic-update-slice_fusion.28), channel_id=1, source_target_pairs={{0,8},{4,12},{8,0},{12,4},{16,24},{20,28},{24,16},{28,20},{1,9},{5... | collective-permute-start | bytes 1425416 | tf_op jit(solution)/shard_map/ppermute | solution.py:87
  71.7 9.2 %slice-start.1 = ((s8[5324800]{0:T(1024)(128)(4,1)}), s8[1130496]{0:T(1024)(128)(4,1)S(1)}, s32[]{:S(2)}) async-start(s8[5324800]{0:T(1024)(128)(4,1)} %bitcast.76), calls=%async_computation.1 | async-start | bytes 2260992
  79.2 1.1 copy-start.1
  84.2 36.9 %collective-permute-start.17 = (f32[896,128]{1,0:T(8,128)}, f32[896,128]{1,0:T(8,128)}, u32[]{:S(2)}, u32[]{:S(2)}) collective-permute-start(f32[896,128]{1,0:T(8,128)} %pad_dynamic-slice_fusion.4), channel_id=1, source_target_pairs={{0,1},{1,0},{2,3},{3,2},{4,5},{5,4},{6,7},{7,6},{8,9},{9,8},{10,11... | collective-permute-start | bytes 1376264 | tf_op jit(solution)/shard_map/ppermute | solution.py:87
  87.2 5.7 %collective-permute-start.12 = (f32[8,128]{1,0:T(8,128)S(1)}, f32[8,128]{1,0:T(8,128)S(1)}, u32[]{:S(2)}, u32[]{:S(2)}) collective-permute-start(f32[8,128]{1,0:T(8,128)S(1)} %broadcast_in_dim.15), channel_id=1, source_target_pairs={{0,1},{1,0},{2,3},{3,2},{4,5},{5,4},{6,7},{7,6},{8,9},{9,8},{10,11... | collective-permute-start | bytes 12296 | tf_op jit(solution)/shard_map/ppermute | solution.py:87
  92.7 5.7 %copy-start.5 = (f32[1,1,4,1600]{3,2,1,0:T(4,128)S(1)}, f32[1,1,4,1600]{3,2,1,0:T(4,128)}, u32[]{:S(2)}) copy-start(f32[1,1,4,1600]{3,2,1,0:T(4,128)} %param.26) | copy-start | bytes 76804
  92.8 5.7 %copy-start.6 = (f32[1,1,4,1600]{3,2,1,0:T(4,128)S(1)}, f32[1,1,4,1600]{3,2,1,0:T(4,128)}, u32[]{:S(2)}) copy-start(f32[1,1,4,1600]{3,2,1,0:T(4,128)} %param.25) | copy-start | bytes 76804
  92.9 3.7 %collective-permute-start.13 = (f32[8,128]{1,0:T(8,128)S(1)}, f32[8,128]{1,0:T(8,128)S(1)}, u32[]{:S(2)}, u32[]{:S(2)}) collective-permute-start(f32[8,128]{1,0:T(8,128)S(1)} %broadcast_add_fusion), channel_id=1, source_target_pairs={{0,2},{1,3},{2,0},{3,1},{4,6},{5,7},{6,4},{7,5},{8,10},{9,11},{10,... | collective-permute-start | bytes 12296 | tf_op jit(solution)/shard_map/ppermute | solution.py:87
  95.3 27.0 %collective-permute-start.27 = (f32[896,128]{1,0:T(8,128)}, f32[896,128]{1,0:T(8,128)}, u32[]{:S(2)}, u32[]{:S(2)}) collective-permute-start(f32[896,128]{1,0:T(8,128)} %pad_dynamic-slice_fusion.2), channel_id=1, source_target_pairs={{0,1},{1,0},{2,3},{3,2},{4,5},{5,4},{6,7},{7,6},{8,9},{9,8},{10,11... | collective-permute-start | bytes 1376264 | tf_op jit(solution)/shard_map/ppermute | solution.py:87
  100.0 12.3 %copy-start.7 = (f32[4,1600]{1,0:T(4,128)S(1)}, f32[4,1600]{1,0:T(4,128)}, u32[]{:S(2)}) copy-start(f32[4,1600]{1,0:T(4,128)} %param.21) | copy-start | bytes 76804
  100.0 12.3 %copy-start.8 = (f32[4,1600]{1,0:T(4,128)S(1)}, f32[4,1600]{1,0:T(4,128)}, u32[]{:S(2)}) copy-start(f32[4,1600]{1,0:T(4,128)} %param.23) | copy-start | bytes 76804
  100.0 12.3 %copy-start.9 = (f32[4,1600]{1,0:T(4,128)S(1)}, f32[4,1600]{1,0:T(4,128)}, u32[]{:S(2)}) copy-start(f32[4,1600]{1,0:T(4,128)} %param.22) | copy-start | bytes 76804
  102.0 9.5 %collective-permute-start.14 = (bf16[1,250,256]{2,1,0:T(8,128)(2,1)S(1)}, bf16[1,250,256]{2,1,0:T(8,128)(2,1)S(1)}, u32[]{:S(2)}, u32[]{:S(2)}) collective-permute-start(bf16[1,250,256]{2,1,0:T(8,128)(2,1)S(1)} %maximum_bitcast_fusion.1), channel_id=1, source_target_pairs={{0,16},{4,20},{8,24},{12,28},{16,0},{20,4},{24,8},{28,12},{1,17},{... | collective-permute-start | bytes 384008 | tf_op jit(solution)/shard_map/ppermute | solution.py:87
  111.5 7.8 %collective-permute-start.15 = (bf16[2,250,256]{2,1,0:T(8,128)(2,1)S(1)}, bf16[2,250,256]{2,1,0:T(8,128)(2,1)S(1)}, u32[]{:S(2)}, u32[]{:S(2)}) collective-permute-start(bf16[2,250,256]{2,1,0:T(8,128)(2,1)S(1)} %constant_dynamic-update-slice_fusion.24), channel_id=1, source_target_pairs={{0,8},{4,12},{8,0},{12,4},{16,24},{20,28},{24,16},{28,20},{1,9},{5... | collective-permute-start | bytes 768008 | tf_op jit(solution)/shard_map/ppermute | solution.py:87
  119.3 36.7 %collective-permute-start.16 = (bf16[4,250,256]{2,1,0:T(8,128)(2,1)S(1)}, bf16[4,250,256]{2,1,0:T(8,128)(2,1)S(1)}, u32[]{:S(2)}, u32[]{:S(2)}) collective-permute-start(bf16[4,250,256]{2,1,0:T(8,128)(2,1)S(1)} %constant_dynamic-update-slice_fusion.22), channel_id=1, source_target_pairs={{0,4},{4,0},{8,12},{12,8},{16,20},{20,16},{24,28},{28,24},{1,5},{5... | collective-permute-start | bytes 1536008 | tf_op jit(solution)/shard_map/ppermute | solution.py:87
  122.2 6.1 %collective-permute-start.18 = (f32[448,128]{1,0:T(8,128)S(1)}, f32[448,128]{1,0:T(8,128)S(1)}, u32[]{:S(2)}, u32[]{:S(2)}) collective-permute-start(f32[448,128]{1,0:T(8,128)S(1)} %constant_dynamic-slice_fusion.7), channel_id=1, source_target_pairs={{0,2},{1,3},{2,0},{3,1},{4,6},{5,7},{6,4},{7,5},{8,10},{9,11},{10,... | collective-permute-start | bytes 688136 | tf_op jit(solution)/shard_map/ppermute | solution.py:87
  123.4 14.6 %collective-permute-start.28 = (f32[448,128]{1,0:T(8,128)S(1)}, f32[448,128]{1,0:T(8,128)S(1)}, u32[]{:S(2)}, u32[]{:S(2)}) collective-permute-start(f32[448,128]{1,0:T(8,128)S(1)} %constant_dynamic-slice_fusion.3), channel_id=1, source_target_pairs={{0,4},{4,0},{8,12},{12,8},{16,20},{20,16},{24,28},{28,24},{1,5},{5... | collective-permute-start | bytes 688136 | tf_op jit(solution)/shard_map/ppermute | solution.py:87
  128.3 11.6 %collective-permute-start.19 = (f32[224,128]{1,0:T(8,128)S(1)}, f32[224,128]{1,0:T(8,128)S(1)}, u32[]{:S(2)}, u32[]{:S(2)}) collective-permute-start(f32[224,128]{1,0:T(8,128)S(1)} %constant_dynamic-slice_fusion.6), channel_id=1, source_target_pairs={{0,4},{4,0},{8,12},{12,8},{16,20},{20,16},{24,28},{28,24},{1,5},{5... | collective-permute-start | bytes 344072 | tf_op jit(solution)/shard_map/ppermute | solution.py:87
  138.0 4.9 %collective-permute-start.29 = (f32[224,128]{1,0:T(8,128)S(1)}, f32[224,128]{1,0:T(8,128)S(1)}, u32[]{:S(2)}, u32[]{:S(2)}) collective-permute-start(f32[224,128]{1,0:T(8,128)S(1)} %constant_dynamic-slice_fusion.2), channel_id=1, source_target_pairs={{0,8},{4,12},{8,0},{12,4},{16,24},{20,28},{24,16},{28,20},{1,9},{5... | collective-permute-start | bytes 344072 | tf_op jit(solution)/shard_map/ppermute | solution.py:87
  139.9 4.2 %collective-permute-start.20 = (f32[112,128]{1,0:T(8,128)S(1)}, f32[112,128]{1,0:T(8,128)S(1)}, u32[]{:S(2)}, u32[]{:S(2)}) collective-permute-start(f32[112,128]{1,0:T(8,128)S(1)} %constant_dynamic-slice_fusion.5), channel_id=1, source_target_pairs={{0,8},{4,12},{8,0},{12,4},{16,24},{20,28},{24,16},{28,20},{1,9},{5... | collective-permute-start | bytes 172040 | tf_op jit(solution)/shard_map/ppermute | solution.py:87
  142.9 4.9 %collective-permute-start.30 = (f32[112,128]{1,0:T(8,128)S(1)}, f32[112,128]{1,0:T(8,128)S(1)}, u32[]{:S(2)}, u32[]{:S(2)}) collective-permute-start(f32[112,128]{1,0:T(8,128)S(1)} %constant_dynamic-slice_fusion.1), channel_id=1, source_target_pairs={{0,2},{1,3},{2,0},{3,1},{4,6},{5,7},{6,4},{7,5},{8,10},{9,11},{10,... | collective-permute-start | bytes 172040 | tf_op jit(solution)/shard_map/ppermute | solution.py:87
  144.2 6.8 %collective-permute-start.21 = (f32[56,128]{1,0:T(8,128)S(1)}, f32[56,128]{1,0:T(8,128)S(1)}, u32[]{:S(2)}, u32[]{:S(2)}) collective-permute-start(f32[56,128]{1,0:T(8,128)S(1)} %constant_dynamic-slice_fusion.4), channel_id=1, source_target_pairs={{0,16},{4,20},{8,24},{12,28},{16,0},{20,4},{24,8},{28,12},{1,17},{... | collective-permute-start | bytes 86024 | tf_op jit(solution)/shard_map/ppermute | solution.py:87
  147.8 5.2 %collective-permute-start.31 = (f32[56,128]{1,0:T(8,128)S(1)}, f32[56,128]{1,0:T(8,128)S(1)}, u32[]{:S(2)}, u32[]{:S(2)}) collective-permute-start(f32[56,128]{1,0:T(8,128)S(1)} %constant_dynamic-slice_fusion), channel_id=1, source_target_pairs={{0,16},{4,20},{8,24},{12,28},{16,0},{20,4},{24,8},{28,12},{1,17},{... | collective-permute-start | bytes 86024 | tf_op jit(solution)/shard_map/ppermute | solution.py:87
  151.0 6.7 %collective-permute-start.22 = (f32[56,128]{1,0:T(8,128)S(1)}, f32[56,128]{1,0:T(8,128)S(1)}, u32[]{:S(2)}, u32[]{:S(2)}) collective-permute-start(f32[56,128]{1,0:T(8,128)S(1)} %get-tuple-element.15), channel_id=1, source_target_pairs={{0,16},{4,20},{8,24},{12,28},{16,0},{20,4},{24,8},{28,12},{1,17},{... | collective-permute-start | bytes 86024 | tf_op jit(solution)/shard_map/ppermute | solution.py:87
  152.9 6.5 %collective-permute-start.32 = (f32[56,128]{1,0:T(8,128)S(1)}, f32[56,128]{1,0:T(8,128)S(1)}, u32[]{:S(2)}, u32[]{:S(2)}) collective-permute-start(f32[56,128]{1,0:T(8,128)S(1)} %get-tuple-element.19), channel_id=1, source_target_pairs={{0,16},{4,20},{8,24},{12,28},{16,0},{20,4},{24,8},{28,12},{1,17},{... | collective-permute-start | bytes 86024 | tf_op jit(solution)/shard_map/ppermute | solution.py:87
  156.0 0.9 copy-start.4
  157.7 4.2 %collective-permute-start.23 = (f32[112,128]{1,0:T(8,128)S(1)}, f32[112,128]{1,0:T(8,128)S(1)}, u32[]{:S(2)}, u32[]{:S(2)}) collective-permute-start(f32[112,128]{1,0:T(8,128)S(1)} %constant_dynamic-update-slice_fusion.18), channel_id=1, source_target_pairs={{0,8},{4,12},{8,0},{12,4},{16,24},{20,28},{24,16},{28,20},{1,9},{5... | collective-permute-start | bytes 172040 | tf_op jit(solution)/shard_map/ppermute | solution.py:87
  159.5 4.9 %collective-permute-start.33 = (f32[112,128]{1,0:T(8,128)S(1)}, f32[112,128]{1,0:T(8,128)S(1)}, u32[]{:S(2)}, u32[]{:S(2)}) collective-permute-start(f32[112,128]{1,0:T(8,128)S(1)} %constant_dynamic-update-slice_fusion.8), channel_id=1, source_target_pairs={{0,2},{1,3},{2,0},{3,1},{4,6},{5,7},{6,4},{7,5},{8,10},{9,11},{10,... | collective-permute-start | bytes 172040 | tf_op jit(solution)/shard_map/ppermute | solution.py:87
  162.0 4.9 %collective-permute-start.24 = (f32[224,128]{1,0:T(8,128)S(1)}, f32[224,128]{1,0:T(8,128)S(1)}, u32[]{:S(2)}, u32[]{:S(2)}) collective-permute-start(f32[224,128]{1,0:T(8,128)S(1)} %constant_dynamic-update-slice_fusion.16), channel_id=1, source_target_pairs={{0,4},{4,0},{8,12},{12,8},{16,20},{20,16},{24,28},{28,24},{1,5},{5... | collective-permute-start | bytes 344072 | tf_op jit(solution)/shard_map/ppermute | solution.py:87
  164.4 4.9 %collective-permute-start.34 = (f32[224,128]{1,0:T(8,128)S(1)}, f32[224,128]{1,0:T(8,128)S(1)}, u32[]{:S(2)}, u32[]{:S(2)}) collective-permute-start(f32[224,128]{1,0:T(8,128)S(1)} %constant_dynamic-update-slice_fusion.6), channel_id=1, source_target_pairs={{0,8},{4,12},{8,0},{12,4},{16,24},{20,28},{24,16},{28,20},{1,9},{5... | collective-permute-start | bytes 344072 | tf_op jit(solution)/shard_map/ppermute | solution.py:87
  166.9 6.1 %collective-permute-start.25 = (f32[448,128]{1,0:T(8,128)S(1)}, f32[448,128]{1,0:T(8,128)S(1)}, u32[]{:S(2)}, u32[]{:S(2)}) collective-permute-start(f32[448,128]{1,0:T(8,128)S(1)} %constant_dynamic-update-slice_fusion.14), channel_id=1, source_target_pairs={{0,2},{1,3},{2,0},{3,1},{4,6},{5,7},{6,4},{7,5},{8,10},{9,11},{10,... | collective-permute-start | bytes 688136 | tf_op jit(solution)/shard_map/ppermute | solution.py:87
  169.2 6.1 %collective-permute-start.35 = (f32[448,128]{1,0:T(8,128)S(1)}, f32[448,128]{1,0:T(8,128)S(1)}, u32[]{:S(2)}, u32[]{:S(2)}) collective-permute-start(f32[448,128]{1,0:T(8,128)S(1)} %constant_dynamic-update-slice_fusion.4), channel_id=1, source_target_pairs={{0,4},{4,0},{8,12},{12,8},{16,20},{20,16},{24,28},{28,24},{1,5},{5... | collective-permute-start | bytes 688136 | tf_op jit(solution)/shard_map/ppermute | solution.py:87
  173.0 11.5 %collective-permute-start.26 = (f32[896,128]{1,0:T(8,128)S(1)}, f32[896,128]{1,0:T(8,128)S(1)}, u32[]{:S(2)}, u32[]{:S(2)}) collective-permute-start(f32[896,128]{1,0:T(8,128)S(1)} %constant_dynamic-update-slice_fusion.12), channel_id=1, source_target_pairs={{0,1},{1,0},{2,3},{3,2},{4,5},{5,4},{6,7},{7,6},{8,9},{9,8},{10,11... | collective-permute-start | bytes 1376264 | tf_op jit(solution)/shard_map/ppermute | solution.py:87
  175.3 9.2 %collective-permute-start.36 = (f32[896,128]{1,0:T(8,128)S(1)}, f32[896,128]{1,0:T(8,128)S(1)}, u32[]{:S(2)}, u32[]{:S(2)}) collective-permute-start(f32[896,128]{1,0:T(8,128)S(1)} %constant_dynamic-update-slice_fusion.2), channel_id=1, source_target_pairs={{0,1},{1,0},{2,3},{3,2},{4,5},{5,4},{6,7},{7,6},{8,9},{9,8},{10,11... | collective-permute-start | bytes 1376264 | tf_op jit(solution)/shard_map/ppermute | solution.py:87

commit v10 on v9

--- a/solution.py
+++ b/solution.py
@@ -34,11 +34,9 @@
     product = None
     for sweep_index in range(NS_STEPS):
         step = 1.5 * identity - 0.5 * gram_matrix
-        product = step if product is None else jnp.dot(product, step, precision=highest)
+        product = step if product is None else jnp.dot(product, step, precision=high)
         if sweep_index + 1 < NS_STEPS:
-            gram_matrix = jnp.dot(
-                step, jnp.dot(gram_matrix, step, precision=highest), precision=highest
-            )
+            gram_matrix = jnp.dot(step, jnp.dot(gram_matrix, step, precision=high), precision=high)
     return jnp.dot(iterate, product, precision=high)
 
 

time: 197 us -> 196 us (level)
  no operation moved by 1% of the time
where the time goes in v10:
time: 196 us; the launch traced here: 195 us
  waiting for transfers between devices  75.8 us (39%)
  starting transfers between devices  44 us (22%)
  other arithmetic  24.8 us (13%)
  matrix products  24 us (12%)
  local copies, waits for them, and re-layouts  12.8 us (7%)
  Pallas kernels  7.5 us (4%)
  between operations  5.82 us (3%)
    ppermute x37, waiting for transfers between devices, swap_with(): lax.ppermute(values, name, [(index, index ^ bit) for index in range(size)])  75.8 us
    ppermute x37, starting transfers between devices, swap_with(): lax.ppermute(values, name, [(index, index ^ bit) for index in range(size)])  44 us
    dot_general x4, matrix products, exact_dot(): lax.dot_general(lhs_bf16, split2(rhs_f32), ((contract, (0,)), ((), ())),...  15.7 us
    pallas_call x1, Pallas kernels, updated_weights(): pl.pallas_call(update_kernel, out_shape=jax.ShapeDtypeStruct(weights.shap...  7.5 us
    convert_element_type x4, other arithmetic, split2(): second = (values - first.astype(jnp.float32)).astype(jnp.bfloat16)  5.03 us
    add x12, other arithmetic, run_steps(): parts = keep + swap_with(send, name, bit, size)  4.49 us
  transfers between devices with their start and end apart: 37, of which 25 were waited for; matrix products, arithmetic and copies ran while one was open for 19% of the time, Pallas kernels for 4%

profile of v10, /device:TPU:0, one launch (start us, length us, event | category | flops | bytes accessed | tf_op | source)
XLA Modules:
  0.0 194.8 jit_solution(18138151070681811113)
XLA Ops:
  0.7 2.2 %subtract_convert_fusion.4 = (bf16[1600,128]{1,0:T(8,128)(2,1)S(1)}, bf16[1600,128]{1,0:T(8,128)(2,1)S(1)}, bf16[1600,128]{1,0:T(8,128)(2,1)S(1)}, bf16[1600,128]{1,0:T(8,128)(2,1)S(1)}) fusion(f32[1600,256]{1,0:T(8,128)} %param.18), kind=kLoop, calls=%fused_computation.52 | loop fusion | flops 1228800 | bytes 4096000 | tf_op jit(solution)/shard_map/convert_element_type | solution.py:214
  2.8 4.2 %convolution_bitcast_fusion.1 = f32[1600,256]{1,0:T(8,128)S(1)} fusion(bf16[1600,1600]{1,0:T(8,128)(2,1)} %bitcast.73, bf16[1600,128]{1,0:T(8,128)(2,1)S(1)} %get-tuple-element.35, bf16[1600,128]{1,0:T(8,128)(2,1)S(1)} %get-tuple-element.36), kind=kOutput, calls=%fused_computation.1 | convolution fusion | flops 1312358400 | bytes 7577600 | tf_op jit(solution)/shard_map/dot_general | solution.py:220
  9.6 2.9 %collective-permute-start = (f32[928,128]{1,0:T(8,128)}, f32[928,128]{1,0:T(8,128)}, u32[]{:S(2)}, u32[]{:S(2)}) collective-permute-start(f32[928,128]{1,0:T(8,128)} %constant_dynamic-slice_fusion.12), channel_id=1, source_target_pairs={{0,4},{4,0},{8,12},{12,8},{16,20},{20,16},{24,28},{28,24},{1,5},{5... | collective-permute-start | bytes 1425416 | tf_op jit(solution)/shard_map/ppermute | solution.py:85
  12.6 4.2 %convolution_bitcast_fusion = f32[1600,256]{1,0:T(8,128)S(1)} fusion(bf16[1600,1600]{1,0:T(8,128)(2,1)} %bitcast.74, bf16[1600,128]{1,0:T(8,128)(2,1)S(1)} %get-tuple-element.41, bf16[1600,128]{1,0:T(8,128)(2,1)S(1)} %get-tuple-element.42), kind=kOutput, calls=%fused_computation | convolution fusion | flops 1312358400 | bytes 7577600 | tf_op jit(solution)/shard_map/dot_general | solution.py:220
  16.8 1.0 slice_add_fusion.2
  17.9 1.4 fusion.7
  20.1 1.6 collective-permute-start.6
  21.7 1.0 convert_element_type.154
  22.7 1.6 copy.34
  24.3 1.7 copy.35
  26.0 1.6 subtract_convert_fusion
  27.7 1.4 maximum_bitcast_fusion.basis_ref
  29.0 1.1 dynamic-slice_add_fusion
  30.7 2.7 %collective-permute-done.6 = f32[928,128]{1,0:T(8,128)} collective-permute-done((f32[928,128]{1,0:T(8,128)}, f32[928,128]{1,0:T(8,128)}, u32[]{:S(2)}, u32[]{:S(2)}) %collective-permute-start.6) | collective-permute-done | bytes 475168 | tf_op jit(solution)/shard_map/ppermute | solution.py:85
  33.3 1.1 fusion.22
  35.1 2.7 %collective-permute-done.1 = f32[464,128]{1,0:T(8,128)S(1)} collective-permute-done((f32[464,128]{1,0:T(8,128)S(1)}, f32[464,128]{1,0:T(8,128)S(1)}, u32[]{:S(2)}, u32[]{:S(2)}) %collective-permute-start.1) | collective-permute-done | bytes 237600 | tf_op jit(solution)/shard_map/ppermute | solution.py:85
  37.8 2.7 %collective-permute-start.2 = (f32[232,128]{1,0:T(8,128)S(1)}, f32[232,128]{1,0:T(8,128)S(1)}, u32[]{:S(2)}, u32[]{:S(2)}) collective-permute-start(f32[232,128]{1,0:T(8,128)S(1)} %constant_dynamic-slice_fusion.10), channel_id=1, source_target_pairs={{0,16},{4,20},{8,24},{12,28},{16,0},{20,4},{24,8},{28,12},{1,17},{... | collective-permute-start | bytes 356360 | tf_op jit(solution)/shard_map/ppermute | solution.py:85
  40.7 2.7 %collective-permute-start.8 = (f32[232,128]{1,0:T(8,128)S(1)}, f32[232,128]{1,0:T(8,128)S(1)}, u32[]{:S(2)}, u32[]{:S(2)}) collective-permute-start(f32[232,128]{1,0:T(8,128)S(1)} %constant_dynamic-slice_fusion.8), channel_id=1, source_target_pairs={{0,16},{4,20},{8,24},{12,28},{16,0},{20,4},{24,8},{28,12},{1,17},{... | collective-permute-start | bytes 356360 | tf_op jit(solution)/shard_map/ppermute | solution.py:85
  43.4 5.5 %collective-permute-done.2 = f32[232,128]{1,0:T(8,128)S(1)} collective-permute-done((f32[232,128]{1,0:T(8,128)S(1)}, f32[232,128]{1,0:T(8,128)S(1)}, u32[]{:S(2)}, u32[]{:S(2)}) %collective-permute-start.2) | collective-permute-done | bytes 118816 | tf_op jit(solution)/shard_map/ppermute | solution.py:85
  49.0 2.4 %collective-permute-done.8 = f32[232,128]{1,0:T(8,128)S(1)} collective-permute-done((f32[232,128]{1,0:T(8,128)S(1)}, f32[232,128]{1,0:T(8,128)S(1)}, u32[]{:S(2)}, u32[]{:S(2)}) %collective-permute-start.8) | collective-permute-done | bytes 118816 | tf_op jit(solution)/shard_map/ppermute | solution.py:85
  52.0 6.4 %collective-permute-done.3 = f32[232,128]{1,0:T(8,128)S(1)} collective-permute-done((f32[232,128]{1,0:T(8,128)S(1)}, f32[232,128]{1,0:T(8,128)S(1)}, u32[]{:S(2)}, u32[]{:S(2)}) %collective-permute-start.3) | collective-permute-done | bytes 118816 | tf_op jit(solution)/shard_map/ppermute | solution.py:85
  58.4 1.5 collective-permute-start.4
  60.8 1.6 collective-permute-done.9
  62.6 3.1 %collective-permute-done.4 = f32[464,128]{1,0:T(8,128)S(1)} collective-permute-done((f32[464,128]{1,0:T(8,128)S(1)}, f32[464,128]{1,0:T(8,128)S(1)}, u32[]{:S(2)}, u32[]{:S(2)}) %collective-permute-start.4) | collective-permute-done | bytes 237600 | tf_op jit(solution)/shard_map/ppermute | solution.py:85
  66.2 4.2 %collective-permute-done.10 = f32[464,128]{1,0:T(8,128)S(1)} collective-permute-done((f32[464,128]{1,0:T(8,128)S(1)}, f32[464,128]{1,0:T(8,128)S(1)}, u32[]{:S(2)}, u32[]{:S(2)}) %collective-permute-start.10) | collective-permute-done | bytes 237600 | tf_op jit(solution)/shard_map/ppermute | solution.py:85
  70.4 1.0 collective-permute-start.11
  71.7 7.1 %collective-permute-done.5 = f32[928,128]{1,0:T(8,128)S(1)} collective-permute-done((f32[928,128]{1,0:T(8,128)S(1)}, f32[928,128]{1,0:T(8,128)S(1)}, u32[]{:S(2)}, u32[]{:S(2)}) %collective-permute-start.5) | collective-permute-done | bytes 475168 | tf_op jit(solution)/shard_map/ppermute | solution.py:85
  79.2 1.1 subtract_convert_fusion.1
  80.9 2.4 %convolution_bitcast_fusion.3 = f32[1600,256]{1,0:T(8,128)S(1)} fusion(bf16[1600,1600]{1,0:T(8,128)(2,1)S(1)} %bitcast.78, bf16[1600,128]{1,0:T(8,128)(2,1)S(1)} %get-tuple-element.16, bf16[1600,128]{1,0:T(8,128)(2,1)S(1)} %get-tuple-element.17), kind=kOutput, calls=%fused_computation.3 | convolution fusion | flops 1312358400 | bytes 7577600 | tf_op jit(solution)/shard_map/dot_general | solution.py:220
  84.9 1.0 fusion.1
  87.8 5.0 %convolution_bitcast_fusion.2 = f32[1600,256]{1,0:T(8,128)S(1)} fusion(bf16[1600,1600]{1,0:T(8,128)(2,1)} %bitcast.75, bf16[1600,128]{1,0:T(8,128)(2,1)S(1)} %get-tuple-element.20, bf16[1600,128]{1,0:T(8,128)(2,1)} %get-tuple-element.21), kind=kOutput, calls=%fused_computation.2 | convolution fusion | flops 1312358400 | bytes 7577600 | tf_op jit(solution)/shard_map/dot_general | solution.py:220
  92.9 1.6 collective-permute-start.13
  98.4 1.4 multiply_divide_fusion.2
  100.0 1.9 convert_bitcast_fusion
  102.0 2.9 %collective-permute-start.14 = (bf16[1,250,256]{2,1,0:T(8,128)(2,1)S(1)}, bf16[1,250,256]{2,1,0:T(8,128)(2,1)S(1)}, u32[]{:S(2)}, u32[]{:S(2)}) collective-permute-start(bf16[1,250,256]{2,1,0:T(8,128)(2,1)S(1)} %maximum_bitcast_fusion.1), channel_id=1, source_target_pairs={{0,16},{4,20},{8,24},{12,28},{16,0},{20,4},{24,8},{28,12},{1,17},{... | collective-permute-start | bytes 384008 | tf_op jit(solution)/shard_map/ppermute | solution.py:85
  105.8 5.7 %collective-permute-done.14 = bf16[1,250,256]{2,1,0:T(8,128)(2,1)S(1)} collective-permute-done((bf16[1,250,256]{2,1,0:T(8,128)(2,1)S(1)}, bf16[1,250,256]{2,1,0:T(8,128)(2,1)S(1)}, u32[]{:S(2)}, u32[]{:S(2)}) %collective-permute-start.14) | collective-permute-done | bytes 128032 | tf_op jit(solution)/shard_map/ppermute | solution.py:85
  113.0 6.3 %collective-permute-done.15 = bf16[2,250,256]{2,1,0:T(8,128)(2,1)S(1)} collective-permute-done((bf16[2,250,256]{2,1,0:T(8,128)(2,1)S(1)}, bf16[2,250,256]{2,1,0:T(8,128)(2,1)S(1)}, u32[]{:S(2)}, u32[]{:S(2)}) %collective-permute-start.15) | collective-permute-done | bytes 256032 | tf_op jit(solution)/shard_map/ppermute | solution.py:85
  119.3 1.6 collective-permute-start.16
  121.1 1.1 fusion.23
  122.3 1.1 fusion.24
  123.9 4.4 %collective-permute-done.18 = f32[448,128]{1,0:T(8,128)S(1)} collective-permute-done((f32[448,128]{1,0:T(8,128)S(1)}, f32[448,128]{1,0:T(8,128)S(1)}, u32[]{:S(2)}, u32[]{:S(2)}) %collective-permute-start.18) | collective-permute-done | bytes 229408 | tf_op jit(solution)/shard_map/ppermute | solution.py:85
  128.8 9.1 %collective-permute-done.28 = f32[448,128]{1,0:T(8,128)S(1)} collective-permute-done((f32[448,128]{1,0:T(8,128)S(1)}, f32[448,128]{1,0:T(8,128)S(1)}, u32[]{:S(2)}, u32[]{:S(2)}) %collective-permute-start.28) | collective-permute-done | bytes 229408 | tf_op jit(solution)/shard_map/ppermute | solution.py:85
  138.0 1.9 collective-permute-start.29
  139.9 1.2 collective-permute-start.20
  141.1 1.7 collective-permute-done.29
  143.0 1.2 collective-permute-done.20
  144.2 3.5 %collective-permute-start.21 = (f32[56,128]{1,0:T(8,128)S(1)}, f32[56,128]{1,0:T(8,128)S(1)}, u32[]{:S(2)}, u32[]{:S(2)}) collective-permute-start(f32[56,128]{1,0:T(8,128)S(1)} %constant_dynamic-slice_fusion.4), channel_id=1, source_target_pairs={{0,16},{4,20},{8,24},{12,28},{16,0},{20,4},{24,8},{28,12},{1,17},{... | collective-permute-start | bytes 86024 | tf_op jit(solution)/shard_map/ppermute | solution.py:85
  147.8 3.2 %collective-permute-start.31 = (f32[56,128]{1,0:T(8,128)S(1)}, f32[56,128]{1,0:T(8,128)S(1)}, u32[]{:S(2)}, u32[]{:S(2)}) collective-permute-start(f32[56,128]{1,0:T(8,128)S(1)} %constant_dynamic-slice_fusion), channel_id=1, source_target_pairs={{0,16},{4,20},{8,24},{12,28},{16,0},{20,4},{24,8},{28,12},{1,17},{... | collective-permute-start | bytes 86024 | tf_op jit(solution)/shard_map/ppermute | solution.py:85
  151.0 1.7 collective-permute-start.22
  152.9 3.0 %collective-permute-start.32 = (f32[56,128]{1,0:T(8,128)S(1)}, f32[56,128]{1,0:T(8,128)S(1)}, u32[]{:S(2)}, u32[]{:S(2)}) collective-permute-start(f32[56,128]{1,0:T(8,128)S(1)} %get-tuple-element.19), channel_id=1, source_target_pairs={{0,16},{4,20},{8,24},{12,28},{16,0},{20,4},{24,8},{28,12},{1,17},{... | collective-permute-start | bytes 86024 | tf_op jit(solution)/shard_map/ppermute | solution.py:85
  157.7 1.7 collective-permute-start.23
  159.6 2.4 %collective-permute-done.23 = f32[112,128]{1,0:T(8,128)S(1)} collective-permute-done((f32[112,128]{1,0:T(8,128)S(1)}, f32[112,128]{1,0:T(8,128)S(1)}, u32[]{:S(2)}, u32[]{:S(2)}) %collective-permute-start.23) | collective-permute-done | bytes 57376 | tf_op jit(solution)/shard_map/ppermute | solution.py:85
  162.0 1.6 collective-permute-start.24
  164.4 1.0 collective-permute-start.34
  165.4 1.5 collective-permute-done.24
  166.9 2.3 %collective-permute-done.34 = f32[224,128]{1,0:T(8,128)S(1)} collective-permute-done((f32[224,128]{1,0:T(8,128)S(1)}, f32[224,128]{1,0:T(8,128)S(1)}, u32[]{:S(2)}, u32[]{:S(2)}) %collective-permute-start.34) | collective-permute-done | bytes 114720 | tf_op jit(solution)/shard_map/ppermute | solution.py:85
  169.2 1.6 collective-permute-start.35
  171.1 1.8 collective-permute-done.25
  173.0 2.3 %collective-permute-done.35 = f32[448,128]{1,0:T(8,128)S(1)} collective-permute-done((f32[448,128]{1,0:T(8,128)S(1)}, f32[448,128]{1,0:T(8,128)S(1)}, u32[]{:S(2)}, u32[]{:S(2)}) %collective-permute-start.35) | collective-permute-done | bytes 229408 | tf_op jit(solution)/shard_map/ppermute | solution.py:85
  175.4 1.3 pad_maximum_fusion.1.direction_ref
  176.7 7.5 %shard_map.221 = bf16[8,200,1600]{2,1,0:T(8,128)(2,1)} custom-call(bf16[8,200,512]{2,1,0:T(8,128)(2,1)} %pad_maximum_fusion.1.direction_ref, bf16[512,1600]{1,0:T(8,128)(2,1)} %maximum_bitcast_fusion.basis_ref, bf16[8,200,1600]{2,1,0:T(8,128)(2,1)} %bitcast.68), custom_call_target="tpu_custom_call" | custom-call | tf_op jit(solution)/shard_map/pallas_call | solution.py:199
  184.7 1.0 multiply_reduce_fusion
  186.4 2.9 %fusion.4 = f32[256,256]{1,0:T(8,128)S(1)} fusion(f32[1600,128]{1,0:T(8,128)S(1)} %slice.124, f32[1600,128]{1,0:T(8,128)S(1)} %slice.121, f32[]{:T(128)S(6)} %rsqrt.4), kind=kOutput, calls=%fused_computation.16 | convolution fusion | flops 1259110400 | bytes 1900548 | tf_op jit(solution)/shard_map/dot_general | solution.py:32
  192.8 2.0 %fusion.2 = f32[1600,256]{1,0:T(8,128)} fusion(f32[256,256]{1,0:T(8,128)S(1)} %fusion.120, f32[1600,128]{1,0:T(8,128)S(1)} %slice.124, f32[1600,128]{1,0:T(8,128)S(1)} %slice.121, f32[]{:T(128)S(6)} %rsqrt.4), kind=kOutput, calls=%fused_computation.14 | convolution fusion | flops 629964800 | bytes 3538948 | tf_op jit(solution)/shard_map/dot_general | solution.py:40
  (186 shorter events, 24.0 us)
Async XLA Ops:
  7.0 0.9 copy-start.3
  8.1 0.7 copy-start.2
  9.6 19.4 %collective-permute-start = (f32[928,128]{1,0:T(8,128)}, f32[928,128]{1,0:T(8,128)}, u32[]{:S(2)}, u32[]{:S(2)}) collective-permute-start(f32[928,128]{1,0:T(8,128)} %constant_dynamic-slice_fusion.12), channel_id=1, source_target_pairs={{0,4},{4,0},{8,12},{12,8},{16,20},{20,16},{24,28},{28,24},{1,5},{5... | collective-permute-start | bytes 1425416 | tf_op jit(solution)/shard_map/ppermute | solution.py:85
  16.8 1.0 copy-start.10
  17.8 3.9 %copy-start = (f32[1600,256]{1,0:T(8,128)S(1)}, f32[1600,256]{1,0:T(8,128)}, u32[]{:S(2)}) copy-start(f32[1600,256]{1,0:T(8,128)} %param.18) | copy-start | bytes 4915204
  20.1 13.2 %collective-permute-start.6 = (f32[928,128]{1,0:T(8,128)}, f32[928,128]{1,0:T(8,128)}, u32[]{:S(2)}, u32[]{:S(2)}) collective-permute-start(f32[928,128]{1,0:T(8,128)} %pad_dynamic-slice_fusion.6), channel_id=1, source_target_pairs={{0,8},{4,12},{8,0},{12,4},{16,24},{20,28},{24,16},{28,20},{1,9},{5... | collective-permute-start | bytes 1425416 | tf_op jit(solution)/shard_map/ppermute | solution.py:85
  30.2 7.6 %collective-permute-start.1 = (f32[464,128]{1,0:T(8,128)S(1)}, f32[464,128]{1,0:T(8,128)S(1)}, u32[]{:S(2)}, u32[]{:S(2)}) collective-permute-start(f32[464,128]{1,0:T(8,128)S(1)} %constant_dynamic-slice_fusion.11), channel_id=1, source_target_pairs={{0,8},{4,12},{8,0},{12,4},{16,24},{20,28},{24,16},{28,20},{1,9},{5... | collective-permute-start | bytes 712712 | tf_op jit(solution)/shard_map/ppermute | solution.py:85
  34.5 6.2 %collective-permute-start.7 = (f32[464,128]{1,0:T(8,128)S(1)}, f32[464,128]{1,0:T(8,128)S(1)}, u32[]{:S(2)}, u32[]{:S(2)}) collective-permute-start(f32[464,128]{1,0:T(8,128)S(1)} %constant_dynamic-slice_fusion.9), channel_id=1, source_target_pairs={{0,4},{4,0},{8,12},{12,8},{16,20},{20,16},{24,28},{28,24},{1,5},{5... | collective-permute-start | bytes 712712 | tf_op jit(solution)/shard_map/ppermute | solution.py:85
  37.8 11.0 %collective-permute-start.2 = (f32[232,128]{1,0:T(8,128)S(1)}, f32[232,128]{1,0:T(8,128)S(1)}, u32[]{:S(2)}, u32[]{:S(2)}) collective-permute-start(f32[232,128]{1,0:T(8,128)S(1)} %constant_dynamic-slice_fusion.10), channel_id=1, source_target_pairs={{0,16},{4,20},{8,24},{12,28},{16,0},{20,4},{24,8},{28,12},{1,17},{... | collective-permute-start | bytes 356360 | tf_op jit(solution)/shard_map/ppermute | solution.py:85
  40.7 10.7 %collective-permute-start.8 = (f32[232,128]{1,0:T(8,128)S(1)}, f32[232,128]{1,0:T(8,128)S(1)}, u32[]{:S(2)}, u32[]{:S(2)}) collective-permute-start(f32[232,128]{1,0:T(8,128)S(1)} %constant_dynamic-slice_fusion.8), channel_id=1, source_target_pairs={{0,16},{4,20},{8,24},{12,28},{16,0},{20,4},{24,8},{28,12},{1,17},{... | collective-permute-start | bytes 356360 | tf_op jit(solution)/shard_map/ppermute | solution.py:85
  48.9 9.5 %collective-permute-start.3 = (f32[232,128]{1,0:T(8,128)S(1)}, f32[232,128]{1,0:T(8,128)S(1)}, u32[]{:S(2)}, u32[]{:S(2)}) collective-permute-start(f32[232,128]{1,0:T(8,128)S(1)} %get-tuple-element.34), channel_id=1, source_target_pairs={{0,16},{4,20},{8,24},{12,28},{16,0},{20,4},{24,8},{28,12},{1,17},{... | collective-permute-start | bytes 356360 | tf_op jit(solution)/shard_map/ppermute | solution.py:85
  51.4 11.0 %collective-permute-start.9 = (f32[232,128]{1,0:T(8,128)S(1)}, f32[232,128]{1,0:T(8,128)S(1)}, u32[]{:S(2)}, u32[]{:S(2)}) collective-permute-start(f32[232,128]{1,0:T(8,128)S(1)} %get-tuple-element.38), channel_id=1, source_target_pairs={{0,16},{4,20},{8,24},{12,28},{16,0},{20,4},{24,8},{28,12},{1,17},{... | collective-permute-start | bytes 356360 | tf_op jit(solution)/shard_map/ppermute | solution.py:85
  58.4 7.2 %collective-permute-start.4 = (f32[464,128]{1,0:T(8,128)S(1)}, f32[464,128]{1,0:T(8,128)S(1)}, u32[]{:S(2)}, u32[]{:S(2)}) collective-permute-start(f32[464,128]{1,0:T(8,128)S(1)} %constant_dynamic-update-slice_fusion.36), channel_id=1, source_target_pairs={{0,8},{4,12},{8,0},{12,4},{16,24},{20,28},{24,16},{28,20},{1,9},{5... | collective-permute-start | bytes 712712 | tf_op jit(solution)/shard_map/ppermute | solution.py:85
  62.4 8.0 %collective-permute-start.10 = (f32[464,128]{1,0:T(8,128)S(1)}, f32[464,128]{1,0:T(8,128)S(1)}, u32[]{:S(2)}, u32[]{:S(2)}) collective-permute-start(f32[464,128]{1,0:T(8,128)S(1)} %constant_dynamic-update-slice_fusion.30), channel_id=1, source_target_pairs={{0,4},{4,0},{8,12},{12,8},{16,20},{20,16},{24,28},{28,24},{1,5},{5... | collective-permute-start | bytes 712712 | tf_op jit(solution)/shard_map/ppermute | solution.py:85
  62.5 18.4 %slice-start = ((s8[5324800]{0:T(1024)(128)(4,1)}), s8[4194304]{0:T(1024)(128)(4,1)S(1)}, s32[]{:S(2)}) async-start(s8[5324800]{0:T(1024)(128)(4,1)} %bitcast.76), calls=%async_computation | async-start | bytes 8388608
  65.7 13.1 %collective-permute-start.5 = (f32[928,128]{1,0:T(8,128)S(1)}, f32[928,128]{1,0:T(8,128)S(1)}, u32[]{:S(2)}, u32[]{:S(2)}) collective-permute-start(f32[928,128]{1,0:T(8,128)S(1)} %constant_dynamic-update-slice_fusion.34), channel_id=1, source_target_pairs={{0,4},{4,0},{8,12},{12,8},{16,20},{20,16},{24,28},{28,24},{1,5},{5... | collective-permute-start | bytes 1425416 | tf_op jit(solution)/shard_map/ppermute | solution.py:85
  70.4 8.7 %collective-permute-start.11 = (f32[928,128]{1,0:T(8,128)S(1)}, f32[928,128]{1,0:T(8,128)S(1)}, u32[]{:S(2)}, u32[]{:S(2)}) collective-permute-start(f32[928,128]{1,0:T(8,128)S(1)} %constant_dynamic-update-slice_fusion.28), channel_id=1, source_target_pairs={{0,8},{4,12},{8,0},{12,4},{16,24},{20,28},{24,16},{28,20},{1,9},{5... | collective-permute-start | bytes 1425416 | tf_op jit(solution)/shard_map/ppermute | solution.py:85
  71.7 9.2 %slice-start.1 = ((s8[5324800]{0:T(1024)(128)(4,1)}), s8[1130496]{0:T(1024)(128)(4,1)S(1)}, s32[]{:S(2)}) async-start(s8[5324800]{0:T(1024)(128)(4,1)} %bitcast.76), calls=%async_computation.1 | async-start | bytes 2260992
  79.2 1.1 copy-start.1
  84.2 36.9 %collective-permute-start.17 = (f32[896,128]{1,0:T(8,128)}, f32[896,128]{1,0:T(8,128)}, u32[]{:S(2)}, u32[]{:S(2)}) collective-permute-start(f32[896,128]{1,0:T(8,128)} %pad_dynamic-slice_fusion.4), channel_id=1, source_target_pairs={{0,1},{1,0},{2,3},{3,2},{4,5},{5,4},{6,7},{7,6},{8,9},{9,8},{10,11... | collective-permute-start | bytes 1376264 | tf_op jit(solution)/shard_map/ppermute | solution.py:85
  87.2 5.7 %collective-permute-start.12 = (f32[8,128]{1,0:T(8,128)S(1)}, f32[8,128]{1,0:T(8,128)S(1)}, u32[]{:S(2)}, u32[]{:S(2)}) collective-permute-start(f32[8,128]{1,0:T(8,128)S(1)} %broadcast_in_dim.15), channel_id=1, source_target_pairs={{0,1},{1,0},{2,3},{3,2},{4,5},{5,4},{6,7},{7,6},{8,9},{9,8},{10,11... | collective-permute-start | bytes 12296 | tf_op jit(solution)/shard_map/ppermute | solution.py:85
  92.7 5.7 %copy-start.5 = (f32[1,1,4,1600]{3,2,1,0:T(4,128)S(1)}, f32[1,1,4,1600]{3,2,1,0:T(4,128)}, u32[]{:S(2)}) copy-start(f32[1,1,4,1600]{3,2,1,0:T(4,128)} %param.26) | copy-start | bytes 76804
  92.8 5.7 %copy-start.6 = (f32[1,1,4,1600]{3,2,1,0:T(4,128)S(1)}, f32[1,1,4,1600]{3,2,1,0:T(4,128)}, u32[]{:S(2)}) copy-start(f32[1,1,4,1600]{3,2,1,0:T(4,128)} %param.25) | copy-start | bytes 76804
  92.9 3.7 %collective-permute-start.13 = (f32[8,128]{1,0:T(8,128)S(1)}, f32[8,128]{1,0:T(8,128)S(1)}, u32[]{:S(2)}, u32[]{:S(2)}) collective-permute-start(f32[8,128]{1,0:T(8,128)S(1)} %broadcast_add_fusion), channel_id=1, source_target_pairs={{0,2},{1,3},{2,0},{3,1},{4,6},{5,7},{6,4},{7,5},{8,10},{9,11},{10,... | collective-permute-start | bytes 12296 | tf_op jit(solution)/shard_map/ppermute | solution.py:85
  95.3 27.0 %collective-permute-start.27 = (f32[896,128]{1,0:T(8,128)}, f32[896,128]{1,0:T(8,128)}, u32[]{:S(2)}, u32[]{:S(2)}) collective-permute-start(f32[896,128]{1,0:T(8,128)} %pad_dynamic-slice_fusion.2), channel_id=1, source_target_pairs={{0,1},{1,0},{2,3},{3,2},{4,5},{5,4},{6,7},{7,6},{8,9},{9,8},{10,11... | collective-permute-start | bytes 1376264 | tf_op jit(solution)/shard_map/ppermute | solution.py:85
  100.0 12.3 %copy-start.7 = (f32[4,1600]{1,0:T(4,128)S(1)}, f32[4,1600]{1,0:T(4,128)}, u32[]{:S(2)}) copy-start(f32[4,1600]{1,0:T(4,128)} %param.21) | copy-start | bytes 76804
  100.0 12.3 %copy-start.8 = (f32[4,1600]{1,0:T(4,128)S(1)}, f32[4,1600]{1,0:T(4,128)}, u32[]{:S(2)}) copy-start(f32[4,1600]{1,0:T(4,128)} %param.23) | copy-start | bytes 76804
  100.0 12.3 %copy-start.9 = (f32[4,1600]{1,0:T(4,128)S(1)}, f32[4,1600]{1,0:T(4,128)}, u32[]{:S(2)}) copy-start(f32[4,1600]{1,0:T(4,128)} %param.22) | copy-start | bytes 76804
  102.0 9.5 %collective-permute-start.14 = (bf16[1,250,256]{2,1,0:T(8,128)(2,1)S(1)}, bf16[1,250,256]{2,1,0:T(8,128)(2,1)S(1)}, u32[]{:S(2)}, u32[]{:S(2)}) collective-permute-start(bf16[1,250,256]{2,1,0:T(8,128)(2,1)S(1)} %maximum_bitcast_fusion.1), channel_id=1, source_target_pairs={{0,16},{4,20},{8,24},{12,28},{16,0},{20,4},{24,8},{28,12},{1,17},{... | collective-permute-start | bytes 384008 | tf_op jit(solution)/shard_map/ppermute | solution.py:85
  111.5 7.8 %collective-permute-start.15 = (bf16[2,250,256]{2,1,0:T(8,128)(2,1)S(1)}, bf16[2,250,256]{2,1,0:T(8,128)(2,1)S(1)}, u32[]{:S(2)}, u32[]{:S(2)}) collective-permute-start(bf16[2,250,256]{2,1,0:T(8,128)(2,1)S(1)} %constant_dynamic-update-slice_fusion.24), channel_id=1, source_target_pairs={{0,8},{4,12},{8,0},{12,4},{16,24},{20,28},{24,16},{28,20},{1,9},{5... | collective-permute-start | bytes 768008 | tf_op jit(solution)/shard_map/ppermute | solution.py:85
  119.3 36.7 %collective-permute-start.16 = (bf16[4,250,256]{2,1,0:T(8,128)(2,1)S(1)}, bf16[4,250,256]{2,1,0:T(8,128)(2,1)S(1)}, u32[]{:S(2)}, u32[]{:S(2)}) collective-permute-start(bf16[4,250,256]{2,1,0:T(8,128)(2,1)S(1)} %constant_dynamic-update-slice_fusion.22), channel_id=1, source_target_pairs={{0,4},{4,0},{8,12},{12,8},{16,20},{20,16},{24,28},{28,24},{1,5},{5... | collective-permute-start | bytes 1536008 | tf_op jit(solution)/shard_map/ppermute | solution.py:85
  122.2 6.1 %collective-permute-start.18 = (f32[448,128]{1,0:T(8,128)S(1)}, f32[448,128]{1,0:T(8,128)S(1)}, u32[]{:S(2)}, u32[]{:S(2)}) collective-permute-start(f32[448,128]{1,0:T(8,128)S(1)} %constant_dynamic-slice_fusion.7), channel_id=1, source_target_pairs={{0,2},{1,3},{2,0},{3,1},{4,6},{5,7},{6,4},{7,5},{8,10},{9,11},{10,... | collective-permute-start | bytes 688136 | tf_op jit(solution)/shard_map/ppermute | solution.py:85
  123.4 14.6 %collective-permute-start.28 = (f32[448,128]{1,0:T(8,128)S(1)}, f32[448,128]{1,0:T(8,128)S(1)}, u32[]{:S(2)}, u32[]{:S(2)}) collective-permute-start(f32[448,128]{1,0:T(8,128)S(1)} %constant_dynamic-slice_fusion.3), channel_id=1, source_target_pairs={{0,4},{4,0},{8,12},{12,8},{16,20},{20,16},{24,28},{28,24},{1,5},{5... | collective-permute-start | bytes 688136 | tf_op jit(solution)/shard_map/ppermute | solution.py:85
  128.3 11.6 %collective-permute-start.19 = (f32[224,128]{1,0:T(8,128)S(1)}, f32[224,128]{1,0:T(8,128)S(1)}, u32[]{:S(2)}, u32[]{:S(2)}) collective-permute-start(f32[224,128]{1,0:T(8,128)S(1)} %constant_dynamic-slice_fusion.6), channel_id=1, source_target_pairs={{0,4},{4,0},{8,12},{12,8},{16,20},{20,16},{24,28},{28,24},{1,5},{5... | collective-permute-start | bytes 344072 | tf_op jit(solution)/shard_map/ppermute | solution.py:85
  138.0 4.9 %collective-permute-start.29 = (f32[224,128]{1,0:T(8,128)S(1)}, f32[224,128]{1,0:T(8,128)S(1)}, u32[]{:S(2)}, u32[]{:S(2)}) collective-permute-start(f32[224,128]{1,0:T(8,128)S(1)} %constant_dynamic-slice_fusion.2), channel_id=1, source_target_pairs={{0,8},{4,12},{8,0},{12,4},{16,24},{20,28},{24,16},{28,20},{1,9},{5... | collective-permute-start | bytes 344072 | tf_op jit(solution)/shard_map/ppermute | solution.py:85
  139.9 4.2 %collective-permute-start.20 = (f32[112,128]{1,0:T(8,128)S(1)}, f32[112,128]{1,0:T(8,128)S(1)}, u32[]{:S(2)}, u32[]{:S(2)}) collective-permute-start(f32[112,128]{1,0:T(8,128)S(1)} %constant_dynamic-slice_fusion.5), channel_id=1, source_target_pairs={{0,8},{4,12},{8,0},{12,4},{16,24},{20,28},{24,16},{28,20},{1,9},{5... | collective-permute-start | bytes 172040 | tf_op jit(solution)/shard_map/ppermute | solution.py:85
  142.9 4.9 %collective-permute-start.30 = (f32[112,128]{1,0:T(8,128)S(1)}, f32[112,128]{1,0:T(8,128)S(1)}, u32[]{:S(2)}, u32[]{:S(2)}) collective-permute-start(f32[112,128]{1,0:T(8,128)S(1)} %constant_dynamic-slice_fusion.1), channel_id=1, source_target_pairs={{0,2},{1,3},{2,0},{3,1},{4,6},{5,7},{6,4},{7,5},{8,10},{9,11},{10,... | collective-permute-start | bytes 172040 | tf_op jit(solution)/shard_map/ppermute | solution.py:85
  144.2 6.8 %collective-permute-start.21 = (f32[56,128]{1,0:T(8,128)S(1)}, f32[56,128]{1,0:T(8,128)S(1)}, u32[]{:S(2)}, u32[]{:S(2)}) collective-permute-start(f32[56,128]{1,0:T(8,128)S(1)} %constant_dynamic-slice_fusion.4), channel_id=1, source_target_pairs={{0,16},{4,20},{8,24},{12,28},{16,0},{20,4},{24,8},{28,12},{1,17},{... | collective-permute-start | bytes 86024 | tf_op jit(solution)/shard_map/ppermute | solution.py:85
  147.8 5.2 %collective-permute-start.31 = (f32[56,128]{1,0:T(8,128)S(1)}, f32[56,128]{1,0:T(8,128)S(1)}, u32[]{:S(2)}, u32[]{:S(2)}) collective-permute-start(f32[56,128]{1,0:T(8,128)S(1)} %constant_dynamic-slice_fusion), channel_id=1, source_target_pairs={{0,16},{4,20},{8,24},{12,28},{16,0},{20,4},{24,8},{28,12},{1,17},{... | collective-permute-start | bytes 86024 | tf_op jit(solution)/shard_map/ppermute | solution.py:85
  151.0 6.7 %collective-permute-start.22 = (f32[56,128]{1,0:T(8,128)S(1)}, f32[56,128]{1,0:T(8,128)S(1)}, u32[]{:S(2)}, u32[]{:S(2)}) collective-permute-start(f32[56,128]{1,0:T(8,128)S(1)} %get-tuple-element.15), channel_id=1, source_target_pairs={{0,16},{4,20},{8,24},{12,28},{16,0},{20,4},{24,8},{28,12},{1,17},{... | collective-permute-start | bytes 86024 | tf_op jit(solution)/shard_map/ppermute | solution.py:85
  152.9 6.5 %collective-permute-start.32 = (f32[56,128]{1,0:T(8,128)S(1)}, f32[56,128]{1,0:T(8,128)S(1)}, u32[]{:S(2)}, u32[]{:S(2)}) collective-permute-start(f32[56,128]{1,0:T(8,128)S(1)} %get-tuple-element.19), channel_id=1, source_target_pairs={{0,16},{4,20},{8,24},{12,28},{16,0},{20,4},{24,8},{28,12},{1,17},{... | collective-permute-start | bytes 86024 | tf_op jit(solution)/shard_map/ppermute | solution.py:85
  156.0 0.9 copy-start.4
  157.7 4.2 %collective-permute-start.23 = (f32[112,128]{1,0:T(8,128)S(1)}, f32[112,128]{1,0:T(8,128)S(1)}, u32[]{:S(2)}, u32[]{:S(2)}) collective-permute-start(f32[112,128]{1,0:T(8,128)S(1)} %constant_dynamic-update-slice_fusion.18), channel_id=1, source_target_pairs={{0,8},{4,12},{8,0},{12,4},{16,24},{20,28},{24,16},{28,20},{1,9},{5... | collective-permute-start | bytes 172040 | tf_op jit(solution)/shard_map/ppermute | solution.py:85
  159.5 4.9 %collective-permute-start.33 = (f32[112,128]{1,0:T(8,128)S(1)}, f32[112,128]{1,0:T(8,128)S(1)}, u32[]{:S(2)}, u32[]{:S(2)}) collective-permute-start(f32[112,128]{1,0:T(8,128)S(1)} %constant_dynamic-update-slice_fusion.8), channel_id=1, source_target_pairs={{0,2},{1,3},{2,0},{3,1},{4,6},{5,7},{6,4},{7,5},{8,10},{9,11},{10,... | collective-permute-start | bytes 172040 | tf_op jit(solution)/shard_map/ppermute | solution.py:85
  162.0 4.9 %collective-permute-start.24 = (f32[224,128]{1,0:T(8,128)S(1)}, f32[224,128]{1,0:T(8,128)S(1)}, u32[]{:S(2)}, u32[]{:S(2)}) collective-permute-start(f32[224,128]{1,0:T(8,128)S(1)} %constant_dynamic-update-slice_fusion.16), channel_id=1, source_target_pairs={{0,4},{4,0},{8,12},{12,8},{16,20},{20,16},{24,28},{28,24},{1,5},{5... | collective-permute-start | bytes 344072 | tf_op jit(solution)/shard_map/ppermute | solution.py:85
  164.4 4.9 %collective-permute-start.34 = (f32[224,128]{1,0:T(8,128)S(1)}, f32[224,128]{1,0:T(8,128)S(1)}, u32[]{:S(2)}, u32[]{:S(2)}) collective-permute-start(f32[224,128]{1,0:T(8,128)S(1)} %constant_dynamic-update-slice_fusion.6), channel_id=1, source_target_pairs={{0,8},{4,12},{8,0},{12,4},{16,24},{20,28},{24,16},{28,20},{1,9},{5... | collective-permute-start | bytes 344072 | tf_op jit(solution)/shard_map/ppermute | solution.py:85
  166.9 6.1 %collective-permute-start.25 = (f32[448,128]{1,0:T(8,128)S(1)}, f32[448,128]{1,0:T(8,128)S(1)}, u32[]{:S(2)}, u32[]{:S(2)}) collective-permute-start(f32[448,128]{1,0:T(8,128)S(1)} %constant_dynamic-update-slice_fusion.14), channel_id=1, source_target_pairs={{0,2},{1,3},{2,0},{3,1},{4,6},{5,7},{6,4},{7,5},{8,10},{9,11},{10,... | collective-permute-start | bytes 688136 | tf_op jit(solution)/shard_map/ppermute | solution.py:85
  169.2 6.1 %collective-permute-start.35 = (f32[448,128]{1,0:T(8,128)S(1)}, f32[448,128]{1,0:T(8,128)S(1)}, u32[]{:S(2)}, u32[]{:S(2)}) collective-permute-start(f32[448,128]{1,0:T(8,128)S(1)} %constant_dynamic-update-slice_fusion.4), channel_id=1, source_target_pairs={{0,4},{4,0},{8,12},{12,8},{16,20},{20,16},{24,28},{28,24},{1,5},{5... | collective-permute-start | bytes 688136 | tf_op jit(solution)/shard_map/ppermute | solution.py:85
  173.0 11.5 %collective-permute-start.26 = (f32[896,128]{1,0:T(8,128)S(1)}, f32[896,128]{1,0:T(8,128)S(1)}, u32[]{:S(2)}, u32[]{:S(2)}) collective-permute-start(f32[896,128]{1,0:T(8,128)S(1)} %constant_dynamic-update-slice_fusion.12), channel_id=1, source_target_pairs={{0,1},{1,0},{2,3},{3,2},{4,5},{5,4},{6,7},{7,6},{8,9},{9,8},{10,11... | collective-permute-start | bytes 1376264 | tf_op jit(solution)/shard_map/ppermute | solution.py:85
  175.3 9.2 %collective-permute-start.36 = (f32[896,128]{1,0:T(8,128)S(1)}, f32[896,128]{1,0:T(8,128)S(1)}, u32[]{:S(2)}, u32[]{:S(2)}) collective-permute-start(f32[896,128]{1,0:T(8,128)S(1)} %constant_dynamic-update-slice_fusion.2), channel_id=1, source_target_pairs={{0,1},{1,0},{2,3},{3,2},{4,5},{5,4},{6,7},{7,6},{8,9},{9,8},{10,11... | collective-permute-start | bytes 1376264 | tf_op jit(solution)/shard_map/ppermute | solution.py:85

commit v11 on v10

--- a/solution.py
+++ b/solution.py
@@ -27,9 +27,8 @@
 
 def orthogonalize(subspace):
     high = lax.Precision.HIGH
-    highest = lax.Precision.HIGHEST
     iterate = subspace * lax.rsqrt(jnp.sum(subspace * subspace) + 1e-06)
-    gram_matrix = jnp.dot(iterate.T, iterate, precision=highest)
+    gram_matrix = jnp.dot(iterate.T, iterate, precision=high)
     identity = jnp.eye(gram_matrix.shape[0], dtype=gram_matrix.dtype)
     product = None
     for sweep_index in range(NS_STEPS):

time: 196 us -> 194 us (0.990)
  transfers between devices with their start and end apart: 37 -> 37, of which waited for: 25 -> 25; matrix products, arithmetic and copies ran while one was open for 19% -> 20% of each run, Pallas kernels for 4% -> 4%
where the time goes in v11:
time: 194 us; the launch traced here: 193 us
  waiting for transfers between devices  75.8 us (39%)
  starting transfers between devices  44 us (23%)
  other arithmetic  24.8 us (13%)
  matrix products  22.7 us (12%)
  local copies, waits for them, and re-layouts  12.8 us (7%)
  Pallas kernels  7.5 us (4%)
  between operations  5.82 us (3%)
    ppermute x37, waiting for transfers between devices, swap_with(): lax.ppermute(values, name, [(index, index ^ bit) for index in range(size)])  75.8 us
    ppermute x37, starting transfers between devices, swap_with(): lax.ppermute(values, name, [(index, index ^ bit) for index in range(size)])  44 us
    dot_general x4, matrix products, exact_dot(): lax.dot_general(lhs_bf16, split2(rhs_f32), ((contract, (0,)), ((), ())),...  15.7 us
    pallas_call x1, Pallas kernels, updated_weights(): pl.pallas_call(update_kernel, out_shape=jax.ShapeDtypeStruct(weights.shap...  7.5 us
    convert_element_type x4, other arithmetic, split2(): second = (values - first.astype(jnp.float32)).astype(jnp.bfloat16)  5.03 us
    add x12, other arithmetic, run_steps(): parts = keep + swap_with(send, name, bit, size)  4.49 us
  transfers between devices with their start and end apart: 37, of which 25 were waited for; matrix products, arithmetic and copies ran while one was open for 20% of the time, Pallas kernels for 4%

profile of v11, /device:TPU:0, one launch (start us, length us, event | category | flops | bytes accessed | tf_op | source)
XLA Modules:
  0.0 193.4 jit_solution(3679609024918766818)
XLA Ops:
  0.7 2.2 %subtract_convert_fusion.4 = (bf16[1600,128]{1,0:T(8,128)(2,1)S(1)}, bf16[1600,128]{1,0:T(8,128)(2,1)S(1)}, bf16[1600,128]{1,0:T(8,128)(2,1)S(1)}, bf16[1600,128]{1,0:T(8,128)(2,1)S(1)}) fusion(f32[1600,256]{1,0:T(8,128)} %param.18), kind=kLoop, calls=%fused_computation.52 | loop fusion | flops 1228800 | bytes 4096000 | tf_op jit(solution)/shard_map/convert_element_type | solution.py:213
  2.8 4.2 %convolution_bitcast_fusion.1 = f32[1600,256]{1,0:T(8,128)S(1)} fusion(bf16[1600,1600]{1,0:T(8,128)(2,1)} %bitcast.73, bf16[1600,128]{1,0:T(8,128)(2,1)S(1)} %get-tuple-element.35, bf16[1600,128]{1,0:T(8,128)(2,1)S(1)} %get-tuple-element.36), kind=kOutput, calls=%fused_computation.1 | convolution fusion | flops 1312358400 | bytes 7577600 | tf_op jit(solution)/shard_map/dot_general | solution.py:219
  9.6 2.9 %collective-permute-start = (f32[928,128]{1,0:T(8,128)}, f32[928,128]{1,0:T(8,128)}, u32[]{:S(2)}, u32[]{:S(2)}) collective-permute-start(f32[928,128]{1,0:T(8,128)} %constant_dynamic-slice_fusion.12), channel_id=1, source_target_pairs={{0,4},{4,0},{8,12},{12,8},{16,20},{20,16},{24,28},{28,24},{1,5},{5... | collective-permute-start | bytes 1425416 | tf_op jit(solution)/shard_map/ppermute | solution.py:84
  12.6 4.2 %convolution_bitcast_fusion = f32[1600,256]{1,0:T(8,128)S(1)} fusion(bf16[1600,1600]{1,0:T(8,128)(2,1)} %bitcast.74, bf16[1600,128]{1,0:T(8,128)(2,1)S(1)} %get-tuple-element.41, bf16[1600,128]{1,0:T(8,128)(2,1)S(1)} %get-tuple-element.42), kind=kOutput, calls=%fused_computation | convolution fusion | flops 1312358400 | bytes 7577600 | tf_op jit(solution)/shard_map/dot_general | solution.py:219
  16.8 1.0 slice_add_fusion.2
  17.9 1.4 fusion.7
  20.1 1.6 collective-permute-start.6
  21.7 1.0 convert_element_type.154
  22.7 1.6 copy.34
  24.3 1.7 copy.35
  26.0 1.6 subtract_convert_fusion
  27.7 1.4 maximum_bitcast_fusion.basis_ref
  29.0 1.1 dynamic-slice_add_fusion
  30.7 2.7 %collective-permute-done.6 = f32[928,128]{1,0:T(8,128)} collective-permute-done((f32[928,128]{1,0:T(8,128)}, f32[928,128]{1,0:T(8,128)}, u32[]{:S(2)}, u32[]{:S(2)}) %collective-permute-start.6) | collective-permute-done | bytes 475168 | tf_op jit(solution)/shard_map/ppermute | solution.py:84
  33.3 1.1 fusion.22
  35.1 2.7 %collective-permute-done.1 = f32[464,128]{1,0:T(8,128)S(1)} collective-permute-done((f32[464,128]{1,0:T(8,128)S(1)}, f32[464,128]{1,0:T(8,128)S(1)}, u32[]{:S(2)}, u32[]{:S(2)}) %collective-permute-start.1) | collective-permute-done | bytes 237600 | tf_op jit(solution)/shard_map/ppermute | solution.py:84
  37.8 2.7 %collective-permute-start.2 = (f32[232,128]{1,0:T(8,128)S(1)}, f32[232,128]{1,0:T(8,128)S(1)}, u32[]{:S(2)}, u32[]{:S(2)}) collective-permute-start(f32[232,128]{1,0:T(8,128)S(1)} %constant_dynamic-slice_fusion.10), channel_id=1, source_target_pairs={{0,16},{4,20},{8,24},{12,28},{16,0},{20,4},{24,8},{28,12},{1,17},{... | collective-permute-start | bytes 356360 | tf_op jit(solution)/shard_map/ppermute | solution.py:84
  40.7 2.7 %collective-permute-start.8 = (f32[232,128]{1,0:T(8,128)S(1)}, f32[232,128]{1,0:T(8,128)S(1)}, u32[]{:S(2)}, u32[]{:S(2)}) collective-permute-start(f32[232,128]{1,0:T(8,128)S(1)} %constant_dynamic-slice_fusion.8), channel_id=1, source_target_pairs={{0,16},{4,20},{8,24},{12,28},{16,0},{20,4},{24,8},{28,12},{1,17},{... | collective-permute-start | bytes 356360 | tf_op jit(solution)/shard_map/ppermute | solution.py:84
  43.4 5.5 %collective-permute-done.2 = f32[232,128]{1,0:T(8,128)S(1)} collective-permute-done((f32[232,128]{1,0:T(8,128)S(1)}, f32[232,128]{1,0:T(8,128)S(1)}, u32[]{:S(2)}, u32[]{:S(2)}) %collective-permute-start.2) | collective-permute-done | bytes 118816 | tf_op jit(solution)/shard_map/ppermute | solution.py:84
  49.0 2.4 %collective-permute-done.8 = f32[232,128]{1,0:T(8,128)S(1)} collective-permute-done((f32[232,128]{1,0:T(8,128)S(1)}, f32[232,128]{1,0:T(8,128)S(1)}, u32[]{:S(2)}, u32[]{:S(2)}) %collective-permute-start.8) | collective-permute-done | bytes 118816 | tf_op jit(solution)/shard_map/ppermute | solution.py:84
  52.0 6.4 %collective-permute-done.3 = f32[232,128]{1,0:T(8,128)S(1)} collective-permute-done((f32[232,128]{1,0:T(8,128)S(1)}, f32[232,128]{1,0:T(8,128)S(1)}, u32[]{:S(2)}, u32[]{:S(2)}) %collective-permute-start.3) | collective-permute-done | bytes 118816 | tf_op jit(solution)/shard_map/ppermute | solution.py:84
  58.4 1.5 collective-permute-start.4
  60.8 1.6 collective-permute-done.9
  62.6 3.1 %collective-permute-done.4 = f32[464,128]{1,0:T(8,128)S(1)} collective-permute-done((f32[464,128]{1,0:T(8,128)S(1)}, f32[464,128]{1,0:T(8,128)S(1)}, u32[]{:S(2)}, u32[]{:S(2)}) %collective-permute-start.4) | collective-permute-done | bytes 237600 | tf_op jit(solution)/shard_map/ppermute | solution.py:84
  66.2 4.2 %collective-permute-done.10 = f32[464,128]{1,0:T(8,128)S(1)} collective-permute-done((f32[464,128]{1,0:T(8,128)S(1)}, f32[464,128]{1,0:T(8,128)S(1)}, u32[]{:S(2)}, u32[]{:S(2)}) %collective-permute-start.10) | collective-permute-done | bytes 237600 | tf_op jit(solution)/shard_map/ppermute | solution.py:84
  70.4 1.0 collective-permute-start.11
  71.7 7.1 %collective-permute-done.5 = f32[928,128]{1,0:T(8,128)S(1)} collective-permute-done((f32[928,128]{1,0:T(8,128)S(1)}, f32[928,128]{1,0:T(8,128)S(1)}, u32[]{:S(2)}, u32[]{:S(2)}) %collective-permute-start.5) | collective-permute-done | bytes 475168 | tf_op jit(solution)/shard_map/ppermute | solution.py:84
  79.2 1.1 subtract_convert_fusion.1
  80.9 2.4 %convolution_bitcast_fusion.3 = f32[1600,256]{1,0:T(8,128)S(1)} fusion(bf16[1600,1600]{1,0:T(8,128)(2,1)S(1)} %bitcast.78, bf16[1600,128]{1,0:T(8,128)(2,1)S(1)} %get-tuple-element.16, bf16[1600,128]{1,0:T(8,128)(2,1)S(1)} %get-tuple-element.17), kind=kOutput, calls=%fused_computation.3 | convolution fusion | flops 1312358400 | bytes 7577600 | tf_op jit(solution)/shard_map/dot_general | solution.py:219
  84.9 1.0 fusion.1
  87.8 5.0 %convolution_bitcast_fusion.2 = f32[1600,256]{1,0:T(8,128)S(1)} fusion(bf16[1600,1600]{1,0:T(8,128)(2,1)} %bitcast.75, bf16[1600,128]{1,0:T(8,128)(2,1)S(1)} %get-tuple-element.20, bf16[1600,128]{1,0:T(8,128)(2,1)} %get-tuple-element.21), kind=kOutput, calls=%fused_computation.2 | convolution fusion | flops 1312358400 | bytes 7577600 | tf_op jit(solution)/shard_map/dot_general | solution.py:219
  92.9 1.6 collective-permute-start.13
  98.4 1.4 multiply_divide_fusion.2
  100.0 1.9 convert_bitcast_fusion
  102.0 2.9 %collective-permute-start.14 = (bf16[1,250,256]{2,1,0:T(8,128)(2,1)S(1)}, bf16[1,250,256]{2,1,0:T(8,128)(2,1)S(1)}, u32[]{:S(2)}, u32[]{:S(2)}) collective-permute-start(bf16[1,250,256]{2,1,0:T(8,128)(2,1)S(1)} %maximum_bitcast_fusion.1), channel_id=1, source_target_pairs={{0,16},{4,20},{8,24},{12,28},{16,0},{20,4},{24,8},{28,12},{1,17},{... | collective-permute-start | bytes 384008 | tf_op jit(solution)/shard_map/ppermute | solution.py:84
  105.8 5.7 %collective-permute-done.14 = bf16[1,250,256]{2,1,0:T(8,128)(2,1)S(1)} collective-permute-done((bf16[1,250,256]{2,1,0:T(8,128)(2,1)S(1)}, bf16[1,250,256]{2,1,0:T(8,128)(2,1)S(1)}, u32[]{:S(2)}, u32[]{:S(2)}) %collective-permute-start.14) | collective-permute-done | bytes 128032 | tf_op jit(solution)/shard_map/ppermute | solution.py:84
  113.0 6.3 %collective-permute-done.15 = bf16[2,250,256]{2,1,0:T(8,128)(2,1)S(1)} collective-permute-done((bf16[2,250,256]{2,1,0:T(8,128)(2,1)S(1)}, bf16[2,250,256]{2,1,0:T(8,128)(2,1)S(1)}, u32[]{:S(2)}, u32[]{:S(2)}) %collective-permute-start.15) | collective-permute-done | bytes 256032 | tf_op jit(solution)/shard_map/ppermute | solution.py:84
  119.3 1.6 collective-permute-start.16
  121.1 1.1 fusion.23
  122.3 1.1 fusion.24
  123.9 4.4 %collective-permute-done.18 = f32[448,128]{1,0:T(8,128)S(1)} collective-permute-done((f32[448,128]{1,0:T(8,128)S(1)}, f32[448,128]{1,0:T(8,128)S(1)}, u32[]{:S(2)}, u32[]{:S(2)}) %collective-permute-start.18) | collective-permute-done | bytes 229408 | tf_op jit(solution)/shard_map/ppermute | solution.py:84
  128.8 9.1 %collective-permute-done.28 = f32[448,128]{1,0:T(8,128)S(1)} collective-permute-done((f32[448,128]{1,0:T(8,128)S(1)}, f32[448,128]{1,0:T(8,128)S(1)}, u32[]{:S(2)}, u32[]{:S(2)}) %collective-permute-start.28) | collective-permute-done | bytes 229408 | tf_op jit(solution)/shard_map/ppermute | solution.py:84
  138.0 1.9 collective-permute-start.29
  139.9 1.2 collective-permute-start.20
  141.1 1.7 collective-permute-done.29
  143.0 1.2 collective-permute-done.20
  144.2 3.5 %collective-permute-start.21 = (f32[56,128]{1,0:T(8,128)S(1)}, f32[56,128]{1,0:T(8,128)S(1)}, u32[]{:S(2)}, u32[]{:S(2)}) collective-permute-start(f32[56,128]{1,0:T(8,128)S(1)} %constant_dynamic-slice_fusion.4), channel_id=1, source_target_pairs={{0,16},{4,20},{8,24},{12,28},{16,0},{20,4},{24,8},{28,12},{1,17},{... | collective-permute-start | bytes 86024 | tf_op jit(solution)/shard_map/ppermute | solution.py:84
  147.8 3.2 %collective-permute-start.31 = (f32[56,128]{1,0:T(8,128)S(1)}, f32[56,128]{1,0:T(8,128)S(1)}, u32[]{:S(2)}, u32[]{:S(2)}) collective-permute-start(f32[56,128]{1,0:T(8,128)S(1)} %constant_dynamic-slice_fusion), channel_id=1, source_target_pairs={{0,16},{4,20},{8,24},{12,28},{16,0},{20,4},{24,8},{28,12},{1,17},{... | collective-permute-start | bytes 86024 | tf_op jit(solution)/shard_map/ppermute | solution.py:84
  151.0 1.7 collective-permute-start.22
  152.9 3.0 %collective-permute-start.32 = (f32[56,128]{1,0:T(8,128)S(1)}, f32[56,128]{1,0:T(8,128)S(1)}, u32[]{:S(2)}, u32[]{:S(2)}) collective-permute-start(f32[56,128]{1,0:T(8,128)S(1)} %get-tuple-element.19), channel_id=1, source_target_pairs={{0,16},{4,20},{8,24},{12,28},{16,0},{20,4},{24,8},{28,12},{1,17},{... | collective-permute-start | bytes 86024 | tf_op jit(solution)/shard_map/ppermute | solution.py:84
  157.7 1.7 collective-permute-start.23
  159.6 2.4 %collective-permute-done.23 = f32[112,128]{1,0:T(8,128)S(1)} collective-permute-done((f32[112,128]{1,0:T(8,128)S(1)}, f32[112,128]{1,0:T(8,128)S(1)}, u32[]{:S(2)}, u32[]{:S(2)}) %collective-permute-start.23) | collective-permute-done | bytes 57376 | tf_op jit(solution)/shard_map/ppermute | solution.py:84
  162.0 1.6 collective-permute-start.24
  164.4 1.0 collective-permute-start.34
  165.4 1.5 collective-permute-done.24
  166.9 2.3 %collective-permute-done.34 = f32[224,128]{1,0:T(8,128)S(1)} collective-permute-done((f32[224,128]{1,0:T(8,128)S(1)}, f32[224,128]{1,0:T(8,128)S(1)}, u32[]{:S(2)}, u32[]{:S(2)}) %collective-permute-start.34) | collective-permute-done | bytes 114720 | tf_op jit(solution)/shard_map/ppermute | solution.py:84
  169.2 1.6 collective-permute-start.35
  171.1 1.8 collective-permute-done.25
  173.0 2.3 %collective-permute-done.35 = f32[448,128]{1,0:T(8,128)S(1)} collective-permute-done((f32[448,128]{1,0:T(8,128)S(1)}, f32[448,128]{1,0:T(8,128)S(1)}, u32[]{:S(2)}, u32[]{:S(2)}) %collective-permute-start.35) | collective-permute-done | bytes 229408 | tf_op jit(solution)/shard_map/ppermute | solution.py:84
  175.4 1.3 pad_maximum_fusion.1.direction_ref
  176.7 7.5 %shard_map.221 = bf16[8,200,1600]{2,1,0:T(8,128)(2,1)} custom-call(bf16[8,200,512]{2,1,0:T(8,128)(2,1)} %pad_maximum_fusion.1.direction_ref, bf16[512,1600]{1,0:T(8,128)(2,1)} %maximum_bitcast_fusion.basis_ref, bf16[8,200,1600]{2,1,0:T(8,128)(2,1)} %bitcast.68), custom_call_target="tpu_custom_call" | custom-call | tf_op jit(solution)/shard_map/pallas_call | solution.py:198
  184.7 1.0 multiply_reduce_fusion
  186.4 1.5 fusion.4
  191.4 2.0 %fusion.2 = f32[1600,256]{1,0:T(8,128)} fusion(f32[256,256]{1,0:T(8,128)S(1)} %fusion.120, f32[1600,128]{1,0:T(8,128)S(1)} %slice.124, f32[1600,128]{1,0:T(8,128)S(1)} %slice.121, f32[]{:T(128)S(6)} %rsqrt.4), kind=kOutput, calls=%fused_computation.14 | convolution fusion | flops 629964800 | bytes 3538948 | tf_op jit(solution)/shard_map/dot_general | solution.py:39
  (186 shorter events, 24.0 us)
Async XLA Ops:
  7.0 0.9 copy-start.3
  8.1 0.7 copy-start.2
  9.6 19.4 %collective-permute-start = (f32[928,128]{1,0:T(8,128)}, f32[928,128]{1,0:T(8,128)}, u32[]{:S(2)}, u32[]{:S(2)}) collective-permute-start(f32[928,128]{1,0:T(8,128)} %constant_dynamic-slice_fusion.12), channel_id=1, source_target_pairs={{0,4},{4,0},{8,12},{12,8},{16,20},{20,16},{24,28},{28,24},{1,5},{5... | collective-permute-start | bytes 1425416 | tf_op jit(solution)/shard_map/ppermute | solution.py:84
  16.8 1.0 copy-start.10
  17.8 3.9 %copy-start = (f32[1600,256]{1,0:T(8,128)S(1)}, f32[1600,256]{1,0:T(8,128)}, u32[]{:S(2)}) copy-start(f32[1600,256]{1,0:T(8,128)} %param.18) | copy-start | bytes 4915204
  20.1 13.2 %collective-permute-start.6 = (f32[928,128]{1,0:T(8,128)}, f32[928,128]{1,0:T(8,128)}, u32[]{:S(2)}, u32[]{:S(2)}) collective-permute-start(f32[928,128]{1,0:T(8,128)} %pad_dynamic-slice_fusion.6), channel_id=1, source_target_pairs={{0,8},{4,12},{8,0},{12,4},{16,24},{20,28},{24,16},{28,20},{1,9},{5... | collective-permute-start | bytes 1425416 | tf_op jit(solution)/shard_map/ppermute | solution.py:84
  30.2 7.6 %collective-permute-start.1 = (f32[464,128]{1,0:T(8,128)S(1)}, f32[464,128]{1,0:T(8,128)S(1)}, u32[]{:S(2)}, u32[]{:S(2)}) collective-permute-start(f32[464,128]{1,0:T(8,128)S(1)} %constant_dynamic-slice_fusion.11), channel_id=1, source_target_pairs={{0,8},{4,12},{8,0},{12,4},{16,24},{20,28},{24,16},{28,20},{1,9},{5... | collective-permute-start | bytes 712712 | tf_op jit(solution)/shard_map/ppermute | solution.py:84
  34.5 6.2 %collective-permute-start.7 = (f32[464,128]{1,0:T(8,128)S(1)}, f32[464,128]{1,0:T(8,128)S(1)}, u32[]{:S(2)}, u32[]{:S(2)}) collective-permute-start(f32[464,128]{1,0:T(8,128)S(1)} %constant_dynamic-slice_fusion.9), channel_id=1, source_target_pairs={{0,4},{4,0},{8,12},{12,8},{16,20},{20,16},{24,28},{28,24},{1,5},{5... | collective-permute-start | bytes 712712 | tf_op jit(solution)/shard_map/ppermute | solution.py:84
  37.8 11.0 %collective-permute-start.2 = (f32[232,128]{1,0:T(8,128)S(1)}, f32[232,128]{1,0:T(8,128)S(1)}, u32[]{:S(2)}, u32[]{:S(2)}) collective-permute-start(f32[232,128]{1,0:T(8,128)S(1)} %constant_dynamic-slice_fusion.10), channel_id=1, source_target_pairs={{0,16},{4,20},{8,24},{12,28},{16,0},{20,4},{24,8},{28,12},{1,17},{... | collective-permute-start | bytes 356360 | tf_op jit(solution)/shard_map/ppermute | solution.py:84
  40.7 10.7 %collective-permute-start.8 = (f32[232,128]{1,0:T(8,128)S(1)}, f32[232,128]{1,0:T(8,128)S(1)}, u32[]{:S(2)}, u32[]{:S(2)}) collective-permute-start(f32[232,128]{1,0:T(8,128)S(1)} %constant_dynamic-slice_fusion.8), channel_id=1, source_target_pairs={{0,16},{4,20},{8,24},{12,28},{16,0},{20,4},{24,8},{28,12},{1,17},{... | collective-permute-start | bytes 356360 | tf_op jit(solution)/shard_map/ppermute | solution.py:84
  48.9 9.5 %collective-permute-start.3 = (f32[232,128]{1,0:T(8,128)S(1)}, f32[232,128]{1,0:T(8,128)S(1)}, u32[]{:S(2)}, u32[]{:S(2)}) collective-permute-start(f32[232,128]{1,0:T(8,128)S(1)} %get-tuple-element.34), channel_id=1, source_target_pairs={{0,16},{4,20},{8,24},{12,28},{16,0},{20,4},{24,8},{28,12},{1,17},{... | collective-permute-start | bytes 356360 | tf_op jit(solution)/shard_map/ppermute | solution.py:84
  51.4 11.0 %collective-permute-start.9 = (f32[232,128]{1,0:T(8,128)S(1)}, f32[232,128]{1,0:T(8,128)S(1)}, u32[]{:S(2)}, u32[]{:S(2)}) collective-permute-start(f32[232,128]{1,0:T(8,128)S(1)} %get-tuple-element.38), channel_id=1, source_target_pairs={{0,16},{4,20},{8,24},{12,28},{16,0},{20,4},{24,8},{28,12},{1,17},{... | collective-permute-start | bytes 356360 | tf_op jit(solution)/shard_map/ppermute | solution.py:84
  58.4 7.2 %collective-permute-start.4 = (f32[464,128]{1,0:T(8,128)S(1)}, f32[464,128]{1,0:T(8,128)S(1)}, u32[]{:S(2)}, u32[]{:S(2)}) collective-permute-start(f32[464,128]{1,0:T(8,128)S(1)} %constant_dynamic-update-slice_fusion.36), channel_id=1, source_target_pairs={{0,8},{4,12},{8,0},{12,4},{16,24},{20,28},{24,16},{28,20},{1,9},{5... | collective-permute-start | bytes 712712 | tf_op jit(solution)/shard_map/ppermute | solution.py:84
  62.4 8.0 %collective-permute-start.10 = (f32[464,128]{1,0:T(8,128)S(1)}, f32[464,128]{1,0:T(8,128)S(1)}, u32[]{:S(2)}, u32[]{:S(2)}) collective-permute-start(f32[464,128]{1,0:T(8,128)S(1)} %constant_dynamic-update-slice_fusion.30), channel_id=1, source_target_pairs={{0,4},{4,0},{8,12},{12,8},{16,20},{20,16},{24,28},{28,24},{1,5},{5... | collective-permute-start | bytes 712712 | tf_op jit(solution)/shard_map/ppermute | solution.py:84
  62.5 18.4 %slice-start = ((s8[5324800]{0:T(1024)(128)(4,1)}), s8[4194304]{0:T(1024)(128)(4,1)S(1)}, s32[]{:S(2)}) async-start(s8[5324800]{0:T(1024)(128)(4,1)} %bitcast.76), calls=%async_computation | async-start | bytes 8388608
  65.7 13.1 %collective-permute-start.5 = (f32[928,128]{1,0:T(8,128)S(1)}, f32[928,128]{1,0:T(8,128)S(1)}, u32[]{:S(2)}, u32[]{:S(2)}) collective-permute-start(f32[928,128]{1,0:T(8,128)S(1)} %constant_dynamic-update-slice_fusion.34), channel_id=1, source_target_pairs={{0,4},{4,0},{8,12},{12,8},{16,20},{20,16},{24,28},{28,24},{1,5},{5... | collective-permute-start | bytes 1425416 | tf_op jit(solution)/shard_map/ppermute | solution.py:84
  70.4 8.7 %collective-permute-start.11 = (f32[928,128]{1,0:T(8,128)S(1)}, f32[928,128]{1,0:T(8,128)S(1)}, u32[]{:S(2)}, u32[]{:S(2)}) collective-permute-start(f32[928,128]{1,0:T(8,128)S(1)} %constant_dynamic-update-slice_fusion.28), channel_id=1, source_target_pairs={{0,8},{4,12},{8,0},{12,4},{16,24},{20,28},{24,16},{28,20},{1,9},{5... | collective-permute-start | bytes 1425416 | tf_op jit(solution)/shard_map/ppermute | solution.py:84
  71.7 9.2 %slice-start.1 = ((s8[5324800]{0:T(1024)(128)(4,1)}), s8[1130496]{0:T(1024)(128)(4,1)S(1)}, s32[]{:S(2)}) async-start(s8[5324800]{0:T(1024)(128)(4,1)} %bitcast.76), calls=%async_computation.1 | async-start | bytes 2260992
  79.2 1.1 copy-start.1
  84.2 36.9 %collective-permute-start.17 = (f32[896,128]{1,0:T(8,128)}, f32[896,128]{1,0:T(8,128)}, u32[]{:S(2)}, u32[]{:S(2)}) collective-permute-start(f32[896,128]{1,0:T(8,128)} %pad_dynamic-slice_fusion.4), channel_id=1, source_target_pairs={{0,1},{1,0},{2,3},{3,2},{4,5},{5,4},{6,7},{7,6},{8,9},{9,8},{10,11... | collective-permute-start | bytes 1376264 | tf_op jit(solution)/shard_map/ppermute | solution.py:84
  87.2 5.7 %collective-permute-start.12 = (f32[8,128]{1,0:T(8,128)S(1)}, f32[8,128]{1,0:T(8,128)S(1)}, u32[]{:S(2)}, u32[]{:S(2)}) collective-permute-start(f32[8,128]{1,0:T(8,128)S(1)} %broadcast_in_dim.15), channel_id=1, source_target_pairs={{0,1},{1,0},{2,3},{3,2},{4,5},{5,4},{6,7},{7,6},{8,9},{9,8},{10,11... | collective-permute-start | bytes 12296 | tf_op jit(solution)/shard_map/ppermute | solution.py:84
  92.7 5.7 %copy-start.5 = (f32[1,1,4,1600]{3,2,1,0:T(4,128)S(1)}, f32[1,1,4,1600]{3,2,1,0:T(4,128)}, u32[]{:S(2)}) copy-start(f32[1,1,4,1600]{3,2,1,0:T(4,128)} %param.26) | copy-start | bytes 76804
  92.8 5.7 %copy-start.6 = (f32[1,1,4,1600]{3,2,1,0:T(4,128)S(1)}, f32[1,1,4,1600]{3,2,1,0:T(4,128)}, u32[]{:S(2)}) copy-start(f32[1,1,4,1600]{3,2,1,0:T(4,128)} %param.25) | copy-start | bytes 76804
  92.9 3.7 %collective-permute-start.13 = (f32[8,128]{1,0:T(8,128)S(1)}, f32[8,128]{1,0:T(8,128)S(1)}, u32[]{:S(2)}, u32[]{:S(2)}) collective-permute-start(f32[8,128]{1,0:T(8,128)S(1)} %broadcast_add_fusion), channel_id=1, source_target_pairs={{0,2},{1,3},{2,0},{3,1},{4,6},{5,7},{6,4},{7,5},{8,10},{9,11},{10,... | collective-permute-start | bytes 12296 | tf_op jit(solution)/shard_map/ppermute | solution.py:84
  95.3 27.0 %collective-permute-start.27 = (f32[896,128]{1,0:T(8,128)}, f32[896,128]{1,0:T(8,128)}, u32[]{:S(2)}, u32[]{:S(2)}) collective-permute-start(f32[896,128]{1,0:T(8,128)} %pad_dynamic-slice_fusion.2), channel_id=1, source_target_pairs={{0,1},{1,0},{2,3},{3,2},{4,5},{5,4},{6,7},{7,6},{8,9},{9,8},{10,11... | collective-permute-start | bytes 1376264 | tf_op jit(solution)/shard_map/ppermute | solution.py:84
  100.0 12.3 %copy-start.7 = (f32[4,1600]{1,0:T(4,128)S(1)}, f32[4,1600]{1,0:T(4,128)}, u32[]{:S(2)}) copy-start(f32[4,1600]{1,0:T(4,128)} %param.21) | copy-start | bytes 76804
  100.0 12.3 %copy-start.8 = (f32[4,1600]{1,0:T(4,128)S(1)}, f32[4,1600]{1,0:T(4,128)}, u32[]{:S(2)}) copy-start(f32[4,1600]{1,0:T(4,128)} %param.23) | copy-start | bytes 76804
  100.0 12.3 %copy-start.9 = (f32[4,1600]{1,0:T(4,128)S(1)}, f32[4,1600]{1,0:T(4,128)}, u32[]{:S(2)}) copy-start(f32[4,1600]{1,0:T(4,128)} %param.22) | copy-start | bytes 76804
  102.0 9.5 %collective-permute-start.14 = (bf16[1,250,256]{2,1,0:T(8,128)(2,1)S(1)}, bf16[1,250,256]{2,1,0:T(8,128)(2,1)S(1)}, u32[]{:S(2)}, u32[]{:S(2)}) collective-permute-start(bf16[1,250,256]{2,1,0:T(8,128)(2,1)S(1)} %maximum_bitcast_fusion.1), channel_id=1, source_target_pairs={{0,16},{4,20},{8,24},{12,28},{16,0},{20,4},{24,8},{28,12},{1,17},{... | collective-permute-start | bytes 384008 | tf_op jit(solution)/shard_map/ppermute | solution.py:84
  111.5 7.8 %collective-permute-start.15 = (bf16[2,250,256]{2,1,0:T(8,128)(2,1)S(1)}, bf16[2,250,256]{2,1,0:T(8,128)(2,1)S(1)}, u32[]{:S(2)}, u32[]{:S(2)}) collective-permute-start(bf16[2,250,256]{2,1,0:T(8,128)(2,1)S(1)} %constant_dynamic-update-slice_fusion.24), channel_id=1, source_target_pairs={{0,8},{4,12},{8,0},{12,4},{16,24},{20,28},{24,16},{28,20},{1,9},{5... | collective-permute-start | bytes 768008 | tf_op jit(solution)/shard_map/ppermute | solution.py:84
  119.3 36.7 %collective-permute-start.16 = (bf16[4,250,256]{2,1,0:T(8,128)(2,1)S(1)}, bf16[4,250,256]{2,1,0:T(8,128)(2,1)S(1)}, u32[]{:S(2)}, u32[]{:S(2)}) collective-permute-start(bf16[4,250,256]{2,1,0:T(8,128)(2,1)S(1)} %constant_dynamic-update-slice_fusion.22), channel_id=1, source_target_pairs={{0,4},{4,0},{8,12},{12,8},{16,20},{20,16},{24,28},{28,24},{1,5},{5... | collective-permute-start | bytes 1536008 | tf_op jit(solution)/shard_map/ppermute | solution.py:84
  122.2 6.1 %collective-permute-start.18 = (f32[448,128]{1,0:T(8,128)S(1)}, f32[448,128]{1,0:T(8,128)S(1)}, u32[]{:S(2)}, u32[]{:S(2)}) collective-permute-start(f32[448,128]{1,0:T(8,128)S(1)} %constant_dynamic-slice_fusion.7), channel_id=1, source_target_pairs={{0,2},{1,3},{2,0},{3,1},{4,6},{5,7},{6,4},{7,5},{8,10},{9,11},{10,... | collective-permute-start | bytes 688136 | tf_op jit(solution)/shard_map/ppermute | solution.py:84
  123.4 14.6 %collective-permute-start.28 = (f32[448,128]{1,0:T(8,128)S(1)}, f32[448,128]{1,0:T(8,128)S(1)}, u32[]{:S(2)}, u32[]{:S(2)}) collective-permute-start(f32[448,128]{1,0:T(8,128)S(1)} %constant_dynamic-slice_fusion.3), channel_id=1, source_target_pairs={{0,4},{4,0},{8,12},{12,8},{16,20},{20,16},{24,28},{28,24},{1,5},{5... | collective-permute-start | bytes 688136 | tf_op jit(solution)/shard_map/ppermute | solution.py:84
  128.3 11.6 %collective-permute-start.19 = (f32[224,128]{1,0:T(8,128)S(1)}, f32[224,128]{1,0:T(8,128)S(1)}, u32[]{:S(2)}, u32[]{:S(2)}) collective-permute-start(f32[224,128]{1,0:T(8,128)S(1)} %constant_dynamic-slice_fusion.6), channel_id=1, source_target_pairs={{0,4},{4,0},{8,12},{12,8},{16,20},{20,16},{24,28},{28,24},{1,5},{5... | collective-permute-start | bytes 344072 | tf_op jit(solution)/shard_map/ppermute | solution.py:84
  138.0 4.9 %collective-permute-start.29 = (f32[224,128]{1,0:T(8,128)S(1)}, f32[224,128]{1,0:T(8,128)S(1)}, u32[]{:S(2)}, u32[]{:S(2)}) collective-permute-start(f32[224,128]{1,0:T(8,128)S(1)} %constant_dynamic-slice_fusion.2), channel_id=1, source_target_pairs={{0,8},{4,12},{8,0},{12,4},{16,24},{20,28},{24,16},{28,20},{1,9},{5... | collective-permute-start | bytes 344072 | tf_op jit(solution)/shard_map/ppermute | solution.py:84
  139.9 4.2 %collective-permute-start.20 = (f32[112,128]{1,0:T(8,128)S(1)}, f32[112,128]{1,0:T(8,128)S(1)}, u32[]{:S(2)}, u32[]{:S(2)}) collective-permute-start(f32[112,128]{1,0:T(8,128)S(1)} %constant_dynamic-slice_fusion.5), channel_id=1, source_target_pairs={{0,8},{4,12},{8,0},{12,4},{16,24},{20,28},{24,16},{28,20},{1,9},{5... | collective-permute-start | bytes 172040 | tf_op jit(solution)/shard_map/ppermute | solution.py:84
  142.9 4.9 %collective-permute-start.30 = (f32[112,128]{1,0:T(8,128)S(1)}, f32[112,128]{1,0:T(8,128)S(1)}, u32[]{:S(2)}, u32[]{:S(2)}) collective-permute-start(f32[112,128]{1,0:T(8,128)S(1)} %constant_dynamic-slice_fusion.1), channel_id=1, source_target_pairs={{0,2},{1,3},{2,0},{3,1},{4,6},{5,7},{6,4},{7,5},{8,10},{9,11},{10,... | collective-permute-start | bytes 172040 | tf_op jit(solution)/shard_map/ppermute | solution.py:84
  144.2 6.8 %collective-permute-start.21 = (f32[56,128]{1,0:T(8,128)S(1)}, f32[56,128]{1,0:T(8,128)S(1)}, u32[]{:S(2)}, u32[]{:S(2)}) collective-permute-start(f32[56,128]{1,0:T(8,128)S(1)} %constant_dynamic-slice_fusion.4), channel_id=1, source_target_pairs={{0,16},{4,20},{8,24},{12,28},{16,0},{20,4},{24,8},{28,12},{1,17},{... | collective-permute-start | bytes 86024 | tf_op jit(solution)/shard_map/ppermute | solution.py:84
  147.8 5.2 %collective-permute-start.31 = (f32[56,128]{1,0:T(8,128)S(1)}, f32[56,128]{1,0:T(8,128)S(1)}, u32[]{:S(2)}, u32[]{:S(2)}) collective-permute-start(f32[56,128]{1,0:T(8,128)S(1)} %constant_dynamic-slice_fusion), channel_id=1, source_target_pairs={{0,16},{4,20},{8,24},{12,28},{16,0},{20,4},{24,8},{28,12},{1,17},{... | collective-permute-start | bytes 86024 | tf_op jit(solution)/shard_map/ppermute | solution.py:84
  151.0 6.7 %collective-permute-start.22 = (f32[56,128]{1,0:T(8,128)S(1)}, f32[56,128]{1,0:T(8,128)S(1)}, u32[]{:S(2)}, u32[]{:S(2)}) collective-permute-start(f32[56,128]{1,0:T(8,128)S(1)} %get-tuple-element.15), channel_id=1, source_target_pairs={{0,16},{4,20},{8,24},{12,28},{16,0},{20,4},{24,8},{28,12},{1,17},{... | collective-permute-start | bytes 86024 | tf_op jit(solution)/shard_map/ppermute | solution.py:84
  152.9 6.5 %collective-permute-start.32 = (f32[56,128]{1,0:T(8,128)S(1)}, f32[56,128]{1,0:T(8,128)S(1)}, u32[]{:S(2)}, u32[]{:S(2)}) collective-permute-start(f32[56,128]{1,0:T(8,128)S(1)} %get-tuple-element.19), channel_id=1, source_target_pairs={{0,16},{4,20},{8,24},{12,28},{16,0},{20,4},{24,8},{28,12},{1,17},{... | collective-permute-start | bytes 86024 | tf_op jit(solution)/shard_map/ppermute | solution.py:84
  156.0 0.9 copy-start.4
  157.7 4.2 %collective-permute-start.23 = (f32[112,128]{1,0:T(8,128)S(1)}, f32[112,128]{1,0:T(8,128)S(1)}, u32[]{:S(2)}, u32[]{:S(2)}) collective-permute-start(f32[112,128]{1,0:T(8,128)S(1)} %constant_dynamic-update-slice_fusion.18), channel_id=1, source_target_pairs={{0,8},{4,12},{8,0},{12,4},{16,24},{20,28},{24,16},{28,20},{1,9},{5... | collective-permute-start | bytes 172040 | tf_op jit(solution)/shard_map/ppermute | solution.py:84
  159.5 4.9 %collective-permute-start.33 = (f32[112,128]{1,0:T(8,128)S(1)}, f32[112,128]{1,0:T(8,128)S(1)}, u32[]{:S(2)}, u32[]{:S(2)}) collective-permute-start(f32[112,128]{1,0:T(8,128)S(1)} %constant_dynamic-update-slice_fusion.8), channel_id=1, source_target_pairs={{0,2},{1,3},{2,0},{3,1},{4,6},{5,7},{6,4},{7,5},{8,10},{9,11},{10,... | collective-permute-start | bytes 172040 | tf_op jit(solution)/shard_map/ppermute | solution.py:84
  162.0 4.9 %collective-permute-start.24 = (f32[224,128]{1,0:T(8,128)S(1)}, f32[224,128]{1,0:T(8,128)S(1)}, u32[]{:S(2)}, u32[]{:S(2)}) collective-permute-start(f32[224,128]{1,0:T(8,128)S(1)} %constant_dynamic-update-slice_fusion.16), channel_id=1, source_target_pairs={{0,4},{4,0},{8,12},{12,8},{16,20},{20,16},{24,28},{28,24},{1,5},{5... | collective-permute-start | bytes 344072 | tf_op jit(solution)/shard_map/ppermute | solution.py:84
  164.4 4.9 %collective-permute-start.34 = (f32[224,128]{1,0:T(8,128)S(1)}, f32[224,128]{1,0:T(8,128)S(1)}, u32[]{:S(2)}, u32[]{:S(2)}) collective-permute-start(f32[224,128]{1,0:T(8,128)S(1)} %constant_dynamic-update-slice_fusion.6), channel_id=1, source_target_pairs={{0,8},{4,12},{8,0},{12,4},{16,24},{20,28},{24,16},{28,20},{1,9},{5... | collective-permute-start | bytes 344072 | tf_op jit(solution)/shard_map/ppermute | solution.py:84
  166.9 6.1 %collective-permute-start.25 = (f32[448,128]{1,0:T(8,128)S(1)}, f32[448,128]{1,0:T(8,128)S(1)}, u32[]{:S(2)}, u32[]{:S(2)}) collective-permute-start(f32[448,128]{1,0:T(8,128)S(1)} %constant_dynamic-update-slice_fusion.14), channel_id=1, source_target_pairs={{0,2},{1,3},{2,0},{3,1},{4,6},{5,7},{6,4},{7,5},{8,10},{9,11},{10,... | collective-permute-start | bytes 688136 | tf_op jit(solution)/shard_map/ppermute | solution.py:84
  169.2 6.1 %collective-permute-start.35 = (f32[448,128]{1,0:T(8,128)S(1)}, f32[448,128]{1,0:T(8,128)S(1)}, u32[]{:S(2)}, u32[]{:S(2)}) collective-permute-start(f32[448,128]{1,0:T(8,128)S(1)} %constant_dynamic-update-slice_fusion.4), channel_id=1, source_target_pairs={{0,4},{4,0},{8,12},{12,8},{16,20},{20,16},{24,28},{28,24},{1,5},{5... | collective-permute-start | bytes 688136 | tf_op jit(solution)/shard_map/ppermute | solution.py:84
  173.0 11.5 %collective-permute-start.26 = (f32[896,128]{1,0:T(8,128)S(1)}, f32[896,128]{1,0:T(8,128)S(1)}, u32[]{:S(2)}, u32[]{:S(2)}) collective-permute-start(f32[896,128]{1,0:T(8,128)S(1)} %constant_dynamic-update-slice_fusion.12), channel_id=1, source_target_pairs={{0,1},{1,0},{2,3},{3,2},{4,5},{5,4},{6,7},{7,6},{8,9},{9,8},{10,11... | collective-permute-start | bytes 1376264 | tf_op jit(solution)/shard_map/ppermute | solution.py:84
  175.3 9.2 %collective-permute-start.36 = (f32[896,128]{1,0:T(8,128)S(1)}, f32[896,128]{1,0:T(8,128)S(1)}, u32[]{:S(2)}, u32[]{:S(2)}) collective-permute-start(f32[896,128]{1,0:T(8,128)S(1)} %constant_dynamic-update-slice_fusion.2), channel_id=1, source_target_pairs={{0,1},{1,0},{2,3},{3,2},{4,5},{5,4},{6,7},{7,6},{8,9},{9,8},{10,11... | collective-permute-start | bytes 1376264 | tf_op jit(solution)/shard_map/ppermute | solution.py:84
